TPU v7x, 32 devices: a whole 2x2x4 slice. The times are simulated.
32 devices in a mesh: row: 4 (over y, core), col: 8 (over z, x).
Axes of the slice: x: 2, y: 2, z: 4, core: 2. Of those that a mesh axis runs over, the one named last changes fastest.
Arguments:
- block_x: float32 [64, 24576], P(None, ('row', 'col')), may hold values from -6 to 6
- block_p: float32 [64, 24576], P(None, ('row', 'col')), may hold values from -6 to 6
- tile_rows: int32 [4, 8, 576], P('row', 'col'), may hold values from 0 to 47, as said below
- tile_cols: int32 [4, 8, 576], P('row', 'col'), may hold values from 0 to 23, as said below
- tile_count: int32 [4, 8], P('row', 'col'), may hold values from 1 to 576, as said below
- tile_vals: bfloat16 [4, 8, 576, 128, 128], P('row', 'col'), may hold values from -0.125 to 0.125
Outputs:
- residual: float32 [64, 24576], P(None, ('row', 'col'))
- image_r: float32 [64, 24576], P(None, ('row', 'col'))
- gram_a: float32 [192, 192], replicated
- gram_b: float32 [192, 192], replicated
Inputs may be any that keep to these rules, and one draw needn't show every extreme that they name: `tile_rows`: within one grid cell the live slots name distinct tiles, all with i <= j; slots at and beyond the cell's count are ignored. `tile_cols`: paired with tile_rows slot by slot. `tile_count`: some grid cell is full in every draw.
All inputs are finite; a program needn't handle non-finite values.
Results may differ from a plain program's by a relative error of at most 0.0035.
Values may be sent and summed in bfloat16 or wider, within the bound.
No kernel may reach another device: no remote copies, remote signals or barrier semaphores. Data moves between devices by JAX's collectives and lax.ppermute only.
A program may use at most 128 MiB of HBM per device.

v0:
```python
import math

import jax
import jax.numpy as jnp
from jax import lax
from jax.sharding import PartitionSpec as P


def apply_graph(vectors, tile_rows, tile_cols, live_count, tile_vals):
    vec_width = vectors.shape[0]
    tile_size = tile_vals.shape[-1]
    row_range = lax.all_gather(vectors, "col", axis=1, tiled=True)
    col_group = lax.all_gather(vectors, "row", axis=1, tiled=True)
    row_blocks = row_range.reshape(vec_width, -1, tile_size)
    col_blocks = col_group.reshape(vec_width, -1, tile_size)
    group_size = math.gcd(tile_vals.shape[0], 64)
    offsets = jnp.arange(group_size, dtype=jnp.int32)
    turn_count = (live_count + group_size - 1) // group_size

    def slot_group(turn_index):
        first_slot = turn_index * group_size
        row_index = lax.dynamic_slice_in_dim(tile_rows, first_slot, group_size)
        col_index = lax.dynamic_slice_in_dim(tile_cols, first_slot, group_size)
        values = lax.dynamic_slice_in_dim(tile_vals, first_slot, group_size, 0)
        live_slots = first_slot + offsets < live_count
        return (row_index, col_index, values, live_slots)

    def turn(turn_index, totals):
        row_totals, col_totals = totals
        row_index, col_index, values, live_slots = slot_group(turn_index)
        values = jnp.where(live_slots[:, None, None], values, jnp.zeros_like(values))
        col_inputs = jnp.take(col_blocks, col_index, axis=1)
        row_inputs = jnp.take(row_blocks, row_index, axis=1)
        forward = jnp.einsum("wgb,gab->wga", col_inputs, values, preferred_element_type=jnp.float32)
        backward = jnp.einsum(
            "wga,gab->wgb", row_inputs, values, preferred_element_type=jnp.float32
        )
        return (row_totals.at[:, row_index].add(forward), col_totals.at[:, col_index].add(backward))

    start_rows = jnp.zeros(row_blocks.shape, jnp.float32)
    start_cols = jnp.zeros(col_blocks.shape, jnp.float32)
    row_totals, col_totals = lax.fori_loop(0, turn_count, turn, (start_rows, start_cols))
    own_rows = lax.psum_scatter(
        row_totals.reshape(vec_width, -1), "col", scatter_dimension=1, tiled=True
    )
    own_cols = lax.psum_scatter(
        col_totals.reshape(vec_width, -1), "row", scatter_dimension=1, tiled=True
    )
    return own_rows + own_cols


def per_device(block_x, block_p, tile_rows, tile_cols, tile_count, tile_vals):
    highest = lax.Precision.HIGHEST
    width_k = block_x.shape[0]
    node_count = block_x.shape[1] * lax.axis_size("row") * lax.axis_size("col")
    slot_rows = tile_rows[0, 0]
    slot_cols = tile_cols[0, 0]
    live_count = tile_count[0, 0]
    slot_vals = tile_vals[0, 0]

    def product(left, right):
        return (
            jnp.dot(left, right.T, precision=highest, preferred_element_type=jnp.float32)
            / node_count
        )

    gram_x = lax.psum(product(block_x, block_x), ("row", "col"))
    cholesky_factor = jnp.linalg.cholesky(gram_x)
    orthonormal = lax.linalg.triangular_solve(cholesky_factor, block_x, left_side=True, lower=True)
    ortho_low = orthonormal.astype(jnp.bfloat16)
    dir_low = block_p.astype(jnp.bfloat16)
    both_images = apply_graph(
        jnp.concatenate([ortho_low, dir_low], axis=0), slot_rows, slot_cols, live_count, slot_vals
    )
    image_x = both_images[:width_k]
    image_p = both_images[width_k:]
    rayleigh = lax.psum(product(orthonormal, image_x), ("row", "col"))
    residual = image_x - jnp.dot(
        rayleigh.T, orthonormal, precision=highest, preferred_element_type=jnp.float32
    )
    residual_low = residual.astype(jnp.bfloat16)
    image_r = apply_graph(residual_low, slot_rows, slot_cols, live_count, slot_vals)
    basis = jnp.concatenate([orthonormal, residual, block_p], axis=0)
    images = jnp.concatenate([image_x, image_r, image_p], axis=0)
    gram_a, gram_b = lax.psum((product(basis, images), product(basis, basis)), ("row", "col"))
    return (residual, image_r, gram_a, gram_b)


def solution(mesh):
    in_specs = (
        P(None, ("row", "col")),
        P(None, ("row", "col")),
        P("row", "col", None),
        P("row", "col", None),
        P("row", "col"),
        P("row", "col", None, None, None),
    )
    out_specs = (P(None, ("row", "col")), P(None, ("row", "col")), P(), P())
    return jax.shard_map(
        per_device, mesh=mesh, in_specs=in_specs, out_specs=out_specs, check_vma=False
    )
```

profile of v0, /device:TPU:0, one launch (start us, length us, event | category | flops | bytes accessed | tf_op | source)
XLA Modules:
  0.0 1113.2 jit_solution(1400629160734229322)
XLA Ops:
  8.4 42.2 %psum.28 = f32[64,64]{0,1:T(8,128)S(1)} all-reduce(f32[64,64]{0,1:T(8,128)S(1)} %convolution_multiply_fusion.3), channel_id=1, replica_groups=mesh['row'=4,'col'=8] {'row','col'}, use_global_device_ids=true, to_apply=%region_0.0 | all-reduce | flops 4096 | bytes 32768 | tf_op jit(solution)/shard_map/psum | solution.py:67
  50.7 5.8 cholesky.16
  57.9 4.9 custom-call.6
  65.7 9.6 all_gather.12
  75.5 33.8 %all-gather.2.cloned.1.call-done = bf16[128,6144]{1,0:T(8,128)(2,1)} async-done(((bf16[128,768]{1,0:T(8,128)(2,1)}), bf16[128,6144]{1,0:T(8,128)(2,1)}) %all-gather.2.cloned.1.call-update) | async-done | bytes 1572880 | tf_op jit(solution)/shard_map/all_gather | solution.py:12
  114.6 317.1 %while.26 = (s32[]{:T(128)}, f32[128,48,128]{2,0,1:T(8,128)}, f32[128,24,128]{2,0,1:T(8,128)S(1)}, s32[]{:T(128)}, s32[576]{0:T(1024)S(1)}, /*index=5*/s32[]{:T(...) while((s32[]{:T(128)}, f32[128,48,128]{2,0,1:T(8,128)}, ...), condition=%wide.region_6.7_spmd.clone, body=%wide.region_3.6_spmd.clone.sunk | while | flops 543165312 | bytes 50343056 | solution.py:42
  117.5 5.8 fusion.80
  123.4 13.6 %scatter_fusion = f32[128,48,128]{2,0,1:T(8,128)} fusion(f32[128,48,128]{2,0,1:T(8,128)} %get-tuple-element.407, s32[64]{0:T(128)S(1)} %get-tuple-element.374, f32[64,128,128]{2,1,0:T(8,128)} %fusion.80), kind=kCustom, calls=%fused_computation.4.clone.clone.1 | custom fusion | flops 1048576 | bytes 12583168 | tf_op jit(solution)/shard_map/while/body/scatter-add | solution.py:38
  140.5 4.9 fusion.81
  145.5 8.8 scatter_fusion.1
  157.2 5.8 fusion.80
  163.1 13.5 %scatter_fusion = f32[128,48,128]{2,0,1:T(8,128)} fusion(f32[128,48,128]{2,0,1:T(8,128)} %get-tuple-element.407, s32[64]{0:T(128)S(1)} %get-tuple-element.374, f32[64,128,128]{2,1,0:T(8,128)} %fusion.80), kind=kCustom, calls=%fused_computation.4.clone.clone.1 | custom fusion | flops 1048576 | bytes 12583168 | tf_op jit(solution)/shard_map/while/body/scatter-add | solution.py:38
  180.1 4.9 fusion.81
  185.1 8.8 scatter_fusion.1
  196.8 5.8 fusion.80
  202.6 13.5 %scatter_fusion = f32[128,48,128]{2,0,1:T(8,128)} fusion(f32[128,48,128]{2,0,1:T(8,128)} %get-tuple-element.407, s32[64]{0:T(128)S(1)} %get-tuple-element.374, f32[64,128,128]{2,1,0:T(8,128)} %fusion.80), kind=kCustom, calls=%fused_computation.4.clone.clone.1 | custom fusion | flops 1048576 | bytes 12583168 | tf_op jit(solution)/shard_map/while/body/scatter-add | solution.py:38
  219.8 4.9 fusion.81
  224.7 8.8 scatter_fusion.1
  236.5 5.8 fusion.80
  242.3 13.6 %scatter_fusion = f32[128,48,128]{2,0,1:T(8,128)} fusion(f32[128,48,128]{2,0,1:T(8,128)} %get-tuple-element.407, s32[64]{0:T(128)S(1)} %get-tuple-element.374, f32[64,128,128]{2,1,0:T(8,128)} %fusion.80), kind=kCustom, calls=%fused_computation.4.clone.clone.1 | custom fusion | flops 1048576 | bytes 12583168 | tf_op jit(solution)/shard_map/while/body/scatter-add | solution.py:38
  259.5 4.9 fusion.81
  264.4 8.8 scatter_fusion.1
  276.2 5.8 fusion.80
  282.0 13.5 %scatter_fusion = f32[128,48,128]{2,0,1:T(8,128)} fusion(f32[128,48,128]{2,0,1:T(8,128)} %get-tuple-element.407, s32[64]{0:T(128)S(1)} %get-tuple-element.374, f32[64,128,128]{2,1,0:T(8,128)} %fusion.80), kind=kCustom, calls=%fused_computation.4.clone.clone.1 | custom fusion | flops 1048576 | bytes 12583168 | tf_op jit(solution)/shard_map/while/body/scatter-add | solution.py:38
  299.1 4.9 fusion.81
  304.1 8.8 scatter_fusion.1
  315.8 5.8 fusion.80
  321.6 13.5 %scatter_fusion = f32[128,48,128]{2,0,1:T(8,128)} fusion(f32[128,48,128]{2,0,1:T(8,128)} %get-tuple-element.407, s32[64]{0:T(128)S(1)} %get-tuple-element.374, f32[64,128,128]{2,1,0:T(8,128)} %fusion.80), kind=kCustom, calls=%fused_computation.4.clone.clone.1 | custom fusion | flops 1048576 | bytes 12583168 | tf_op jit(solution)/shard_map/while/body/scatter-add | solution.py:38
  338.8 4.9 fusion.81
  343.7 8.8 scatter_fusion.1
  355.5 5.8 fusion.80
  361.3 13.5 %scatter_fusion = f32[128,48,128]{2,0,1:T(8,128)} fusion(f32[128,48,128]{2,0,1:T(8,128)} %get-tuple-element.407, s32[64]{0:T(128)S(1)} %get-tuple-element.374, f32[64,128,128]{2,1,0:T(8,128)} %fusion.80), kind=kCustom, calls=%fused_computation.4.clone.clone.1 | custom fusion | flops 1048576 | bytes 12583168 | tf_op jit(solution)/shard_map/while/body/scatter-add | solution.py:38
  378.4 4.9 fusion.81
  383.3 8.8 scatter_fusion.1
  395.1 5.8 fusion.80
  400.9 13.5 %scatter_fusion = f32[128,48,128]{2,0,1:T(8,128)} fusion(f32[128,48,128]{2,0,1:T(8,128)} %get-tuple-element.407, s32[64]{0:T(128)S(1)} %get-tuple-element.374, f32[64,128,128]{2,1,0:T(8,128)} %fusion.80), kind=kCustom, calls=%fused_computation.4.clone.clone.1 | custom fusion | flops 1048576 | bytes 12583168 | tf_op jit(solution)/shard_map/while/body/scatter-add | solution.py:38
  418.0 4.9 fusion.81
  422.9 8.8 scatter_fusion.1
  433.2 3.9 copy_bitcast_fusion
  437.1 61.4 %reduce-scatter.7.cloned.1.call-done = f32[128,768]{1,0:T(8,128)} async-done(((f32[128,3072]{1,0:T(8,128)}), f32[128,768]{1,0:T(8,128)}) %reduce-scatter.7.cloned.1.call-update) | async-done | bytes 393232 | tf_op jit(solution)/shard_map/reduce_scatter | solution.py:46
  498.5 78.4 %reduce-scatter.5.cloned.1.call-done = f32[128,768]{1,0:T(8,128)} async-done(((f32[128,6144]{1,0:T(8,128)}), f32[128,768]{1,0:T(8,128)}) %reduce-scatter.5.cloned.1.call-update) | async-done | bytes 393232 | tf_op jit(solution)/shard_map/reduce_scatter | solution.py:43
  578.4 39.8 %psum.29 = f32[64,64]{0,1:T(8,128)S(1)} all-reduce(f32[64,64]{0,1:T(8,128)S(1)} %convolution_multiply_fusion.2), channel_id=1, replica_groups=mesh['row'=4,'col'=8] {'row','col'}, use_global_device_ids=true, to_apply=%region_9.10 | all-reduce | flops 4096 | bytes 32768 | tf_op jit(solution)/shard_map/psum | solution.py:77
  619.3 7.2 all_gather.14
  626.5 32.1 %all_gather.15 = bf16[64,6144]{1,0:T(8,128)(2,1)S(1)} all-gather(bf16[64,768]{1,0:T(8,128)(2,1)S(1)} %get-tuple-element.250), channel_id=1, replica_groups=mesh['row'=4,'col'=8] {'col'}, dimensions={1}, use_global_device_ids=true | all-gather | bytes 884736 | tf_op jit(solution)/shard_map/all_gather | solution.py:12
  661.2 193.0 %while.27 = (s32[]{:T(128)}, f32[64,48,128]{2,0,1:T(8,128)}, f32[64,24,128]{2,0,1:T(8,128)S(1)}, s32[]{:T(128)}, s32[576]{0:T(1024)S(1)}, /*index=5*/s32[]{:T(12...) while((s32[]{:T(128)}, f32[64,48,128]{2,0,1:T(8,128)}, ...), condition=%wide.region_13.14_spmd.clone, body=%wide.region_10.13_spmd.clone.sunk | while | flops 272632704 | bytes 27274384 | solution.py:42
  667.3 9.0 scatter_fusion.2
  681.8 3.7 scatter_fusion.3
  691.4 9.0 scatter_fusion.2
  705.8 3.7 scatter_fusion.3
  715.5 9.0 scatter_fusion.2
  730.0 3.7 scatter_fusion.3
  739.6 9.0 scatter_fusion.2
  754.1 3.7 scatter_fusion.3
  763.7 9.0 scatter_fusion.2
  778.2 3.7 scatter_fusion.3
  787.9 9.0 scatter_fusion.2
  802.3 3.7 scatter_fusion.3
  812.0 9.0 scatter_fusion.2
  826.4 3.7 scatter_fusion.3
  836.1 9.0 scatter_fusion.2
  850.5 3.7 scatter_fusion.3
  858.8 42.1 %reduce-scatter.11.cloned.1.call-done = f32[64,768]{1,0:T(8,128)} async-done(((f32[64,3072]{1,0:T(8,128)}), f32[64,768]{1,0:T(8,128)}) %reduce-scatter.11.cloned.1.call-update) | async-done | bytes 196624 | tf_op jit(solution)/shard_map/reduce_scatter | solution.py:46
  900.8 68.6 %reduce-scatter.9.cloned.1.call-done = f32[64,768]{1,0:T(8,128)} async-done(((f32[64,6144]{1,0:T(8,128)}), f32[64,768]{1,0:T(8,128)}) %reduce-scatter.9.cloned.1.call-update) | async-done | bytes 196624 | tf_op jit(solution)/shard_map/reduce_scatter | solution.py:43
  971.9 131.3 %all-reduce.3.cloned.1.call-done = (f32[192,192]{1,0:T(8,128)}, f32[192,192]{1,0:T(8,128)}) async-done(((f32[192,192]{1,0:T(8,128)}, f32[192,192]{1,0:T(8,128)}), (f32[192,192]{1,0:T(8,128)}, f32[192,192]{1,0:T(8,128)})) %all-reduce.3.cloned.1.call-update) | async-done | bytes 294928 | tf_op jit(solution)/shard_map/psum | solution.py:85
  (177 shorter events, 170.0 us)
Async XLA Ops:
  7.2 0.9 copy-start
  7.2 58.4 %copy-start.9 = (s32[1,1,576]{2,1,0:T(1,128)S(1)}, s32[1,1,576]{2,1,0:T(1,128)}, u32[]{:S(2)}) copy-start(s32[1,1,576]{2,1,0:T(1,128)} %param.12) | copy-start | bytes 6916
  7.2 58.5 %copy-start.10 = (s32[1,1,576]{2,1,0:T(1,128)S(1)}, s32[1,1,576]{2,1,0:T(1,128)}, u32[]{:S(2)}) copy-start(s32[1,1,576]{2,1,0:T(1,128)} %param.13) | copy-start | bytes 6916
  7.2 102.1 %all-gather.2.cloned.1.call-start = ((), (), s32[]{:S(2)}) async-start(), calls=%async_computation.4 | async-start | bytes 1769472 | tf_op jit(solution)/shard_map/all_gather | solution.py:12
  63.2 555.1 %copy-start.4 = (f32[64,768]{1,0:T(8,128)}, f32[64,768]{1,0:T(8,128)S(1)}, u32[]{:S(2)}) copy-start(f32[64,768]{1,0:T(8,128)S(1)} %get-tuple-element.249) | copy-start | bytes 589828
  64.9 433.6 %reduce-scatter.7.cloned.1.call-start = ((), (), s32[]{:S(2)}) async-start(), calls=%async_computation.6 | async-start | bytes 1966080 | tf_op jit(solution)/shard_map/reduce_scatter | solution.py:46
  433.1 143.8 %reduce-scatter.5.cloned.1.call-start = ((), (), s32[]{:S(2)}) async-start(), calls=%async_computation.5 | async-start | bytes 3538944 | tf_op jit(solution)/shard_map/reduce_scatter | solution.py:43
  437.1 463.8 %reduce-scatter.11.cloned.1.call-start = ((), (), s32[]{:S(2)}) async-start(), calls=%async_computation.8 | async-start | bytes 983040 | tf_op jit(solution)/shard_map/reduce_scatter | solution.py:46
  578.1 81.7 %copy-start.2 = (f32[128,768]{1,0:T(8,128)}, f32[128,768]{1,0:T(8,128)S(1)}, u32[]{:S(2)}) copy-start(f32[128,768]{1,0:T(8,128)S(1)} %add.116) | copy-start | bytes 1179652
  854.2 1.7 copy-start.1
  855.2 114.2 %reduce-scatter.9.cloned.1.call-start = ((), (), s32[]{:S(2)}) async-start(), calls=%async_computation.7 | async-start | bytes 1769472 | tf_op jit(solution)/shard_map/reduce_scatter | solution.py:43
  855.9 1.3 copy-start.5
  855.9 1.4 copy-start.6
  855.9 1.5 copy-start.7
  855.9 2.8 copy-start.3
  857.2 245.9 %all-reduce.3.cloned.1.call-start = ((), (), s32[]{:S(2)}) async-start(), calls=%async_computation.9 | async-start | bytes 786432 | tf_op jit(solution)/shard_map/psum | solution.py:85
  970.5 135.9 %copy-start.8 = (f32[64,768]{1,0:T(8,128)}, f32[64,768]{1,0:T(8,128)S(1)}, u32[]{:S(2)}) copy-start(f32[64,768]{1,0:T(8,128)S(1)} %add.117) | copy-start | bytes 589828
Sparse Core Ops, SparseCore 0:
  65.0 44.2 all-gather.1
  433.3 65.2 reduce-scatter.6
  502.6 74.3 reduce-scatter.4
  855.3 45.4 reduce-scatter.10
  904.1 65.2 reduce-scatter.8
  976.3 126.8 all-reduce.2
where the time goes:
time: 1120 us; the launch traced here: 1110 us
  waiting for transfers between devices  416 us (37%)
  other arithmetic  308 us (28%)
  matrix products  140 us (12%)
  blocking collectives  131 us (12%)
  local copies, waits for them, and re-layouts  102 us (9%)
  between operations  15 us (1%)
    scatter-add x16, other arithmetic, turn(): row_totals.at[:, row_index].add(forward)  180 us
    reduce_scatter x2, waiting for transfers between devices, apply_graph(): lax.psum_scatter(row_totals.reshape(vec_width, -1), 'col', scatter_dimens...  147 us
    psum x1, waiting for transfers between devices, per_device(): lax.psum((product(basis, images), product(basis, basis)), ('row', 'col'))  131 us
    reduce_scatter x2, waiting for transfers between devices, apply_graph(): lax.psum_scatter(col_totals.reshape(vec_width, -1), 'row', scatter_dimens...  103 us
    scatter-add x16, other arithmetic, turn(): col_totals.at[:, col_index].add(backward)  100 us
    dot_general x16, matrix products, turn(): jnp.einsum('wgb,gab->wga', col_inputs, values, preferred_element_type=jnp...  74.4 us
    dot_general x16, matrix products, turn(): jnp.einsum('wga,gab->wgb', row_inputs, values, preferred_element_type=jnp...  60.7 us
    gather x16, local copies, waits for them, and re-layouts, turn(): row_inputs = jnp.take(row_blocks, row_index, axis=1)  51 us
  transfers between devices with their start and end apart: 6, of which 6 were waited for; matrix products, arithmetic and copies ran while one was open for 1% of the time, Pallas kernels for 0%

commit v1 on v0

v1 whole, which is shorter than its diff:
```python
import functools

import jax
import jax.numpy as jnp
from jax import lax
from jax.experimental import pallas as pl
from jax.experimental.pallas import tpu as pltpu
from jax.sharding import PartitionSpec as P

GROUP = 64


def tile_kernel(rows_ref, cols_ref, cnt_ref, vals_ref, rin_ref, cin_ref, rout_ref, cout_ref):
    g = pl.program_id(0)
    group = vals_ref.shape[0]

    @pl.when(g == 0)
    def _():
        rout_ref[...] = jnp.zeros_like(rout_ref)
        cout_ref[...] = jnp.zeros_like(cout_ref)

    base = g * group
    live = cnt_ref[0]

    def body(t, carry):
        slot = base + t

        @pl.when(slot < live)
        def _():
            a = rows_ref[slot]
            b = cols_ref[slot]
            v = vals_ref[t]
            fwd = lax.dot_general(
                cin_ref[b], v, (((1,), (1,)), ((), ())), preferred_element_type=jnp.float32
            )
            bwd = jnp.dot(rin_ref[a], v, preferred_element_type=jnp.float32)
            rout_ref[a] += fwd
            cout_ref[b] += bwd

        return carry

    lax.fori_loop(0, group, body, 0)


def tile_products(row_blocks, col_blocks, tile_rows, tile_cols, live_count, tile_vals):
    n_rows, width, tile = row_blocks.shape
    n_cols = col_blocks.shape[0]
    slots = tile_vals.shape[0]
    group = GROUP if slots % GROUP == 0 else slots
    steps = slots // group

    def vals_map(g, rows, cols, cnt):
        last = jnp.maximum(cnt[0] - 1, 0) // group
        return (jnp.minimum(g, last), 0, 0)

    grid_spec = pltpu.PrefetchScalarGridSpec(
        num_scalar_prefetch=3,
        grid=(steps,),
        in_specs=[
            pl.BlockSpec((group, tile, tile), vals_map),
            pl.BlockSpec((n_rows, width, tile), lambda g, r, c, n: (0, 0, 0)),
            pl.BlockSpec((n_cols, width, tile), lambda g, r, c, n: (0, 0, 0)),
        ],
        out_specs=[
            pl.BlockSpec((n_rows, width, tile), lambda g, r, c, n: (0, 0, 0)),
            pl.BlockSpec((n_cols, width, tile), lambda g, r, c, n: (0, 0, 0)),
        ],
    )
    flops = 4 * slots * width * tile * tile
    bytes_accessed = (
        tile_vals.size * 2 + (row_blocks.size + col_blocks.size) * 2
        + (row_blocks.size + col_blocks.size) * 4
    )
    return pl.pallas_call(
        tile_kernel,
        grid_spec=grid_spec,
        out_shape=[
            jax.ShapeDtypeStruct((n_rows, width, tile), jnp.float32),
            jax.ShapeDtypeStruct((n_cols, width, tile), jnp.float32),
        ],
        compiler_params=pltpu.CompilerParams(
            dimension_semantics=("arbitrary",), vmem_limit_bytes=48 * 1024 * 1024
        ),
        cost_estimate=pl.CostEstimate(
            flops=flops, bytes_accessed=bytes_accessed, transcendentals=0
        ),
    )(tile_rows, tile_cols, live_count.reshape(1), tile_vals, row_blocks, col_blocks)


def apply_graph(vectors, tile_rows, tile_cols, live_count, tile_vals):
    vec_width, local_nodes = vectors.shape
    tile = tile_vals.shape[-1]
    local = vectors.reshape(vec_width, local_nodes // tile, tile).transpose(1, 0, 2)
    row_blocks = lax.all_gather(local, "col", axis=0, tiled=True)
    col_blocks = lax.all_gather(local, "row", axis=0, tiled=True)
    row_totals, col_totals = tile_products(
        row_blocks, col_blocks, tile_rows, tile_cols, live_count, tile_vals
    )
    own_rows = lax.psum_scatter(row_totals, "col", scatter_dimension=0, tiled=True)
    own_cols = lax.psum_scatter(col_totals, "row", scatter_dimension=0, tiled=True)
    return (own_rows + own_cols).transpose(1, 0, 2).reshape(vec_width, local_nodes)


def per_device(block_x, block_p, tile_rows, tile_cols, tile_count, tile_vals):
    highest = lax.Precision.HIGHEST
    width_k = block_x.shape[0]
    node_count = block_x.shape[1] * lax.axis_size("row") * lax.axis_size("col")
    slot_rows = tile_rows[0, 0]
    slot_cols = tile_cols[0, 0]
    live_count = tile_count[0, 0]
    slot_vals = tile_vals[0, 0]

    def product(left, right):
        return (
            jnp.dot(left, right.T, precision=highest, preferred_element_type=jnp.float32)
            / node_count
        )

    gram_x = lax.psum(product(block_x, block_x), ("row", "col"))
    cholesky_factor = jnp.linalg.cholesky(gram_x)
    orthonormal = lax.linalg.triangular_solve(cholesky_factor, block_x, left_side=True, lower=True)
    ortho_low = orthonormal.astype(jnp.bfloat16)
    dir_low = block_p.astype(jnp.bfloat16)
    both_images = apply_graph(
        jnp.concatenate([ortho_low, dir_low], axis=0), slot_rows, slot_cols, live_count, slot_vals
    )
    image_x = both_images[:width_k]
    image_p = both_images[width_k:]
    rayleigh = lax.psum(product(orthonormal, image_x), ("row", "col"))
    residual = image_x - jnp.dot(
        rayleigh.T, orthonormal, precision=highest, preferred_element_type=jnp.float32
    )
    residual_low = residual.astype(jnp.bfloat16)
    image_r = apply_graph(residual_low, slot_rows, slot_cols, live_count, slot_vals)
    basis = jnp.concatenate([orthonormal, residual, block_p], axis=0)
    images = jnp.concatenate([image_x, image_r, image_p], axis=0)
    gram_a, gram_b = lax.psum((product(basis, images), product(basis, basis)), ("row", "col"))
    return (residual, image_r, gram_a, gram_b)


def solution(mesh):
    in_specs = (
        P(None, ("row", "col")),
        P(None, ("row", "col")),
        P("row", "col", None),
        P("row", "col", None),
        P("row", "col"),
        P("row", "col", None, None, None),
    )
    out_specs = (P(None, ("row", "col")), P(None, ("row", "col")), P(), P())
    return jax.shard_map(
        per_device, mesh=mesh, in_specs=in_specs, out_specs=out_specs, check_vma=False
    )
```

time: 1120 us -> 723 us (0.65)
  other arithmetic: 308 us -> 15.3 us
  Pallas kernels: 0 us -> 189 us
  matrix products: 140 us -> 3.97 us
  local copies, waits for them, and re-layouts: 102 us -> 7.05 us
  waiting for transfers between devices: 416 us -> 362 us
    scatter-add x32 -> x0, other arithmetic: 280 us -> none  [the longest x16 180 us: turn(): row_totals.at[:, row_index].add(forward)]
    pallas_call x0 -> x2, Pallas kernels: none -> 189 us  [tile_products(): pl.pallas_call(tile_kernel, grid_spec=grid_spec, out_shape=[jax.ShapeDtyp...]
    dot_general x32 -> x0, matrix products: 135 us -> none  [the longest x16 74.4 us: turn(): jnp.einsum('wgb,gab->wga', col_inputs, values, preferred_element_type=jnp...]
    gather x32 -> x0, local copies, waits for them, and re-layouts: 81.8 us -> none  [the longest x16 51 us: turn(): row_inputs = jnp.take(row_blocks, row_index, axis=1)]
    reduce_scatter x4, waiting for transfers between devices: 250 us -> 196 us  [the longest x2 147 us: apply_graph(): lax.psum_scatter(row_totals, 'col', scatter_dimension=0, tiled=True)]
  transfers between devices with their start and end apart: 6 -> 6, of which waited for: 6 -> 6; matrix products, arithmetic and copies ran while one was open for 1% -> 0% of each run, Pallas kernels for 0% -> 0%
where the time goes in v1:
time: 723 us
  waiting for transfers between devices  362 us (50%)
  Pallas kernels  189 us (26%)
  blocking collectives  131 us (18%)
  other arithmetic  15.3 us (2%)
  between operations  15 us (2%)
    pallas_call x2, Pallas kernels, tile_products(): pl.pallas_call(tile_kernel, grid_spec=grid_spec, out_shape=[jax.ShapeDtyp...  189 us
    reduce_scatter x2, waiting for transfers between devices, apply_graph(): lax.psum_scatter(row_totals, 'col', scatter_dimension=0, tiled=True)  147 us
    psum x1, waiting for transfers between devices, per_device(): lax.psum((product(basis, images), product(basis, basis)), ('row', 'col'))  131 us
    reduce_scatter x2, waiting for transfers between devices, apply_graph(): lax.psum_scatter(col_totals, 'row', scatter_dimension=0, tiled=True)  49.2 us
    psum x1, blocking collectives, per_device(): gram_x = lax.psum(product(block_x, block_x), ('row', 'col'))  42.2 us
    psum x1, blocking collectives, per_device(): rayleigh = lax.psum(product(orthonormal, image_x), ('row', 'col'))  39.9 us
    all_gather x1, waiting for transfers between devices, apply_graph(): row_blocks = lax.all_gather(local, 'col', axis=0, tiled=True)  33.8 us
    all_gather x1, blocking collectives, apply_graph(): row_blocks = lax.all_gather(local, 'col', axis=0, tiled=True)  32.2 us
  transfers between devices with their start and end apart: 6, of which 6 were waited for; matrix products, arithmetic and copies ran while one was open for 0% of the time, Pallas kernels for 0%

profile of v1, /device:TPU:0, one launch (start us, length us, event | category | flops | bytes accessed | tf_op | source)
XLA Modules:
  0.0 723.5 jit_solution(12046427706844615295)
XLA Ops:
  7.2 0.0 copy-start
  7.2 0.0 copy-start.5
  7.2 0.0 copy-start.6
  7.2 0.0 all-gather.2.cloned.1.call-start
  7.2 0.9 copy-done
  8.1 0.3 convolution_multiply_fusion.3
  8.4 42.2 %psum.28 = f32[64,64]{0,1:T(8,128)S(1)} all-reduce(f32[64,64]{0,1:T(8,128)S(1)} %convolution_multiply_fusion.3), channel_id=1, replica_groups=mesh['row'=4,'col'=8] {'row','col'}, use_global_device_ids=true, to_apply=%region_0.0 | all-reduce | flops 4096 | bytes 32768 | tf_op jit(solution)/shard_map/psum | solution.py:119
  50.6 0.1 copy.21
  50.7 5.8 cholesky.16
  56.6 0.6 compare_reduce_fusion
  57.2 0.7 fusion.5
  57.9 4.9 custom-call.6
  62.8 1.0 convert_element_type.10
  63.7 0.4 fusion.11
  64.1 0.2 copy.22
  64.3 0.8 copy.23
  65.1 0.0 all-gather.2.cloned.1.call-update
  65.1 0.0 reduce-scatter.7.cloned.1.call-start
  65.8 0.0 copy-done.5
  65.9 0.0 copy-done.6
  65.9 9.6 %all_gather.13.cin_ref = bf16[24,128,128]{2,1,0:T(8,128)(2,1)S(1)} all-gather(bf16[6,128,128]{2,1,0:T(8,128)(2,1)} %copy.23), channel_id=1, replica_groups=mesh['row'=4,'col'=8] {'row'}, dimensions={0}, use_global_device_ids=true | all-gather | bytes 983040 | tf_op jit(solution)/shard_map/all_gather | solution.py:95
  75.5 33.8 %all-gather.2.cloned.1.call-done.rin_ref = bf16[48,128,128]{2,1,0:T(8,128)(2,1)} async-done(((bf16[6,128,128]{2,1,0:T(8,128)(2,1)}), bf16[48,128,128]{2,1,0:T(8,128)(2,1)}) %all-gather.2.cloned.1.call-update) | async-done | bytes 1572880 | tf_op jit(solution)/shard_map/all_gather | solution.py:94
  109.3 0.0 copy-start.1
  109.3 1.4 copy-done.1
  110.7 98.6 %shard_map.93 = (f32[48,128,128]{2,1,0:T(8,128)}, f32[24,128,128]{2,1,0:T(8,128)}) custom-call(s32[576]{0:T(1024)S(1)} %reduce.6.rows_ref, s32[576]{0:T(1024)S(1)} %reduce.7.cols_ref, s32[1]{0:T(128)} %bitcast.42.cnt_ref, bf16[576,128,128]{2,1,0:T(8,128)(2,1)} %bitcast.44, bf16[48,128,128]{2,1,0:T(8,128)(2,1)S(1)} %copy-done.1, ...), custom_call_target="tpu_custom_call" | custom-call | flops 4831838208 | bytes 25952256 | tf_op jit(solution)/shard_map/pallas_call | solution.py:74
  209.3 0.0 reduce-scatter.7.cloned.1.call-update
  209.3 0.0 reduce-scatter.5.cloned.1.call-start
  209.4 0.7 reduce-scatter.5.cloned.1.call-update
  210.1 0.0 reduce-scatter.11.cloned.1.call-start
  210.1 28.8 %reduce-scatter.7.cloned.1.call-done = f32[6,128,128]{2,1,0:T(8,128)} async-done(((f32[24,128,128]{2,1,0:T(8,128)}), f32[6,128,128]{2,1,0:T(8,128)}) %reduce-scatter.7.cloned.1.call-update) | async-done | bytes 393232 | tf_op jit(solution)/shard_map/reduce_scatter | solution.py:100
  238.9 78.5 %reduce-scatter.5.cloned.1.call-done = f32[6,128,128]{2,1,0:T(8,128)} async-done(((f32[48,128,128]{2,1,0:T(8,128)}), f32[6,128,128]{2,1,0:T(8,128)}) %reduce-scatter.5.cloned.1.call-update) | async-done | bytes 393232 | tf_op jit(solution)/shard_map/reduce_scatter | solution.py:99
  317.3 1.2 add_bitcast_fusion
  318.5 0.3 convolution_multiply_fusion.2
  318.9 39.9 %psum.29 = f32[64,64]{0,1:T(8,128)S(1)} all-reduce(f32[64,64]{0,1:T(8,128)S(1)} %convolution_multiply_fusion.2), channel_id=1, replica_groups=mesh['row'=4,'col'=8] {'row','col'}, use_global_device_ids=true, to_apply=%region_5.6 | all-reduce | flops 4096 | bytes 32768 | tf_op jit(solution)/shard_map/psum | solution.py:129
  358.7 0.3 fusion.12
  359.0 0.0 copy-start.3
  359.1 0.1 reshape.30
  359.2 7.3 %all_gather.15.cin_ref = bf16[24,64,128]{2,1,0:T(8,128)(2,1)S(1)} all-gather(bf16[6,64,128]{2,1,0:T(8,128)(2,1)S(1)} %copy.27), channel_id=1, replica_groups=mesh['row'=4,'col'=8] {'row'}, dimensions={0}, use_global_device_ids=true | all-gather | bytes 491520 | tf_op jit(solution)/shard_map/all_gather | solution.py:95
  366.5 32.2 %all_gather.14.rin_ref = bf16[48,64,128]{2,1,0:T(8,128)(2,1)S(1)} all-gather(bf16[6,64,128]{2,1,0:T(8,128)(2,1)S(1)} %copy.27), channel_id=1, replica_groups=mesh['row'=4,'col'=8] {'col'}, dimensions={0}, use_global_device_ids=true | all-gather | bytes 884736 | tf_op jit(solution)/shard_map/all_gather | solution.py:94
  398.6 90.1 %shard_map.94 = (f32[48,64,128]{2,1,0:T(8,128)}, f32[24,64,128]{2,1,0:T(8,128)}) custom-call(s32[576]{0:T(1024)S(1)} %reduce.6.rows_ref, s32[576]{0:T(1024)S(1)} %reduce.7.cols_ref, s32[1]{0:T(128)} %bitcast.43.cnt_ref, bf16[576,128,128]{2,1,0:T(8,128)(2,1)} %bitcast.45, bf16[48,64,128]{2,1,0:T(8,128)(2,1)S(1)} %all_gather.14.rin_ref, ...), custom_call_target="tpu_custom_call" | custom-call | flops 2415919104 | bytes 22413312 | tf_op jit(solution)/shard_map/pallas_call | solution.py:74
  488.7 0.0 copy-start.2
  488.7 0.0 reduce-scatter.11.cloned.1.call-update
  488.7 0.0 reduce-scatter.9.cloned.1.call-start
  488.8 0.5 reduce-scatter.9.cloned.1.call-update
  489.3 0.0 all-reduce.3.cloned.1.call-start
  489.4 0.3 copy-done.2
  489.6 1.3 convolution_multiply_fusion
  491.0 20.5 %reduce-scatter.11.cloned.1.call-done = f32[6,64,128]{2,1,0:T(8,128)} async-done(((f32[24,64,128]{2,1,0:T(8,128)}), f32[6,64,128]{2,1,0:T(8,128)}) %reduce-scatter.11.cloned.1.call-update) | async-done | bytes 196624 | tf_op jit(solution)/shard_map/reduce_scatter | solution.py:100
  511.5 68.2 %reduce-scatter.9.cloned.1.call-done = f32[6,64,128]{2,1,0:T(8,128)} async-done(((f32[48,64,128]{2,1,0:T(8,128)}), f32[6,64,128]{2,1,0:T(8,128)}) %reduce-scatter.9.cloned.1.call-update) | async-done | bytes 196624 | tf_op jit(solution)/shard_map/reduce_scatter | solution.py:99
  579.7 1.0 copy_bitcast_fusion.1
  580.7 0.0 copy-start.4
  580.7 0.0 copy-done.3
  580.7 1.3 convolution_multiply_fusion.1
  582.1 0.0 all-reduce.3.cloned.1.call-update
  582.1 131.3 %all-reduce.3.cloned.1.call-done = (f32[192,192]{1,0:T(8,128)}, f32[192,192]{1,0:T(8,128)}) async-done(((f32[192,192]{1,0:T(8,128)}, f32[192,192]{1,0:T(8,128)}), (f32[192,192]{1,0:T(8,128)}, f32[192,192]{1,0:T(8,128)})) %all-reduce.3.cloned.1.call-update) | async-done | bytes 294928 | tf_op jit(solution)/shard_map/psum | solution.py:137
  713.4 1.6 copy.45
  715.0 1.6 copy.46
  716.6 0.0 copy-done.4
  (8 shorter events, 0.2 us)
Async XLA Ops:
  7.2 0.9 copy-start
  7.2 58.7 %copy-start.5 = (s32[1,1,576]{2,1,0:T(1,128)S(1)}, s32[1,1,576]{2,1,0:T(1,128)}, u32[]{:S(2)}) copy-start(s32[1,1,576]{2,1,0:T(1,128)} %param.8) | copy-start | bytes 6916
  7.2 58.7 %copy-start.6 = (s32[1,1,576]{2,1,0:T(1,128)S(1)}, s32[1,1,576]{2,1,0:T(1,128)}, u32[]{:S(2)}) copy-start(s32[1,1,576]{2,1,0:T(1,128)} %param.9) | copy-start | bytes 6916
  7.2 102.1 %all-gather.2.cloned.1.call-start = ((), (), s32[]{:S(2)}) async-start(), calls=%async_computation.4 | async-start | bytes 1769472 | tf_op jit(solution)/shard_map/all_gather | solution.py:94
  65.1 173.7 %reduce-scatter.7.cloned.1.call-start = ((), (), s32[]{:S(2)}) async-start(), calls=%async_computation.6 | async-start | bytes 1966080 | tf_op jit(solution)/shard_map/reduce_scatter | solution.py:100
  109.3 1.4 copy-start.1
  209.3 108.0 %reduce-scatter.5.cloned.1.call-start = ((), (), s32[]{:S(2)}) async-start(), calls=%async_computation.5 | async-start | bytes 3538944 | tf_op jit(solution)/shard_map/reduce_scatter | solution.py:99
  210.1 301.4 %reduce-scatter.11.cloned.1.call-start = ((), (), s32[]{:S(2)}) async-start(), calls=%async_computation.8 | async-start | bytes 983040 | tf_op jit(solution)/shard_map/reduce_scatter | solution.py:100
  359.0 221.7 %copy-start.3 = (f32[64,768]{1,0:T(8,128)}, f32[64,768]{1,0:T(8,128)S(1)}, u32[]{:S(2)}) copy-start(f32[64,768]{1,0:T(8,128)S(1)} %get-tuple-element.22) | copy-start | bytes 589828
  488.7 0.9 copy-start.2
  488.7 90.9 %reduce-scatter.9.cloned.1.call-start = ((), (), s32[]{:S(2)}) async-start(), calls=%async_computation.7 | async-start | bytes 1769472 | tf_op jit(solution)/shard_map/reduce_scatter | solution.py:99
  489.3 224.1 %all-reduce.3.cloned.1.call-start = ((), (), s32[]{:S(2)}) async-start(), calls=%async_computation.9 | async-start | bytes 786432 | tf_op jit(solution)/shard_map/psum | solution.py:137
  580.7 135.9 %copy-start.4 = (f32[64,768]{1,0:T(8,128)}, f32[64,768]{1,0:T(8,128)S(1)}, u32[]{:S(2)}) copy-start(f32[64,768]{1,0:T(8,128)S(1)} %copy_bitcast_fusion.1) | copy-start | bytes 589828
Sparse Core Ops, SparseCore 0:
  65.3 43.9 all-gather.1
  209.5 29.3 reduce-scatter.6
  242.9 74.3 reduce-scatter.4
  488.8 22.5 reduce-scatter.10
  514.7 64.8 reduce-scatter.8
  586.5 126.8 all-reduce.2

commit v2 on v1

--- a/solution.py
+++ b/solution.py
@@ -87,17 +87,68 @@
     )(tile_rows, tile_cols, live_count.reshape(1), tile_vals, row_blocks, col_blocks)
 
 
+def exchange_pairs(size, step):
+    return [(i, i ^ step) for i in range(size)]
+
+
+def reversed_bits(value, bits):
+    result = jnp.zeros_like(value)
+    for k in range(bits):
+        result = result | (((value >> k) & 1) << (bits - 1 - k))
+    return result
+
+
+def gather_blocks(local, axis):
+    size = lax.axis_size(axis)
+    held = local
+    step = size // 2
+    while step >= 1:
+        held = jnp.concatenate([held, lax.ppermute(held, axis, exchange_pairs(size, step))], axis=0)
+        step //= 2
+    return held
+
+
+def scatter_sum(totals, axis):
+    size = lax.axis_size(axis)
+    held = totals
+    step = 1
+    while step < size:
+        half = held.shape[0] // 2
+        held = held[:half] + lax.ppermute(held[half:], axis, exchange_pairs(size, step))
+        step *= 2
+    return held
+
+
+def all_sum(value):
+    for axis in ("row", "col"):
+        size = lax.axis_size(axis)
+        step = 1
+        while step < size:
+            value = value + lax.ppermute(value, axis, exchange_pairs(size, step))
+            step *= 2
+    return value
+
+
+def held_position(index, axis, blocks_each):
+    size = lax.axis_size(axis)
+    bits = size.bit_length() - 1
+    me = lax.axis_index(axis)
+    owner = index // blocks_each
+    return reversed_bits(me ^ owner, bits) * blocks_each + index % blocks_each
+
+
 def apply_graph(vectors, tile_rows, tile_cols, live_count, tile_vals):
     vec_width, local_nodes = vectors.shape
     tile = tile_vals.shape[-1]
-    local = vectors.reshape(vec_width, local_nodes // tile, tile).transpose(1, 0, 2)
-    row_blocks = lax.all_gather(local, "col", axis=0, tiled=True)
-    col_blocks = lax.all_gather(local, "row", axis=0, tiled=True)
+    blocks_each = local_nodes // tile
+    local = vectors.reshape(vec_width, blocks_each, tile).transpose(1, 0, 2)
+    row_blocks = gather_blocks(local, "col")
+    col_blocks = gather_blocks(local, "row")
     row_totals, col_totals = tile_products(
         row_blocks, col_blocks, tile_rows, tile_cols, live_count, tile_vals
     )
-    own_rows = lax.psum_scatter(row_totals, "col", scatter_dimension=0, tiled=True)
-    own_cols = lax.psum_scatter(col_totals, "row", scatter_dimension=0, tiled=True)
+    own_rows = scatter_sum(row_totals, "col")
+    own_cols = scatter_sum(col_totals, "row")
     return (own_rows + own_cols).transpose(1, 0, 2).reshape(vec_width, local_nodes)
 
 
@@ -105,8 +156,9 @@
     highest = lax.Precision.HIGHEST
     width_k = block_x.shape[0]
     node_count = block_x.shape[1] * lax.axis_size("row") * lax.axis_size("col")
-    slot_rows = tile_rows[0, 0]
-    slot_cols = tile_cols[0, 0]
+    blocks_each = block_x.shape[1] // tile_vals.shape[-1]
+    slot_rows = held_position(tile_rows[0, 0], "col", blocks_each)
+    slot_cols = held_position(tile_cols[0, 0], "row", blocks_each)
     live_count = tile_count[0, 0]
     slot_vals = tile_vals[0, 0]
 
@@ -116,7 +168,7 @@
             / node_count
         )
 
-    gram_x = lax.psum(product(block_x, block_x), ("row", "col"))
+    gram_x = all_sum(product(block_x, block_x))
     cholesky_factor = jnp.linalg.cholesky(gram_x)
     orthonormal = lax.linalg.triangular_solve(cholesky_factor, block_x, left_side=True, lower=True)
     ortho_low = orthonormal.astype(jnp.bfloat16)
@@ -126,7 +178,7 @@
     )
     image_x = both_images[:width_k]
     image_p = both_images[width_k:]
-    rayleigh = lax.psum(product(orthonormal, image_x), ("row", "col"))
+    rayleigh = all_sum(product(orthonormal, image_x))
     residual = image_x - jnp.dot(
         rayleigh.T, orthonormal, precision=highest, preferred_element_type=jnp.float32
     )
@@ -134,7 +186,7 @@
     image_r = apply_graph(residual_low, slot_rows, slot_cols, live_count, slot_vals)
     basis = jnp.concatenate([orthonormal, residual, block_p], axis=0)
     images = jnp.concatenate([image_x, image_r, image_p], axis=0)
-    gram_a, gram_b = lax.psum((product(basis, images), product(basis, basis)), ("row", "col"))
+    gram_a, gram_b = all_sum(jnp.stack([product(basis, images), product(basis, basis)]))
     return (residual, image_r, gram_a, gram_b)
 
 

time: 723 us -> 442 us (0.61)
  waiting for transfers between devices: 362 us -> 199 us
  blocking collectives: 131 us -> 0 us
  starting transfers between devices: 0.24 us -> 40 us
  between operations: 15 us -> 1.89 us
  Pallas kernels: 189 us -> 178 us
    ppermute x0 -> x35, waiting for transfers between devices: none -> 199 us  [the longest x15 74.3 us: all_sum(): value = value + lax.ppermute(value, axis, exchange_pairs(size, step))]
    reduce_scatter x4 -> x0, waiting for transfers between devices: 196 us -> none  [the longest x2 147 us: apply_graph(): lax.psum_scatter(row_totals, 'col', scatter_dimension=0, tiled=True)]
    psum x1 -> x0, waiting for transfers between devices: 131 us -> none  [per_device(): lax.psum((product(basis, images), product(basis, basis)), ('row', 'col'))]
    psum x2 -> x0, blocking collectives: 82 us -> none  [the longest x1 42.2 us: per_device(): gram_x = lax.psum(product(block_x, block_x), ('row', 'col'))]
    all_gather x3 -> x0, blocking collectives: 49 us -> none  [the longest x1 32.2 us: apply_graph(): row_blocks = lax.all_gather(local, 'col', axis=0, tiled=True)]
    ppermute x0 -> x35, starting transfers between devices: none -> 40 us  [the longest x10 18 us: scatter_sum(): lax.ppermute(held[half:], axis, exchange_pairs(size, step))]
    all_gather x1 -> x0, waiting for transfers between devices: 33.8 us -> none  [apply_graph(): row_blocks = lax.all_gather(local, 'col', axis=0, tiled=True)]
    pallas_call x2, Pallas kernels: 189 us -> 178 us  [tile_products(): pl.pallas_call(tile_kernel, grid_spec=grid_spec, out_shape=[jax.ShapeDtyp...]
  transfers between devices with their start and end apart: 6 -> 35, of which waited for: 6 -> 31; matrix products, arithmetic and copies ran while one was open for 0% -> 1% of each run, Pallas kernels for 0% -> 0%
where the time goes in v2:
time: 442 us; the launch traced here: 441 us
  waiting for transfers between devices  199 us (45%)
  Pallas kernels  178 us (40%)
  starting transfers between devices  40 us (9%)
  other arithmetic  14.8 us (3%)
    pallas_call x2, Pallas kernels, tile_products(): pl.pallas_call(tile_kernel, grid_spec=grid_spec, out_shape=[jax.ShapeDtyp...  178 us
    ppermute x15, waiting for transfers between devices, all_sum(): value = value + lax.ppermute(value, axis, exchange_pairs(size, step))  74.3 us
    ppermute x10, waiting for transfers between devices, scatter_sum(): lax.ppermute(held[half:], axis, exchange_pairs(size, step))  68.5 us
    ppermute x10, waiting for transfers between devices, gather_blocks(): lax.ppermute(held, axis, exchange_pairs(size, step))  55.9 us
    ppermute x10, starting transfers between devices, scatter_sum(): lax.ppermute(held[half:], axis, exchange_pairs(size, step))  18 us
    ppermute x15, starting transfers between devices, all_sum(): value = value + lax.ppermute(value, axis, exchange_pairs(size, step))  13.6 us
  transfers between devices with their start and end apart: 35, of which 31 were waited for; matrix products, arithmetic and copies ran while one was open for 1% of the time, Pallas kernels for 0%

profile of v2, /device:TPU:0, one launch (start us, length us, event | category | flops | bytes accessed | tf_op | source)
XLA Modules:
  0.0 440.6 jit_solution(724367766726321698)
XLA Ops:
  0.6 0.9 copy-done
  1.6 0.3 convolution_multiply_fusion.3
  1.9 0.5 collective-permute-start
  2.4 0.9 collective-permute-done
  3.3 2.9 collective-permute-start.1
  6.1 1.9 collective-permute-done.1
  8.0 2.0 collective-permute-start.2
  10.0 1.9 collective-permute-done.2
  11.9 2.1 collective-permute-start.3
  14.0 1.9 collective-permute-done.3
  15.9 3.0 collective-permute-start.4
  19.0 0.9 convert_element_type.10
  19.9 0.9 collective-permute-done.4
  21.0 5.8 %cholesky.16 = f32[64,64]{1,0:T(8,128)S(1)} custom-call(f32[64,64]{1,0:T(8,128)S(1)} %fusion.18), custom_call_target="Cholesky" | custom-call | tf_op jit(solution)/shard_map/jit(cholesky)/cholesky | solution.py:172
  26.8 0.6 compare_reduce_fusion.2
  27.5 0.7 fusion.15
  28.1 4.9 %custom-call.6 = f32[1,64,64]{1,2,0:T(8,128)S(1)} custom-call(f32[1,64,64]{2,1,0:T(8,128)S(1)} %fusion.15), custom_call_target="InvertDiagBlocksLowerTriangular" | custom-call | tf_op jit(solution)/shard_map/triangular_solve | solution.py:173
  33.0 0.4 fusion.27
  33.5 0.2 copy.15
  33.6 0.2 copy.16
  33.8 1.9 collective-permute-start.8
  35.7 2.6 collective-permute-start.5
  38.3 1.2 collective-permute-done.8
  39.5 4.9 %collective-permute-done.5 = bf16[6,128,128]{2,1,0:T(8,128)(2,1)S(1)} collective-permute-done((bf16[6,128,128]{2,1,0:T(8,128)(2,1)S(1)}, bf16[6,128,128]{2,1,0:T(8,128)(2,1)S(1)}, u32[]{:S(2)}, u32[]{:S(2)}) %collective-permute-start.5) | collective-permute-done | bytes 196640 | tf_op jit(solution)/shard_map/ppermute | solution.py:106
  44.6 0.8 collective-permute-start.6
  45.3 0.9 collective-permute-done.9
  46.3 9.8 %collective-permute-done.6 = bf16[12,128,128]{2,1,0:T(8,128)(2,1)S(1)} collective-permute-done((bf16[12,128,128]{2,1,0:T(8,128)(2,1)S(1)}, bf16[12,128,128]{2,1,0:T(8,128)(2,1)S(1)}, u32[]{:S(2)}, u32[]{:S(2)}) %collective-permute-start.6) | collective-permute-done | bytes 393248 | tf_op jit(solution)/shard_map/ppermute | solution.py:106
  56.2 1.6 collective-permute-start.7
  58.6 16.8 %collective-permute-done.7 = bf16[24,128,128]{2,1,0:T(8,128)(2,1)S(1)} collective-permute-done((bf16[24,128,128]{2,1,0:T(8,128)(2,1)S(1)}, bf16[24,128,128]{2,1,0:T(8,128)(2,1)S(1)}, u32[]{:S(2)}, u32[]{:S(2)}) %collective-permute-start.7) | collective-permute-done | bytes 786464 | tf_op jit(solution)/shard_map/ppermute | solution.py:106
  75.6 93.7 %shard_map.93 = (f32[48,128,128]{2,1,0:T(8,128)}, f32[24,128,128]{2,1,0:T(8,128)S(1)}) custom-call(s32[576]{0:T(1024)S(1)} %get-tuple-element.30.rows_ref, s32[576]{0:T(1024)S(1)} %get-tuple-element.31.cols_ref, s32[1]{0:T(128)} %bitcast.56.cnt_ref, bf16[576,128,128]{2,1,0:T(8,128)(2,1)} %bitcast.58, bf16[48,128,128]{2,1,0:T(8,128)(2,1)S(1)} %pad_maximum_fusion.rin_ref, ...), custom_call_target="tpu_custom_call" | custom-call | flops 4831838208 | bytes 25952256 | tf_op jit(solution)/shard_map/pallas_call | solution.py:74
  169.2 1.7 slice.83
  170.9 9.2 %collective-permute-start.10 = (f32[24,128,128]{2,1,0:T(8,128)S(1)}, f32[24,128,128]{2,1,0:T(8,128)S(1)}, u32[]{:S(2)}, u32[]{:S(2)}) collective-permute-start(f32[24,128,128]{2,1,0:T(8,128)S(1)} %slice.83), channel_id=1, source_target_pairs={{0,1},{1,0},{2,3},{3,2},{4,5},{5,4},{6,7},{7,6},{8,9},{9,8},{10,11... | collective-permute-start | bytes 4718600 | tf_op jit(solution)/shard_map/ppermute | solution.py:117
  180.3 18.3 %collective-permute-done.10 = f32[24,128,128]{2,1,0:T(8,128)S(1)} collective-permute-done((f32[24,128,128]{2,1,0:T(8,128)S(1)}, f32[24,128,128]{2,1,0:T(8,128)S(1)}, u32[]{:S(2)}, u32[]{:S(2)}) %collective-permute-start.10) | collective-permute-done | bytes 1572896 | tf_op jit(solution)/shard_map/ppermute | solution.py:117
  198.6 0.2 slice_add_fusion
  199.1 13.1 %collective-permute-done.11 = f32[12,128,128]{2,1,0:T(8,128)S(1)} collective-permute-done((f32[12,128,128]{2,1,0:T(8,128)S(1)}, f32[12,128,128]{2,1,0:T(8,128)S(1)}, u32[]{:S(2)}, u32[]{:S(2)}) %collective-permute-start.11) | collective-permute-done | bytes 786464 | tf_op jit(solution)/shard_map/ppermute | solution.py:117
  212.5 11.8 %collective-permute-done.12 = f32[6,128,128]{2,1,0:T(8,128)S(1)} collective-permute-done((f32[6,128,128]{2,1,0:T(8,128)S(1)}, f32[6,128,128]{2,1,0:T(8,128)S(1)}, u32[]{:S(2)}, u32[]{:S(2)}) %collective-permute-start.12) | collective-permute-done | bytes 393248 | tf_op jit(solution)/shard_map/ppermute | solution.py:117
  224.5 0.3 convolution_multiply_fusion.2
  224.9 1.2 collective-permute-done.15
  226.1 3.9 collective-permute-done.16
  230.0 1.1 collective-permute-start.17
  231.1 2.8 collective-permute-done.17
  233.9 3.9 collective-permute-done.18
  237.9 6.2 %collective-permute-done.19 = f32[64,64]{0,1:T(8,128)S(1)} collective-permute-done((f32[64,64]{0,1:T(8,128)S(1)}, f32[64,64]{0,1:T(8,128)S(1)}, u32[]{:S(2)}, u32[]{:S(2)}) %collective-permute-start.19) | collective-permute-done | bytes 16416 | tf_op jit(solution)/shard_map/ppermute | solution.py:127
  244.1 0.3 convolution_subtract_fusion
  244.6 4.5 %collective-permute-done.23 = bf16[6,64,128]{2,1,0:T(8,128)(2,1)S(1)} collective-permute-done((bf16[6,64,128]{2,1,0:T(8,128)(2,1)S(1)}, bf16[6,64,128]{2,1,0:T(8,128)(2,1)S(1)}, u32[]{:S(2)}, u32[]{:S(2)}) %collective-permute-start.23) | collective-permute-done | bytes 98336 | tf_op jit(solution)/shard_map/ppermute | solution.py:106
  249.1 1.0 collective-permute-done.20
  250.3 1.3 collective-permute-done.24
  251.6 5.9 %collective-permute-done.21 = bf16[12,64,128]{2,1,0:T(8,128)(2,1)S(1)} collective-permute-done((bf16[12,64,128]{2,1,0:T(8,128)(2,1)S(1)}, bf16[12,64,128]{2,1,0:T(8,128)(2,1)S(1)}, u32[]{:S(2)}, u32[]{:S(2)}) %collective-permute-start.21) | collective-permute-done | bytes 196640 | tf_op jit(solution)/shard_map/ppermute | solution.py:106
  257.6 1.2 collective-permute-start.22
  258.8 9.6 %collective-permute-done.22 = bf16[24,64,128]{2,1,0:T(8,128)(2,1)S(1)} collective-permute-done((bf16[24,64,128]{2,1,0:T(8,128)(2,1)S(1)}, bf16[24,64,128]{2,1,0:T(8,128)(2,1)S(1)}, u32[]{:S(2)}, u32[]{:S(2)}) %collective-permute-start.22) | collective-permute-done | bytes 393248 | tf_op jit(solution)/shard_map/ppermute | solution.py:106
  268.4 84.6 %shard_map.94 = (f32[48,64,128]{2,1,0:T(8,128)S(1)}, f32[24,64,128]{2,1,0:T(8,128)S(1)}) custom-call(s32[576]{0:T(1024)S(1)} %get-tuple-element.30.rows_ref, s32[576]{0:T(1024)S(1)} %get-tuple-element.31.cols_ref, s32[1]{0:T(128)} %bitcast.57.cnt_ref, bf16[576,128,128]{2,1,0:T(8,128)(2,1)} %bitcast.59, bf16[48,64,128]{2,1,0:T(8,128)(2,1)S(1)} %pad_maximum_fusion.3.rin_ref, ...), custom_call_target="tpu_custom_call" | custom-call | flops 2415919104 | bytes 22413312 | tf_op jit(solution)/shard_map/pallas_call | solution.py:74
  353.1 8.2 %collective-permute-start.25 = (f32[24,64,128]{2,1,0:T(8,128)S(1)}, f32[24,64,128]{2,1,0:T(8,128)S(1)}, u32[]{:S(2)}, u32[]{:S(2)}) collective-permute-start(f32[24,64,128]{2,1,0:T(8,128)S(1)} %slice.95), channel_id=1, source_target_pairs={{0,1},{1,0},{2,3},{3,2},{4,5},{5,4},{6,7},{7,6},{8,9},{9,8},{10,11... | collective-permute-start | bytes 2359304 | tf_op jit(solution)/shard_map/ppermute | solution.py:117
  361.4 9.9 %collective-permute-done.25 = f32[24,64,128]{2,1,0:T(8,128)S(1)} collective-permute-done((f32[24,64,128]{2,1,0:T(8,128)S(1)}, f32[24,64,128]{2,1,0:T(8,128)S(1)}, u32[]{:S(2)}, u32[]{:S(2)}) %collective-permute-start.25) | collective-permute-done | bytes 786464 | tf_op jit(solution)/shard_map/ppermute | solution.py:117
  371.7 8.5 %collective-permute-done.26 = f32[12,64,128]{2,1,0:T(8,128)S(1)} collective-permute-done((f32[12,64,128]{2,1,0:T(8,128)S(1)}, f32[12,64,128]{2,1,0:T(8,128)S(1)}, u32[]{:S(2)}, u32[]{:S(2)}) %collective-permute-start.26) | collective-permute-done | bytes 393248 | tf_op jit(solution)/shard_map/ppermute | solution.py:117
  380.4 0.7 fusion
  381.1 6.9 %collective-permute-done.27 = f32[6,64,128]{2,1,0:T(8,128)S(1)} collective-permute-done((f32[6,64,128]{2,1,0:T(8,128)S(1)}, f32[6,64,128]{2,1,0:T(8,128)S(1)}, u32[]{:S(2)}, u32[]{:S(2)}) %collective-permute-start.27) | collective-permute-done | bytes 196640 | tf_op jit(solution)/shard_map/ppermute | solution.py:117
  388.1 0.7 fusion.1
  388.9 1.7 collective-permute-done.30
  390.7 11.1 %collective-permute-done.31 = f32[2,192,192]{2,1,0:T(8,128)S(1)} collective-permute-done((f32[2,192,192]{2,1,0:T(8,128)S(1)}, f32[2,192,192]{2,1,0:T(8,128)S(1)}, u32[]{:S(2)}, u32[]{:S(2)}) %collective-permute-start.31) | collective-permute-done | bytes 294944 | tf_op jit(solution)/shard_map/ppermute | solution.py:127
  401.9 1.6 collective-permute-start.32
  403.6 8.8 %collective-permute-done.32 = f32[2,192,192]{2,1,0:T(8,128)S(1)} collective-permute-done((f32[2,192,192]{2,1,0:T(8,128)S(1)}, f32[2,192,192]{2,1,0:T(8,128)S(1)}, u32[]{:S(2)}, u32[]{:S(2)}) %collective-permute-start.32) | collective-permute-done | bytes 294944 | tf_op jit(solution)/shard_map/ppermute | solution.py:127
  412.5 9.4 %collective-permute-done.33 = f32[2,192,192]{2,1,0:T(8,128)S(1)} collective-permute-done((f32[2,192,192]{2,1,0:T(8,128)S(1)}, f32[2,192,192]{2,1,0:T(8,128)S(1)}, u32[]{:S(2)}, u32[]{:S(2)}) %collective-permute-start.33) | collective-permute-done | bytes 294944 | tf_op jit(solution)/shard_map/ppermute | solution.py:127
  422.0 17.8 %collective-permute-done.34 = f32[2,192,192]{2,1,0:T(8,128)S(1)} collective-permute-done((f32[2,192,192]{2,1,0:T(8,128)S(1)}, f32[2,192,192]{2,1,0:T(8,128)S(1)}, u32[]{:S(2)}, u32[]{:S(2)}) %collective-permute-start.34) | collective-permute-done | bytes 294944 | tf_op jit(solution)/shard_map/ppermute | solution.py:127
  439.8 0.8 slice_bitcast_fusion
  (88 shorter events, 3.5 us)
Async XLA Ops:
  0.6 0.9 copy-start
  1.9 1.4 collective-permute-start
  3.3 4.8 %collective-permute-start.1 = (f32[64,64]{0,1:T(8,128)S(1)}, f32[64,64]{0,1:T(8,128)S(1)}, u32[]{:S(2)}, u32[]{:S(2)}) collective-permute-start(f32[64,64]{0,1:T(8,128)S(1)} %add.114), channel_id=1, source_target_pairs={{0,16},{8,24},{16,0},{24,8},{1,17},{9,25},{17,1},{25,9},{2,18},{10... | collective-permute-start | bytes 49160 | tf_op jit(solution)/shard_map/ppermute | solution.py:127
  8.0 3.9 collective-permute-start.2
  11.9 4.0 collective-permute-start.3
  15.9 4.9 %collective-permute-start.4 = (f32[64,64]{0,1:T(8,128)S(1)}, f32[64,64]{0,1:T(8,128)S(1)}, u32[]{:S(2)}, u32[]{:S(2)}) collective-permute-start(f32[64,64]{0,1:T(8,128)S(1)} %add.117), channel_id=1, source_target_pairs={{0,4},{1,5},{2,6},{3,7},{4,0},{5,1},{6,2},{7,3},{8,12},{9,13},{10,... | collective-permute-start | bytes 49160 | tf_op jit(solution)/shard_map/ppermute | solution.py:127
  33.8 5.7 %collective-permute-start.8 = (bf16[6,128,128]{2,1,0:T(8,128)(2,1)S(1)}, bf16[6,128,128]{2,1,0:T(8,128)(2,1)S(1)}, u32[]{:S(2)}, u32[]{:S(2)}) collective-permute-start(bf16[6,128,128]{2,1,0:T(8,128)(2,1)S(1)} %bitcast.60), channel_id=1, source_target_pairs={{0,16},{8,24},{16,0},{24,8},{1,17},{9,25},{17,1},{25,9},{2,18},{10... | collective-permute-start | bytes 589832 | tf_op jit(solution)/shard_map/ppermute | solution.py:106
  35.7 8.7 %collective-permute-start.5 = (bf16[6,128,128]{2,1,0:T(8,128)(2,1)S(1)}, bf16[6,128,128]{2,1,0:T(8,128)(2,1)S(1)}, u32[]{:S(2)}, u32[]{:S(2)}) collective-permute-start(bf16[6,128,128]{2,1,0:T(8,128)(2,1)S(1)} %bitcast.61), channel_id=1, source_target_pairs={{0,4},{1,5},{2,6},{3,7},{4,0},{5,1},{6,2},{7,3},{8,12},{9,13},{10,... | collective-permute-start | bytes 589832 | tf_op jit(solution)/shard_map/ppermute | solution.py:106
  44.5 14.0 %copy-start.5 = (s32[1,1,576]{2,1,0:T(1,128)S(1)}, s32[1,1,576]{2,1,0:T(1,128)}, u32[]{:S(2)}) copy-start(s32[1,1,576]{2,1,0:T(1,128)} %param.8) | copy-start | bytes 6916
  44.5 14.0 %copy-start.6 = (s32[1,1,576]{2,1,0:T(1,128)S(1)}, s32[1,1,576]{2,1,0:T(1,128)}, u32[]{:S(2)}) copy-start(s32[1,1,576]{2,1,0:T(1,128)} %param.9) | copy-start | bytes 6916
  44.5 1.8 collective-permute-start.9
  44.6 11.5 %collective-permute-start.6 = (bf16[12,128,128]{2,1,0:T(8,128)(2,1)S(1)}, bf16[12,128,128]{2,1,0:T(8,128)(2,1)S(1)}, u32[]{:S(2)}, u32[]{:S(2)}) collective-permute-start(bf16[12,128,128]{2,1,0:T(8,128)(2,1)S(1)} %get-tuple-element.23), channel_id=1, source_target_pairs={{0,2},{1,3},{2,0},{3,1},{4,6},{5,7},{6,4},{7,5},{8,10},{9,11},{10,... | collective-permute-start | bytes 1179656 | tf_op jit(solution)/shard_map/ppermute | solution.py:106
  56.2 19.2 %collective-permute-start.7 = (bf16[24,128,128]{2,1,0:T(8,128)(2,1)S(1)}, bf16[24,128,128]{2,1,0:T(8,128)(2,1)S(1)}, u32[]{:S(2)}, u32[]{:S(2)}) collective-permute-start(bf16[24,128,128]{2,1,0:T(8,128)(2,1)S(1)} %get-tuple-element.21), channel_id=1, source_target_pairs={{0,1},{1,0},{2,3},{3,2},{4,5},{5,4},{6,7},{7,6},{8,9},{9,8},{10,11... | collective-permute-start | bytes 2359304 | tf_op jit(solution)/shard_map/ppermute | solution.py:106
  169.2 29.4 %copy-start.1 = (f32[48,128,128]{2,1,0:T(8,128)S(1)}, f32[48,128,128]{2,1,0:T(8,128)}, u32[]{:S(2)}) copy-start(f32[48,128,128]{2,1,0:T(8,128)} %get-tuple-element.8) | copy-start | bytes 9437188
  170.9 27.6 %collective-permute-start.10 = (f32[24,128,128]{2,1,0:T(8,128)S(1)}, f32[24,128,128]{2,1,0:T(8,128)S(1)}, u32[]{:S(2)}, u32[]{:S(2)}) collective-permute-start(f32[24,128,128]{2,1,0:T(8,128)S(1)} %slice.83), channel_id=1, source_target_pairs={{0,1},{1,0},{2,3},{3,2},{4,5},{5,4},{6,7},{7,6},{8,9},{9,8},{10,11... | collective-permute-start | bytes 4718600 | tf_op jit(solution)/shard_map/ppermute | solution.py:117
  180.2 18.7 %collective-permute-start.13 = (f32[12,128,128]{2,1,0:T(8,128)S(1)}, f32[12,128,128]{2,1,0:T(8,128)S(1)}, u32[]{:S(2)}, u32[]{:S(2)}) collective-permute-start(f32[12,128,128]{2,1,0:T(8,128)S(1)} %slice.89), channel_id=1, source_target_pairs={{0,8},{8,0},{16,24},{24,16},{1,9},{9,1},{17,25},{25,17},{2,10},{10... | collective-permute-start | bytes 2359304 | tf_op jit(solution)/shard_map/ppermute | solution.py:117
  198.8 13.4 %collective-permute-start.11 = (f32[12,128,128]{2,1,0:T(8,128)S(1)}, f32[12,128,128]{2,1,0:T(8,128)S(1)}, u32[]{:S(2)}, u32[]{:S(2)}) collective-permute-start(f32[12,128,128]{2,1,0:T(8,128)S(1)} %slice.107), channel_id=1, source_target_pairs={{0,2},{1,3},{2,0},{3,1},{4,6},{5,7},{6,4},{7,5},{8,10},{9,11},{10,... | collective-permute-start | bytes 2359304 | tf_op jit(solution)/shard_map/ppermute | solution.py:117
  199.1 13.4 %collective-permute-start.14 = (f32[6,128,128]{2,1,0:T(8,128)S(1)}, f32[6,128,128]{2,1,0:T(8,128)S(1)}, u32[]{:S(2)}, u32[]{:S(2)}) collective-permute-start(f32[6,128,128]{2,1,0:T(8,128)S(1)} %slice.111), channel_id=1, source_target_pairs={{0,16},{8,24},{16,0},{24,8},{1,17},{9,25},{17,1},{25,9},{2,18},{10... | collective-permute-start | bytes 1179656 | tf_op jit(solution)/shard_map/ppermute | solution.py:117
  212.4 11.9 %collective-permute-start.12 = (f32[6,128,128]{2,1,0:T(8,128)S(1)}, f32[6,128,128]{2,1,0:T(8,128)S(1)}, u32[]{:S(2)}, u32[]{:S(2)}) collective-permute-start(f32[6,128,128]{2,1,0:T(8,128)S(1)} %slice.109), channel_id=1, source_target_pairs={{0,4},{1,5},{2,6},{3,7},{4,0},{5,1},{6,2},{7,3},{8,12},{9,13},{10,... | collective-permute-start | bytes 1179656 | tf_op jit(solution)/shard_map/ppermute | solution.py:117
  224.8 1.3 collective-permute-start.15
  226.1 3.9 collective-permute-start.16
  230.0 3.9 collective-permute-start.17
  233.9 3.9 collective-permute-start.18
  237.9 6.2 %collective-permute-start.19 = (f32[64,64]{0,1:T(8,128)S(1)}, f32[64,64]{0,1:T(8,128)S(1)}, u32[]{:S(2)}, u32[]{:S(2)}) collective-permute-start(f32[64,64]{0,1:T(8,128)S(1)} %add.129), channel_id=1, source_target_pairs={{0,4},{1,5},{2,6},{3,7},{4,0},{5,1},{6,2},{7,3},{8,12},{9,13},{10,... | collective-permute-start | bytes 49160 | tf_op jit(solution)/shard_map/ppermute | solution.py:127
  244.4 143.7 %copy-start.2 = (f32[64,768]{1,0:T(8,128)}, f32[64,768]{1,0:T(8,128)S(1)}, u32[]{:S(2)}) copy-start(f32[64,768]{1,0:T(8,128)S(1)} %convolution_subtract_fusion) | copy-start | bytes 589828
  244.4 4.7 %collective-permute-start.23 = (bf16[6,64,128]{2,1,0:T(8,128)(2,1)S(1)}, bf16[6,64,128]{2,1,0:T(8,128)(2,1)S(1)}, u32[]{:S(2)}, u32[]{:S(2)}) collective-permute-start(bf16[6,64,128]{2,1,0:T(8,128)(2,1)S(1)} %bitcast_bitcast_fusion), channel_id=1, source_target_pairs={{0,16},{8,24},{16,0},{24,8},{1,17},{9,25},{17,1},{25,9},{2,18},{10... | collective-permute-start | bytes 294920 | tf_op jit(solution)/shard_map/ppermute | solution.py:106
  244.5 5.6 %collective-permute-start.20 = (bf16[6,64,128]{2,1,0:T(8,128)(2,1)S(1)}, bf16[6,64,128]{2,1,0:T(8,128)(2,1)S(1)}, u32[]{:S(2)}, u32[]{:S(2)}) collective-permute-start(bf16[6,64,128]{2,1,0:T(8,128)(2,1)S(1)} %bitcast_bitcast_fusion), channel_id=1, source_target_pairs={{0,4},{1,5},{2,6},{3,7},{4,0},{5,1},{6,2},{7,3},{8,12},{9,13},{10,... | collective-permute-start | bytes 294920 | tf_op jit(solution)/shard_map/ppermute | solution.py:106
  250.1 1.5 collective-permute-start.24
  250.2 7.3 %collective-permute-start.21 = (bf16[12,64,128]{2,1,0:T(8,128)(2,1)S(1)}, bf16[12,64,128]{2,1,0:T(8,128)(2,1)S(1)}, u32[]{:S(2)}, u32[]{:S(2)}) collective-permute-start(bf16[12,64,128]{2,1,0:T(8,128)(2,1)S(1)} %get-tuple-element.27), channel_id=1, source_target_pairs={{0,2},{1,3},{2,0},{3,1},{4,6},{5,7},{6,4},{7,5},{8,10},{9,11},{10,... | collective-permute-start | bytes 589832 | tf_op jit(solution)/shard_map/ppermute | solution.py:106
  257.6 10.7 %collective-permute-start.22 = (bf16[24,64,128]{2,1,0:T(8,128)(2,1)S(1)}, bf16[24,64,128]{2,1,0:T(8,128)(2,1)S(1)}, u32[]{:S(2)}, u32[]{:S(2)}) collective-permute-start(bf16[24,64,128]{2,1,0:T(8,128)(2,1)S(1)} %get-tuple-element.25), channel_id=1, source_target_pairs={{0,1},{1,0},{2,3},{3,2},{4,5},{5,4},{6,7},{7,6},{8,9},{9,8},{10,11... | collective-permute-start | bytes 1179656 | tf_op jit(solution)/shard_map/ppermute | solution.py:106
  353.1 18.2 %collective-permute-start.25 = (f32[24,64,128]{2,1,0:T(8,128)S(1)}, f32[24,64,128]{2,1,0:T(8,128)S(1)}, u32[]{:S(2)}, u32[]{:S(2)}) collective-permute-start(f32[24,64,128]{2,1,0:T(8,128)S(1)} %slice.95), channel_id=1, source_target_pairs={{0,1},{1,0},{2,3},{3,2},{4,5},{5,4},{6,7},{7,6},{8,9},{9,8},{10,11... | collective-permute-start | bytes 2359304 | tf_op jit(solution)/shard_map/ppermute | solution.py:117
  361.4 10.2 %collective-permute-start.28 = (f32[12,64,128]{2,1,0:T(8,128)S(1)}, f32[12,64,128]{2,1,0:T(8,128)S(1)}, u32[]{:S(2)}, u32[]{:S(2)}) collective-permute-start(f32[12,64,128]{2,1,0:T(8,128)S(1)} %slice.101), channel_id=1, source_target_pairs={{0,8},{8,0},{16,24},{24,16},{1,9},{9,1},{17,25},{25,17},{2,10},{10... | collective-permute-start | bytes 1179656 | tf_op jit(solution)/shard_map/ppermute | solution.py:117
  371.4 8.8 %collective-permute-start.26 = (f32[12,64,128]{2,1,0:T(8,128)S(1)}, f32[12,64,128]{2,1,0:T(8,128)S(1)}, u32[]{:S(2)}, u32[]{:S(2)}) collective-permute-start(f32[12,64,128]{2,1,0:T(8,128)S(1)} %slice.114), channel_id=1, source_target_pairs={{0,2},{1,3},{2,0},{3,1},{4,6},{5,7},{6,4},{7,5},{8,10},{9,11},{10,... | collective-permute-start | bytes 1179656 | tf_op jit(solution)/shard_map/ppermute | solution.py:117
  371.6 8.8 %copy-start.3 = (f32[64,768]{1,0:T(8,128)S(1)}, f32[64,768]{1,0:T(8,128)}, u32[]{:S(2)}) copy-start(f32[64,768]{1,0:T(8,128)} %param.7) | copy-start | bytes 589828
  371.6 9.5 %collective-permute-start.29 = (f32[6,64,128]{2,1,0:T(8,128)S(1)}, f32[6,64,128]{2,1,0:T(8,128)S(1)}, u32[]{:S(2)}, u32[]{:S(2)}) collective-permute-start(f32[6,64,128]{2,1,0:T(8,128)S(1)} %slice.118), channel_id=1, source_target_pairs={{0,16},{8,24},{16,0},{24,8},{1,17},{9,25},{17,1},{25,9},{2,18},{10... | collective-permute-start | bytes 589832 | tf_op jit(solution)/shard_map/ppermute | solution.py:117
  380.3 7.7 %collective-permute-start.27 = (f32[6,64,128]{2,1,0:T(8,128)S(1)}, f32[6,64,128]{2,1,0:T(8,128)S(1)}, u32[]{:S(2)}, u32[]{:S(2)}) collective-permute-start(f32[6,64,128]{2,1,0:T(8,128)S(1)} %slice.116), channel_id=1, source_target_pairs={{0,4},{1,5},{2,6},{3,7},{4,0},{5,1},{6,2},{7,3},{8,12},{9,13},{10,... | collective-permute-start | bytes 589832 | tf_op jit(solution)/shard_map/ppermute | solution.py:117
  388.1 2.6 copy-start.4
  388.8 1.8 collective-permute-start.30
  390.6 11.2 %collective-permute-start.31 = (f32[2,192,192]{2,1,0:T(8,128)S(1)}, f32[2,192,192]{2,1,0:T(8,128)S(1)}, u32[]{:S(2)}, u32[]{:S(2)}) collective-permute-start(f32[2,192,192]{2,1,0:T(8,128)S(1)} %fusion.26), channel_id=1, source_target_pairs={{0,16},{8,24},{16,0},{24,8},{1,17},{9,25},{17,1},{25,9},{2,18},{10... | collective-permute-start | bytes 884744 | tf_op jit(solution)/shard_map/ppermute | solution.py:127
  401.9 10.4 %collective-permute-start.32 = (f32[2,192,192]{2,1,0:T(8,128)S(1)}, f32[2,192,192]{2,1,0:T(8,128)S(1)}, u32[]{:S(2)}, u32[]{:S(2)}) collective-permute-start(f32[2,192,192]{2,1,0:T(8,128)S(1)} %fusion.33), channel_id=1, source_target_pairs={{0,1},{1,0},{2,3},{3,2},{4,5},{5,4},{6,7},{7,6},{8,9},{9,8},{10,11... | collective-permute-start | bytes 884744 | tf_op jit(solution)/shard_map/ppermute | solution.py:127
  412.4 9.5 %collective-permute-start.33 = (f32[2,192,192]{2,1,0:T(8,128)S(1)}, f32[2,192,192]{2,1,0:T(8,128)S(1)}, u32[]{:S(2)}, u32[]{:S(2)}) collective-permute-start(f32[2,192,192]{2,1,0:T(8,128)S(1)} %add.139), channel_id=1, source_target_pairs={{0,2},{1,3},{2,0},{3,1},{4,6},{5,7},{6,4},{7,5},{8,10},{9,11},{10,... | collective-permute-start | bytes 884744 | tf_op jit(solution)/shard_map/ppermute | solution.py:127
  421.9 17.9 %collective-permute-start.34 = (f32[2,192,192]{2,1,0:T(8,128)S(1)}, f32[2,192,192]{2,1,0:T(8,128)S(1)}, u32[]{:S(2)}, u32[]{:S(2)}) collective-permute-start(f32[2,192,192]{2,1,0:T(8,128)S(1)} %add.140), channel_id=1, source_target_pairs={{0,4},{1,5},{2,6},{3,7},{4,0},{5,1},{6,2},{7,3},{8,12},{9,13},{10,... | collective-permute-start | bytes 884744 | tf_op jit(solution)/shard_map/ppermute | solution.py:127

commit v3 on v2

--- a/solution.py
+++ b/solution.py
@@ -8,6 +8,7 @@
 from jax.sharding import PartitionSpec as P
 
 GROUP = 64
+UNROLL = 32
 
 
 def tile_kernel(rows_ref, cols_ref, cnt_ref, vals_ref, rin_ref, cin_ref, rout_ref, cout_ref):
@@ -22,24 +23,36 @@
     base = g * group
     live = cnt_ref[0]
 
-    def body(t, carry):
+    def tile_step(t):
         slot = base + t
-
-        @pl.when(slot < live)
+        a = rows_ref[slot]
+        b = cols_ref[slot]
+        v = vals_ref[t]
+        fwd = lax.dot_general(
+            cin_ref[b], v, (((1,), (1,)), ((), ())), preferred_element_type=jnp.float32
+        )
+        bwd = jnp.dot(rin_ref[a], v, preferred_element_type=jnp.float32)
+        rout_ref[a] += fwd
+        cout_ref[b] += bwd
+
+    def full_body(t, carry):
+        tile_step(t)
+        return carry
+
+    def part_body(t, carry):
+        @pl.when(base + t < live)
         def _():
-            a = rows_ref[slot]
-            b = cols_ref[slot]
-            v = vals_ref[t]
-            fwd = lax.dot_general(
-                cin_ref[b], v, (((1,), (1,)), ((), ())), preferred_element_type=jnp.float32
-            )
-            bwd = jnp.dot(rin_ref[a], v, preferred_element_type=jnp.float32)
-            rout_ref[a] += fwd
-            cout_ref[b] += bwd
+            tile_step(t)
 
         return carry
 
-    lax.fori_loop(0, group, body, 0)
+    @pl.when(base + group <= live)
+    def _():
+        lax.fori_loop(0, group, full_body, 0, unroll=UNROLL)
+
+    @pl.when(jnp.logical_and(base < live, base + group > live))
+    def _():
+        lax.fori_loop(0, group, part_body, 0)
 
 
 def tile_products(row_blocks, col_blocks, tile_rows, tile_cols, live_count, tile_vals):

time: 442 us -> 322 us (0.73); the launches traced: 441 us -> 325 us
  Pallas kernels: 178 us -> 52 us
  starting transfers between devices: 40 us -> 49.6 us
    pallas_call x2, Pallas kernels: 178 us -> 52 us  [tile_products(): pl.pallas_call(tile_kernel, grid_spec=grid_spec, out_shape=[jax.ShapeDtyp...]
    ppermute x10, starting transfers between devices: 18 us -> 28 us  [scatter_sum(): lax.ppermute(held[half:], axis, exchange_pairs(size, step))]
where the time goes in v3:
time: 322 us; the launch traced here: 325 us
  waiting for transfers between devices  200 us (62%)
  Pallas kernels  52 us (16%)
  starting transfers between devices  49.6 us (15%)
  other arithmetic  14.8 us (5%)
  local copies, waits for them, and re-layouts  4.21 us (1%)
    ppermute x15, waiting for transfers between devices, all_sum(): value = value + lax.ppermute(value, axis, exchange_pairs(size, step))  74 us
    ppermute x10, waiting for transfers between devices, scatter_sum(): lax.ppermute(held[half:], axis, exchange_pairs(size, step))  68.8 us
    ppermute x10, waiting for transfers between devices, gather_blocks(): lax.ppermute(held, axis, exchange_pairs(size, step))  57.3 us
    pallas_call x2, Pallas kernels, tile_products(): pl.pallas_call(tile_kernel, grid_spec=grid_spec, out_shape=[jax.ShapeDtyp...  52 us
    ppermute x10, starting transfers between devices, scatter_sum(): lax.ppermute(held[half:], axis, exchange_pairs(size, step))  28 us
    ppermute x15, starting transfers between devices, all_sum(): value = value + lax.ppermute(value, axis, exchange_pairs(size, step))  13.9 us
    ppermute x10, starting transfers between devices, gather_blocks(): lax.ppermute(held, axis, exchange_pairs(size, step))  7.81 us
    another operation x3, other arithmetic, per_device(): cholesky_factor = jnp.linalg.cholesky(gram_x)  6.52 us
  transfers between devices with their start and end apart: 35, of which 31 were waited for; matrix products, arithmetic and copies ran while one was open for 1% of the time, Pallas kernels for 0%

profile of v3, /device:TPU:0, one launch (start us, length us, event | category | flops | bytes accessed | tf_op | source)
XLA Modules:
  0.0 325.3 jit_solution(10912858457221990340)
XLA Ops:
  0.6 0.9 copy-done
  1.9 0.5 collective-permute-start
  2.4 0.9 collective-permute-done
  3.3 2.9 collective-permute-start.1
  6.1 1.9 collective-permute-done.1
  8.0 2.0 collective-permute-start.2
  10.0 1.9 collective-permute-done.2
  11.9 2.1 collective-permute-start.3
  14.0 1.9 collective-permute-done.3
  15.9 3.0 collective-permute-start.4
  19.0 0.9 convert_element_type.10
  19.9 0.9 collective-permute-done.4
  21.0 5.8 %cholesky.16 = f32[64,64]{1,0:T(8,128)S(1)} custom-call(f32[64,64]{1,0:T(8,128)S(1)} %fusion.18), custom_call_target="Cholesky" | custom-call | tf_op jit(solution)/shard_map/jit(cholesky)/cholesky | solution.py:185
  26.8 0.6 compare_reduce_fusion.2
  27.5 0.7 fusion.15
  28.1 4.9 %custom-call.6 = f32[1,64,64]{1,2,0:T(8,128)S(1)} custom-call(f32[1,64,64]{2,1,0:T(8,128)S(1)} %fusion.15), custom_call_target="InvertDiagBlocksLowerTriangular" | custom-call | tf_op jit(solution)/shard_map/triangular_solve | solution.py:186
  33.0 0.4 fusion.27
  33.8 1.9 collective-permute-start.8
  35.7 2.6 collective-permute-start.5
  38.3 1.2 collective-permute-done.8
  39.5 4.9 %collective-permute-done.5 = bf16[6,128,128]{2,1,0:T(8,128)(2,1)S(1)} collective-permute-done((bf16[6,128,128]{2,1,0:T(8,128)(2,1)S(1)}, bf16[6,128,128]{2,1,0:T(8,128)(2,1)S(1)}, u32[]{:S(2)}, u32[]{:S(2)}) %collective-permute-start.5) | collective-permute-done | bytes 196640 | tf_op jit(solution)/shard_map/ppermute | solution.py:119
  44.6 0.8 collective-permute-start.6
  45.3 0.9 collective-permute-done.9
  46.3 9.8 %collective-permute-done.6 = bf16[12,128,128]{2,1,0:T(8,128)(2,1)S(1)} collective-permute-done((bf16[12,128,128]{2,1,0:T(8,128)(2,1)S(1)}, bf16[12,128,128]{2,1,0:T(8,128)(2,1)S(1)}, u32[]{:S(2)}, u32[]{:S(2)}) %collective-permute-start.6) | collective-permute-done | bytes 393248 | tf_op jit(solution)/shard_map/ppermute | solution.py:119
  56.2 1.6 collective-permute-start.7
  58.6 16.8 %collective-permute-done.7 = bf16[24,128,128]{2,1,0:T(8,128)(2,1)S(1)} collective-permute-done((bf16[24,128,128]{2,1,0:T(8,128)(2,1)S(1)}, bf16[24,128,128]{2,1,0:T(8,128)(2,1)S(1)}, u32[]{:S(2)}, u32[]{:S(2)}) %collective-permute-start.7) | collective-permute-done | bytes 786464 | tf_op jit(solution)/shard_map/ppermute | solution.py:119
  75.6 27.6 %shard_map.93 = (f32[48,128,128]{2,1,0:T(8,128)}, f32[24,128,128]{2,1,0:T(8,128)S(1)}) custom-call(s32[576]{0:T(1024)S(1)} %get-tuple-element.30.rows_ref, s32[576]{0:T(1024)S(1)} %get-tuple-element.31.cols_ref, s32[1]{0:T(128)} %bitcast.56.cnt_ref, bf16[576,128,128]{2,1,0:T(8,128)(2,1)} %bitcast.58, bf16[48,128,128]{2,1,0:T(8,128)(2,1)S(1)} %pad_maximum_fusion.rin_ref, ...), custom_call_target="tpu_custom_call" | custom-call | flops 4831838208 | bytes 25952256 | tf_op jit(solution)/shard_map/pallas_call | solution.py:87
  103.2 1.7 slice.83
  104.9 2.9 collective-permute-start.10
  108.0 23.1 %collective-permute-done.10 = f32[24,128,128]{2,1,0:T(8,128)S(1)} collective-permute-done((f32[24,128,128]{2,1,0:T(8,128)S(1)}, f32[24,128,128]{2,1,0:T(8,128)S(1)}, u32[]{:S(2)}, u32[]{:S(2)}) %collective-permute-start.10) | collective-permute-done | bytes 1572896 | tf_op jit(solution)/shard_map/ppermute | solution.py:130
  131.3 3.8 %collective-permute-start.11 = (f32[12,128,128]{2,1,0:T(8,128)S(1)}, f32[12,128,128]{2,1,0:T(8,128)S(1)}, u32[]{:S(2)}, u32[]{:S(2)}) collective-permute-start(f32[12,128,128]{2,1,0:T(8,128)S(1)} %slice.107), channel_id=1, source_target_pairs={{0,2},{1,3},{2,0},{3,1},{4,6},{5,7},{6,4},{7,5},{8,10},{9,11},{10,... | collective-permute-start | bytes 2359304 | tf_op jit(solution)/shard_map/ppermute | solution.py:130
  135.3 9.7 %collective-permute-done.11 = f32[12,128,128]{2,1,0:T(8,128)S(1)} collective-permute-done((f32[12,128,128]{2,1,0:T(8,128)S(1)}, f32[12,128,128]{2,1,0:T(8,128)S(1)}, u32[]{:S(2)}, u32[]{:S(2)}) %collective-permute-start.11) | collective-permute-done | bytes 786464 | tf_op jit(solution)/shard_map/ppermute | solution.py:130
  145.2 11.8 %collective-permute-start.12 = (f32[6,128,128]{2,1,0:T(8,128)S(1)}, f32[6,128,128]{2,1,0:T(8,128)S(1)}, u32[]{:S(2)}, u32[]{:S(2)}) collective-permute-start(f32[6,128,128]{2,1,0:T(8,128)S(1)} %slice.109), channel_id=1, source_target_pairs={{0,4},{1,5},{2,6},{3,7},{4,0},{5,1},{6,2},{7,3},{8,12},{9,13},{10,... | collective-permute-start | bytes 1179656 | tf_op jit(solution)/shard_map/ppermute | solution.py:130
  157.0 15.4 %collective-permute-done.12 = f32[6,128,128]{2,1,0:T(8,128)S(1)} collective-permute-done((f32[6,128,128]{2,1,0:T(8,128)S(1)}, f32[6,128,128]{2,1,0:T(8,128)S(1)}, u32[]{:S(2)}, u32[]{:S(2)}) %collective-permute-start.12) | collective-permute-done | bytes 393248 | tf_op jit(solution)/shard_map/ppermute | solution.py:130
  172.6 0.3 convolution_multiply_fusion.2
  173.0 1.2 collective-permute-done.15
  174.2 3.9 %collective-permute-done.16 = f32[64,64]{0,1:T(8,128)S(1)} collective-permute-done((f32[64,64]{0,1:T(8,128)S(1)}, f32[64,64]{0,1:T(8,128)S(1)}, u32[]{:S(2)}, u32[]{:S(2)}) %collective-permute-start.16) | collective-permute-done | bytes 16416 | tf_op jit(solution)/shard_map/ppermute | solution.py:140
  178.1 3.9 %collective-permute-done.17 = f32[64,64]{0,1:T(8,128)S(1)} collective-permute-done((f32[64,64]{0,1:T(8,128)S(1)}, f32[64,64]{0,1:T(8,128)S(1)}, u32[]{:S(2)}, u32[]{:S(2)}) %collective-permute-start.17) | collective-permute-done | bytes 16416 | tf_op jit(solution)/shard_map/ppermute | solution.py:140
  182.0 3.9 %collective-permute-done.18 = f32[64,64]{0,1:T(8,128)S(1)} collective-permute-done((f32[64,64]{0,1:T(8,128)S(1)}, f32[64,64]{0,1:T(8,128)S(1)}, u32[]{:S(2)}, u32[]{:S(2)}) %collective-permute-start.18) | collective-permute-done | bytes 16416 | tf_op jit(solution)/shard_map/ppermute | solution.py:140
  185.9 1.5 collective-permute-start.19
  187.4 4.7 %collective-permute-done.19 = f32[64,64]{0,1:T(8,128)S(1)} collective-permute-done((f32[64,64]{0,1:T(8,128)S(1)}, f32[64,64]{0,1:T(8,128)S(1)}, u32[]{:S(2)}, u32[]{:S(2)}) %collective-permute-start.19) | collective-permute-done | bytes 16416 | tf_op jit(solution)/shard_map/ppermute | solution.py:140
  192.1 0.3 convolution_subtract_fusion
  192.5 0.6 collective-permute-start.20
  193.1 4.0 %collective-permute-done.23 = bf16[6,64,128]{2,1,0:T(8,128)(2,1)S(1)} collective-permute-done((bf16[6,64,128]{2,1,0:T(8,128)(2,1)S(1)}, bf16[6,64,128]{2,1,0:T(8,128)(2,1)S(1)}, u32[]{:S(2)}, u32[]{:S(2)}) %collective-permute-start.23) | collective-permute-done | bytes 98336 | tf_op jit(solution)/shard_map/ppermute | solution.py:119
  197.1 1.8 collective-permute-done.20
  199.1 1.3 collective-permute-done.24
  200.5 5.9 %collective-permute-done.21 = bf16[12,64,128]{2,1,0:T(8,128)(2,1)S(1)} collective-permute-done((bf16[12,64,128]{2,1,0:T(8,128)(2,1)S(1)}, bf16[12,64,128]{2,1,0:T(8,128)(2,1)S(1)}, u32[]{:S(2)}, u32[]{:S(2)}) %collective-permute-start.21) | collective-permute-done | bytes 196640 | tf_op jit(solution)/shard_map/ppermute | solution.py:119
  206.5 10.7 %collective-permute-done.22 = bf16[24,64,128]{2,1,0:T(8,128)(2,1)S(1)} collective-permute-done((bf16[24,64,128]{2,1,0:T(8,128)(2,1)S(1)}, bf16[24,64,128]{2,1,0:T(8,128)(2,1)S(1)}, u32[]{:S(2)}, u32[]{:S(2)}) %collective-permute-start.22) | collective-permute-done | bytes 393248 | tf_op jit(solution)/shard_map/ppermute | solution.py:119
  217.3 24.4 %shard_map.94 = (f32[48,64,128]{2,1,0:T(8,128)S(1)}, f32[24,64,128]{2,1,0:T(8,128)S(1)}) custom-call(s32[576]{0:T(1024)S(1)} %get-tuple-element.30.rows_ref, s32[576]{0:T(1024)S(1)} %get-tuple-element.31.cols_ref, s32[1]{0:T(128)} %bitcast.57.cnt_ref, bf16[576,128,128]{2,1,0:T(8,128)(2,1)} %bitcast.59, bf16[48,64,128]{2,1,0:T(8,128)(2,1)S(1)} %pad_maximum_fusion.3.rin_ref, ...), custom_call_target="tpu_custom_call" | custom-call | flops 2415919104 | bytes 22413312 | tf_op jit(solution)/shard_map/pallas_call | solution.py:87
  241.7 1.8 collective-permute-start.25
  243.6 10.2 %collective-permute-done.25 = f32[24,64,128]{2,1,0:T(8,128)S(1)} collective-permute-done((f32[24,64,128]{2,1,0:T(8,128)S(1)}, f32[24,64,128]{2,1,0:T(8,128)S(1)}, u32[]{:S(2)}, u32[]{:S(2)}) %collective-permute-start.25) | collective-permute-done | bytes 786464 | tf_op jit(solution)/shard_map/ppermute | solution.py:130
  253.9 2.5 collective-permute-start.26
  256.6 5.6 %collective-permute-done.26 = f32[12,64,128]{2,1,0:T(8,128)S(1)} collective-permute-done((f32[12,64,128]{2,1,0:T(8,128)S(1)}, f32[12,64,128]{2,1,0:T(8,128)S(1)}, u32[]{:S(2)}, u32[]{:S(2)}) %collective-permute-start.26) | collective-permute-done | bytes 393248 | tf_op jit(solution)/shard_map/ppermute | solution.py:130
  262.3 4.8 %collective-permute-start.27 = (f32[6,64,128]{2,1,0:T(8,128)S(1)}, f32[6,64,128]{2,1,0:T(8,128)S(1)}, u32[]{:S(2)}, u32[]{:S(2)}) collective-permute-start(f32[6,64,128]{2,1,0:T(8,128)S(1)} %slice.116), channel_id=1, source_target_pairs={{0,4},{1,5},{2,6},{3,7},{4,0},{5,1},{6,2},{7,3},{8,12},{9,13},{10,... | collective-permute-start | bytes 589832 | tf_op jit(solution)/shard_map/ppermute | solution.py:130
  267.2 0.7 fusion
  267.9 4.8 %collective-permute-done.27 = f32[6,64,128]{2,1,0:T(8,128)S(1)} collective-permute-done((f32[6,64,128]{2,1,0:T(8,128)S(1)}, f32[6,64,128]{2,1,0:T(8,128)S(1)}, u32[]{:S(2)}, u32[]{:S(2)}) %collective-permute-start.27) | collective-permute-done | bytes 196640 | tf_op jit(solution)/shard_map/ppermute | solution.py:130
  272.8 0.7 fusion.1
  273.5 1.7 collective-permute-done.30
  275.4 11.1 %collective-permute-done.31 = f32[2,192,192]{2,1,0:T(8,128)S(1)} collective-permute-done((f32[2,192,192]{2,1,0:T(8,128)S(1)}, f32[2,192,192]{2,1,0:T(8,128)S(1)}, u32[]{:S(2)}, u32[]{:S(2)}) %collective-permute-start.31) | collective-permute-done | bytes 294944 | tf_op jit(solution)/shard_map/ppermute | solution.py:140
  286.7 10.3 %collective-permute-done.32 = f32[2,192,192]{2,1,0:T(8,128)S(1)} collective-permute-done((f32[2,192,192]{2,1,0:T(8,128)S(1)}, f32[2,192,192]{2,1,0:T(8,128)S(1)}, u32[]{:S(2)}, u32[]{:S(2)}) %collective-permute-start.32) | collective-permute-done | bytes 294944 | tf_op jit(solution)/shard_map/ppermute | solution.py:140
  297.2 9.4 %collective-permute-done.33 = f32[2,192,192]{2,1,0:T(8,128)S(1)} collective-permute-done((f32[2,192,192]{2,1,0:T(8,128)S(1)}, f32[2,192,192]{2,1,0:T(8,128)S(1)}, u32[]{:S(2)}, u32[]{:S(2)}) %collective-permute-start.33) | collective-permute-done | bytes 294944 | tf_op jit(solution)/shard_map/ppermute | solution.py:140
  306.6 1.5 collective-permute-start.34
  308.1 16.3 %collective-permute-done.34 = f32[2,192,192]{2,1,0:T(8,128)S(1)} collective-permute-done((f32[2,192,192]{2,1,0:T(8,128)S(1)}, f32[2,192,192]{2,1,0:T(8,128)S(1)}, u32[]{:S(2)}, u32[]{:S(2)}) %collective-permute-start.34) | collective-permute-done | bytes 294944 | tf_op jit(solution)/shard_map/ppermute | solution.py:140
  324.5 0.8 slice_bitcast_fusion
  (88 shorter events, 4.0 us)
Async XLA Ops:
  0.6 0.9 copy-start
  1.9 1.4 collective-permute-start
  3.3 4.8 %collective-permute-start.1 = (f32[64,64]{0,1:T(8,128)S(1)}, f32[64,64]{0,1:T(8,128)S(1)}, u32[]{:S(2)}, u32[]{:S(2)}) collective-permute-start(f32[64,64]{0,1:T(8,128)S(1)} %add.114), channel_id=1, source_target_pairs={{0,16},{8,24},{16,0},{24,8},{1,17},{9,25},{17,1},{25,9},{2,18},{10... | collective-permute-start | bytes 49160 | tf_op jit(solution)/shard_map/ppermute | solution.py:140
  8.0 3.9 %collective-permute-start.2 = (f32[64,64]{0,1:T(8,128)S(1)}, f32[64,64]{0,1:T(8,128)S(1)}, u32[]{:S(2)}, u32[]{:S(2)}) collective-permute-start(f32[64,64]{0,1:T(8,128)S(1)} %add.115), channel_id=1, source_target_pairs={{0,1},{1,0},{2,3},{3,2},{4,5},{5,4},{6,7},{7,6},{8,9},{9,8},{10,11... | collective-permute-start | bytes 49160 | tf_op jit(solution)/shard_map/ppermute | solution.py:140
  11.9 4.0 %collective-permute-start.3 = (f32[64,64]{0,1:T(8,128)S(1)}, f32[64,64]{0,1:T(8,128)S(1)}, u32[]{:S(2)}, u32[]{:S(2)}) collective-permute-start(f32[64,64]{0,1:T(8,128)S(1)} %add.116), channel_id=1, source_target_pairs={{0,2},{1,3},{2,0},{3,1},{4,6},{5,7},{6,4},{7,5},{8,10},{9,11},{10,... | collective-permute-start | bytes 49160 | tf_op jit(solution)/shard_map/ppermute | solution.py:140
  15.9 4.9 %collective-permute-start.4 = (f32[64,64]{0,1:T(8,128)S(1)}, f32[64,64]{0,1:T(8,128)S(1)}, u32[]{:S(2)}, u32[]{:S(2)}) collective-permute-start(f32[64,64]{0,1:T(8,128)S(1)} %add.117), channel_id=1, source_target_pairs={{0,4},{1,5},{2,6},{3,7},{4,0},{5,1},{6,2},{7,3},{8,12},{9,13},{10,... | collective-permute-start | bytes 49160 | tf_op jit(solution)/shard_map/ppermute | solution.py:140
  33.8 5.7 %collective-permute-start.8 = (bf16[6,128,128]{2,1,0:T(8,128)(2,1)S(1)}, bf16[6,128,128]{2,1,0:T(8,128)(2,1)S(1)}, u32[]{:S(2)}, u32[]{:S(2)}) collective-permute-start(bf16[6,128,128]{2,1,0:T(8,128)(2,1)S(1)} %bitcast.60), channel_id=1, source_target_pairs={{0,16},{8,24},{16,0},{24,8},{1,17},{9,25},{17,1},{25,9},{2,18},{10... | collective-permute-start | bytes 589832 | tf_op jit(solution)/shard_map/ppermute | solution.py:119
  35.7 8.7 %collective-permute-start.5 = (bf16[6,128,128]{2,1,0:T(8,128)(2,1)S(1)}, bf16[6,128,128]{2,1,0:T(8,128)(2,1)S(1)}, u32[]{:S(2)}, u32[]{:S(2)}) collective-permute-start(bf16[6,128,128]{2,1,0:T(8,128)(2,1)S(1)} %bitcast.61), channel_id=1, source_target_pairs={{0,4},{1,5},{2,6},{3,7},{4,0},{5,1},{6,2},{7,3},{8,12},{9,13},{10,... | collective-permute-start | bytes 589832 | tf_op jit(solution)/shard_map/ppermute | solution.py:119
  44.5 14.0 %copy-start.5 = (s32[1,1,576]{2,1,0:T(1,128)S(1)}, s32[1,1,576]{2,1,0:T(1,128)}, u32[]{:S(2)}) copy-start(s32[1,1,576]{2,1,0:T(1,128)} %param.8) | copy-start | bytes 6916
  44.5 14.0 %copy-start.6 = (s32[1,1,576]{2,1,0:T(1,128)S(1)}, s32[1,1,576]{2,1,0:T(1,128)}, u32[]{:S(2)}) copy-start(s32[1,1,576]{2,1,0:T(1,128)} %param.9) | copy-start | bytes 6916
  44.5 1.8 collective-permute-start.9
  44.6 11.5 %collective-permute-start.6 = (bf16[12,128,128]{2,1,0:T(8,128)(2,1)S(1)}, bf16[12,128,128]{2,1,0:T(8,128)(2,1)S(1)}, u32[]{:S(2)}, u32[]{:S(2)}) collective-permute-start(bf16[12,128,128]{2,1,0:T(8,128)(2,1)S(1)} %get-tuple-element.23), channel_id=1, source_target_pairs={{0,2},{1,3},{2,0},{3,1},{4,6},{5,7},{6,4},{7,5},{8,10},{9,11},{10,... | collective-permute-start | bytes 1179656 | tf_op jit(solution)/shard_map/ppermute | solution.py:119
  56.2 19.2 %collective-permute-start.7 = (bf16[24,128,128]{2,1,0:T(8,128)(2,1)S(1)}, bf16[24,128,128]{2,1,0:T(8,128)(2,1)S(1)}, u32[]{:S(2)}, u32[]{:S(2)}) collective-permute-start(bf16[24,128,128]{2,1,0:T(8,128)(2,1)S(1)} %get-tuple-element.21), channel_id=1, source_target_pairs={{0,1},{1,0},{2,3},{3,2},{4,5},{5,4},{6,7},{7,6},{8,9},{9,8},{10,11... | collective-permute-start | bytes 2359304 | tf_op jit(solution)/shard_map/ppermute | solution.py:119
  103.2 27.9 %copy-start.1 = (f32[48,128,128]{2,1,0:T(8,128)S(1)}, f32[48,128,128]{2,1,0:T(8,128)}, u32[]{:S(2)}) copy-start(f32[48,128,128]{2,1,0:T(8,128)} %get-tuple-element.8) | copy-start | bytes 9437188
  104.9 26.2 %collective-permute-start.10 = (f32[24,128,128]{2,1,0:T(8,128)S(1)}, f32[24,128,128]{2,1,0:T(8,128)S(1)}, u32[]{:S(2)}, u32[]{:S(2)}) collective-permute-start(f32[24,128,128]{2,1,0:T(8,128)S(1)} %slice.83), channel_id=1, source_target_pairs={{0,1},{1,0},{2,3},{3,2},{4,5},{5,4},{6,7},{7,6},{8,9},{9,8},{10,11... | collective-permute-start | bytes 4718600 | tf_op jit(solution)/shard_map/ppermute | solution.py:130
  107.9 27.2 %collective-permute-start.13 = (f32[12,128,128]{2,1,0:T(8,128)S(1)}, f32[12,128,128]{2,1,0:T(8,128)S(1)}, u32[]{:S(2)}, u32[]{:S(2)}) collective-permute-start(f32[12,128,128]{2,1,0:T(8,128)S(1)} %slice.89), channel_id=1, source_target_pairs={{0,8},{8,0},{16,24},{24,16},{1,9},{9,1},{17,25},{25,17},{2,10},{10... | collective-permute-start | bytes 2359304 | tf_op jit(solution)/shard_map/ppermute | solution.py:130
  131.3 13.7 %collective-permute-start.11 = (f32[12,128,128]{2,1,0:T(8,128)S(1)}, f32[12,128,128]{2,1,0:T(8,128)S(1)}, u32[]{:S(2)}, u32[]{:S(2)}) collective-permute-start(f32[12,128,128]{2,1,0:T(8,128)S(1)} %slice.107), channel_id=1, source_target_pairs={{0,2},{1,3},{2,0},{3,1},{4,6},{5,7},{6,4},{7,5},{8,10},{9,11},{10,... | collective-permute-start | bytes 2359304 | tf_op jit(solution)/shard_map/ppermute | solution.py:130
  135.2 21.8 %collective-permute-start.14 = (f32[6,128,128]{2,1,0:T(8,128)S(1)}, f32[6,128,128]{2,1,0:T(8,128)S(1)}, u32[]{:S(2)}, u32[]{:S(2)}) collective-permute-start(f32[6,128,128]{2,1,0:T(8,128)S(1)} %slice.111), channel_id=1, source_target_pairs={{0,16},{8,24},{16,0},{24,8},{1,17},{9,25},{17,1},{25,9},{2,18},{10... | collective-permute-start | bytes 1179656 | tf_op jit(solution)/shard_map/ppermute | solution.py:130
  145.2 27.2 %collective-permute-start.12 = (f32[6,128,128]{2,1,0:T(8,128)S(1)}, f32[6,128,128]{2,1,0:T(8,128)S(1)}, u32[]{:S(2)}, u32[]{:S(2)}) collective-permute-start(f32[6,128,128]{2,1,0:T(8,128)S(1)} %slice.109), channel_id=1, source_target_pairs={{0,4},{1,5},{2,6},{3,7},{4,0},{5,1},{6,2},{7,3},{8,12},{9,13},{10,... | collective-permute-start | bytes 1179656 | tf_op jit(solution)/shard_map/ppermute | solution.py:130
  172.9 1.3 collective-permute-start.15
  174.2 3.9 %collective-permute-start.16 = (f32[64,64]{0,1:T(8,128)S(1)}, f32[64,64]{0,1:T(8,128)S(1)}, u32[]{:S(2)}, u32[]{:S(2)}) collective-permute-start(f32[64,64]{0,1:T(8,128)S(1)} %add.126), channel_id=1, source_target_pairs={{0,16},{8,24},{16,0},{24,8},{1,17},{9,25},{17,1},{25,9},{2,18},{10... | collective-permute-start | bytes 49160 | tf_op jit(solution)/shard_map/ppermute | solution.py:140
  178.1 3.9 %collective-permute-start.17 = (f32[64,64]{0,1:T(8,128)S(1)}, f32[64,64]{0,1:T(8,128)S(1)}, u32[]{:S(2)}, u32[]{:S(2)}) collective-permute-start(f32[64,64]{0,1:T(8,128)S(1)} %add.127), channel_id=1, source_target_pairs={{0,1},{1,0},{2,3},{3,2},{4,5},{5,4},{6,7},{7,6},{8,9},{9,8},{10,11... | collective-permute-start | bytes 49160 | tf_op jit(solution)/shard_map/ppermute | solution.py:140
  182.0 3.9 %collective-permute-start.18 = (f32[64,64]{0,1:T(8,128)S(1)}, f32[64,64]{0,1:T(8,128)S(1)}, u32[]{:S(2)}, u32[]{:S(2)}) collective-permute-start(f32[64,64]{0,1:T(8,128)S(1)} %add.128), channel_id=1, source_target_pairs={{0,2},{1,3},{2,0},{3,1},{4,6},{5,7},{6,4},{7,5},{8,10},{9,11},{10,... | collective-permute-start | bytes 49160 | tf_op jit(solution)/shard_map/ppermute | solution.py:140
  185.9 6.1 %collective-permute-start.19 = (f32[64,64]{0,1:T(8,128)S(1)}, f32[64,64]{0,1:T(8,128)S(1)}, u32[]{:S(2)}, u32[]{:S(2)}) collective-permute-start(f32[64,64]{0,1:T(8,128)S(1)} %add.129), channel_id=1, source_target_pairs={{0,4},{1,5},{2,6},{3,7},{4,0},{5,1},{6,2},{7,3},{8,12},{9,13},{10,... | collective-permute-start | bytes 49160 | tf_op jit(solution)/shard_map/ppermute | solution.py:140
  192.4 80.4 %copy-start.2 = (f32[64,768]{1,0:T(8,128)}, f32[64,768]{1,0:T(8,128)S(1)}, u32[]{:S(2)}) copy-start(f32[64,768]{1,0:T(8,128)S(1)} %convolution_subtract_fusion) | copy-start | bytes 589828
  192.4 4.7 %collective-permute-start.23 = (bf16[6,64,128]{2,1,0:T(8,128)(2,1)S(1)}, bf16[6,64,128]{2,1,0:T(8,128)(2,1)S(1)}, u32[]{:S(2)}, u32[]{:S(2)}) collective-permute-start(bf16[6,64,128]{2,1,0:T(8,128)(2,1)S(1)} %bitcast_bitcast_fusion), channel_id=1, source_target_pairs={{0,16},{8,24},{16,0},{24,8},{1,17},{9,25},{17,1},{25,9},{2,18},{10... | collective-permute-start | bytes 294920 | tf_op jit(solution)/shard_map/ppermute | solution.py:119
  192.5 6.4 %collective-permute-start.20 = (bf16[6,64,128]{2,1,0:T(8,128)(2,1)S(1)}, bf16[6,64,128]{2,1,0:T(8,128)(2,1)S(1)}, u32[]{:S(2)}, u32[]{:S(2)}) collective-permute-start(bf16[6,64,128]{2,1,0:T(8,128)(2,1)S(1)} %bitcast_bitcast_fusion), channel_id=1, source_target_pairs={{0,4},{1,5},{2,6},{3,7},{4,0},{5,1},{6,2},{7,3},{8,12},{9,13},{10,... | collective-permute-start | bytes 294920 | tf_op jit(solution)/shard_map/ppermute | solution.py:119
  199.0 1.5 collective-permute-start.24
  199.0 7.3 %collective-permute-start.21 = (bf16[12,64,128]{2,1,0:T(8,128)(2,1)S(1)}, bf16[12,64,128]{2,1,0:T(8,128)(2,1)S(1)}, u32[]{:S(2)}, u32[]{:S(2)}) collective-permute-start(bf16[12,64,128]{2,1,0:T(8,128)(2,1)S(1)} %get-tuple-element.27), channel_id=1, source_target_pairs={{0,2},{1,3},{2,0},{3,1},{4,6},{5,7},{6,4},{7,5},{8,10},{9,11},{10,... | collective-permute-start | bytes 589832 | tf_op jit(solution)/shard_map/ppermute | solution.py:119
  206.4 10.7 %collective-permute-start.22 = (bf16[24,64,128]{2,1,0:T(8,128)(2,1)S(1)}, bf16[24,64,128]{2,1,0:T(8,128)(2,1)S(1)}, u32[]{:S(2)}, u32[]{:S(2)}) collective-permute-start(bf16[24,64,128]{2,1,0:T(8,128)(2,1)S(1)} %get-tuple-element.25), channel_id=1, source_target_pairs={{0,1},{1,0},{2,3},{3,2},{4,5},{5,4},{6,7},{7,6},{8,9},{9,8},{10,11... | collective-permute-start | bytes 1179656 | tf_op jit(solution)/shard_map/ppermute | solution.py:119
  241.7 12.1 %collective-permute-start.25 = (f32[24,64,128]{2,1,0:T(8,128)S(1)}, f32[24,64,128]{2,1,0:T(8,128)S(1)}, u32[]{:S(2)}, u32[]{:S(2)}) collective-permute-start(f32[24,64,128]{2,1,0:T(8,128)S(1)} %slice.95), channel_id=1, source_target_pairs={{0,1},{1,0},{2,3},{3,2},{4,5},{5,4},{6,7},{7,6},{8,9},{9,8},{10,11... | collective-permute-start | bytes 2359304 | tf_op jit(solution)/shard_map/ppermute | solution.py:130
  243.5 12.9 %collective-permute-start.28 = (f32[12,64,128]{2,1,0:T(8,128)S(1)}, f32[12,64,128]{2,1,0:T(8,128)S(1)}, u32[]{:S(2)}, u32[]{:S(2)}) collective-permute-start(f32[12,64,128]{2,1,0:T(8,128)S(1)} %slice.101), channel_id=1, source_target_pairs={{0,8},{8,0},{16,24},{24,16},{1,9},{9,1},{17,25},{25,17},{2,10},{10... | collective-permute-start | bytes 1179656 | tf_op jit(solution)/shard_map/ppermute | solution.py:130
  253.9 8.3 %collective-permute-start.26 = (f32[12,64,128]{2,1,0:T(8,128)S(1)}, f32[12,64,128]{2,1,0:T(8,128)S(1)}, u32[]{:S(2)}, u32[]{:S(2)}) collective-permute-start(f32[12,64,128]{2,1,0:T(8,128)S(1)} %slice.114), channel_id=1, source_target_pairs={{0,2},{1,3},{2,0},{3,1},{4,6},{5,7},{6,4},{7,5},{8,10},{9,11},{10,... | collective-permute-start | bytes 1179656 | tf_op jit(solution)/shard_map/ppermute | solution.py:130
  256.5 10.7 %copy-start.3 = (f32[64,768]{1,0:T(8,128)S(1)}, f32[64,768]{1,0:T(8,128)}, u32[]{:S(2)}) copy-start(f32[64,768]{1,0:T(8,128)} %param.7) | copy-start | bytes 589828
  256.5 11.3 %collective-permute-start.29 = (f32[6,64,128]{2,1,0:T(8,128)S(1)}, f32[6,64,128]{2,1,0:T(8,128)S(1)}, u32[]{:S(2)}, u32[]{:S(2)}) collective-permute-start(f32[6,64,128]{2,1,0:T(8,128)S(1)} %slice.118), channel_id=1, source_target_pairs={{0,16},{8,24},{16,0},{24,8},{1,17},{9,25},{17,1},{25,9},{2,18},{10... | collective-permute-start | bytes 589832 | tf_op jit(solution)/shard_map/ppermute | solution.py:130
  262.3 10.4 %collective-permute-start.27 = (f32[6,64,128]{2,1,0:T(8,128)S(1)}, f32[6,64,128]{2,1,0:T(8,128)S(1)}, u32[]{:S(2)}, u32[]{:S(2)}) collective-permute-start(f32[6,64,128]{2,1,0:T(8,128)S(1)} %slice.116), channel_id=1, source_target_pairs={{0,4},{1,5},{2,6},{3,7},{4,0},{5,1},{6,2},{7,3},{8,12},{9,13},{10,... | collective-permute-start | bytes 589832 | tf_op jit(solution)/shard_map/ppermute | solution.py:130
  272.7 2.6 copy-start.4
  273.5 1.8 collective-permute-start.30
  275.3 11.2 %collective-permute-start.31 = (f32[2,192,192]{2,1,0:T(8,128)S(1)}, f32[2,192,192]{2,1,0:T(8,128)S(1)}, u32[]{:S(2)}, u32[]{:S(2)}) collective-permute-start(f32[2,192,192]{2,1,0:T(8,128)S(1)} %fusion.26), channel_id=1, source_target_pairs={{0,16},{8,24},{16,0},{24,8},{1,17},{9,25},{17,1},{25,9},{2,18},{10... | collective-permute-start | bytes 884744 | tf_op jit(solution)/shard_map/ppermute | solution.py:140
  286.6 10.4 %collective-permute-start.32 = (f32[2,192,192]{2,1,0:T(8,128)S(1)}, f32[2,192,192]{2,1,0:T(8,128)S(1)}, u32[]{:S(2)}, u32[]{:S(2)}) collective-permute-start(f32[2,192,192]{2,1,0:T(8,128)S(1)} %fusion.33), channel_id=1, source_target_pairs={{0,1},{1,0},{2,3},{3,2},{4,5},{5,4},{6,7},{7,6},{8,9},{9,8},{10,11... | collective-permute-start | bytes 884744 | tf_op jit(solution)/shard_map/ppermute | solution.py:140
  297.1 9.5 %collective-permute-start.33 = (f32[2,192,192]{2,1,0:T(8,128)S(1)}, f32[2,192,192]{2,1,0:T(8,128)S(1)}, u32[]{:S(2)}, u32[]{:S(2)}) collective-permute-start(f32[2,192,192]{2,1,0:T(8,128)S(1)} %add.139), channel_id=1, source_target_pairs={{0,2},{1,3},{2,0},{3,1},{4,6},{5,7},{6,4},{7,5},{8,10},{9,11},{10,... | collective-permute-start | bytes 884744 | tf_op jit(solution)/shard_map/ppermute | solution.py:140
  306.6 17.9 %collective-permute-start.34 = (f32[2,192,192]{2,1,0:T(8,128)S(1)}, f32[2,192,192]{2,1,0:T(8,128)S(1)}, u32[]{:S(2)}, u32[]{:S(2)}) collective-permute-start(f32[2,192,192]{2,1,0:T(8,128)S(1)} %add.140), channel_id=1, source_target_pairs={{0,4},{1,5},{2,6},{3,7},{4,0},{5,1},{6,2},{7,3},{8,12},{9,13},{10,... | collective-permute-start | bytes 884744 | tf_op jit(solution)/shard_map/ppermute | solution.py:140

commit v4 on v3

--- a/solution.py
+++ b/solution.py
@@ -11,14 +11,19 @@
 UNROLL = 32
 
 
-def tile_kernel(rows_ref, cols_ref, cnt_ref, vals_ref, rin_ref, cin_ref, rout_ref, cout_ref):
+def tile_kernel(rows_ref, cols_ref, cnt_ref, vals_ref, rin_ref, cin_ref, *out_refs):
     g = pl.program_id(0)
     group = vals_ref.shape[0]
+    row_outs = out_refs[0::2]
+    col_outs = out_refs[1::2]
+    edges = [0]
+    for ref in row_outs:
+        edges.append(edges[-1] + ref.shape[1])
 
     @pl.when(g == 0)
     def _():
-        rout_ref[...] = jnp.zeros_like(rout_ref)
-        cout_ref[...] = jnp.zeros_like(cout_ref)
+        for ref in out_refs:
+            ref[...] = jnp.zeros_like(ref)
 
     base = g * group
     live = cnt_ref[0]
@@ -32,8 +37,9 @@
             cin_ref[b], v, (((1,), (1,)), ((), ())), preferred_element_type=jnp.float32
         )
         bwd = jnp.dot(rin_ref[a], v, preferred_element_type=jnp.float32)
-        rout_ref[a] += fwd
-        cout_ref[b] += bwd
+        for k in range(len(row_outs)):
+            row_outs[k][a] += fwd[edges[k]:edges[k + 1]]
+            col_outs[k][b] += bwd[edges[k]:edges[k + 1]]
 
     def full_body(t, carry):
         tile_step(t)
@@ -55,7 +61,7 @@
         lax.fori_loop(0, group, part_body, 0)
 
 
-def tile_products(row_blocks, col_blocks, tile_rows, tile_cols, live_count, tile_vals):
+def tile_products(row_blocks, col_blocks, tile_rows, tile_cols, live_count, tile_vals, widths):
     n_rows, width, tile = row_blocks.shape
     n_cols = col_blocks.shape[0]
     slots = tile_vals.shape[0]
@@ -75,8 +81,9 @@
             pl.BlockSpec((n_cols, width, tile), lambda g, r, c, n: (0, 0, 0)),
         ],
         out_specs=[
-            pl.BlockSpec((n_rows, width, tile), lambda g, r, c, n: (0, 0, 0)),
-            pl.BlockSpec((n_cols, width, tile), lambda g, r, c, n: (0, 0, 0)),
+            pl.BlockSpec((n, w, tile), lambda g, r, c, k: (0, 0, 0))
+            for w in widths
+            for n in (n_rows, n_cols)
         ],
     )
     flops = 4 * slots * width * tile * tile
@@ -88,8 +95,7 @@
         tile_kernel,
         grid_spec=grid_spec,
         out_shape=[
-            jax.ShapeDtypeStruct((n_rows, width, tile), jnp.float32),
-            jax.ShapeDtypeStruct((n_cols, width, tile), jnp.float32),
+            jax.ShapeDtypeStruct((n, w, tile), jnp.float32) for w in widths for n in (n_rows, n_cols)
         ],
         compiler_params=pltpu.CompilerParams(
             dimension_semantics=("arbitrary",), vmem_limit_bytes=48 * 1024 * 1024
@@ -150,19 +156,23 @@
     return reversed_bits(me ^ owner, bits) * blocks_each + index % blocks_each
 
 
-def apply_graph(vectors, tile_rows, tile_cols, live_count, tile_vals):
+def to_blocks(vectors, tile):
     vec_width, local_nodes = vectors.shape
-    tile = tile_vals.shape[-1]
-    blocks_each = local_nodes // tile
-    local = vectors.reshape(vec_width, blocks_each, tile).transpose(1, 0, 2)
-    row_blocks = gather_blocks(local, "col")
-    col_blocks = gather_blocks(local, "row")
-    row_totals, col_totals = tile_products(
-        row_blocks, col_blocks, tile_rows, tile_cols, live_count, tile_vals
-    )
-    own_rows = scatter_sum(row_totals, "col")
-    own_cols = scatter_sum(col_totals, "row")
-    return (own_rows + own_cols).transpose(1, 0, 2).reshape(vec_width, local_nodes)
+    return vectors.reshape(vec_width, local_nodes // tile, tile).transpose(1, 0, 2)
+
+
+def from_blocks(blocks):
+    count, vec_width, tile = blocks.shape
+    return blocks.transpose(1, 0, 2).reshape(vec_width, count * tile)
+
+
+def gathered(vectors, tile):
+    local = to_blocks(vectors, tile)
+    return gather_blocks(local, "col"), gather_blocks(local, "row")
+
+
+def owned(row_totals, col_totals):
+    return from_blocks(scatter_sum(row_totals, "col") + scatter_sum(col_totals, "row"))
 
 
 def per_device(block_x, block_p, tile_rows, tile_cols, tile_count, tile_vals):
@@ -184,22 +194,37 @@
     gram_x = all_sum(product(block_x, block_x))
     cholesky_factor = jnp.linalg.cholesky(gram_x)
     orthonormal = lax.linalg.triangular_solve(cholesky_factor, block_x, left_side=True, lower=True)
-    ortho_low = orthonormal.astype(jnp.bfloat16)
-    dir_low = block_p.astype(jnp.bfloat16)
-    both_images = apply_graph(
-        jnp.concatenate([ortho_low, dir_low], axis=0), slot_rows, slot_cols, live_count, slot_vals
-    )
-    image_x = both_images[:width_k]
-    image_p = both_images[width_k:]
+    tile = tile_vals.shape[-1]
+    dir_rows, dir_cols = gathered(block_p.astype(jnp.bfloat16), tile)
+    ortho_rows, ortho_cols = gathered(orthonormal.astype(jnp.bfloat16), tile)
+    x_rows, x_cols, p_rows, p_cols = tile_products(
+        jnp.concatenate([ortho_rows, dir_rows], axis=1),
+        jnp.concatenate([ortho_cols, dir_cols], axis=1),
+        slot_rows, slot_cols, live_count, slot_vals, (width_k, block_p.shape[0]),
+    )
+    image_x = owned(x_rows, x_cols)
     rayleigh = all_sum(product(orthonormal, image_x))
     residual = image_x - jnp.dot(
         rayleigh.T, orthonormal, precision=highest, preferred_element_type=jnp.float32
     )
-    residual_low = residual.astype(jnp.bfloat16)
-    image_r = apply_graph(residual_low, slot_rows, slot_cols, live_count, slot_vals)
+    res_rows, res_cols = gathered(residual.astype(jnp.bfloat16), tile)
+    image_p = owned(p_rows, p_cols)
     basis = jnp.concatenate([orthonormal, residual, block_p], axis=0)
-    images = jnp.concatenate([image_x, image_r, image_p], axis=0)
-    gram_a, gram_b = all_sum(jnp.stack([product(basis, images), product(basis, basis)]))
+    early = all_sum(
+        jnp.concatenate(
+            [product(basis, basis), product(basis, image_x), product(basis, image_p)], axis=1
+        )
+    )
+    r_rows, r_cols = tile_products(
+        res_rows, res_cols, slot_rows, slot_cols, live_count, slot_vals, (residual.shape[0],)
+    )
+    image_r = owned(r_rows, r_cols)
+    late = all_sum(product(basis, image_r))
+    span = basis.shape[0]
+    gram_b = early[:, :span]
+    gram_a = jnp.concatenate(
+        [early[:, span:span + width_k], late, early[:, span + width_k:]], axis=1
+    )
     return (residual, image_r, gram_a, gram_b)
 
 

time: 322 us -> 269 us (0.84); the launches traced: 325 us -> 267 us
  waiting for transfers between devices: 200 us -> 129 us
  starting transfers between devices: 49.6 us -> 57.3 us
  other arithmetic: 14.8 us -> 21.3 us
    ppermute x10 -> x15, waiting for transfers between devices: 68.8 us -> 34.1 us  [scatter_sum(): lax.ppermute(held[half:], axis, exchange_pairs(size, step))]
    ppermute x10 -> x15, waiting for transfers between devices: 57.3 us -> 31.4 us  [gather_blocks(): lax.ppermute(held, axis, exchange_pairs(size, step))]
    ppermute x10 -> x15, starting transfers between devices: 7.81 us -> 19.2 us  [gather_blocks(): lax.ppermute(held, axis, exchange_pairs(size, step))]
    ppermute x15 -> x20, waiting for transfers between devices: 74 us -> 63.6 us  [all_sum(): value = value + lax.ppermute(value, axis, exchange_pairs(size, step))]
    ppermute x10 -> x15, starting transfers between devices: 28 us -> 21.3 us  [scatter_sum(): lax.ppermute(held[half:], axis, exchange_pairs(size, step))]
    concatenate x1 -> x4, other arithmetic: 0.02 us -> 5.41 us  [the longest x1 4.43 us: per_device(): jnp.concatenate([ortho_rows, dir_rows], axis=1)]
    ppermute x15 -> x20, starting transfers between devices: 13.9 us -> 16.8 us  [all_sum(): value = value + lax.ppermute(value, axis, exchange_pairs(size, step))]
  transfers between devices with their start and end apart: 35 -> 50, of which waited for: 31 -> 35; matrix products, arithmetic and copies ran while one was open for 1% -> 8% of each run, Pallas kernels for 0% -> 0%
where the time goes in v4:
time: 269 us; the launch traced here: 267 us
  waiting for transfers between devices  129 us (48%)
  starting transfers between devices  57.3 us (21%)
  Pallas kernels  51.3 us (19%)
  other arithmetic  21.3 us (8%)
  matrix products  3.82 us (1%)
    ppermute x20, waiting for transfers between devices, all_sum(): value = value + lax.ppermute(value, axis, exchange_pairs(size, step))  63.6 us
    pallas_call x2, Pallas kernels, tile_products(): pl.pallas_call(tile_kernel, grid_spec=grid_spec, out_shape=[jax.ShapeDtyp...  51.3 us
    ppermute x15, waiting for transfers between devices, scatter_sum(): lax.ppermute(held[half:], axis, exchange_pairs(size, step))  34.1 us
    ppermute x15, waiting for transfers between devices, gather_blocks(): lax.ppermute(held, axis, exchange_pairs(size, step))  31.4 us
    ppermute x15, starting transfers between devices, scatter_sum(): lax.ppermute(held[half:], axis, exchange_pairs(size, step))  21.3 us
    ppermute x15, starting transfers between devices, gather_blocks(): lax.ppermute(held, axis, exchange_pairs(size, step))  19.2 us
    ppermute x20, starting transfers between devices, all_sum(): value = value + lax.ppermute(value, axis, exchange_pairs(size, step))  16.8 us
    another operation x3, other arithmetic, per_device(): cholesky_factor = jnp.linalg.cholesky(gram_x)  6.52 us
  transfers between devices with their start and end apart: 50, of which 35 were waited for; matrix products, arithmetic and copies ran while one was open for 8% of the time, Pallas kernels for 0%

profile of v4, /device:TPU:0, one launch (start us, length us, event | category | flops | bytes accessed | tf_op | source)
XLA Modules:
  0.0 267.0 jit_solution(14026106542366759852)
XLA Ops:
  0.6 0.9 copy-done
  2.4 0.9 collective-permute-done
  3.3 2.9 %collective-permute-start.1 = (f32[64,64]{0,1:T(8,128)S(1)}, f32[64,64]{0,1:T(8,128)S(1)}, u32[]{:S(2)}, u32[]{:S(2)}) collective-permute-start(f32[64,64]{0,1:T(8,128)S(1)} %add.147), channel_id=1, source_target_pairs={{0,16},{8,24},{16,0},{24,8},{1,17},{9,25},{17,1},{25,9},{2,18},{10... | collective-permute-start | bytes 49160 | tf_op jit(solution)/shard_map/ppermute | solution.py:146
  6.1 1.9 collective-permute-done.1
  8.0 2.0 collective-permute-start.2
  10.0 0.9 bitcast_bitcast_fusion.1
  11.0 1.6 collective-permute-start.13
  12.6 2.6 collective-permute-start.8
  15.2 1.6 collective-permute-start.3
  17.5 1.6 collective-permute-done.3
  19.1 0.9 collective-permute-start.4
  20.7 3.2 %collective-permute-done.4 = f32[64,64]{0,1:T(8,128)S(1)} collective-permute-done((f32[64,64]{0,1:T(8,128)S(1)}, f32[64,64]{0,1:T(8,128)S(1)}, u32[]{:S(2)}, u32[]{:S(2)}) %collective-permute-start.4) | collective-permute-done | bytes 16416 | tf_op jit(solution)/shard_map/ppermute | solution.py:146
  24.1 5.8 %cholesky.16 = f32[64,64]{1,0:T(8,128)S(1)} custom-call(f32[64,64]{1,0:T(8,128)S(1)} %fusion.17), custom_call_target="Cholesky" | custom-call | tf_op jit(solution)/shard_map/jit(cholesky)/cholesky | solution.py:195
  31.2 4.9 %custom-call.6 = f32[1,64,64]{1,2,0:T(8,128)S(1)} custom-call(f32[1,64,64]{2,1,0:T(8,128)S(1)} %fusion.14), custom_call_target="InvertDiagBlocksLowerTriangular" | custom-call | tf_op jit(solution)/shard_map/triangular_solve | solution.py:196
  37.1 0.9 collective-permute-start.5
  38.1 1.9 collective-permute-start.9
  39.9 1.3 collective-permute-done.11
  41.3 1.5 collective-permute-done.5
  42.8 2.6 collective-permute-start.6
  45.5 0.8 collective-permute-start.10
  46.3 2.7 %collective-permute-done.6 = bf16[12,64,128]{2,1,0:T(8,128)(2,1)S(1)} collective-permute-done((bf16[12,64,128]{2,1,0:T(8,128)(2,1)S(1)}, bf16[12,64,128]{2,1,0:T(8,128)(2,1)S(1)}, u32[]{:S(2)}, u32[]{:S(2)}) %collective-permute-start.6) | collective-permute-done | bytes 196640 | tf_op jit(solution)/shard_map/ppermute | solution.py:125
  49.1 0.8 collective-permute-start.7
  51.2 0.9 collective-permute-done.14
  52.5 2.6 collective-permute-done.10
  55.1 4.2 %collective-permute-done.7 = bf16[24,64,128]{2,1,0:T(8,128)(2,1)S(1)} collective-permute-done((bf16[24,64,128]{2,1,0:T(8,128)(2,1)S(1)}, bf16[24,64,128]{2,1,0:T(8,128)(2,1)S(1)}, u32[]{:S(2)}, u32[]{:S(2)}) %collective-permute-start.7) | collective-permute-done | bytes 393248 | tf_op jit(solution)/shard_map/ppermute | solution.py:125
  59.3 4.4 %maximum_maximum_fusion.rin_ref = bf16[48,128,128]{2,1,0:T(8,128)(2,1)} fusion(bf16[24,64,128]{2,1,0:T(8,128)(2,1)S(1)} %collective-permute-done.10, bf16[12,64,128]{2,1,0:T(8,128)(2,1)S(1)} %collective-permute-done.9, bf16[6,64,128]{2,1,0:T(8,128)(2,1)S(1)} %collective-permute-done.8, bf16[6,64,128]{2,1,0:T(8,128)(2,1)S(1)} %bitcast_bitcast_fusion.1, ...), kind=kLoop, calls=%fused_computation | loop fusion | flops 12582912 | bytes 3145728 | tf_op jit(solution)/shard_map/concatenate | solution.py:201
  63.7 26.9 %shard_map.93 = (f32[48,64,128]{2,1,0:T(8,128)S(1)}, f32[24,64,128]{2,1,0:T(8,128)S(1)}, f32[48,64,128]{2,1,0:T(8,128)S(1)}, f32[24,64,128]{2,1,0:T(8,128)S(1)}) custom-call(s32[576]{0:T(1024)S(1)} %get-tuple-element.30.rows_ref, s32[576]{0:T(1024)S(1)} %get-tuple-element.31.cols_ref, s32[1]{0:T(128)} %bitcast.61.cnt_ref, bf16[576,128,128]{2,1,0:T(8,128)(2,1)} %bitcast.63, ...), custom_call_target="tpu_custom_call" | custom-call | flops 4831838208 | bytes 25952256 | tf_op jit(solution)/shard_map/pallas_call | solution.py:94
  90.7 4.3 %collective-permute-start.15 = (f32[24,64,128]{2,1,0:T(8,128)S(1)}, f32[24,64,128]{2,1,0:T(8,128)S(1)}, u32[]{:S(2)}, u32[]{:S(2)}) collective-permute-start(f32[24,64,128]{2,1,0:T(8,128)S(1)} %slice.110), channel_id=1, source_target_pairs={{0,1},{1,0},{2,3},{3,2},{4,5},{5,4},{6,7},{7,6},{8,9},{9,8},{10,11... | collective-permute-start | bytes 2359304 | tf_op jit(solution)/shard_map/ppermute | solution.py:136
  95.1 17.5 %collective-permute-done.15 = f32[24,64,128]{2,1,0:T(8,128)S(1)} collective-permute-done((f32[24,64,128]{2,1,0:T(8,128)S(1)}, f32[24,64,128]{2,1,0:T(8,128)S(1)}, u32[]{:S(2)}, u32[]{:S(2)}) %collective-permute-start.15) | collective-permute-done | bytes 786464 | tf_op jit(solution)/shard_map/ppermute | solution.py:136
  112.9 2.5 collective-permute-start.35
  115.6 5.0 %collective-permute-done.16 = f32[12,64,128]{2,1,0:T(8,128)S(1)} collective-permute-done((f32[12,64,128]{2,1,0:T(8,128)S(1)}, f32[12,64,128]{2,1,0:T(8,128)S(1)}, u32[]{:S(2)}, u32[]{:S(2)}) %collective-permute-start.16) | collective-permute-done | bytes 393248 | tf_op jit(solution)/shard_map/ppermute | solution.py:136
  120.7 2.5 collective-permute-start.17
  123.2 6.3 %collective-permute-done.17 = f32[6,64,128]{2,1,0:T(8,128)S(1)} collective-permute-done((f32[6,64,128]{2,1,0:T(8,128)S(1)}, f32[6,64,128]{2,1,0:T(8,128)S(1)}, u32[]{:S(2)}, u32[]{:S(2)}) %collective-permute-start.17) | collective-permute-done | bytes 196640 | tf_op jit(solution)/shard_map/ppermute | solution.py:136
  129.9 1.2 collective-permute-done.20
  131.1 3.9 %collective-permute-done.21 = f32[64,64]{0,1:T(8,128)S(1)} collective-permute-done((f32[64,64]{0,1:T(8,128)S(1)}, f32[64,64]{0,1:T(8,128)S(1)}, u32[]{:S(2)}, u32[]{:S(2)}) %collective-permute-start.21) | collective-permute-done | bytes 16416 | tf_op jit(solution)/shard_map/ppermute | solution.py:146
  135.0 2.5 collective-permute-start.22
  137.5 1.9 collective-permute-done.22
  140.0 3.3 %collective-permute-done.23 = f32[64,64]{0,1:T(8,128)S(1)} collective-permute-done((f32[64,64]{0,1:T(8,128)S(1)}, f32[64,64]{0,1:T(8,128)S(1)}, u32[]{:S(2)}, u32[]{:S(2)}) %collective-permute-start.23) | collective-permute-done | bytes 16416 | tf_op jit(solution)/shard_map/ppermute | solution.py:146
  143.3 1.9 collective-permute-start.24
  145.3 2.1 collective-permute-start.36
  147.4 0.8 collective-permute-done.24
  148.7 2.2 collective-permute-start.25
  151.0 2.0 collective-permute-start.39
  153.7 1.6 collective-permute-done.25
  155.4 2.4 collective-permute-start.26
  157.9 1.1 collective-permute-start.37
  159.0 8.3 %collective-permute-done.26 = bf16[12,64,128]{2,1,0:T(8,128)(2,1)S(1)} collective-permute-done((bf16[12,64,128]{2,1,0:T(8,128)(2,1)S(1)}, bf16[12,64,128]{2,1,0:T(8,128)(2,1)S(1)}, u32[]{:S(2)}, u32[]{:S(2)}) %collective-permute-start.26) | collective-permute-done | bytes 196640 | tf_op jit(solution)/shard_map/ppermute | solution.py:125
  167.4 2.1 collective-permute-start.27
  171.4 7.2 %collective-permute-done.27 = bf16[24,64,128]{2,1,0:T(8,128)(2,1)S(1)} collective-permute-done((bf16[24,64,128]{2,1,0:T(8,128)(2,1)S(1)}, bf16[24,64,128]{2,1,0:T(8,128)(2,1)S(1)}, u32[]{:S(2)}, u32[]{:S(2)}) %collective-permute-start.27) | collective-permute-done | bytes 393248 | tf_op jit(solution)/shard_map/ppermute | solution.py:125
  178.7 24.4 %shard_map.94 = (f32[48,64,128]{2,1,0:T(8,128)S(1)}, f32[24,64,128]{2,1,0:T(8,128)S(1)}) custom-call(s32[576]{0:T(1024)S(1)} %get-tuple-element.30.rows_ref, s32[576]{0:T(1024)S(1)} %get-tuple-element.31.cols_ref, s32[1]{0:T(128)} %bitcast.62.cnt_ref, bf16[576,128,128]{2,1,0:T(8,128)(2,1)} %bitcast.64, bf16[48,64,128]{2,1,0:T(8,128)(2,1)S(1)} %pad_maximum_fusion.rin_ref, ...), custom_call_target="tpu_custom_call" | custom-call | flops 2415919104 | bytes 22413312 | tf_op jit(solution)/shard_map/pallas_call | solution.py:94
  203.2 5.5 %collective-permute-start.30 = (f32[24,64,128]{2,1,0:T(8,128)S(1)}, f32[24,64,128]{2,1,0:T(8,128)S(1)}, u32[]{:S(2)}, u32[]{:S(2)}) collective-permute-start(f32[24,64,128]{2,1,0:T(8,128)S(1)} %slice.120), channel_id=1, source_target_pairs={{0,1},{1,0},{2,3},{3,2},{4,5},{5,4},{6,7},{7,6},{8,9},{9,8},{10,11... | collective-permute-start | bytes 2359304 | tf_op jit(solution)/shard_map/ppermute | solution.py:136
  208.8 1.6 collective-permute-done.40
  210.6 9.0 %collective-permute-done.41 = f32[192,320]{1,0:T(8,128)S(1)} collective-permute-done((f32[192,320]{1,0:T(8,128)S(1)}, f32[192,320]{1,0:T(8,128)S(1)}, u32[]{:S(2)}, u32[]{:S(2)}) %collective-permute-start.41) | collective-permute-done | bytes 245792 | tf_op jit(solution)/shard_map/ppermute | solution.py:146
  220.1 7.9 %collective-permute-done.42 = f32[192,320]{1,0:T(8,128)S(1)} collective-permute-done((f32[192,320]{1,0:T(8,128)S(1)}, f32[192,320]{1,0:T(8,128)S(1)}, u32[]{:S(2)}, u32[]{:S(2)}) %collective-permute-start.42) | collective-permute-done | bytes 245792 | tf_op jit(solution)/shard_map/ppermute | solution.py:146
  228.8 3.2 %collective-permute-done.31 = f32[12,64,128]{2,1,0:T(8,128)S(1)} collective-permute-done((f32[12,64,128]{2,1,0:T(8,128)S(1)}, f32[12,64,128]{2,1,0:T(8,128)S(1)}, u32[]{:S(2)}, u32[]{:S(2)}) %collective-permute-start.31) | collective-permute-done | bytes 393248 | tf_op jit(solution)/shard_map/ppermute | solution.py:136
  232.2 8.5 %collective-permute-done.43 = f32[192,320]{1,0:T(8,128)S(1)} collective-permute-done((f32[192,320]{1,0:T(8,128)S(1)}, f32[192,320]{1,0:T(8,128)S(1)}, u32[]{:S(2)}, u32[]{:S(2)}) %collective-permute-start.43) | collective-permute-done | bytes 245792 | tf_op jit(solution)/shard_map/ppermute | solution.py:146
  241.2 2.2 collective-permute-done.32
  244.2 1.3 collective-permute-done.45
  245.8 4.6 %collective-permute-done.46 = f32[192,64]{1,0:T(8,128)S(1)} collective-permute-done((f32[192,64]{1,0:T(8,128)S(1)}, f32[192,64]{1,0:T(8,128)S(1)}, u32[]{:S(2)}, u32[]{:S(2)}) %collective-permute-start.46) | collective-permute-done | bytes 49184 | tf_op jit(solution)/shard_map/ppermute | solution.py:146
  250.4 2.1 collective-permute-start.47
  252.5 2.6 collective-permute-done.47
  255.5 0.9 collective-permute-done.44
  256.4 3.4 %collective-permute-done.48 = f32[192,64]{1,0:T(8,128)S(1)} collective-permute-done((f32[192,64]{1,0:T(8,128)S(1)}, f32[192,64]{1,0:T(8,128)S(1)}, u32[]{:S(2)}, u32[]{:S(2)}) %collective-permute-start.48) | collective-permute-done | bytes 49184 | tf_op jit(solution)/shard_map/ppermute | solution.py:146
  261.0 5.2 %collective-permute-done.49 = f32[192,64]{1,0:T(8,128)S(1)} collective-permute-done((f32[192,64]{1,0:T(8,128)S(1)}, f32[192,64]{1,0:T(8,128)S(1)}, u32[]{:S(2)}, u32[]{:S(2)}) %collective-permute-start.49) | collective-permute-done | bytes 49184 | tf_op jit(solution)/shard_map/ppermute | solution.py:146
  (131 shorter events, 17.1 us)
Async XLA Ops:
  0.6 0.9 copy-start
  1.9 43.5 %copy-start.4 = (s32[1,1,576]{2,1,0:T(1,128)S(1)}, s32[1,1,576]{2,1,0:T(1,128)}, u32[]{:S(2)}) copy-start(s32[1,1,576]{2,1,0:T(1,128)} %param.8) | copy-start | bytes 6916
  1.9 1.4 collective-permute-start
  3.3 4.8 %collective-permute-start.1 = (f32[64,64]{0,1:T(8,128)S(1)}, f32[64,64]{0,1:T(8,128)S(1)}, u32[]{:S(2)}, u32[]{:S(2)}) collective-permute-start(f32[64,64]{0,1:T(8,128)S(1)} %add.147), channel_id=1, source_target_pairs={{0,16},{8,24},{16,0},{24,8},{1,17},{9,25},{17,1},{25,9},{2,18},{10... | collective-permute-start | bytes 49160 | tf_op jit(solution)/shard_map/ppermute | solution.py:146
  8.0 7.1 %collective-permute-start.2 = (f32[64,64]{0,1:T(8,128)S(1)}, f32[64,64]{0,1:T(8,128)S(1)}, u32[]{:S(2)}, u32[]{:S(2)}) collective-permute-start(f32[64,64]{0,1:T(8,128)S(1)} %add.148), channel_id=1, source_target_pairs={{0,1},{1,0},{2,3},{3,2},{4,5},{5,4},{6,7},{7,6},{8,9},{9,8},{10,11... | collective-permute-start | bytes 49160 | tf_op jit(solution)/shard_map/ppermute | solution.py:146
  11.0 27.1 %collective-permute-start.13 = (bf16[6,64,128]{2,1,0:T(8,128)(2,1)S(1)}, bf16[6,64,128]{2,1,0:T(8,128)(2,1)S(1)}, u32[]{:S(2)}, u32[]{:S(2)}) collective-permute-start(bf16[6,64,128]{2,1,0:T(8,128)(2,1)S(1)} %bitcast_bitcast_fusion.1), channel_id=1, source_target_pairs={{0,16},{8,24},{16,0},{24,8},{1,17},{9,25},{17,1},{25,9},{2,18},{10... | collective-permute-start | bytes 294920 | tf_op jit(solution)/shard_map/ppermute | solution.py:125
  12.6 25.5 %collective-permute-start.8 = (bf16[6,64,128]{2,1,0:T(8,128)(2,1)S(1)}, bf16[6,64,128]{2,1,0:T(8,128)(2,1)S(1)}, u32[]{:S(2)}, u32[]{:S(2)}) collective-permute-start(bf16[6,64,128]{2,1,0:T(8,128)(2,1)S(1)} %bitcast_bitcast_fusion.1), channel_id=1, source_target_pairs={{0,4},{1,5},{2,6},{3,7},{4,0},{5,1},{6,2},{7,3},{8,12},{9,13},{10,... | collective-permute-start | bytes 294920 | tf_op jit(solution)/shard_map/ppermute | solution.py:125
  15.2 4.0 %collective-permute-start.3 = (f32[64,64]{0,1:T(8,128)S(1)}, f32[64,64]{0,1:T(8,128)S(1)}, u32[]{:S(2)}, u32[]{:S(2)}) collective-permute-start(f32[64,64]{0,1:T(8,128)S(1)} %add.149), channel_id=1, source_target_pairs={{0,2},{1,3},{2,0},{3,1},{4,6},{5,7},{6,4},{7,5},{8,10},{9,11},{10,... | collective-permute-start | bytes 49160 | tf_op jit(solution)/shard_map/ppermute | solution.py:146
  19.1 4.8 %collective-permute-start.4 = (f32[64,64]{0,1:T(8,128)S(1)}, f32[64,64]{0,1:T(8,128)S(1)}, u32[]{:S(2)}, u32[]{:S(2)}) collective-permute-start(f32[64,64]{0,1:T(8,128)S(1)} %add.150), channel_id=1, source_target_pairs={{0,4},{1,5},{2,6},{3,7},{4,0},{5,1},{6,2},{7,3},{8,12},{9,13},{10,... | collective-permute-start | bytes 49160 | tf_op jit(solution)/shard_map/ppermute | solution.py:146
  36.5 13.4 %copy-start.5 = (s32[1,1,576]{2,1,0:T(1,128)S(1)}, s32[1,1,576]{2,1,0:T(1,128)}, u32[]{:S(2)}) copy-start(s32[1,1,576]{2,1,0:T(1,128)} %param.9) | copy-start | bytes 6916
  36.6 4.7 %collective-permute-start.11 = (bf16[6,64,128]{2,1,0:T(8,128)(2,1)S(1)}, bf16[6,64,128]{2,1,0:T(8,128)(2,1)S(1)}, u32[]{:S(2)}, u32[]{:S(2)}) collective-permute-start(bf16[6,64,128]{2,1,0:T(8,128)(2,1)S(1)} %bitcast_bitcast_fusion.2), channel_id=1, source_target_pairs={{0,16},{8,24},{16,0},{24,8},{1,17},{9,25},{17,1},{25,9},{2,18},{10... | collective-permute-start | bytes 294920 | tf_op jit(solution)/shard_map/ppermute | solution.py:125
  37.1 5.6 %collective-permute-start.5 = (bf16[6,64,128]{2,1,0:T(8,128)(2,1)S(1)}, bf16[6,64,128]{2,1,0:T(8,128)(2,1)S(1)}, u32[]{:S(2)}, u32[]{:S(2)}) collective-permute-start(bf16[6,64,128]{2,1,0:T(8,128)(2,1)S(1)} %bitcast_bitcast_fusion.2), channel_id=1, source_target_pairs={{0,4},{1,5},{2,6},{3,7},{4,0},{5,1},{6,2},{7,3},{8,12},{9,13},{10,... | collective-permute-start | bytes 294920 | tf_op jit(solution)/shard_map/ppermute | solution.py:125
  38.1 7.4 %collective-permute-start.9 = (bf16[12,64,128]{2,1,0:T(8,128)(2,1)S(1)}, bf16[12,64,128]{2,1,0:T(8,128)(2,1)S(1)}, u32[]{:S(2)}, u32[]{:S(2)}) collective-permute-start(bf16[12,64,128]{2,1,0:T(8,128)(2,1)S(1)} %get-tuple-element.29), channel_id=1, source_target_pairs={{0,2},{1,3},{2,0},{3,1},{4,6},{5,7},{6,4},{7,5},{8,10},{9,11},{10,... | collective-permute-start | bytes 589832 | tf_op jit(solution)/shard_map/ppermute | solution.py:125
  42.8 6.2 %collective-permute-start.6 = (bf16[12,64,128]{2,1,0:T(8,128)(2,1)S(1)}, bf16[12,64,128]{2,1,0:T(8,128)(2,1)S(1)}, u32[]{:S(2)}, u32[]{:S(2)}) collective-permute-start(bf16[12,64,128]{2,1,0:T(8,128)(2,1)S(1)} %get-tuple-element.27), channel_id=1, source_target_pairs={{0,2},{1,3},{2,0},{3,1},{4,6},{5,7},{6,4},{7,5},{8,10},{9,11},{10,... | collective-permute-start | bytes 589832 | tf_op jit(solution)/shard_map/ppermute | solution.py:125
  45.5 9.6 %collective-permute-start.10 = (bf16[24,64,128]{2,1,0:T(8,128)(2,1)S(1)}, bf16[24,64,128]{2,1,0:T(8,128)(2,1)S(1)}, u32[]{:S(2)}, u32[]{:S(2)}) collective-permute-start(bf16[24,64,128]{2,1,0:T(8,128)(2,1)S(1)} %pad_maximum_fusion.5), channel_id=1, source_target_pairs={{0,1},{1,0},{2,3},{3,2},{4,5},{5,4},{6,7},{7,6},{8,9},{9,8},{10,11... | collective-permute-start | bytes 1179656 | tf_op jit(solution)/shard_map/ppermute | solution.py:125
  49.1 10.2 %collective-permute-start.7 = (bf16[24,64,128]{2,1,0:T(8,128)(2,1)S(1)}, bf16[24,64,128]{2,1,0:T(8,128)(2,1)S(1)}, u32[]{:S(2)}, u32[]{:S(2)}) collective-permute-start(bf16[24,64,128]{2,1,0:T(8,128)(2,1)S(1)} %pad_maximum_fusion.4), channel_id=1, source_target_pairs={{0,1},{1,0},{2,3},{3,2},{4,5},{5,4},{6,7},{7,6},{8,9},{9,8},{10,11... | collective-permute-start | bytes 1179656 | tf_op jit(solution)/shard_map/ppermute | solution.py:125
  50.6 1.5 collective-permute-start.14
  50.7 1.7 collective-permute-start.12
  90.7 21.9 %collective-permute-start.15 = (f32[24,64,128]{2,1,0:T(8,128)S(1)}, f32[24,64,128]{2,1,0:T(8,128)S(1)}, u32[]{:S(2)}, u32[]{:S(2)}) collective-permute-start(f32[24,64,128]{2,1,0:T(8,128)S(1)} %slice.110), channel_id=1, source_target_pairs={{0,1},{1,0},{2,3},{3,2},{4,5},{5,4},{6,7},{7,6},{8,9},{9,8},{10,11... | collective-permute-start | bytes 2359304 | tf_op jit(solution)/shard_map/ppermute | solution.py:136
  95.0 20.5 %collective-permute-start.18 = (f32[12,64,128]{2,1,0:T(8,128)S(1)}, f32[12,64,128]{2,1,0:T(8,128)S(1)}, u32[]{:S(2)}, u32[]{:S(2)}) collective-permute-start(f32[12,64,128]{2,1,0:T(8,128)S(1)} %slice.116), channel_id=1, source_target_pairs={{0,8},{8,0},{16,24},{24,16},{1,9},{9,1},{17,25},{25,17},{2,10},{10... | collective-permute-start | bytes 1179656 | tf_op jit(solution)/shard_map/ppermute | solution.py:136
  112.8 7.8 %collective-permute-start.16 = (f32[12,64,128]{2,1,0:T(8,128)S(1)}, f32[12,64,128]{2,1,0:T(8,128)S(1)}, u32[]{:S(2)}, u32[]{:S(2)}) collective-permute-start(f32[12,64,128]{2,1,0:T(8,128)S(1)} %slice.143), channel_id=1, source_target_pairs={{0,2},{1,3},{2,0},{3,1},{4,6},{5,7},{6,4},{7,5},{8,10},{9,11},{10,... | collective-permute-start | bytes 1179656 | tf_op jit(solution)/shard_map/ppermute | solution.py:136
  112.9 32.2 %collective-permute-start.35 = (f32[24,64,128]{2,1,0:T(8,128)S(1)}, f32[24,64,128]{2,1,0:T(8,128)S(1)}, u32[]{:S(2)}, u32[]{:S(2)}) collective-permute-start(f32[24,64,128]{2,1,0:T(8,128)S(1)} %slice.130), channel_id=1, source_target_pairs={{0,1},{1,0},{2,3},{3,2},{4,5},{5,4},{6,7},{7,6},{8,9},{9,8},{10,11... | collective-permute-start | bytes 2359304 | tf_op jit(solution)/shard_map/ppermute | solution.py:136
  115.6 7.6 %collective-permute-start.19 = (f32[6,64,128]{2,1,0:T(8,128)S(1)}, f32[6,64,128]{2,1,0:T(8,128)S(1)}, u32[]{:S(2)}, u32[]{:S(2)}) collective-permute-start(f32[6,64,128]{2,1,0:T(8,128)S(1)} %slice.147), channel_id=1, source_target_pairs={{0,16},{8,24},{16,0},{24,8},{1,17},{9,25},{17,1},{25,9},{2,18},{10... | collective-permute-start | bytes 589832 | tf_op jit(solution)/shard_map/ppermute | solution.py:136
  120.7 8.7 %collective-permute-start.17 = (f32[6,64,128]{2,1,0:T(8,128)S(1)}, f32[6,64,128]{2,1,0:T(8,128)S(1)}, u32[]{:S(2)}, u32[]{:S(2)}) collective-permute-start(f32[6,64,128]{2,1,0:T(8,128)S(1)} %slice.145), channel_id=1, source_target_pairs={{0,4},{1,5},{2,6},{3,7},{4,0},{5,1},{6,2},{7,3},{8,12},{9,13},{10,... | collective-permute-start | bytes 589832 | tf_op jit(solution)/shard_map/ppermute | solution.py:136
  129.8 1.3 collective-permute-start.20
  131.1 3.9 %collective-permute-start.21 = (f32[64,64]{0,1:T(8,128)S(1)}, f32[64,64]{0,1:T(8,128)S(1)}, u32[]{:S(2)}, u32[]{:S(2)}) collective-permute-start(f32[64,64]{0,1:T(8,128)S(1)} %add.159), channel_id=1, source_target_pairs={{0,16},{8,24},{16,0},{24,8},{1,17},{9,25},{17,1},{25,9},{2,18},{10... | collective-permute-start | bytes 49160 | tf_op jit(solution)/shard_map/ppermute | solution.py:146
  135.0 4.4 %collective-permute-start.22 = (f32[64,64]{0,1:T(8,128)S(1)}, f32[64,64]{0,1:T(8,128)S(1)}, u32[]{:S(2)}, u32[]{:S(2)}) collective-permute-start(f32[64,64]{0,1:T(8,128)S(1)} %add.160), channel_id=1, source_target_pairs={{0,1},{1,0},{2,3},{3,2},{4,5},{5,4},{6,7},{7,6},{8,9},{9,8},{10,11... | collective-permute-start | bytes 49160 | tf_op jit(solution)/shard_map/ppermute | solution.py:146
  139.4 3.9 %collective-permute-start.23 = (f32[64,64]{0,1:T(8,128)S(1)}, f32[64,64]{0,1:T(8,128)S(1)}, u32[]{:S(2)}, u32[]{:S(2)}) collective-permute-start(f32[64,64]{0,1:T(8,128)S(1)} %add.161), channel_id=1, source_target_pairs={{0,2},{1,3},{2,0},{3,1},{4,6},{5,7},{6,4},{7,5},{8,10},{9,11},{10,... | collective-permute-start | bytes 49160 | tf_op jit(solution)/shard_map/ppermute | solution.py:146
  139.9 11.0 %collective-permute-start.38 = (f32[12,64,128]{2,1,0:T(8,128)S(1)}, f32[12,64,128]{2,1,0:T(8,128)S(1)}, u32[]{:S(2)}, u32[]{:S(2)}) collective-permute-start(f32[12,64,128]{2,1,0:T(8,128)S(1)} %slice.136), channel_id=1, source_target_pairs={{0,8},{8,0},{16,24},{24,16},{1,9},{9,1},{17,25},{25,17},{2,10},{10... | collective-permute-start | bytes 1179656 | tf_op jit(solution)/shard_map/ppermute | solution.py:136
  143.3 4.9 %collective-permute-start.24 = (f32[64,64]{0,1:T(8,128)S(1)}, f32[64,64]{0,1:T(8,128)S(1)}, u32[]{:S(2)}, u32[]{:S(2)}) collective-permute-start(f32[64,64]{0,1:T(8,128)S(1)} %add.162), channel_id=1, source_target_pairs={{0,4},{1,5},{2,6},{3,7},{4,0},{5,1},{6,2},{7,3},{8,12},{9,13},{10,... | collective-permute-start | bytes 49160 | tf_op jit(solution)/shard_map/ppermute | solution.py:146
  145.3 12.5 %collective-permute-start.36 = (f32[12,64,128]{2,1,0:T(8,128)S(1)}, f32[12,64,128]{2,1,0:T(8,128)S(1)}, u32[]{:S(2)}, u32[]{:S(2)}) collective-permute-start(f32[12,64,128]{2,1,0:T(8,128)S(1)} %slice.155), channel_id=1, source_target_pairs={{0,2},{1,3},{2,0},{3,1},{4,6},{5,7},{6,4},{7,5},{8,10},{9,11},{10,... | collective-permute-start | bytes 1179656 | tf_op jit(solution)/shard_map/ppermute | solution.py:136
  148.6 94.9 %copy-start.1 = (f32[64,768]{1,0:T(8,128)}, f32[64,768]{1,0:T(8,128)S(1)}, u32[]{:S(2)}) copy-start(f32[64,768]{1,0:T(8,128)S(1)} %convolution_subtract_fusion) | copy-start | bytes 589828
  148.6 5.1 %collective-permute-start.28 = (bf16[6,64,128]{2,1,0:T(8,128)(2,1)S(1)}, bf16[6,64,128]{2,1,0:T(8,128)(2,1)S(1)}, u32[]{:S(2)}, u32[]{:S(2)}) collective-permute-start(bf16[6,64,128]{2,1,0:T(8,128)(2,1)S(1)} %bitcast_bitcast_fusion), channel_id=1, source_target_pairs={{0,16},{8,24},{16,0},{24,8},{1,17},{9,25},{17,1},{25,9},{2,18},{10... | collective-permute-start | bytes 294920 | tf_op jit(solution)/shard_map/ppermute | solution.py:125
  148.7 6.6 %collective-permute-start.25 = (bf16[6,64,128]{2,1,0:T(8,128)(2,1)S(1)}, bf16[6,64,128]{2,1,0:T(8,128)(2,1)S(1)}, u32[]{:S(2)}, u32[]{:S(2)}) collective-permute-start(bf16[6,64,128]{2,1,0:T(8,128)(2,1)S(1)} %bitcast_bitcast_fusion), channel_id=1, source_target_pairs={{0,4},{1,5},{2,6},{3,7},{4,0},{5,1},{6,2},{7,3},{8,12},{9,13},{10,... | collective-permute-start | bytes 294920 | tf_op jit(solution)/shard_map/ppermute | solution.py:125
  151.0 19.8 %collective-permute-start.39 = (f32[6,64,128]{2,1,0:T(8,128)S(1)}, f32[6,64,128]{2,1,0:T(8,128)S(1)}, u32[]{:S(2)}, u32[]{:S(2)}) collective-permute-start(f32[6,64,128]{2,1,0:T(8,128)S(1)} %slice.159), channel_id=1, source_target_pairs={{0,16},{8,24},{16,0},{24,8},{1,17},{9,25},{17,1},{25,9},{2,18},{10... | collective-permute-start | bytes 589832 | tf_op jit(solution)/shard_map/ppermute | solution.py:136
  155.3 14.1 %copy-start.2 = (f32[64,768]{1,0:T(8,128)S(1)}, f32[64,768]{1,0:T(8,128)}, u32[]{:S(2)}) copy-start(f32[64,768]{1,0:T(8,128)} %param.7) | copy-start | bytes 589828
  155.3 3.7 %collective-permute-start.29 = (bf16[12,64,128]{2,1,0:T(8,128)(2,1)S(1)}, bf16[12,64,128]{2,1,0:T(8,128)(2,1)S(1)}, u32[]{:S(2)}, u32[]{:S(2)}) collective-permute-start(bf16[12,64,128]{2,1,0:T(8,128)(2,1)S(1)} %get-tuple-element.24), channel_id=1, source_target_pairs={{0,8},{8,0},{16,24},{24,16},{1,9},{9,1},{17,25},{25,17},{2,10},{10... | collective-permute-start | bytes 589832 | tf_op jit(solution)/shard_map/ppermute | solution.py:125
  155.4 11.9 %collective-permute-start.26 = (bf16[12,64,128]{2,1,0:T(8,128)(2,1)S(1)}, bf16[12,64,128]{2,1,0:T(8,128)(2,1)S(1)}, u32[]{:S(2)}, u32[]{:S(2)}) collective-permute-start(bf16[12,64,128]{2,1,0:T(8,128)(2,1)S(1)} %get-tuple-element.25), channel_id=1, source_target_pairs={{0,2},{1,3},{2,0},{3,1},{4,6},{5,7},{6,4},{7,5},{8,10},{9,11},{10,... | collective-permute-start | bytes 589832 | tf_op jit(solution)/shard_map/ppermute | solution.py:125
  157.9 12.8 %collective-permute-start.37 = (f32[6,64,128]{2,1,0:T(8,128)S(1)}, f32[6,64,128]{2,1,0:T(8,128)S(1)}, u32[]{:S(2)}, u32[]{:S(2)}) collective-permute-start(f32[6,64,128]{2,1,0:T(8,128)S(1)} %slice.157), channel_id=1, source_target_pairs={{0,4},{1,5},{2,6},{3,7},{4,0},{5,1},{6,2},{7,3},{8,12},{9,13},{10,... | collective-permute-start | bytes 589832 | tf_op jit(solution)/shard_map/ppermute | solution.py:136
  167.4 11.2 %collective-permute-start.27 = (bf16[24,64,128]{2,1,0:T(8,128)(2,1)S(1)}, bf16[24,64,128]{2,1,0:T(8,128)(2,1)S(1)}, u32[]{:S(2)}, u32[]{:S(2)}) collective-permute-start(bf16[24,64,128]{2,1,0:T(8,128)(2,1)S(1)} %get-tuple-element.23), channel_id=1, source_target_pairs={{0,1},{1,0},{2,3},{3,2},{4,5},{5,4},{6,7},{7,6},{8,9},{9,8},{10,11... | collective-permute-start | bytes 1179656 | tf_op jit(solution)/shard_map/ppermute | solution.py:125
  203.2 16.7 %collective-permute-start.30 = (f32[24,64,128]{2,1,0:T(8,128)S(1)}, f32[24,64,128]{2,1,0:T(8,128)S(1)}, u32[]{:S(2)}, u32[]{:S(2)}) collective-permute-start(f32[24,64,128]{2,1,0:T(8,128)S(1)} %slice.120), channel_id=1, source_target_pairs={{0,1},{1,0},{2,3},{3,2},{4,5},{5,4},{6,7},{7,6},{8,9},{9,8},{10,11... | collective-permute-start | bytes 2359304 | tf_op jit(solution)/shard_map/ppermute | solution.py:136
  208.7 1.6 collective-permute-start.40
  210.5 9.1 %collective-permute-start.41 = (f32[192,320]{1,0:T(8,128)S(1)}, f32[192,320]{1,0:T(8,128)S(1)}, u32[]{:S(2)}, u32[]{:S(2)}) collective-permute-start(f32[192,320]{1,0:T(8,128)S(1)} %fusion.34), channel_id=1, source_target_pairs={{0,16},{8,24},{16,0},{24,8},{1,17},{9,25},{17,1},{25,9},{2,18},{10... | collective-permute-start | bytes 737288 | tf_op jit(solution)/shard_map/ppermute | solution.py:146
  219.7 8.3 %collective-permute-start.42 = (f32[192,320]{1,0:T(8,128)S(1)}, f32[192,320]{1,0:T(8,128)S(1)}, u32[]{:S(2)}, u32[]{:S(2)}) collective-permute-start(f32[192,320]{1,0:T(8,128)S(1)} %add.177), channel_id=1, source_target_pairs={{0,1},{1,0},{2,3},{3,2},{4,5},{5,4},{6,7},{7,6},{8,9},{9,8},{10,11... | collective-permute-start | bytes 737288 | tf_op jit(solution)/shard_map/ppermute | solution.py:146
  219.8 8.3 %collective-permute-start.33 = (f32[12,64,128]{2,1,0:T(8,128)S(1)}, f32[12,64,128]{2,1,0:T(8,128)S(1)}, u32[]{:S(2)}, u32[]{:S(2)}) collective-permute-start(f32[12,64,128]{2,1,0:T(8,128)S(1)} %slice.126), channel_id=1, source_target_pairs={{0,8},{8,0},{16,24},{24,16},{1,9},{9,1},{17,25},{25,17},{2,10},{10... | collective-permute-start | bytes 1179656 | tf_op jit(solution)/shard_map/ppermute | solution.py:136
  220.0 12.0 %collective-permute-start.31 = (f32[12,64,128]{2,1,0:T(8,128)S(1)}, f32[12,64,128]{2,1,0:T(8,128)S(1)}, u32[]{:S(2)}, u32[]{:S(2)}) collective-permute-start(f32[12,64,128]{2,1,0:T(8,128)S(1)} %slice.149), channel_id=1, source_target_pairs={{0,2},{1,3},{2,0},{3,1},{4,6},{5,7},{6,4},{7,5},{8,10},{9,11},{10,... | collective-permute-start | bytes 1179656 | tf_op jit(solution)/shard_map/ppermute | solution.py:136
  228.0 12.7 %collective-permute-start.43 = (f32[192,320]{1,0:T(8,128)S(1)}, f32[192,320]{1,0:T(8,128)S(1)}, u32[]{:S(2)}, u32[]{:S(2)}) collective-permute-start(f32[192,320]{1,0:T(8,128)S(1)} %add.178), channel_id=1, source_target_pairs={{0,2},{1,3},{2,0},{3,1},{4,6},{5,7},{6,4},{7,5},{8,10},{9,11},{10,... | collective-permute-start | bytes 737288 | tf_op jit(solution)/shard_map/ppermute | solution.py:146
  228.2 13.1 %collective-permute-start.34 = (f32[6,64,128]{2,1,0:T(8,128)S(1)}, f32[6,64,128]{2,1,0:T(8,128)S(1)}, u32[]{:S(2)}, u32[]{:S(2)}) collective-permute-start(f32[6,64,128]{2,1,0:T(8,128)S(1)} %slice.153), channel_id=1, source_target_pairs={{0,16},{8,24},{16,0},{24,8},{1,17},{9,25},{17,1},{25,9},{2,18},{10... | collective-permute-start | bytes 589832 | tf_op jit(solution)/shard_map/ppermute | solution.py:136
  232.1 11.3 %collective-permute-start.32 = (f32[6,64,128]{2,1,0:T(8,128)S(1)}, f32[6,64,128]{2,1,0:T(8,128)S(1)}, u32[]{:S(2)}, u32[]{:S(2)}) collective-permute-start(f32[6,64,128]{2,1,0:T(8,128)S(1)} %slice.151), channel_id=1, source_target_pairs={{0,4},{1,5},{2,6},{3,7},{4,0},{5,1},{6,2},{7,3},{8,12},{9,13},{10,... | collective-permute-start | bytes 589832 | tf_op jit(solution)/shard_map/ppermute | solution.py:136
  240.7 15.6 %collective-permute-start.44 = (f32[192,320]{1,0:T(8,128)S(1)}, f32[192,320]{1,0:T(8,128)S(1)}, u32[]{:S(2)}, u32[]{:S(2)}) collective-permute-start(f32[192,320]{1,0:T(8,128)S(1)} %add.179), channel_id=1, source_target_pairs={{0,4},{1,5},{2,6},{3,7},{4,0},{5,1},{6,2},{7,3},{8,12},{9,13},{10,... | collective-permute-start | bytes 737288 | tf_op jit(solution)/shard_map/ppermute | solution.py:146
  243.5 16.8 %copy-start.3 = (f32[64,768]{1,0:T(8,128)}, f32[64,768]{1,0:T(8,128)S(1)}, u32[]{:S(2)}) copy-start(f32[64,768]{1,0:T(8,128)S(1)} %copy_bitcast_fusion) | copy-start | bytes 589828
  244.1 1.4 collective-permute-start.45
  245.5 4.9 %collective-permute-start.46 = (f32[192,64]{1,0:T(8,128)S(1)}, f32[192,64]{1,0:T(8,128)S(1)}, u32[]{:S(2)}, u32[]{:S(2)}) collective-permute-start(f32[192,64]{1,0:T(8,128)S(1)} %add.181), channel_id=1, source_target_pairs={{0,16},{8,24},{16,0},{24,8},{1,17},{9,25},{17,1},{25,9},{2,18},{10... | collective-permute-start | bytes 147464 | tf_op jit(solution)/shard_map/ppermute | solution.py:146
  250.4 4.7 %collective-permute-start.47 = (f32[192,64]{1,0:T(8,128)S(1)}, f32[192,64]{1,0:T(8,128)S(1)}, u32[]{:S(2)}, u32[]{:S(2)}) collective-permute-start(f32[192,64]{1,0:T(8,128)S(1)} %add.182), channel_id=1, source_target_pairs={{0,1},{1,0},{2,3},{3,2},{4,5},{5,4},{6,7},{7,6},{8,9},{9,8},{10,11... | collective-permute-start | bytes 147464 | tf_op jit(solution)/shard_map/ppermute | solution.py:146
  255.1 4.7 %collective-permute-start.48 = (f32[192,64]{1,0:T(8,128)S(1)}, f32[192,64]{1,0:T(8,128)S(1)}, u32[]{:S(2)}, u32[]{:S(2)}) collective-permute-start(f32[192,64]{1,0:T(8,128)S(1)} %add.183), channel_id=1, source_target_pairs={{0,2},{1,3},{2,0},{3,1},{4,6},{5,7},{6,4},{7,5},{8,10},{9,11},{10,... | collective-permute-start | bytes 147464 | tf_op jit(solution)/shard_map/ppermute | solution.py:146
  259.8 6.4 %collective-permute-start.49 = (f32[192,64]{1,0:T(8,128)S(1)}, f32[192,64]{1,0:T(8,128)S(1)}, u32[]{:S(2)}, u32[]{:S(2)}) collective-permute-start(f32[192,64]{1,0:T(8,128)S(1)} %add.184), channel_id=1, source_target_pairs={{0,4},{1,5},{2,6},{3,7},{4,0},{5,1},{6,2},{7,3},{8,12},{9,13},{10,... | collective-permute-start | bytes 147464 | tf_op jit(solution)/shard_map/ppermute | solution.py:146

commit v5 on v4

--- a/solution.py
+++ b/solution.py
@@ -133,7 +133,8 @@
     step = 1
     while step < size:
         half = held.shape[0] // 2
-        held = held[:half] + lax.ppermute(held[half:], axis, exchange_pairs(size, step))
+        sent = held[half:].astype(jnp.bfloat16)
+        held = held[:half] + lax.ppermute(sent, axis, exchange_pairs(size, step)).astype(held.dtype)
         step *= 2
     return held
 

time: 269 us -> 238 us (0.88); the launches traced: 267 us -> 239 us
  waiting for transfers between devices: 129 us -> 113 us
  Pallas kernels: 51.3 us -> 44 us
  starting transfers between devices: 57.3 us -> 52.8 us
    ppermute x20, waiting for transfers between devices: 63.6 us -> 51.4 us  [all_sum(): value = value + lax.ppermute(value, axis, exchange_pairs(size, step))]
    ppermute x15, starting transfers between devices: 21.3 us -> 13.8 us  [scatter_sum(): lax.ppermute(sent, axis, exchange_pairs(size, step)).astype(held.dtype)]
    pallas_call x2, Pallas kernels: 51.3 us -> 44 us  [tile_products(): pl.pallas_call(tile_kernel, grid_spec=grid_spec, out_shape=[jax.ShapeDtyp...]
    ppermute x15, waiting for transfers between devices: 31.4 us -> 26.2 us  [gather_blocks(): lax.ppermute(held, axis, exchange_pairs(size, step))]
    ppermute x20, starting transfers between devices: 16.8 us -> 21 us  [all_sum(): value = value + lax.ppermute(value, axis, exchange_pairs(size, step))]
  transfers between devices with their start and end apart: 50 -> 50, of which waited for: 35 -> 31; matrix products, arithmetic and copies ran while one was open for 8% -> 9% of each run, Pallas kernels for 0% -> 9%
where the time goes in v5:
time: 238 us; the launch traced here: 239 us
  waiting for transfers between devices  113 us (47%)
  starting transfers between devices  52.8 us (22%)
  Pallas kernels  44 us (18%)
  other arithmetic  21.3 us (9%)
  matrix products  3.82 us (2%)
    ppermute x20, waiting for transfers between devices, all_sum(): value = value + lax.ppermute(value, axis, exchange_pairs(size, step))  51.4 us
    pallas_call x2, Pallas kernels, tile_products(): pl.pallas_call(tile_kernel, grid_spec=grid_spec, out_shape=[jax.ShapeDtyp...  44 us
    ppermute x15, waiting for transfers between devices, scatter_sum(): lax.ppermute(sent, axis, exchange_pairs(size, step)).astype(held.dtype)  35.7 us
    ppermute x15, waiting for transfers between devices, gather_blocks(): lax.ppermute(held, axis, exchange_pairs(size, step))  26.2 us
    ppermute x20, starting transfers between devices, all_sum(): value = value + lax.ppermute(value, axis, exchange_pairs(size, step))  21 us
    ppermute x15, starting transfers between devices, gather_blocks(): lax.ppermute(held, axis, exchange_pairs(size, step))  17.9 us
    ppermute x15, starting transfers between devices, scatter_sum(): lax.ppermute(sent, axis, exchange_pairs(size, step)).astype(held.dtype)  13.8 us
    another operation x3, other arithmetic, per_device(): cholesky_factor = jnp.linalg.cholesky(gram_x)  6.52 us
  transfers between devices with their start and end apart: 50, of which 31 were waited for; matrix products, arithmetic and copies ran while one was open for 9% of the time, Pallas kernels for 9%

profile of v5, /device:TPU:0, one launch (start us, length us, event | category | flops | bytes accessed | tf_op | source)
XLA Modules:
  0.0 239.4 jit_solution(7030236168900641646)
XLA Ops:
  0.6 0.9 copy-done
  2.4 0.9 collective-permute-done
  3.3 2.9 %collective-permute-start.1 = (f32[64,64]{0,1:T(8,128)S(1)}, f32[64,64]{0,1:T(8,128)S(1)}, u32[]{:S(2)}, u32[]{:S(2)}) collective-permute-start(f32[64,64]{0,1:T(8,128)S(1)} %add.147), channel_id=1, source_target_pairs={{0,16},{8,24},{16,0},{24,8},{1,17},{9,25},{17,1},{25,9},{2,18},{10... | collective-permute-start | bytes 49160 | tf_op jit(solution)/shard_map/ppermute | solution.py:147
  6.1 1.9 collective-permute-done.1
  8.0 2.0 collective-permute-start.2
  10.0 0.9 bitcast_bitcast_fusion.1
  11.0 1.6 collective-permute-start.13
  12.6 2.6 %collective-permute-start.8 = (bf16[6,64,128]{2,1,0:T(8,128)(2,1)S(1)}, bf16[6,64,128]{2,1,0:T(8,128)(2,1)S(1)}, u32[]{:S(2)}, u32[]{:S(2)}) collective-permute-start(bf16[6,64,128]{2,1,0:T(8,128)(2,1)S(1)} %bitcast_bitcast_fusion.1), channel_id=1, source_target_pairs={{0,4},{1,5},{2,6},{3,7},{4,0},{5,1},{6,2},{7,3},{8,12},{9,13},{10,... | collective-permute-start | bytes 294920 | tf_op jit(solution)/shard_map/ppermute | solution.py:125
  15.2 1.6 collective-permute-start.3
  16.8 0.7 divide_reduce_fusion.1
  17.5 1.6 collective-permute-done.3
  19.1 0.9 collective-permute-start.4
  20.0 0.7 divide_reduce_fusion
  20.7 3.2 %collective-permute-done.4 = f32[64,64]{0,1:T(8,128)S(1)} collective-permute-done((f32[64,64]{0,1:T(8,128)S(1)}, f32[64,64]{0,1:T(8,128)S(1)}, u32[]{:S(2)}, u32[]{:S(2)}) %collective-permute-start.4) | collective-permute-done | bytes 16416 | tf_op jit(solution)/shard_map/ppermute | solution.py:147
  24.1 5.8 %cholesky.16 = f32[64,64]{1,0:T(8,128)S(1)} custom-call(f32[64,64]{1,0:T(8,128)S(1)} %fusion.17), custom_call_target="Cholesky" | custom-call | tf_op jit(solution)/shard_map/jit(cholesky)/cholesky | solution.py:196
  31.2 4.9 %custom-call.6 = f32[1,64,64]{1,2,0:T(8,128)S(1)} custom-call(f32[1,64,64]{2,1,0:T(8,128)S(1)} %fusion.14), custom_call_target="InvertDiagBlocksLowerTriangular" | custom-call | tf_op jit(solution)/shard_map/triangular_solve | solution.py:197
  37.1 0.9 collective-permute-start.5
  38.1 1.9 collective-permute-start.9
  39.9 1.3 collective-permute-done.11
  41.3 1.5 collective-permute-done.5
  42.8 2.6 %collective-permute-start.6 = (bf16[12,64,128]{2,1,0:T(8,128)(2,1)S(1)}, bf16[12,64,128]{2,1,0:T(8,128)(2,1)S(1)}, u32[]{:S(2)}, u32[]{:S(2)}) collective-permute-start(bf16[12,64,128]{2,1,0:T(8,128)(2,1)S(1)} %get-tuple-element.27), channel_id=1, source_target_pairs={{0,2},{1,3},{2,0},{3,1},{4,6},{5,7},{6,4},{7,5},{8,10},{9,11},{10,... | collective-permute-start | bytes 589832 | tf_op jit(solution)/shard_map/ppermute | solution.py:125
  45.5 0.8 collective-permute-start.10
  46.3 2.7 %collective-permute-done.6 = bf16[12,64,128]{2,1,0:T(8,128)(2,1)S(1)} collective-permute-done((bf16[12,64,128]{2,1,0:T(8,128)(2,1)S(1)}, bf16[12,64,128]{2,1,0:T(8,128)(2,1)S(1)}, u32[]{:S(2)}, u32[]{:S(2)}) %collective-permute-start.6) | collective-permute-done | bytes 196640 | tf_op jit(solution)/shard_map/ppermute | solution.py:125
  49.1 0.8 collective-permute-start.7
  51.2 0.9 collective-permute-done.14
  52.5 2.6 %collective-permute-done.10 = bf16[24,64,128]{2,1,0:T(8,128)(2,1)S(1)} collective-permute-done((bf16[24,64,128]{2,1,0:T(8,128)(2,1)S(1)}, bf16[24,64,128]{2,1,0:T(8,128)(2,1)S(1)}, u32[]{:S(2)}, u32[]{:S(2)}) %collective-permute-start.10) | collective-permute-done | bytes 393248 | tf_op jit(solution)/shard_map/ppermute | solution.py:125
  55.1 4.2 %collective-permute-done.7 = bf16[24,64,128]{2,1,0:T(8,128)(2,1)S(1)} collective-permute-done((bf16[24,64,128]{2,1,0:T(8,128)(2,1)S(1)}, bf16[24,64,128]{2,1,0:T(8,128)(2,1)S(1)}, u32[]{:S(2)}, u32[]{:S(2)}) %collective-permute-start.7) | collective-permute-done | bytes 393248 | tf_op jit(solution)/shard_map/ppermute | solution.py:125
  59.3 4.4 %maximum_maximum_fusion.rin_ref = bf16[48,128,128]{2,1,0:T(8,128)(2,1)} fusion(bf16[24,64,128]{2,1,0:T(8,128)(2,1)S(1)} %collective-permute-done.10, bf16[12,64,128]{2,1,0:T(8,128)(2,1)S(1)} %collective-permute-done.9, bf16[6,64,128]{2,1,0:T(8,128)(2,1)S(1)} %collective-permute-done.8, bf16[6,64,128]{2,1,0:T(8,128)(2,1)S(1)} %bitcast_bitcast_fusion.1, ...), kind=kLoop, calls=%fused_computation | loop fusion | flops 12582912 | bytes 3145728 | tf_op jit(solution)/shard_map/concatenate | solution.py:202
  63.7 22.9 %shard_map.93 = (f32[48,64,128]{2,1,0:T(8,128)S(1)}, f32[24,64,128]{2,1,0:T(8,128)S(1)}, f32[48,64,128]{2,1,0:T(8,128)S(1)}, f32[24,64,128]{2,1,0:T(8,128)S(1)}) custom-call(s32[576]{0:T(1024)S(1)} %get-tuple-element.30.rows_ref, s32[576]{0:T(1024)S(1)} %get-tuple-element.31.cols_ref, s32[1]{0:T(128)} %bitcast.61.cnt_ref, bf16[576,128,128]{2,1,0:T(8,128)(2,1)} %bitcast.63, ...), custom_call_target="tpu_custom_call" | custom-call | flops 4831838208 | bytes 25952256 | tf_op jit(solution)/shard_map/pallas_call | solution.py:94
  86.8 7.6 %collective-permute-done.15 = bf16[24,64,128]{2,1,0:T(8,128)(2,1)S(1)} collective-permute-done((bf16[24,64,128]{2,1,0:T(8,128)(2,1)S(1)}, bf16[24,64,128]{2,1,0:T(8,128)(2,1)S(1)}, u32[]{:S(2)}, u32[]{:S(2)}) %collective-permute-start.15) | collective-permute-done | bytes 393248 | tf_op jit(solution)/shard_map/ppermute | solution.py:137
  94.6 6.8 %collective-permute-start.16 = (bf16[12,64,128]{2,1,0:T(8,128)(2,1)S(1)}, bf16[12,64,128]{2,1,0:T(8,128)(2,1)S(1)}, u32[]{:S(2)}, u32[]{:S(2)}) collective-permute-start(bf16[12,64,128]{2,1,0:T(8,128)(2,1)S(1)} %slice.240), channel_id=1, source_target_pairs={{0,2},{1,3},{2,0},{3,1},{4,6},{5,7},{6,4},{7,5},{8,10},{9,11},{10,... | collective-permute-start | bytes 589832 | tf_op jit(solution)/shard_map/ppermute | solution.py:137
  101.6 3.5 %collective-permute-done.16 = bf16[12,64,128]{2,1,0:T(8,128)(2,1)S(1)} collective-permute-done((bf16[12,64,128]{2,1,0:T(8,128)(2,1)S(1)}, bf16[12,64,128]{2,1,0:T(8,128)(2,1)S(1)}, u32[]{:S(2)}, u32[]{:S(2)}) %collective-permute-start.16) | collective-permute-done | bytes 196640 | tf_op jit(solution)/shard_map/ppermute | solution.py:137
  105.3 0.9 collective-permute-start.35
  106.2 4.5 %collective-permute-done.17 = bf16[6,64,128]{2,1,0:T(8,128)(2,1)S(1)} collective-permute-done((bf16[6,64,128]{2,1,0:T(8,128)(2,1)S(1)}, bf16[6,64,128]{2,1,0:T(8,128)(2,1)S(1)}, u32[]{:S(2)}, u32[]{:S(2)}) %collective-permute-start.17) | collective-permute-done | bytes 98336 | tf_op jit(solution)/shard_map/ppermute | solution.py:137
  111.2 1.2 collective-permute-done.20
  112.7 3.6 %collective-permute-done.21 = f32[64,64]{0,1:T(8,128)S(1)} collective-permute-done((f32[64,64]{0,1:T(8,128)S(1)}, f32[64,64]{0,1:T(8,128)S(1)}, u32[]{:S(2)}, u32[]{:S(2)}) %collective-permute-start.21) | collective-permute-done | bytes 16416 | tf_op jit(solution)/shard_map/ppermute | solution.py:147
  116.3 1.8 collective-permute-start.22
  118.7 1.6 collective-permute-done.22
  120.3 2.1 collective-permute-start.23
  122.5 2.1 collective-permute-done.23
  124.8 2.9 %collective-permute-start.37 = (bf16[6,64,128]{2,1,0:T(8,128)(2,1)S(1)}, bf16[6,64,128]{2,1,0:T(8,128)(2,1)S(1)}, u32[]{:S(2)}, u32[]{:S(2)}) collective-permute-start(bf16[6,64,128]{2,1,0:T(8,128)(2,1)S(1)} %slice.242), channel_id=1, source_target_pairs={{0,4},{1,5},{2,6},{3,7},{4,0},{5,1},{6,2},{7,3},{8,12},{9,13},{10,... | collective-permute-start | bytes 294920 | tf_op jit(solution)/shard_map/ppermute | solution.py:137
  127.7 1.7 collective-permute-done.24
  130.8 2.4 %collective-permute-done.37 = bf16[6,64,128]{2,1,0:T(8,128)(2,1)S(1)} collective-permute-done((bf16[6,64,128]{2,1,0:T(8,128)(2,1)S(1)}, bf16[6,64,128]{2,1,0:T(8,128)(2,1)S(1)}, u32[]{:S(2)}, u32[]{:S(2)}) %collective-permute-start.37) | collective-permute-done | bytes 98336 | tf_op jit(solution)/shard_map/ppermute | solution.py:137
  134.5 1.2 collective-permute-done.25
  135.8 1.8 collective-permute-start.26
  138.6 4.5 %collective-permute-done.26 = bf16[12,64,128]{2,1,0:T(8,128)(2,1)S(1)} collective-permute-done((bf16[12,64,128]{2,1,0:T(8,128)(2,1)S(1)}, bf16[12,64,128]{2,1,0:T(8,128)(2,1)S(1)}, u32[]{:S(2)}, u32[]{:S(2)}) %collective-permute-start.26) | collective-permute-done | bytes 196640 | tf_op jit(solution)/shard_map/ppermute | solution.py:125
  143.2 2.8 %collective-permute-start.27 = (bf16[24,64,128]{2,1,0:T(8,128)(2,1)S(1)}, bf16[24,64,128]{2,1,0:T(8,128)(2,1)S(1)}, u32[]{:S(2)}, u32[]{:S(2)}) collective-permute-start(bf16[24,64,128]{2,1,0:T(8,128)(2,1)S(1)} %get-tuple-element.23), channel_id=1, source_target_pairs={{0,1},{1,0},{2,3},{3,2},{4,5},{5,4},{6,7},{7,6},{8,9},{9,8},{10,11... | collective-permute-start | bytes 1179656 | tf_op jit(solution)/shard_map/ppermute | solution.py:125
  146.1 1.9 collective-permute-start.41
  148.0 6.9 %collective-permute-done.27 = bf16[24,64,128]{2,1,0:T(8,128)(2,1)S(1)} collective-permute-done((bf16[24,64,128]{2,1,0:T(8,128)(2,1)S(1)}, bf16[24,64,128]{2,1,0:T(8,128)(2,1)S(1)}, u32[]{:S(2)}, u32[]{:S(2)}) %collective-permute-start.27) | collective-permute-done | bytes 393248 | tf_op jit(solution)/shard_map/ppermute | solution.py:125
  155.0 21.1 %shard_map.94 = (f32[48,64,128]{2,1,0:T(8,128)S(1)}, f32[24,64,128]{2,1,0:T(8,128)S(1)}) custom-call(s32[576]{0:T(1024)S(1)} %get-tuple-element.30.rows_ref, s32[576]{0:T(1024)S(1)} %get-tuple-element.31.cols_ref, s32[1]{0:T(128)} %bitcast.62.cnt_ref, bf16[576,128,128]{2,1,0:T(8,128)(2,1)} %bitcast.64, bf16[48,64,128]{2,1,0:T(8,128)(2,1)S(1)} %pad_maximum_fusion.rin_ref, ...), custom_call_target="tpu_custom_call" | custom-call | flops 2415919104 | bytes 22413312 | tf_op jit(solution)/shard_map/pallas_call | solution.py:94
  176.3 2.1 collective-permute-start.42
  178.5 14.4 %collective-permute-done.42 = f32[192,320]{1,0:T(8,128)S(1)} collective-permute-done((f32[192,320]{1,0:T(8,128)S(1)}, f32[192,320]{1,0:T(8,128)S(1)}, u32[]{:S(2)}, u32[]{:S(2)}) %collective-permute-start.42) | collective-permute-done | bytes 245792 | tf_op jit(solution)/shard_map/ppermute | solution.py:147
  193.1 2.1 collective-permute-start.31
  195.3 9.1 %collective-permute-done.31 = bf16[12,64,128]{2,1,0:T(8,128)(2,1)S(1)} collective-permute-done((bf16[12,64,128]{2,1,0:T(8,128)(2,1)S(1)}, bf16[12,64,128]{2,1,0:T(8,128)(2,1)S(1)}, u32[]{:S(2)}, u32[]{:S(2)}) %collective-permute-start.31) | collective-permute-done | bytes 196640 | tf_op jit(solution)/shard_map/ppermute | solution.py:137
  204.6 3.0 %collective-permute-start.44 = (f32[192,320]{1,0:T(8,128)S(1)}, f32[192,320]{1,0:T(8,128)S(1)}, u32[]{:S(2)}, u32[]{:S(2)}) collective-permute-start(f32[192,320]{1,0:T(8,128)S(1)} %add.179), channel_id=1, source_target_pairs={{0,4},{1,5},{2,6},{3,7},{4,0},{5,1},{6,2},{7,3},{8,12},{9,13},{10,... | collective-permute-start | bytes 737288 | tf_op jit(solution)/shard_map/ppermute | solution.py:147
  207.6 8.5 %collective-permute-done.32 = bf16[6,64,128]{2,1,0:T(8,128)(2,1)S(1)} collective-permute-done((bf16[6,64,128]{2,1,0:T(8,128)(2,1)S(1)}, bf16[6,64,128]{2,1,0:T(8,128)(2,1)S(1)}, u32[]{:S(2)}, u32[]{:S(2)}) %collective-permute-start.32) | collective-permute-done | bytes 98336 | tf_op jit(solution)/shard_map/ppermute | solution.py:137
  216.9 1.3 collective-permute-done.45
  218.3 4.8 %collective-permute-done.46 = f32[192,64]{1,0:T(8,128)S(1)} collective-permute-done((f32[192,64]{1,0:T(8,128)S(1)}, f32[192,64]{1,0:T(8,128)S(1)}, u32[]{:S(2)}, u32[]{:S(2)}) %collective-permute-start.46) | collective-permute-done | bytes 49184 | tf_op jit(solution)/shard_map/ppermute | solution.py:147
  223.1 0.9 collective-permute-start.47
  224.0 3.7 %collective-permute-done.47 = f32[192,64]{1,0:T(8,128)S(1)} collective-permute-done((f32[192,64]{1,0:T(8,128)S(1)}, f32[192,64]{1,0:T(8,128)S(1)}, u32[]{:S(2)}, u32[]{:S(2)}) %collective-permute-start.47) | collective-permute-done | bytes 49184 | tf_op jit(solution)/shard_map/ppermute | solution.py:147
  227.9 4.6 %collective-permute-done.48 = f32[192,64]{1,0:T(8,128)S(1)} collective-permute-done((f32[192,64]{1,0:T(8,128)S(1)}, f32[192,64]{1,0:T(8,128)S(1)}, u32[]{:S(2)}, u32[]{:S(2)}) %collective-permute-start.48) | collective-permute-done | bytes 49184 | tf_op jit(solution)/shard_map/ppermute | solution.py:147
  233.3 0.7 slice.183
  233.9 4.6 %collective-permute-done.49 = f32[192,64]{1,0:T(8,128)S(1)} collective-permute-done((f32[192,64]{1,0:T(8,128)S(1)}, f32[192,64]{1,0:T(8,128)S(1)}, u32[]{:S(2)}, u32[]{:S(2)}) %collective-permute-start.49) | collective-permute-done | bytes 49184 | tf_op jit(solution)/shard_map/ppermute | solution.py:147
  238.6 0.8 pad_maximum_fusion.13
  (131 shorter events, 13.1 us)
Async XLA Ops:
  0.6 0.9 copy-start
  1.9 43.5 %copy-start.4 = (s32[1,1,576]{2,1,0:T(1,128)S(1)}, s32[1,1,576]{2,1,0:T(1,128)}, u32[]{:S(2)}) copy-start(s32[1,1,576]{2,1,0:T(1,128)} %param.8) | copy-start | bytes 6916
  1.9 1.4 collective-permute-start
  3.3 4.8 %collective-permute-start.1 = (f32[64,64]{0,1:T(8,128)S(1)}, f32[64,64]{0,1:T(8,128)S(1)}, u32[]{:S(2)}, u32[]{:S(2)}) collective-permute-start(f32[64,64]{0,1:T(8,128)S(1)} %add.147), channel_id=1, source_target_pairs={{0,16},{8,24},{16,0},{24,8},{1,17},{9,25},{17,1},{25,9},{2,18},{10... | collective-permute-start | bytes 49160 | tf_op jit(solution)/shard_map/ppermute | solution.py:147
  8.0 7.1 %collective-permute-start.2 = (f32[64,64]{0,1:T(8,128)S(1)}, f32[64,64]{0,1:T(8,128)S(1)}, u32[]{:S(2)}, u32[]{:S(2)}) collective-permute-start(f32[64,64]{0,1:T(8,128)S(1)} %add.148), channel_id=1, source_target_pairs={{0,1},{1,0},{2,3},{3,2},{4,5},{5,4},{6,7},{7,6},{8,9},{9,8},{10,11... | collective-permute-start | bytes 49160 | tf_op jit(solution)/shard_map/ppermute | solution.py:147
  11.0 27.1 %collective-permute-start.13 = (bf16[6,64,128]{2,1,0:T(8,128)(2,1)S(1)}, bf16[6,64,128]{2,1,0:T(8,128)(2,1)S(1)}, u32[]{:S(2)}, u32[]{:S(2)}) collective-permute-start(bf16[6,64,128]{2,1,0:T(8,128)(2,1)S(1)} %bitcast_bitcast_fusion.1), channel_id=1, source_target_pairs={{0,16},{8,24},{16,0},{24,8},{1,17},{9,25},{17,1},{25,9},{2,18},{10... | collective-permute-start | bytes 294920 | tf_op jit(solution)/shard_map/ppermute | solution.py:125
  12.6 25.5 %collective-permute-start.8 = (bf16[6,64,128]{2,1,0:T(8,128)(2,1)S(1)}, bf16[6,64,128]{2,1,0:T(8,128)(2,1)S(1)}, u32[]{:S(2)}, u32[]{:S(2)}) collective-permute-start(bf16[6,64,128]{2,1,0:T(8,128)(2,1)S(1)} %bitcast_bitcast_fusion.1), channel_id=1, source_target_pairs={{0,4},{1,5},{2,6},{3,7},{4,0},{5,1},{6,2},{7,3},{8,12},{9,13},{10,... | collective-permute-start | bytes 294920 | tf_op jit(solution)/shard_map/ppermute | solution.py:125
  15.2 4.0 %collective-permute-start.3 = (f32[64,64]{0,1:T(8,128)S(1)}, f32[64,64]{0,1:T(8,128)S(1)}, u32[]{:S(2)}, u32[]{:S(2)}) collective-permute-start(f32[64,64]{0,1:T(8,128)S(1)} %add.149), channel_id=1, source_target_pairs={{0,2},{1,3},{2,0},{3,1},{4,6},{5,7},{6,4},{7,5},{8,10},{9,11},{10,... | collective-permute-start | bytes 49160 | tf_op jit(solution)/shard_map/ppermute | solution.py:147
  19.1 4.8 %collective-permute-start.4 = (f32[64,64]{0,1:T(8,128)S(1)}, f32[64,64]{0,1:T(8,128)S(1)}, u32[]{:S(2)}, u32[]{:S(2)}) collective-permute-start(f32[64,64]{0,1:T(8,128)S(1)} %add.150), channel_id=1, source_target_pairs={{0,4},{1,5},{2,6},{3,7},{4,0},{5,1},{6,2},{7,3},{8,12},{9,13},{10,... | collective-permute-start | bytes 49160 | tf_op jit(solution)/shard_map/ppermute | solution.py:147
  36.5 13.4 %copy-start.5 = (s32[1,1,576]{2,1,0:T(1,128)S(1)}, s32[1,1,576]{2,1,0:T(1,128)}, u32[]{:S(2)}) copy-start(s32[1,1,576]{2,1,0:T(1,128)} %param.9) | copy-start | bytes 6916
  36.6 4.7 %collective-permute-start.11 = (bf16[6,64,128]{2,1,0:T(8,128)(2,1)S(1)}, bf16[6,64,128]{2,1,0:T(8,128)(2,1)S(1)}, u32[]{:S(2)}, u32[]{:S(2)}) collective-permute-start(bf16[6,64,128]{2,1,0:T(8,128)(2,1)S(1)} %bitcast_bitcast_fusion.2), channel_id=1, source_target_pairs={{0,16},{8,24},{16,0},{24,8},{1,17},{9,25},{17,1},{25,9},{2,18},{10... | collective-permute-start | bytes 294920 | tf_op jit(solution)/shard_map/ppermute | solution.py:125
  37.1 5.6 %collective-permute-start.5 = (bf16[6,64,128]{2,1,0:T(8,128)(2,1)S(1)}, bf16[6,64,128]{2,1,0:T(8,128)(2,1)S(1)}, u32[]{:S(2)}, u32[]{:S(2)}) collective-permute-start(bf16[6,64,128]{2,1,0:T(8,128)(2,1)S(1)} %bitcast_bitcast_fusion.2), channel_id=1, source_target_pairs={{0,4},{1,5},{2,6},{3,7},{4,0},{5,1},{6,2},{7,3},{8,12},{9,13},{10,... | collective-permute-start | bytes 294920 | tf_op jit(solution)/shard_map/ppermute | solution.py:125
  38.1 7.4 %collective-permute-start.9 = (bf16[12,64,128]{2,1,0:T(8,128)(2,1)S(1)}, bf16[12,64,128]{2,1,0:T(8,128)(2,1)S(1)}, u32[]{:S(2)}, u32[]{:S(2)}) collective-permute-start(bf16[12,64,128]{2,1,0:T(8,128)(2,1)S(1)} %get-tuple-element.29), channel_id=1, source_target_pairs={{0,2},{1,3},{2,0},{3,1},{4,6},{5,7},{6,4},{7,5},{8,10},{9,11},{10,... | collective-permute-start | bytes 589832 | tf_op jit(solution)/shard_map/ppermute | solution.py:125
  42.8 6.2 %collective-permute-start.6 = (bf16[12,64,128]{2,1,0:T(8,128)(2,1)S(1)}, bf16[12,64,128]{2,1,0:T(8,128)(2,1)S(1)}, u32[]{:S(2)}, u32[]{:S(2)}) collective-permute-start(bf16[12,64,128]{2,1,0:T(8,128)(2,1)S(1)} %get-tuple-element.27), channel_id=1, source_target_pairs={{0,2},{1,3},{2,0},{3,1},{4,6},{5,7},{6,4},{7,5},{8,10},{9,11},{10,... | collective-permute-start | bytes 589832 | tf_op jit(solution)/shard_map/ppermute | solution.py:125
  45.5 9.6 %collective-permute-start.10 = (bf16[24,64,128]{2,1,0:T(8,128)(2,1)S(1)}, bf16[24,64,128]{2,1,0:T(8,128)(2,1)S(1)}, u32[]{:S(2)}, u32[]{:S(2)}) collective-permute-start(bf16[24,64,128]{2,1,0:T(8,128)(2,1)S(1)} %pad_maximum_fusion.5), channel_id=1, source_target_pairs={{0,1},{1,0},{2,3},{3,2},{4,5},{5,4},{6,7},{7,6},{8,9},{9,8},{10,11... | collective-permute-start | bytes 1179656 | tf_op jit(solution)/shard_map/ppermute | solution.py:125
  49.1 10.2 %collective-permute-start.7 = (bf16[24,64,128]{2,1,0:T(8,128)(2,1)S(1)}, bf16[24,64,128]{2,1,0:T(8,128)(2,1)S(1)}, u32[]{:S(2)}, u32[]{:S(2)}) collective-permute-start(bf16[24,64,128]{2,1,0:T(8,128)(2,1)S(1)} %pad_maximum_fusion.4), channel_id=1, source_target_pairs={{0,1},{1,0},{2,3},{3,2},{4,5},{5,4},{6,7},{7,6},{8,9},{9,8},{10,11... | collective-permute-start | bytes 1179656 | tf_op jit(solution)/shard_map/ppermute | solution.py:125
  50.6 1.5 collective-permute-start.14
  50.7 1.7 collective-permute-start.12
  86.7 7.8 %collective-permute-start.15 = (bf16[24,64,128]{2,1,0:T(8,128)(2,1)S(1)}, bf16[24,64,128]{2,1,0:T(8,128)(2,1)S(1)}, u32[]{:S(2)}, u32[]{:S(2)}) collective-permute-start(bf16[24,64,128]{2,1,0:T(8,128)(2,1)S(1)} %slice.234), channel_id=1, source_target_pairs={{0,1},{1,0},{2,3},{3,2},{4,5},{5,4},{6,7},{7,6},{8,9},{9,8},{10,11... | collective-permute-start | bytes 1179656 | tf_op jit(solution)/shard_map/ppermute | solution.py:137
  86.8 14.7 %collective-permute-start.18 = (bf16[12,64,128]{2,1,0:T(8,128)(2,1)S(1)}, bf16[12,64,128]{2,1,0:T(8,128)(2,1)S(1)}, u32[]{:S(2)}, u32[]{:S(2)}) collective-permute-start(bf16[12,64,128]{2,1,0:T(8,128)(2,1)S(1)} %slice.239), channel_id=1, source_target_pairs={{0,8},{8,0},{16,24},{24,16},{1,9},{9,1},{17,25},{25,17},{2,10},{10... | collective-permute-start | bytes 589832 | tf_op jit(solution)/shard_map/ppermute | solution.py:137
  94.6 10.5 %collective-permute-start.16 = (bf16[12,64,128]{2,1,0:T(8,128)(2,1)S(1)}, bf16[12,64,128]{2,1,0:T(8,128)(2,1)S(1)}, u32[]{:S(2)}, u32[]{:S(2)}) collective-permute-start(bf16[12,64,128]{2,1,0:T(8,128)(2,1)S(1)} %slice.240), channel_id=1, source_target_pairs={{0,2},{1,3},{2,0},{3,1},{4,6},{5,7},{6,4},{7,5},{8,10},{9,11},{10,... | collective-permute-start | bytes 589832 | tf_op jit(solution)/shard_map/ppermute | solution.py:137
  101.5 4.7 %collective-permute-start.19 = (bf16[6,64,128]{2,1,0:T(8,128)(2,1)S(1)}, bf16[6,64,128]{2,1,0:T(8,128)(2,1)S(1)}, u32[]{:S(2)}, u32[]{:S(2)}) collective-permute-start(bf16[6,64,128]{2,1,0:T(8,128)(2,1)S(1)} %slice.245), channel_id=1, source_target_pairs={{0,16},{8,24},{16,0},{24,8},{1,17},{9,25},{17,1},{25,9},{2,18},{10... | collective-permute-start | bytes 294920 | tf_op jit(solution)/shard_map/ppermute | solution.py:137
  105.2 5.6 %collective-permute-start.17 = (bf16[6,64,128]{2,1,0:T(8,128)(2,1)S(1)}, bf16[6,64,128]{2,1,0:T(8,128)(2,1)S(1)}, u32[]{:S(2)}, u32[]{:S(2)}) collective-permute-start(bf16[6,64,128]{2,1,0:T(8,128)(2,1)S(1)} %slice.246), channel_id=1, source_target_pairs={{0,4},{1,5},{2,6},{3,7},{4,0},{5,1},{6,2},{7,3},{8,12},{9,13},{10,... | collective-permute-start | bytes 294920 | tf_op jit(solution)/shard_map/ppermute | solution.py:137
  105.3 12.8 %collective-permute-start.35 = (bf16[24,64,128]{2,1,0:T(8,128)(2,1)S(1)}, bf16[24,64,128]{2,1,0:T(8,128)(2,1)S(1)}, u32[]{:S(2)}, u32[]{:S(2)}) collective-permute-start(bf16[24,64,128]{2,1,0:T(8,128)(2,1)S(1)} %slice.232), channel_id=1, source_target_pairs={{0,1},{1,0},{2,3},{3,2},{4,5},{5,4},{6,7},{7,6},{8,9},{9,8},{10,11... | collective-permute-start | bytes 1179656 | tf_op jit(solution)/shard_map/ppermute | solution.py:137
  111.1 1.3 collective-permute-start.20
  112.4 3.9 %collective-permute-start.21 = (f32[64,64]{0,1:T(8,128)S(1)}, f32[64,64]{0,1:T(8,128)S(1)}, u32[]{:S(2)}, u32[]{:S(2)}) collective-permute-start(f32[64,64]{0,1:T(8,128)S(1)} %add.159), channel_id=1, source_target_pairs={{0,16},{8,24},{16,0},{24,8},{1,17},{9,25},{17,1},{25,9},{2,18},{10... | collective-permute-start | bytes 49160 | tf_op jit(solution)/shard_map/ppermute | solution.py:147
  112.5 9.9 %collective-permute-start.38 = (bf16[12,64,128]{2,1,0:T(8,128)(2,1)S(1)}, bf16[12,64,128]{2,1,0:T(8,128)(2,1)S(1)}, u32[]{:S(2)}, u32[]{:S(2)}) collective-permute-start(bf16[12,64,128]{2,1,0:T(8,128)(2,1)S(1)} %slice.235), channel_id=1, source_target_pairs={{0,8},{8,0},{16,24},{24,16},{1,9},{9,1},{17,25},{25,17},{2,10},{10... | collective-permute-start | bytes 589832 | tf_op jit(solution)/shard_map/ppermute | solution.py:137
  116.3 3.9 %collective-permute-start.22 = (f32[64,64]{0,1:T(8,128)S(1)}, f32[64,64]{0,1:T(8,128)S(1)}, u32[]{:S(2)}, u32[]{:S(2)}) collective-permute-start(f32[64,64]{0,1:T(8,128)S(1)} %add.160), channel_id=1, source_target_pairs={{0,1},{1,0},{2,3},{3,2},{4,5},{5,4},{6,7},{7,6},{8,9},{9,8},{10,11... | collective-permute-start | bytes 49160 | tf_op jit(solution)/shard_map/ppermute | solution.py:147
  118.3 6.4 %collective-permute-start.36 = (bf16[12,64,128]{2,1,0:T(8,128)(2,1)S(1)}, bf16[12,64,128]{2,1,0:T(8,128)(2,1)S(1)}, u32[]{:S(2)}, u32[]{:S(2)}) collective-permute-start(bf16[12,64,128]{2,1,0:T(8,128)(2,1)S(1)} %slice.236), channel_id=1, source_target_pairs={{0,2},{1,3},{2,0},{3,1},{4,6},{5,7},{6,4},{7,5},{8,10},{9,11},{10,... | collective-permute-start | bytes 589832 | tf_op jit(solution)/shard_map/ppermute | solution.py:137
  120.3 12.9 %copy-start.2 = (f32[64,768]{1,0:T(8,128)S(1)}, f32[64,768]{1,0:T(8,128)}, u32[]{:S(2)}) copy-start(f32[64,768]{1,0:T(8,128)} %param.7) | copy-start | bytes 589828
  120.3 4.4 %collective-permute-start.23 = (f32[64,64]{0,1:T(8,128)S(1)}, f32[64,64]{0,1:T(8,128)S(1)}, u32[]{:S(2)}, u32[]{:S(2)}) collective-permute-start(f32[64,64]{0,1:T(8,128)S(1)} %add.161), channel_id=1, source_target_pairs={{0,2},{1,3},{2,0},{3,1},{4,6},{5,7},{6,4},{7,5},{8,10},{9,11},{10,... | collective-permute-start | bytes 49160 | tf_op jit(solution)/shard_map/ppermute | solution.py:147
  122.4 8.4 %collective-permute-start.39 = (bf16[6,64,128]{2,1,0:T(8,128)(2,1)S(1)}, bf16[6,64,128]{2,1,0:T(8,128)(2,1)S(1)}, u32[]{:S(2)}, u32[]{:S(2)}) collective-permute-start(bf16[6,64,128]{2,1,0:T(8,128)(2,1)S(1)} %slice.241), channel_id=1, source_target_pairs={{0,16},{8,24},{16,0},{24,8},{1,17},{9,25},{17,1},{25,9},{2,18},{10... | collective-permute-start | bytes 294920 | tf_op jit(solution)/shard_map/ppermute | solution.py:137
  124.6 4.8 %collective-permute-start.24 = (f32[64,64]{0,1:T(8,128)S(1)}, f32[64,64]{0,1:T(8,128)S(1)}, u32[]{:S(2)}, u32[]{:S(2)}) collective-permute-start(f32[64,64]{0,1:T(8,128)S(1)} %add.162), channel_id=1, source_target_pairs={{0,4},{1,5},{2,6},{3,7},{4,0},{5,1},{6,2},{7,3},{8,12},{9,13},{10,... | collective-permute-start | bytes 49160 | tf_op jit(solution)/shard_map/ppermute | solution.py:147
  124.8 8.4 %collective-permute-start.37 = (bf16[6,64,128]{2,1,0:T(8,128)(2,1)S(1)}, bf16[6,64,128]{2,1,0:T(8,128)(2,1)S(1)}, u32[]{:S(2)}, u32[]{:S(2)}) collective-permute-start(bf16[6,64,128]{2,1,0:T(8,128)(2,1)S(1)} %slice.242), channel_id=1, source_target_pairs={{0,4},{1,5},{2,6},{3,7},{4,0},{5,1},{6,2},{7,3},{8,12},{9,13},{10,... | collective-permute-start | bytes 294920 | tf_op jit(solution)/shard_map/ppermute | solution.py:137
  129.8 86.4 %copy-start.1 = (f32[64,768]{1,0:T(8,128)}, f32[64,768]{1,0:T(8,128)S(1)}, u32[]{:S(2)}) copy-start(f32[64,768]{1,0:T(8,128)S(1)} %convolution_subtract_fusion) | copy-start | bytes 589828
  129.8 4.7 %collective-permute-start.28 = (bf16[6,64,128]{2,1,0:T(8,128)(2,1)S(1)}, bf16[6,64,128]{2,1,0:T(8,128)(2,1)S(1)}, u32[]{:S(2)}, u32[]{:S(2)}) collective-permute-start(bf16[6,64,128]{2,1,0:T(8,128)(2,1)S(1)} %bitcast_bitcast_fusion), channel_id=1, source_target_pairs={{0,16},{8,24},{16,0},{24,8},{1,17},{9,25},{17,1},{25,9},{2,18},{10... | collective-permute-start | bytes 294920 | tf_op jit(solution)/shard_map/ppermute | solution.py:125
  130.1 5.5 %collective-permute-start.25 = (bf16[6,64,128]{2,1,0:T(8,128)(2,1)S(1)}, bf16[6,64,128]{2,1,0:T(8,128)(2,1)S(1)}, u32[]{:S(2)}, u32[]{:S(2)}) collective-permute-start(bf16[6,64,128]{2,1,0:T(8,128)(2,1)S(1)} %bitcast_bitcast_fusion), channel_id=1, source_target_pairs={{0,4},{1,5},{2,6},{3,7},{4,0},{5,1},{6,2},{7,3},{8,12},{9,13},{10,... | collective-permute-start | bytes 294920 | tf_op jit(solution)/shard_map/ppermute | solution.py:125
  135.7 2.9 %collective-permute-start.29 = (bf16[12,64,128]{2,1,0:T(8,128)(2,1)S(1)}, bf16[12,64,128]{2,1,0:T(8,128)(2,1)S(1)}, u32[]{:S(2)}, u32[]{:S(2)}) collective-permute-start(bf16[12,64,128]{2,1,0:T(8,128)(2,1)S(1)} %get-tuple-element.24), channel_id=1, source_target_pairs={{0,8},{8,0},{16,24},{24,16},{1,9},{9,1},{17,25},{25,17},{2,10},{10... | collective-permute-start | bytes 589832 | tf_op jit(solution)/shard_map/ppermute | solution.py:125
  135.8 7.3 %collective-permute-start.26 = (bf16[12,64,128]{2,1,0:T(8,128)(2,1)S(1)}, bf16[12,64,128]{2,1,0:T(8,128)(2,1)S(1)}, u32[]{:S(2)}, u32[]{:S(2)}) collective-permute-start(bf16[12,64,128]{2,1,0:T(8,128)(2,1)S(1)} %get-tuple-element.25), channel_id=1, source_target_pairs={{0,2},{1,3},{2,0},{3,1},{4,6},{5,7},{6,4},{7,5},{8,10},{9,11},{10,... | collective-permute-start | bytes 589832 | tf_op jit(solution)/shard_map/ppermute | solution.py:125
  138.4 7.5 %collective-permute-start.40 = (f32[192,320]{1,0:T(8,128)S(1)}, f32[192,320]{1,0:T(8,128)S(1)}, u32[]{:S(2)}, u32[]{:S(2)}) collective-permute-start(f32[192,320]{1,0:T(8,128)S(1)} %pad_maximum_fusion.6), channel_id=1, source_target_pairs={{0,8},{8,0},{16,24},{24,16},{1,9},{9,1},{17,25},{25,17},{2,10},{10... | collective-permute-start | bytes 737288 | tf_op jit(solution)/shard_map/ppermute | solution.py:147
  143.2 11.7 %collective-permute-start.27 = (bf16[24,64,128]{2,1,0:T(8,128)(2,1)S(1)}, bf16[24,64,128]{2,1,0:T(8,128)(2,1)S(1)}, u32[]{:S(2)}, u32[]{:S(2)}) collective-permute-start(bf16[24,64,128]{2,1,0:T(8,128)(2,1)S(1)} %get-tuple-element.23), channel_id=1, source_target_pairs={{0,1},{1,0},{2,3},{3,2},{4,5},{5,4},{6,7},{7,6},{8,9},{9,8},{10,11... | collective-permute-start | bytes 1179656 | tf_op jit(solution)/shard_map/ppermute | solution.py:125
  146.1 30.2 %collective-permute-start.41 = (f32[192,320]{1,0:T(8,128)S(1)}, f32[192,320]{1,0:T(8,128)S(1)}, u32[]{:S(2)}, u32[]{:S(2)}) collective-permute-start(f32[192,320]{1,0:T(8,128)S(1)} %fusion.34), channel_id=1, source_target_pairs={{0,16},{8,24},{16,0},{24,8},{1,17},{9,25},{17,1},{25,9},{2,18},{10... | collective-permute-start | bytes 737288 | tf_op jit(solution)/shard_map/ppermute | solution.py:147
  176.2 16.8 %collective-permute-start.30 = (bf16[24,64,128]{2,1,0:T(8,128)(2,1)S(1)}, bf16[24,64,128]{2,1,0:T(8,128)(2,1)S(1)}, u32[]{:S(2)}, u32[]{:S(2)}) collective-permute-start(bf16[24,64,128]{2,1,0:T(8,128)(2,1)S(1)} %slice.233), channel_id=1, source_target_pairs={{0,1},{1,0},{2,3},{3,2},{4,5},{5,4},{6,7},{7,6},{8,9},{9,8},{10,11... | collective-permute-start | bytes 1179656 | tf_op jit(solution)/shard_map/ppermute | solution.py:137
  176.3 16.6 %collective-permute-start.42 = (f32[192,320]{1,0:T(8,128)S(1)}, f32[192,320]{1,0:T(8,128)S(1)}, u32[]{:S(2)}, u32[]{:S(2)}) collective-permute-start(f32[192,320]{1,0:T(8,128)S(1)} %add.177), channel_id=1, source_target_pairs={{0,1},{1,0},{2,3},{3,2},{4,5},{5,4},{6,7},{7,6},{8,9},{9,8},{10,11... | collective-permute-start | bytes 737288 | tf_op jit(solution)/shard_map/ppermute | solution.py:147
  178.4 16.8 %collective-permute-start.33 = (bf16[12,64,128]{2,1,0:T(8,128)(2,1)S(1)}, bf16[12,64,128]{2,1,0:T(8,128)(2,1)S(1)}, u32[]{:S(2)}, u32[]{:S(2)}) collective-permute-start(bf16[12,64,128]{2,1,0:T(8,128)(2,1)S(1)} %slice.237), channel_id=1, source_target_pairs={{0,8},{8,0},{16,24},{24,16},{1,9},{9,1},{17,25},{25,17},{2,10},{10... | collective-permute-start | bytes 589832 | tf_op jit(solution)/shard_map/ppermute | solution.py:137
  192.9 11.7 %collective-permute-start.43 = (f32[192,320]{1,0:T(8,128)S(1)}, f32[192,320]{1,0:T(8,128)S(1)}, u32[]{:S(2)}, u32[]{:S(2)}) collective-permute-start(f32[192,320]{1,0:T(8,128)S(1)} %add.178), channel_id=1, source_target_pairs={{0,2},{1,3},{2,0},{3,1},{4,6},{5,7},{6,4},{7,5},{8,10},{9,11},{10,... | collective-permute-start | bytes 737288 | tf_op jit(solution)/shard_map/ppermute | solution.py:147
  193.1 11.3 %collective-permute-start.31 = (bf16[12,64,128]{2,1,0:T(8,128)(2,1)S(1)}, bf16[12,64,128]{2,1,0:T(8,128)(2,1)S(1)}, u32[]{:S(2)}, u32[]{:S(2)}) collective-permute-start(bf16[12,64,128]{2,1,0:T(8,128)(2,1)S(1)} %slice.238), channel_id=1, source_target_pairs={{0,2},{1,3},{2,0},{3,1},{4,6},{5,7},{6,4},{7,5},{8,10},{9,11},{10,... | collective-permute-start | bytes 589832 | tf_op jit(solution)/shard_map/ppermute | solution.py:137
  195.3 12.3 %collective-permute-start.34 = (bf16[6,64,128]{2,1,0:T(8,128)(2,1)S(1)}, bf16[6,64,128]{2,1,0:T(8,128)(2,1)S(1)}, u32[]{:S(2)}, u32[]{:S(2)}) collective-permute-start(bf16[6,64,128]{2,1,0:T(8,128)(2,1)S(1)} %slice.243), channel_id=1, source_target_pairs={{0,16},{8,24},{16,0},{24,8},{1,17},{9,25},{17,1},{25,9},{2,18},{10... | collective-permute-start | bytes 294920 | tf_op jit(solution)/shard_map/ppermute | solution.py:137
  204.5 11.6 %collective-permute-start.32 = (bf16[6,64,128]{2,1,0:T(8,128)(2,1)S(1)}, bf16[6,64,128]{2,1,0:T(8,128)(2,1)S(1)}, u32[]{:S(2)}, u32[]{:S(2)}) collective-permute-start(bf16[6,64,128]{2,1,0:T(8,128)(2,1)S(1)} %slice.244), channel_id=1, source_target_pairs={{0,4},{1,5},{2,6},{3,7},{4,0},{5,1},{6,2},{7,3},{8,12},{9,13},{10,... | collective-permute-start | bytes 294920 | tf_op jit(solution)/shard_map/ppermute | solution.py:137
  204.6 23.3 %collective-permute-start.44 = (f32[192,320]{1,0:T(8,128)S(1)}, f32[192,320]{1,0:T(8,128)S(1)}, u32[]{:S(2)}, u32[]{:S(2)}) collective-permute-start(f32[192,320]{1,0:T(8,128)S(1)} %add.179), channel_id=1, source_target_pairs={{0,4},{1,5},{2,6},{3,7},{4,0},{5,1},{6,2},{7,3},{8,12},{9,13},{10,... | collective-permute-start | bytes 737288 | tf_op jit(solution)/shard_map/ppermute | solution.py:147
  216.2 17.1 %copy-start.3 = (f32[64,768]{1,0:T(8,128)}, f32[64,768]{1,0:T(8,128)S(1)}, u32[]{:S(2)}) copy-start(f32[64,768]{1,0:T(8,128)S(1)} %copy_bitcast_fusion) | copy-start | bytes 589828
  216.8 1.4 collective-permute-start.45
  218.2 4.9 %collective-permute-start.46 = (f32[192,64]{1,0:T(8,128)S(1)}, f32[192,64]{1,0:T(8,128)S(1)}, u32[]{:S(2)}, u32[]{:S(2)}) collective-permute-start(f32[192,64]{1,0:T(8,128)S(1)} %add.181), channel_id=1, source_target_pairs={{0,16},{8,24},{16,0},{24,8},{1,17},{9,25},{17,1},{25,9},{2,18},{10... | collective-permute-start | bytes 147464 | tf_op jit(solution)/shard_map/ppermute | solution.py:147
  223.1 4.7 %collective-permute-start.47 = (f32[192,64]{1,0:T(8,128)S(1)}, f32[192,64]{1,0:T(8,128)S(1)}, u32[]{:S(2)}, u32[]{:S(2)}) collective-permute-start(f32[192,64]{1,0:T(8,128)S(1)} %add.182), channel_id=1, source_target_pairs={{0,1},{1,0},{2,3},{3,2},{4,5},{5,4},{6,7},{7,6},{8,9},{9,8},{10,11... | collective-permute-start | bytes 147464 | tf_op jit(solution)/shard_map/ppermute | solution.py:147
  227.8 4.7 %collective-permute-start.48 = (f32[192,64]{1,0:T(8,128)S(1)}, f32[192,64]{1,0:T(8,128)S(1)}, u32[]{:S(2)}, u32[]{:S(2)}) collective-permute-start(f32[192,64]{1,0:T(8,128)S(1)} %add.183), channel_id=1, source_target_pairs={{0,2},{1,3},{2,0},{3,1},{4,6},{5,7},{6,4},{7,5},{8,10},{9,11},{10,... | collective-permute-start | bytes 147464 | tf_op jit(solution)/shard_map/ppermute | solution.py:147
  232.5 6.1 %collective-permute-start.49 = (f32[192,64]{1,0:T(8,128)S(1)}, f32[192,64]{1,0:T(8,128)S(1)}, u32[]{:S(2)}, u32[]{:S(2)}) collective-permute-start(f32[192,64]{1,0:T(8,128)S(1)} %add.184), channel_id=1, source_target_pairs={{0,4},{1,5},{2,6},{3,7},{4,0},{5,1},{6,2},{7,3},{8,12},{9,13},{10,... | collective-permute-start | bytes 147464 | tf_op jit(solution)/shard_map/ppermute | solution.py:147

commit v6 on v5

--- a/solution.py
+++ b/solution.py
@@ -133,7 +133,9 @@
     step = 1
     while step < size:
         half = held.shape[0] // 2
-        sent = held[half:].astype(jnp.bfloat16)
+        sent = held[half:]
+        if step == 1 and axis == "col":
+            sent = sent.astype(jnp.bfloat16)
         held = held[:half] + lax.ppermute(sent, axis, exchange_pairs(size, step)).astype(held.dtype)
         step *= 2
     return held

time: 238 us -> 256 us (1.076)
  starting transfers between devices: 52.8 us -> 80.9 us
  waiting for transfers between devices: 113 us -> 98.9 us
    ppermute x20, starting transfers between devices: 21 us -> 37.8 us  [all_sum(): value = value + lax.ppermute(value, axis, exchange_pairs(size, step))]
    ppermute x20, waiting for transfers between devices: 51.4 us -> 40 us  [all_sum(): value = value + lax.ppermute(value, axis, exchange_pairs(size, step))]
    ppermute x15, starting transfers between devices: 13.8 us -> 23.7 us  [scatter_sum(): lax.ppermute(sent, axis, exchange_pairs(size, step)).astype(held.dtype)]
    ppermute x15, waiting for transfers between devices: 35.7 us -> 30.9 us  [scatter_sum(): lax.ppermute(sent, axis, exchange_pairs(size, step)).astype(held.dtype)]
  transfers between devices with their start and end apart: 50 -> 50, of which waited for: 31 -> 29; matrix products, arithmetic and copies ran while one was open for 9% -> 8% of each run, Pallas kernels for 9% -> 9%
where the time goes in v6:
time: 256 us; the launch traced here: 255 us
  waiting for transfers between devices  98.9 us (39%)
  starting transfers between devices  80.9 us (32%)
  Pallas kernels  45.8 us (18%)
  other arithmetic  21.3 us (8%)
  matrix products  3.82 us (1%)
    pallas_call x2, Pallas kernels, tile_products(): pl.pallas_call(tile_kernel, grid_spec=grid_spec, out_shape=[jax.ShapeDtyp...  45.8 us
    ppermute x20, waiting for transfers between devices, all_sum(): value = value + lax.ppermute(value, axis, exchange_pairs(size, step))  40 us
    ppermute x20, starting transfers between devices, all_sum(): value = value + lax.ppermute(value, axis, exchange_pairs(size, step))  37.8 us
    ppermute x15, waiting for transfers between devices, scatter_sum(): lax.ppermute(sent, axis, exchange_pairs(size, step)).astype(held.dtype)  30.9 us
    ppermute x15, waiting for transfers between devices, gather_blocks(): lax.ppermute(held, axis, exchange_pairs(size, step))  27.9 us
    ppermute x15, starting transfers between devices, scatter_sum(): lax.ppermute(sent, axis, exchange_pairs(size, step)).astype(held.dtype)  23.7 us
    ppermute x15, starting transfers between devices, gather_blocks(): lax.ppermute(held, axis, exchange_pairs(size, step))  19.4 us
    another operation x3, other arithmetic, per_device(): cholesky_factor = jnp.linalg.cholesky(gram_x)  6.52 us
  transfers between devices with their start and end apart: 50, of which 29 were waited for; matrix products, arithmetic and copies ran while one was open for 8% of the time, Pallas kernels for 9%

profile of v6, /device:TPU:0, one launch (start us, length us, event | category | flops | bytes accessed | tf_op | source)
XLA Modules:
  0.0 254.9 jit_solution(12558097128307278630)
XLA Ops:
  0.6 0.9 copy-done
  2.4 0.9 collective-permute-done
  3.3 2.9 %collective-permute-start.1 = (f32[64,64]{0,1:T(8,128)S(1)}, f32[64,64]{0,1:T(8,128)S(1)}, u32[]{:S(2)}, u32[]{:S(2)}) collective-permute-start(f32[64,64]{0,1:T(8,128)S(1)} %add.147), channel_id=1, source_target_pairs={{0,16},{8,24},{16,0},{24,8},{1,17},{9,25},{17,1},{25,9},{2,18},{10... | collective-permute-start | bytes 49160 | tf_op jit(solution)/shard_map/ppermute | solution.py:149
  6.1 1.9 collective-permute-done.1
  8.0 2.0 collective-permute-start.2
  10.0 0.9 bitcast_bitcast_fusion.1
  11.0 1.6 collective-permute-start.13
  12.6 2.6 %collective-permute-start.8 = (bf16[6,64,128]{2,1,0:T(8,128)(2,1)S(1)}, bf16[6,64,128]{2,1,0:T(8,128)(2,1)S(1)}, u32[]{:S(2)}, u32[]{:S(2)}) collective-permute-start(bf16[6,64,128]{2,1,0:T(8,128)(2,1)S(1)} %bitcast_bitcast_fusion.1), channel_id=1, source_target_pairs={{0,4},{1,5},{2,6},{3,7},{4,0},{5,1},{6,2},{7,3},{8,12},{9,13},{10,... | collective-permute-start | bytes 294920 | tf_op jit(solution)/shard_map/ppermute | solution.py:125
  15.2 1.6 collective-permute-start.3
  17.5 1.6 collective-permute-done.3
  19.1 0.9 collective-permute-start.4
  20.7 3.2 %collective-permute-done.4 = f32[64,64]{0,1:T(8,128)S(1)} collective-permute-done((f32[64,64]{0,1:T(8,128)S(1)}, f32[64,64]{0,1:T(8,128)S(1)}, u32[]{:S(2)}, u32[]{:S(2)}) %collective-permute-start.4) | collective-permute-done | bytes 16416 | tf_op jit(solution)/shard_map/ppermute | solution.py:149
  24.1 5.8 %cholesky.16 = f32[64,64]{1,0:T(8,128)S(1)} custom-call(f32[64,64]{1,0:T(8,128)S(1)} %fusion.17), custom_call_target="Cholesky" | custom-call | tf_op jit(solution)/shard_map/jit(cholesky)/cholesky | solution.py:198
  31.2 4.9 %custom-call.6 = f32[1,64,64]{1,2,0:T(8,128)S(1)} custom-call(f32[1,64,64]{2,1,0:T(8,128)S(1)} %fusion.14), custom_call_target="InvertDiagBlocksLowerTriangular" | custom-call | tf_op jit(solution)/shard_map/triangular_solve | solution.py:199
  37.1 0.9 collective-permute-start.5
  38.1 1.9 collective-permute-start.9
  39.9 1.3 collective-permute-done.11
  41.3 1.5 collective-permute-done.5
  42.8 2.6 %collective-permute-start.6 = (bf16[12,64,128]{2,1,0:T(8,128)(2,1)S(1)}, bf16[12,64,128]{2,1,0:T(8,128)(2,1)S(1)}, u32[]{:S(2)}, u32[]{:S(2)}) collective-permute-start(bf16[12,64,128]{2,1,0:T(8,128)(2,1)S(1)} %get-tuple-element.27), channel_id=1, source_target_pairs={{0,2},{1,3},{2,0},{3,1},{4,6},{5,7},{6,4},{7,5},{8,10},{9,11},{10,... | collective-permute-start | bytes 589832 | tf_op jit(solution)/shard_map/ppermute | solution.py:125
  45.5 0.8 collective-permute-start.10
  46.3 2.7 %collective-permute-done.6 = bf16[12,64,128]{2,1,0:T(8,128)(2,1)S(1)} collective-permute-done((bf16[12,64,128]{2,1,0:T(8,128)(2,1)S(1)}, bf16[12,64,128]{2,1,0:T(8,128)(2,1)S(1)}, u32[]{:S(2)}, u32[]{:S(2)}) %collective-permute-start.6) | collective-permute-done | bytes 196640 | tf_op jit(solution)/shard_map/ppermute | solution.py:125
  51.2 0.9 collective-permute-done.14
  52.5 2.6 %collective-permute-done.10 = bf16[24,64,128]{2,1,0:T(8,128)(2,1)S(1)} collective-permute-done((bf16[24,64,128]{2,1,0:T(8,128)(2,1)S(1)}, bf16[24,64,128]{2,1,0:T(8,128)(2,1)S(1)}, u32[]{:S(2)}, u32[]{:S(2)}) %collective-permute-start.10) | collective-permute-done | bytes 393248 | tf_op jit(solution)/shard_map/ppermute | solution.py:125
  55.1 4.2 %collective-permute-done.7 = bf16[24,64,128]{2,1,0:T(8,128)(2,1)S(1)} collective-permute-done((bf16[24,64,128]{2,1,0:T(8,128)(2,1)S(1)}, bf16[24,64,128]{2,1,0:T(8,128)(2,1)S(1)}, u32[]{:S(2)}, u32[]{:S(2)}) %collective-permute-start.7) | collective-permute-done | bytes 393248 | tf_op jit(solution)/shard_map/ppermute | solution.py:125
  59.3 4.4 %maximum_maximum_fusion.rin_ref = bf16[48,128,128]{2,1,0:T(8,128)(2,1)} fusion(bf16[24,64,128]{2,1,0:T(8,128)(2,1)S(1)} %collective-permute-done.10, bf16[12,64,128]{2,1,0:T(8,128)(2,1)S(1)} %collective-permute-done.9, bf16[6,64,128]{2,1,0:T(8,128)(2,1)S(1)} %collective-permute-done.8, bf16[6,64,128]{2,1,0:T(8,128)(2,1)S(1)} %bitcast_bitcast_fusion.1, ...), kind=kLoop, calls=%fused_computation | loop fusion | flops 12582912 | bytes 3145728 | tf_op jit(solution)/shard_map/concatenate | solution.py:204
  63.7 23.8 %shard_map.93 = (f32[48,64,128]{2,1,0:T(8,128)S(1)}, f32[24,64,128]{2,1,0:T(8,128)S(1)}, f32[48,64,128]{2,1,0:T(8,128)S(1)}, f32[24,64,128]{2,1,0:T(8,128)S(1)}) custom-call(s32[576]{0:T(1024)S(1)} %get-tuple-element.30.rows_ref, s32[576]{0:T(1024)S(1)} %get-tuple-element.31.cols_ref, s32[1]{0:T(128)} %bitcast.61.cnt_ref, bf16[576,128,128]{2,1,0:T(8,128)(2,1)} %bitcast.63, ...), custom_call_target="tpu_custom_call" | custom-call | flops 4831838208 | bytes 25952256 | tf_op jit(solution)/shard_map/pallas_call | solution.py:94
  87.8 7.6 %collective-permute-done.15 = bf16[24,64,128]{2,1,0:T(8,128)(2,1)S(1)} collective-permute-done((bf16[24,64,128]{2,1,0:T(8,128)(2,1)S(1)}, bf16[24,64,128]{2,1,0:T(8,128)(2,1)S(1)}, u32[]{:S(2)}, u32[]{:S(2)}) %collective-permute-start.15) | collective-permute-done | bytes 393248 | tf_op jit(solution)/shard_map/ppermute | solution.py:139
  95.6 5.4 %collective-permute-start.16 = (f32[12,64,128]{2,1,0:T(8,128)S(1)}, f32[12,64,128]{2,1,0:T(8,128)S(1)}, u32[]{:S(2)}, u32[]{:S(2)}) collective-permute-start(f32[12,64,128]{2,1,0:T(8,128)S(1)} %slice.147), channel_id=1, source_target_pairs={{0,2},{1,3},{2,0},{3,1},{4,6},{5,7},{6,4},{7,5},{8,10},{9,11},{10,... | collective-permute-start | bytes 1179656 | tf_op jit(solution)/shard_map/ppermute | solution.py:139
  101.1 7.7 %collective-permute-done.16 = f32[12,64,128]{2,1,0:T(8,128)S(1)} collective-permute-done((f32[12,64,128]{2,1,0:T(8,128)S(1)}, f32[12,64,128]{2,1,0:T(8,128)S(1)}, u32[]{:S(2)}, u32[]{:S(2)}) %collective-permute-start.16) | collective-permute-done | bytes 393248 | tf_op jit(solution)/shard_map/ppermute | solution.py:139
  108.9 3.6 %collective-permute-start.17 = (f32[6,64,128]{2,1,0:T(8,128)S(1)}, f32[6,64,128]{2,1,0:T(8,128)S(1)}, u32[]{:S(2)}, u32[]{:S(2)}) collective-permute-start(f32[6,64,128]{2,1,0:T(8,128)S(1)} %slice.149), channel_id=1, source_target_pairs={{0,4},{1,5},{2,6},{3,7},{4,0},{5,1},{6,2},{7,3},{8,12},{9,13},{10,... | collective-permute-start | bytes 589832 | tf_op jit(solution)/shard_map/ppermute | solution.py:139
  112.7 1.3 collective-permute-start.35
  114.1 4.3 %collective-permute-done.17 = f32[6,64,128]{2,1,0:T(8,128)S(1)} collective-permute-done((f32[6,64,128]{2,1,0:T(8,128)S(1)}, f32[6,64,128]{2,1,0:T(8,128)S(1)}, u32[]{:S(2)}, u32[]{:S(2)}) %collective-permute-start.17) | collective-permute-done | bytes 196640 | tf_op jit(solution)/shard_map/ppermute | solution.py:139
  118.8 1.2 collective-permute-done.20
  120.0 3.9 %collective-permute-done.21 = f32[64,64]{0,1:T(8,128)S(1)} collective-permute-done((f32[64,64]{0,1:T(8,128)S(1)}, f32[64,64]{0,1:T(8,128)S(1)}, u32[]{:S(2)}, u32[]{:S(2)}) %collective-permute-start.21) | collective-permute-done | bytes 16416 | tf_op jit(solution)/shard_map/ppermute | solution.py:149
  123.9 1.2 collective-permute-start.22
  125.1 2.7 %collective-permute-done.22 = f32[64,64]{0,1:T(8,128)S(1)} collective-permute-done((f32[64,64]{0,1:T(8,128)S(1)}, f32[64,64]{0,1:T(8,128)S(1)}, u32[]{:S(2)}, u32[]{:S(2)}) %collective-permute-start.22) | collective-permute-done | bytes 16416 | tf_op jit(solution)/shard_map/ppermute | solution.py:149
  127.8 1.0 collective-permute-start.23
  129.0 2.8 %collective-permute-done.23 = f32[64,64]{0,1:T(8,128)S(1)} collective-permute-done((f32[64,64]{0,1:T(8,128)S(1)}, f32[64,64]{0,1:T(8,128)S(1)}, u32[]{:S(2)}, u32[]{:S(2)}) %collective-permute-start.23) | collective-permute-done | bytes 16416 | tf_op jit(solution)/shard_map/ppermute | solution.py:149
  131.7 2.7 %collective-permute-start.24 = (f32[64,64]{0,1:T(8,128)S(1)}, f32[64,64]{0,1:T(8,128)S(1)}, u32[]{:S(2)}, u32[]{:S(2)}) collective-permute-start(f32[64,64]{0,1:T(8,128)S(1)} %add.162), channel_id=1, source_target_pairs={{0,4},{1,5},{2,6},{3,7},{4,0},{5,1},{6,2},{7,3},{8,12},{9,13},{10,... | collective-permute-start | bytes 49160 | tf_op jit(solution)/shard_map/ppermute | solution.py:149
  134.6 2.1 collective-permute-start.36
  137.1 3.0 %collective-permute-start.25 = (bf16[6,64,128]{2,1,0:T(8,128)(2,1)S(1)}, bf16[6,64,128]{2,1,0:T(8,128)(2,1)S(1)}, u32[]{:S(2)}, u32[]{:S(2)}) collective-permute-start(bf16[6,64,128]{2,1,0:T(8,128)(2,1)S(1)} %bitcast_bitcast_fusion), channel_id=1, source_target_pairs={{0,4},{1,5},{2,6},{3,7},{4,0},{5,1},{6,2},{7,3},{8,12},{9,13},{10,... | collective-permute-start | bytes 294920 | tf_op jit(solution)/shard_map/ppermute | solution.py:125
  140.2 4.7 %collective-permute-done.36 = f32[12,64,128]{2,1,0:T(8,128)S(1)} collective-permute-done((f32[12,64,128]{2,1,0:T(8,128)S(1)}, f32[12,64,128]{2,1,0:T(8,128)S(1)}, u32[]{:S(2)}, u32[]{:S(2)}) %collective-permute-start.36) | collective-permute-done | bytes 393248 | tf_op jit(solution)/shard_map/ppermute | solution.py:139
  144.9 1.5 collective-permute-start.37
  146.5 2.7 %collective-permute-start.26 = (bf16[12,64,128]{2,1,0:T(8,128)(2,1)S(1)}, bf16[12,64,128]{2,1,0:T(8,128)(2,1)S(1)}, u32[]{:S(2)}, u32[]{:S(2)}) collective-permute-start(bf16[12,64,128]{2,1,0:T(8,128)(2,1)S(1)} %get-tuple-element.25), channel_id=1, source_target_pairs={{0,2},{1,3},{2,0},{3,1},{4,6},{5,7},{6,4},{7,5},{8,10},{9,11},{10,... | collective-permute-start | bytes 589832 | tf_op jit(solution)/shard_map/ppermute | solution.py:125
  149.8 5.9 %collective-permute-done.26 = bf16[12,64,128]{2,1,0:T(8,128)(2,1)S(1)} collective-permute-done((bf16[12,64,128]{2,1,0:T(8,128)(2,1)S(1)}, bf16[12,64,128]{2,1,0:T(8,128)(2,1)S(1)}, u32[]{:S(2)}, u32[]{:S(2)}) %collective-permute-start.26) | collective-permute-done | bytes 196640 | tf_op jit(solution)/shard_map/ppermute | solution.py:125
  155.8 1.3 collective-permute-start.27
  158.6 8.4 %collective-permute-done.27 = bf16[24,64,128]{2,1,0:T(8,128)(2,1)S(1)} collective-permute-done((bf16[24,64,128]{2,1,0:T(8,128)(2,1)S(1)}, bf16[24,64,128]{2,1,0:T(8,128)(2,1)S(1)}, u32[]{:S(2)}, u32[]{:S(2)}) %collective-permute-start.27) | collective-permute-done | bytes 393248 | tf_op jit(solution)/shard_map/ppermute | solution.py:125
  167.1 22.0 %shard_map.94 = (f32[48,64,128]{2,1,0:T(8,128)S(1)}, f32[24,64,128]{2,1,0:T(8,128)S(1)}) custom-call(s32[576]{0:T(1024)S(1)} %get-tuple-element.30.rows_ref, s32[576]{0:T(1024)S(1)} %get-tuple-element.31.cols_ref, s32[1]{0:T(128)} %bitcast.62.cnt_ref, bf16[576,128,128]{2,1,0:T(8,128)(2,1)} %bitcast.64, bf16[48,64,128]{2,1,0:T(8,128)(2,1)S(1)} %pad_maximum_fusion.rin_ref, ...), custom_call_target="tpu_custom_call" | custom-call | flops 2415919104 | bytes 22413312 | tf_op jit(solution)/shard_map/pallas_call | solution.py:94
  189.4 7.6 %collective-permute-done.41 = f32[192,320]{1,0:T(8,128)S(1)} collective-permute-done((f32[192,320]{1,0:T(8,128)S(1)}, f32[192,320]{1,0:T(8,128)S(1)}, u32[]{:S(2)}, u32[]{:S(2)}) %collective-permute-start.41) | collective-permute-done | bytes 245792 | tf_op jit(solution)/shard_map/ppermute | solution.py:149
  197.1 1.2 collective-permute-start.42
  198.5 4.4 %collective-permute-start.31 = (f32[12,64,128]{2,1,0:T(8,128)S(1)}, f32[12,64,128]{2,1,0:T(8,128)S(1)}, u32[]{:S(2)}, u32[]{:S(2)}) collective-permute-start(f32[12,64,128]{2,1,0:T(8,128)S(1)} %slice.154), channel_id=1, source_target_pairs={{0,2},{1,3},{2,0},{3,1},{4,6},{5,7},{6,4},{7,5},{8,10},{9,11},{10,... | collective-permute-start | bytes 1179656 | tf_op jit(solution)/shard_map/ppermute | solution.py:139
  202.9 0.9 collective-permute-done.42
  203.9 2.3 collective-permute-start.43
  206.3 6.6 %collective-permute-done.31 = f32[12,64,128]{2,1,0:T(8,128)S(1)} collective-permute-done((f32[12,64,128]{2,1,0:T(8,128)S(1)}, f32[12,64,128]{2,1,0:T(8,128)S(1)}, u32[]{:S(2)}, u32[]{:S(2)}) %collective-permute-start.31) | collective-permute-done | bytes 393248 | tf_op jit(solution)/shard_map/ppermute | solution.py:139
  213.0 4.8 %collective-permute-start.32 = (f32[6,64,128]{2,1,0:T(8,128)S(1)}, f32[6,64,128]{2,1,0:T(8,128)S(1)}, u32[]{:S(2)}, u32[]{:S(2)}) collective-permute-start(f32[6,64,128]{2,1,0:T(8,128)S(1)} %slice.156), channel_id=1, source_target_pairs={{0,4},{1,5},{2,6},{3,7},{4,0},{5,1},{6,2},{7,3},{8,12},{9,13},{10,... | collective-permute-start | bytes 589832 | tf_op jit(solution)/shard_map/ppermute | solution.py:139
  217.8 6.2 %collective-permute-start.44 = (f32[192,320]{1,0:T(8,128)S(1)}, f32[192,320]{1,0:T(8,128)S(1)}, u32[]{:S(2)}, u32[]{:S(2)}) collective-permute-start(f32[192,320]{1,0:T(8,128)S(1)} %add.179), channel_id=1, source_target_pairs={{0,4},{1,5},{2,6},{3,7},{4,0},{5,1},{6,2},{7,3},{8,12},{9,13},{10,... | collective-permute-start | bytes 737288 | tf_op jit(solution)/shard_map/ppermute | solution.py:149
  224.8 1.3 collective-permute-done.45
  226.2 4.8 %collective-permute-done.46 = f32[192,64]{1,0:T(8,128)S(1)} collective-permute-done((f32[192,64]{1,0:T(8,128)S(1)}, f32[192,64]{1,0:T(8,128)S(1)}, u32[]{:S(2)}, u32[]{:S(2)}) %collective-permute-start.46) | collective-permute-done | bytes 49184 | tf_op jit(solution)/shard_map/ppermute | solution.py:149
  231.1 1.8 collective-permute-start.47
  232.9 2.8 %collective-permute-done.47 = f32[192,64]{1,0:T(8,128)S(1)} collective-permute-done((f32[192,64]{1,0:T(8,128)S(1)}, f32[192,64]{1,0:T(8,128)S(1)}, u32[]{:S(2)}, u32[]{:S(2)}) %collective-permute-start.47) | collective-permute-done | bytes 49184 | tf_op jit(solution)/shard_map/ppermute | solution.py:149
  235.8 9.7 %collective-permute-start.48 = (f32[192,64]{1,0:T(8,128)S(1)}, f32[192,64]{1,0:T(8,128)S(1)}, u32[]{:S(2)}, u32[]{:S(2)}) collective-permute-start(f32[192,64]{1,0:T(8,128)S(1)} %add.183), channel_id=1, source_target_pairs={{0,2},{1,3},{2,0},{3,1},{4,6},{5,7},{6,4},{7,5},{8,10},{9,11},{10,... | collective-permute-start | bytes 147464 | tf_op jit(solution)/shard_map/ppermute | solution.py:149
  245.5 2.6 %collective-permute-done.48 = f32[192,64]{1,0:T(8,128)S(1)} collective-permute-done((f32[192,64]{1,0:T(8,128)S(1)}, f32[192,64]{1,0:T(8,128)S(1)}, u32[]{:S(2)}, u32[]{:S(2)}) %collective-permute-start.48) | collective-permute-done | bytes 49184 | tf_op jit(solution)/shard_map/ppermute | solution.py:149
  248.0 3.4 %collective-permute-start.49 = (f32[192,64]{1,0:T(8,128)S(1)}, f32[192,64]{1,0:T(8,128)S(1)}, u32[]{:S(2)}, u32[]{:S(2)}) collective-permute-start(f32[192,64]{1,0:T(8,128)S(1)} %add.184), channel_id=1, source_target_pairs={{0,4},{1,5},{2,6},{3,7},{4,0},{5,1},{6,2},{7,3},{8,12},{9,13},{10,... | collective-permute-start | bytes 147464 | tf_op jit(solution)/shard_map/ppermute | solution.py:149
  252.3 1.8 collective-permute-done.49
  (131 shorter events, 14.3 us)
Async XLA Ops:
  0.6 0.9 copy-start
  1.9 43.5 %copy-start.4 = (s32[1,1,576]{2,1,0:T(1,128)S(1)}, s32[1,1,576]{2,1,0:T(1,128)}, u32[]{:S(2)}) copy-start(s32[1,1,576]{2,1,0:T(1,128)} %param.8) | copy-start | bytes 6916
  1.9 1.4 collective-permute-start
  3.3 4.8 %collective-permute-start.1 = (f32[64,64]{0,1:T(8,128)S(1)}, f32[64,64]{0,1:T(8,128)S(1)}, u32[]{:S(2)}, u32[]{:S(2)}) collective-permute-start(f32[64,64]{0,1:T(8,128)S(1)} %add.147), channel_id=1, source_target_pairs={{0,16},{8,24},{16,0},{24,8},{1,17},{9,25},{17,1},{25,9},{2,18},{10... | collective-permute-start | bytes 49160 | tf_op jit(solution)/shard_map/ppermute | solution.py:149
  8.0 7.1 %collective-permute-start.2 = (f32[64,64]{0,1:T(8,128)S(1)}, f32[64,64]{0,1:T(8,128)S(1)}, u32[]{:S(2)}, u32[]{:S(2)}) collective-permute-start(f32[64,64]{0,1:T(8,128)S(1)} %add.148), channel_id=1, source_target_pairs={{0,1},{1,0},{2,3},{3,2},{4,5},{5,4},{6,7},{7,6},{8,9},{9,8},{10,11... | collective-permute-start | bytes 49160 | tf_op jit(solution)/shard_map/ppermute | solution.py:149
  11.0 27.1 %collective-permute-start.13 = (bf16[6,64,128]{2,1,0:T(8,128)(2,1)S(1)}, bf16[6,64,128]{2,1,0:T(8,128)(2,1)S(1)}, u32[]{:S(2)}, u32[]{:S(2)}) collective-permute-start(bf16[6,64,128]{2,1,0:T(8,128)(2,1)S(1)} %bitcast_bitcast_fusion.1), channel_id=1, source_target_pairs={{0,16},{8,24},{16,0},{24,8},{1,17},{9,25},{17,1},{25,9},{2,18},{10... | collective-permute-start | bytes 294920 | tf_op jit(solution)/shard_map/ppermute | solution.py:125
  12.6 25.5 %collective-permute-start.8 = (bf16[6,64,128]{2,1,0:T(8,128)(2,1)S(1)}, bf16[6,64,128]{2,1,0:T(8,128)(2,1)S(1)}, u32[]{:S(2)}, u32[]{:S(2)}) collective-permute-start(bf16[6,64,128]{2,1,0:T(8,128)(2,1)S(1)} %bitcast_bitcast_fusion.1), channel_id=1, source_target_pairs={{0,4},{1,5},{2,6},{3,7},{4,0},{5,1},{6,2},{7,3},{8,12},{9,13},{10,... | collective-permute-start | bytes 294920 | tf_op jit(solution)/shard_map/ppermute | solution.py:125
  15.2 4.0 %collective-permute-start.3 = (f32[64,64]{0,1:T(8,128)S(1)}, f32[64,64]{0,1:T(8,128)S(1)}, u32[]{:S(2)}, u32[]{:S(2)}) collective-permute-start(f32[64,64]{0,1:T(8,128)S(1)} %add.149), channel_id=1, source_target_pairs={{0,2},{1,3},{2,0},{3,1},{4,6},{5,7},{6,4},{7,5},{8,10},{9,11},{10,... | collective-permute-start | bytes 49160 | tf_op jit(solution)/shard_map/ppermute | solution.py:149
  19.1 4.8 %collective-permute-start.4 = (f32[64,64]{0,1:T(8,128)S(1)}, f32[64,64]{0,1:T(8,128)S(1)}, u32[]{:S(2)}, u32[]{:S(2)}) collective-permute-start(f32[64,64]{0,1:T(8,128)S(1)} %add.150), channel_id=1, source_target_pairs={{0,4},{1,5},{2,6},{3,7},{4,0},{5,1},{6,2},{7,3},{8,12},{9,13},{10,... | collective-permute-start | bytes 49160 | tf_op jit(solution)/shard_map/ppermute | solution.py:149
  36.5 13.4 %copy-start.5 = (s32[1,1,576]{2,1,0:T(1,128)S(1)}, s32[1,1,576]{2,1,0:T(1,128)}, u32[]{:S(2)}) copy-start(s32[1,1,576]{2,1,0:T(1,128)} %param.9) | copy-start | bytes 6916
  36.6 4.7 %collective-permute-start.11 = (bf16[6,64,128]{2,1,0:T(8,128)(2,1)S(1)}, bf16[6,64,128]{2,1,0:T(8,128)(2,1)S(1)}, u32[]{:S(2)}, u32[]{:S(2)}) collective-permute-start(bf16[6,64,128]{2,1,0:T(8,128)(2,1)S(1)} %bitcast_bitcast_fusion.2), channel_id=1, source_target_pairs={{0,16},{8,24},{16,0},{24,8},{1,17},{9,25},{17,1},{25,9},{2,18},{10... | collective-permute-start | bytes 294920 | tf_op jit(solution)/shard_map/ppermute | solution.py:125
  37.1 5.6 %collective-permute-start.5 = (bf16[6,64,128]{2,1,0:T(8,128)(2,1)S(1)}, bf16[6,64,128]{2,1,0:T(8,128)(2,1)S(1)}, u32[]{:S(2)}, u32[]{:S(2)}) collective-permute-start(bf16[6,64,128]{2,1,0:T(8,128)(2,1)S(1)} %bitcast_bitcast_fusion.2), channel_id=1, source_target_pairs={{0,4},{1,5},{2,6},{3,7},{4,0},{5,1},{6,2},{7,3},{8,12},{9,13},{10,... | collective-permute-start | bytes 294920 | tf_op jit(solution)/shard_map/ppermute | solution.py:125
  38.1 7.4 %collective-permute-start.9 = (bf16[12,64,128]{2,1,0:T(8,128)(2,1)S(1)}, bf16[12,64,128]{2,1,0:T(8,128)(2,1)S(1)}, u32[]{:S(2)}, u32[]{:S(2)}) collective-permute-start(bf16[12,64,128]{2,1,0:T(8,128)(2,1)S(1)} %get-tuple-element.29), channel_id=1, source_target_pairs={{0,2},{1,3},{2,0},{3,1},{4,6},{5,7},{6,4},{7,5},{8,10},{9,11},{10,... | collective-permute-start | bytes 589832 | tf_op jit(solution)/shard_map/ppermute | solution.py:125
  42.8 6.2 %collective-permute-start.6 = (bf16[12,64,128]{2,1,0:T(8,128)(2,1)S(1)}, bf16[12,64,128]{2,1,0:T(8,128)(2,1)S(1)}, u32[]{:S(2)}, u32[]{:S(2)}) collective-permute-start(bf16[12,64,128]{2,1,0:T(8,128)(2,1)S(1)} %get-tuple-element.27), channel_id=1, source_target_pairs={{0,2},{1,3},{2,0},{3,1},{4,6},{5,7},{6,4},{7,5},{8,10},{9,11},{10,... | collective-permute-start | bytes 589832 | tf_op jit(solution)/shard_map/ppermute | solution.py:125
  45.5 9.6 %collective-permute-start.10 = (bf16[24,64,128]{2,1,0:T(8,128)(2,1)S(1)}, bf16[24,64,128]{2,1,0:T(8,128)(2,1)S(1)}, u32[]{:S(2)}, u32[]{:S(2)}) collective-permute-start(bf16[24,64,128]{2,1,0:T(8,128)(2,1)S(1)} %pad_maximum_fusion.5), channel_id=1, source_target_pairs={{0,1},{1,0},{2,3},{3,2},{4,5},{5,4},{6,7},{7,6},{8,9},{9,8},{10,11... | collective-permute-start | bytes 1179656 | tf_op jit(solution)/shard_map/ppermute | solution.py:125
  49.1 10.2 %collective-permute-start.7 = (bf16[24,64,128]{2,1,0:T(8,128)(2,1)S(1)}, bf16[24,64,128]{2,1,0:T(8,128)(2,1)S(1)}, u32[]{:S(2)}, u32[]{:S(2)}) collective-permute-start(bf16[24,64,128]{2,1,0:T(8,128)(2,1)S(1)} %pad_maximum_fusion.4), channel_id=1, source_target_pairs={{0,1},{1,0},{2,3},{3,2},{4,5},{5,4},{6,7},{7,6},{8,9},{9,8},{10,11... | collective-permute-start | bytes 1179656 | tf_op jit(solution)/shard_map/ppermute | solution.py:125
  50.6 1.5 collective-permute-start.14
  50.7 1.7 collective-permute-start.12
  87.6 7.8 %collective-permute-start.15 = (bf16[24,64,128]{2,1,0:T(8,128)(2,1)S(1)}, bf16[24,64,128]{2,1,0:T(8,128)(2,1)S(1)}, u32[]{:S(2)}, u32[]{:S(2)}) collective-permute-start(bf16[24,64,128]{2,1,0:T(8,128)(2,1)S(1)} %slice.207), channel_id=1, source_target_pairs={{0,1},{1,0},{2,3},{3,2},{4,5},{5,4},{6,7},{7,6},{8,9},{9,8},{10,11... | collective-permute-start | bytes 1179656 | tf_op jit(solution)/shard_map/ppermute | solution.py:139
  87.7 13.2 %collective-permute-start.18 = (f32[12,64,128]{2,1,0:T(8,128)S(1)}, f32[12,64,128]{2,1,0:T(8,128)S(1)}, u32[]{:S(2)}, u32[]{:S(2)}) collective-permute-start(f32[12,64,128]{2,1,0:T(8,128)S(1)} %slice.119), channel_id=1, source_target_pairs={{0,8},{8,0},{16,24},{24,16},{1,9},{9,1},{17,25},{25,17},{2,10},{10... | collective-permute-start | bytes 1179656 | tf_op jit(solution)/shard_map/ppermute | solution.py:139
  95.6 13.2 %collective-permute-start.16 = (f32[12,64,128]{2,1,0:T(8,128)S(1)}, f32[12,64,128]{2,1,0:T(8,128)S(1)}, u32[]{:S(2)}, u32[]{:S(2)}) collective-permute-start(f32[12,64,128]{2,1,0:T(8,128)S(1)} %slice.147), channel_id=1, source_target_pairs={{0,2},{1,3},{2,0},{3,1},{4,6},{5,7},{6,4},{7,5},{8,10},{9,11},{10,... | collective-permute-start | bytes 1179656 | tf_op jit(solution)/shard_map/ppermute | solution.py:139
  101.1 13.0 %collective-permute-start.19 = (f32[6,64,128]{2,1,0:T(8,128)S(1)}, f32[6,64,128]{2,1,0:T(8,128)S(1)}, u32[]{:S(2)}, u32[]{:S(2)}) collective-permute-start(f32[6,64,128]{2,1,0:T(8,128)S(1)} %slice.151), channel_id=1, source_target_pairs={{0,16},{8,24},{16,0},{24,8},{1,17},{9,25},{17,1},{25,9},{2,18},{10... | collective-permute-start | bytes 589832 | tf_op jit(solution)/shard_map/ppermute | solution.py:139
  108.9 9.4 %collective-permute-start.17 = (f32[6,64,128]{2,1,0:T(8,128)S(1)}, f32[6,64,128]{2,1,0:T(8,128)S(1)}, u32[]{:S(2)}, u32[]{:S(2)}) collective-permute-start(f32[6,64,128]{2,1,0:T(8,128)S(1)} %slice.149), channel_id=1, source_target_pairs={{0,4},{1,5},{2,6},{3,7},{4,0},{5,1},{6,2},{7,3},{8,12},{9,13},{10,... | collective-permute-start | bytes 589832 | tf_op jit(solution)/shard_map/ppermute | solution.py:139
  112.7 16.1 %collective-permute-start.38 = (f32[12,64,128]{2,1,0:T(8,128)S(1)}, f32[12,64,128]{2,1,0:T(8,128)S(1)}, u32[]{:S(2)}, u32[]{:S(2)}) collective-permute-start(f32[12,64,128]{2,1,0:T(8,128)S(1)} %slice.139), channel_id=1, source_target_pairs={{0,8},{8,0},{16,24},{24,16},{1,9},{9,1},{17,25},{25,17},{2,10},{10... | collective-permute-start | bytes 1179656 | tf_op jit(solution)/shard_map/ppermute | solution.py:139
  112.7 21.7 %collective-permute-start.35 = (bf16[24,64,128]{2,1,0:T(8,128)(2,1)S(1)}, bf16[24,64,128]{2,1,0:T(8,128)(2,1)S(1)}, u32[]{:S(2)}, u32[]{:S(2)}) collective-permute-start(bf16[24,64,128]{2,1,0:T(8,128)(2,1)S(1)} %slice.205), channel_id=1, source_target_pairs={{0,1},{1,0},{2,3},{3,2},{4,5},{5,4},{6,7},{7,6},{8,9},{9,8},{10,11... | collective-permute-start | bytes 1179656 | tf_op jit(solution)/shard_map/ppermute | solution.py:139
  118.7 1.3 collective-permute-start.20
  120.0 3.9 %collective-permute-start.21 = (f32[64,64]{0,1:T(8,128)S(1)}, f32[64,64]{0,1:T(8,128)S(1)}, u32[]{:S(2)}, u32[]{:S(2)}) collective-permute-start(f32[64,64]{0,1:T(8,128)S(1)} %add.159), channel_id=1, source_target_pairs={{0,16},{8,24},{16,0},{24,8},{1,17},{9,25},{17,1},{25,9},{2,18},{10... | collective-permute-start | bytes 49160 | tf_op jit(solution)/shard_map/ppermute | solution.py:149
  123.9 3.9 %collective-permute-start.22 = (f32[64,64]{0,1:T(8,128)S(1)}, f32[64,64]{0,1:T(8,128)S(1)}, u32[]{:S(2)}, u32[]{:S(2)}) collective-permute-start(f32[64,64]{0,1:T(8,128)S(1)} %add.160), channel_id=1, source_target_pairs={{0,1},{1,0},{2,3},{3,2},{4,5},{5,4},{6,7},{7,6},{8,9},{9,8},{10,11... | collective-permute-start | bytes 49160 | tf_op jit(solution)/shard_map/ppermute | solution.py:149
  127.8 3.9 %collective-permute-start.23 = (f32[64,64]{0,1:T(8,128)S(1)}, f32[64,64]{0,1:T(8,128)S(1)}, u32[]{:S(2)}, u32[]{:S(2)}) collective-permute-start(f32[64,64]{0,1:T(8,128)S(1)} %add.161), channel_id=1, source_target_pairs={{0,2},{1,3},{2,0},{3,1},{4,6},{5,7},{6,4},{7,5},{8,10},{9,11},{10,... | collective-permute-start | bytes 49160 | tf_op jit(solution)/shard_map/ppermute | solution.py:149
  128.9 28.9 %collective-permute-start.39 = (f32[6,64,128]{2,1,0:T(8,128)S(1)}, f32[6,64,128]{2,1,0:T(8,128)S(1)}, u32[]{:S(2)}, u32[]{:S(2)}) collective-permute-start(f32[6,64,128]{2,1,0:T(8,128)S(1)} %slice.165), channel_id=1, source_target_pairs={{0,16},{8,24},{16,0},{24,8},{1,17},{9,25},{17,1},{25,9},{2,18},{10... | collective-permute-start | bytes 589832 | tf_op jit(solution)/shard_map/ppermute | solution.py:139
  131.7 5.0 %collective-permute-start.24 = (f32[64,64]{0,1:T(8,128)S(1)}, f32[64,64]{0,1:T(8,128)S(1)}, u32[]{:S(2)}, u32[]{:S(2)}) collective-permute-start(f32[64,64]{0,1:T(8,128)S(1)} %add.162), channel_id=1, source_target_pairs={{0,4},{1,5},{2,6},{3,7},{4,0},{5,1},{6,2},{7,3},{8,12},{9,13},{10,... | collective-permute-start | bytes 49160 | tf_op jit(solution)/shard_map/ppermute | solution.py:149
  134.6 14.6 %copy-start.2 = (f32[64,768]{1,0:T(8,128)S(1)}, f32[64,768]{1,0:T(8,128)}, u32[]{:S(2)}) copy-start(f32[64,768]{1,0:T(8,128)} %param.7) | copy-start | bytes 589828
  134.6 10.2 %collective-permute-start.36 = (f32[12,64,128]{2,1,0:T(8,128)S(1)}, f32[12,64,128]{2,1,0:T(8,128)S(1)}, u32[]{:S(2)}, u32[]{:S(2)}) collective-permute-start(f32[12,64,128]{2,1,0:T(8,128)S(1)} %slice.161), channel_id=1, source_target_pairs={{0,2},{1,3},{2,0},{3,1},{4,6},{5,7},{6,4},{7,5},{8,10},{9,11},{10,... | collective-permute-start | bytes 1179656 | tf_op jit(solution)/shard_map/ppermute | solution.py:139
  137.0 87.1 %copy-start.1 = (f32[64,768]{1,0:T(8,128)}, f32[64,768]{1,0:T(8,128)S(1)}, u32[]{:S(2)}) copy-start(f32[64,768]{1,0:T(8,128)S(1)} %convolution_subtract_fusion) | copy-start | bytes 589828
  137.1 9.3 %collective-permute-start.28 = (bf16[6,64,128]{2,1,0:T(8,128)(2,1)S(1)}, bf16[6,64,128]{2,1,0:T(8,128)(2,1)S(1)}, u32[]{:S(2)}, u32[]{:S(2)}) collective-permute-start(bf16[6,64,128]{2,1,0:T(8,128)(2,1)S(1)} %bitcast_bitcast_fusion), channel_id=1, source_target_pairs={{0,16},{8,24},{16,0},{24,8},{1,17},{9,25},{17,1},{25,9},{2,18},{10... | collective-permute-start | bytes 294920 | tf_op jit(solution)/shard_map/ppermute | solution.py:125
  137.1 9.2 %collective-permute-start.25 = (bf16[6,64,128]{2,1,0:T(8,128)(2,1)S(1)}, bf16[6,64,128]{2,1,0:T(8,128)(2,1)S(1)}, u32[]{:S(2)}, u32[]{:S(2)}) collective-permute-start(bf16[6,64,128]{2,1,0:T(8,128)(2,1)S(1)} %bitcast_bitcast_fusion), channel_id=1, source_target_pairs={{0,4},{1,5},{2,6},{3,7},{4,0},{5,1},{6,2},{7,3},{8,12},{9,13},{10,... | collective-permute-start | bytes 294920 | tf_op jit(solution)/shard_map/ppermute | solution.py:125
  144.9 12.9 %collective-permute-start.37 = (f32[6,64,128]{2,1,0:T(8,128)S(1)}, f32[6,64,128]{2,1,0:T(8,128)S(1)}, u32[]{:S(2)}, u32[]{:S(2)}) collective-permute-start(f32[6,64,128]{2,1,0:T(8,128)S(1)} %slice.163), channel_id=1, source_target_pairs={{0,4},{1,5},{2,6},{3,7},{4,0},{5,1},{6,2},{7,3},{8,12},{9,13},{10,... | collective-permute-start | bytes 589832 | tf_op jit(solution)/shard_map/ppermute | solution.py:139
  146.4 3.4 %collective-permute-start.29 = (bf16[12,64,128]{2,1,0:T(8,128)(2,1)S(1)}, bf16[12,64,128]{2,1,0:T(8,128)(2,1)S(1)}, u32[]{:S(2)}, u32[]{:S(2)}) collective-permute-start(bf16[12,64,128]{2,1,0:T(8,128)(2,1)S(1)} %get-tuple-element.24), channel_id=1, source_target_pairs={{0,8},{8,0},{16,24},{24,16},{1,9},{9,1},{17,25},{25,17},{2,10},{10... | collective-permute-start | bytes 589832 | tf_op jit(solution)/shard_map/ppermute | solution.py:125
  146.5 9.2 %collective-permute-start.26 = (bf16[12,64,128]{2,1,0:T(8,128)(2,1)S(1)}, bf16[12,64,128]{2,1,0:T(8,128)(2,1)S(1)}, u32[]{:S(2)}, u32[]{:S(2)}) collective-permute-start(bf16[12,64,128]{2,1,0:T(8,128)(2,1)S(1)} %get-tuple-element.25), channel_id=1, source_target_pairs={{0,2},{1,3},{2,0},{3,1},{4,6},{5,7},{6,4},{7,5},{8,10},{9,11},{10,... | collective-permute-start | bytes 589832 | tf_op jit(solution)/shard_map/ppermute | solution.py:125
  155.8 11.2 %collective-permute-start.27 = (bf16[24,64,128]{2,1,0:T(8,128)(2,1)S(1)}, bf16[24,64,128]{2,1,0:T(8,128)(2,1)S(1)}, u32[]{:S(2)}, u32[]{:S(2)}) collective-permute-start(bf16[24,64,128]{2,1,0:T(8,128)(2,1)S(1)} %get-tuple-element.23), channel_id=1, source_target_pairs={{0,1},{1,0},{2,3},{3,2},{4,5},{5,4},{6,7},{7,6},{8,9},{9,8},{10,11... | collective-permute-start | bytes 1179656 | tf_op jit(solution)/shard_map/ppermute | solution.py:125
  158.5 30.6 %collective-permute-start.40 = (f32[192,320]{1,0:T(8,128)S(1)}, f32[192,320]{1,0:T(8,128)S(1)}, u32[]{:S(2)}, u32[]{:S(2)}) collective-permute-start(f32[192,320]{1,0:T(8,128)S(1)} %pad_maximum_fusion.6), channel_id=1, source_target_pairs={{0,8},{8,0},{16,24},{24,16},{1,9},{9,1},{17,25},{25,17},{2,10},{10... | collective-permute-start | bytes 737288 | tf_op jit(solution)/shard_map/ppermute | solution.py:149
  189.1 9.2 %collective-permute-start.30 = (bf16[24,64,128]{2,1,0:T(8,128)(2,1)S(1)}, bf16[24,64,128]{2,1,0:T(8,128)(2,1)S(1)}, u32[]{:S(2)}, u32[]{:S(2)}) collective-permute-start(bf16[24,64,128]{2,1,0:T(8,128)(2,1)S(1)} %slice.206), channel_id=1, source_target_pairs={{0,1},{1,0},{2,3},{3,2},{4,5},{5,4},{6,7},{7,6},{8,9},{9,8},{10,11... | collective-permute-start | bytes 1179656 | tf_op jit(solution)/shard_map/ppermute | solution.py:139
  189.3 7.7 %collective-permute-start.41 = (f32[192,320]{1,0:T(8,128)S(1)}, f32[192,320]{1,0:T(8,128)S(1)}, u32[]{:S(2)}, u32[]{:S(2)}) collective-permute-start(f32[192,320]{1,0:T(8,128)S(1)} %fusion.34), channel_id=1, source_target_pairs={{0,16},{8,24},{16,0},{24,8},{1,17},{9,25},{17,1},{25,9},{2,18},{10... | collective-permute-start | bytes 737288 | tf_op jit(solution)/shard_map/ppermute | solution.py:149
  197.1 6.8 %collective-permute-start.42 = (f32[192,320]{1,0:T(8,128)S(1)}, f32[192,320]{1,0:T(8,128)S(1)}, u32[]{:S(2)}, u32[]{:S(2)}) collective-permute-start(f32[192,320]{1,0:T(8,128)S(1)} %add.177), channel_id=1, source_target_pairs={{0,1},{1,0},{2,3},{3,2},{4,5},{5,4},{6,7},{7,6},{8,9},{9,8},{10,11... | collective-permute-start | bytes 737288 | tf_op jit(solution)/shard_map/ppermute | solution.py:149
  198.3 7.9 %collective-permute-start.33 = (f32[12,64,128]{2,1,0:T(8,128)S(1)}, f32[12,64,128]{2,1,0:T(8,128)S(1)}, u32[]{:S(2)}, u32[]{:S(2)}) collective-permute-start(f32[12,64,128]{2,1,0:T(8,128)S(1)} %slice.129), channel_id=1, source_target_pairs={{0,8},{8,0},{16,24},{24,16},{1,9},{9,1},{17,25},{25,17},{2,10},{10... | collective-permute-start | bytes 1179656 | tf_op jit(solution)/shard_map/ppermute | solution.py:139
  198.5 14.4 %collective-permute-start.31 = (f32[12,64,128]{2,1,0:T(8,128)S(1)}, f32[12,64,128]{2,1,0:T(8,128)S(1)}, u32[]{:S(2)}, u32[]{:S(2)}) collective-permute-start(f32[12,64,128]{2,1,0:T(8,128)S(1)} %slice.154), channel_id=1, source_target_pairs={{0,2},{1,3},{2,0},{3,1},{4,6},{5,7},{6,4},{7,5},{8,10},{9,11},{10,... | collective-permute-start | bytes 1179656 | tf_op jit(solution)/shard_map/ppermute | solution.py:139
  203.9 13.9 %collective-permute-start.43 = (f32[192,320]{1,0:T(8,128)S(1)}, f32[192,320]{1,0:T(8,128)S(1)}, u32[]{:S(2)}, u32[]{:S(2)}) collective-permute-start(f32[192,320]{1,0:T(8,128)S(1)} %add.178), channel_id=1, source_target_pairs={{0,2},{1,3},{2,0},{3,1},{4,6},{5,7},{6,4},{7,5},{8,10},{9,11},{10,... | collective-permute-start | bytes 737288 | tf_op jit(solution)/shard_map/ppermute | solution.py:149
  206.2 17.8 %collective-permute-start.34 = (f32[6,64,128]{2,1,0:T(8,128)S(1)}, f32[6,64,128]{2,1,0:T(8,128)S(1)}, u32[]{:S(2)}, u32[]{:S(2)}) collective-permute-start(f32[6,64,128]{2,1,0:T(8,128)S(1)} %slice.158), channel_id=1, source_target_pairs={{0,16},{8,24},{16,0},{24,8},{1,17},{9,25},{17,1},{25,9},{2,18},{10... | collective-permute-start | bytes 589832 | tf_op jit(solution)/shard_map/ppermute | solution.py:139
  213.0 11.0 %collective-permute-start.32 = (f32[6,64,128]{2,1,0:T(8,128)S(1)}, f32[6,64,128]{2,1,0:T(8,128)S(1)}, u32[]{:S(2)}, u32[]{:S(2)}) collective-permute-start(f32[6,64,128]{2,1,0:T(8,128)S(1)} %slice.156), channel_id=1, source_target_pairs={{0,4},{1,5},{2,6},{3,7},{4,0},{5,1},{6,2},{7,3},{8,12},{9,13},{10,... | collective-permute-start | bytes 589832 | tf_op jit(solution)/shard_map/ppermute | solution.py:139
  217.8 27.6 %collective-permute-start.44 = (f32[192,320]{1,0:T(8,128)S(1)}, f32[192,320]{1,0:T(8,128)S(1)}, u32[]{:S(2)}, u32[]{:S(2)}) collective-permute-start(f32[192,320]{1,0:T(8,128)S(1)} %add.179), channel_id=1, source_target_pairs={{0,4},{1,5},{2,6},{3,7},{4,0},{5,1},{6,2},{7,3},{8,12},{9,13},{10,... | collective-permute-start | bytes 737288 | tf_op jit(solution)/shard_map/ppermute | solution.py:149
  224.1 27.5 %copy-start.3 = (f32[64,768]{1,0:T(8,128)}, f32[64,768]{1,0:T(8,128)S(1)}, u32[]{:S(2)}) copy-start(f32[64,768]{1,0:T(8,128)S(1)} %copy_bitcast_fusion) | copy-start | bytes 589828
  224.7 1.4 collective-permute-start.45
  226.1 4.9 %collective-permute-start.46 = (f32[192,64]{1,0:T(8,128)S(1)}, f32[192,64]{1,0:T(8,128)S(1)}, u32[]{:S(2)}, u32[]{:S(2)}) collective-permute-start(f32[192,64]{1,0:T(8,128)S(1)} %add.181), channel_id=1, source_target_pairs={{0,16},{8,24},{16,0},{24,8},{1,17},{9,25},{17,1},{25,9},{2,18},{10... | collective-permute-start | bytes 147464 | tf_op jit(solution)/shard_map/ppermute | solution.py:149
  231.1 4.7 %collective-permute-start.47 = (f32[192,64]{1,0:T(8,128)S(1)}, f32[192,64]{1,0:T(8,128)S(1)}, u32[]{:S(2)}, u32[]{:S(2)}) collective-permute-start(f32[192,64]{1,0:T(8,128)S(1)} %add.182), channel_id=1, source_target_pairs={{0,1},{1,0},{2,3},{3,2},{4,5},{5,4},{6,7},{7,6},{8,9},{9,8},{10,11... | collective-permute-start | bytes 147464 | tf_op jit(solution)/shard_map/ppermute | solution.py:149
  235.8 12.3 %collective-permute-start.48 = (f32[192,64]{1,0:T(8,128)S(1)}, f32[192,64]{1,0:T(8,128)S(1)}, u32[]{:S(2)}, u32[]{:S(2)}) collective-permute-start(f32[192,64]{1,0:T(8,128)S(1)} %add.183), channel_id=1, source_target_pairs={{0,2},{1,3},{2,0},{3,1},{4,6},{5,7},{6,4},{7,5},{8,10},{9,11},{10,... | collective-permute-start | bytes 147464 | tf_op jit(solution)/shard_map/ppermute | solution.py:149
  248.0 6.0 %collective-permute-start.49 = (f32[192,64]{1,0:T(8,128)S(1)}, f32[192,64]{1,0:T(8,128)S(1)}, u32[]{:S(2)}, u32[]{:S(2)}) collective-permute-start(f32[192,64]{1,0:T(8,128)S(1)} %add.184), channel_id=1, source_target_pairs={{0,4},{1,5},{2,6},{3,7},{4,0},{5,1},{6,2},{7,3},{8,12},{9,13},{10,... | collective-permute-start | bytes 147464 | tf_op jit(solution)/shard_map/ppermute | solution.py:149

commit v7 on v6

--- a/solution.py
+++ b/solution.py
@@ -151,6 +151,20 @@
     return value
 
 
+def all_sum_direct(value):
+    for axis in ("row", "col"):
+        size = lax.axis_size(axis)
+        me = lax.axis_index(axis)
+        got = [value] + [
+            lax.ppermute(value, axis, exchange_pairs(size, step)) for step in range(1, size)
+        ]
+        ordered = jnp.take(jnp.stack(got), me ^ jnp.arange(size), axis=0)
+        value = ordered[0]
+        for k in range(1, size):
+            value = value + ordered[k]
+    return value
+
+
 def held_position(index, axis, blocks_each):
     size = lax.axis_size(axis)
     bits = size.bit_length() - 1
@@ -194,7 +208,7 @@
             / node_count
         )
 
-    gram_x = all_sum(product(block_x, block_x))
+    gram_x = all_sum_direct(product(block_x, block_x))
     cholesky_factor = jnp.linalg.cholesky(gram_x)
     orthonormal = lax.linalg.triangular_solve(cholesky_factor, block_x, left_side=True, lower=True)
     tile = tile_vals.shape[-1]
@@ -206,7 +220,7 @@
         slot_rows, slot_cols, live_count, slot_vals, (width_k, block_p.shape[0]),
     )
     image_x = owned(x_rows, x_cols)
-    rayleigh = all_sum(product(orthonormal, image_x))
+    rayleigh = all_sum_direct(product(orthonormal, image_x))
     residual = image_x - jnp.dot(
         rayleigh.T, orthonormal, precision=highest, preferred_element_type=jnp.float32
     )
@@ -222,7 +236,7 @@
         res_rows, res_cols, slot_rows, slot_cols, live_count, slot_vals, (residual.shape[0],)
     )
     image_r = owned(r_rows, r_cols)
-    late = all_sum(product(basis, image_r))
+    late = all_sum_direct(product(basis, image_r))
     span = basis.shape[0]
     gram_b = early[:, :span]
     gram_a = jnp.concatenate(

time: 256 us -> 278 us (1.086)
  waiting for transfers between devices: 98.9 us -> 121 us
  starting transfers between devices: 80.9 us -> 66.5 us
  local copies, waits for them, and re-layouts: 2.25 us -> 11.1 us
  Pallas kernels: 45.8 us -> 49.2 us
  other arithmetic: 21.3 us -> 24.6 us
    ppermute x20 -> x5, starting transfers between devices: 37.8 us -> 0.37 us  [all_sum(): value = value + lax.ppermute(value, axis, exchange_pairs(size, step))]
    ppermute x0 -> x30, starting transfers between devices: none -> 36.4 us  [all_sum_direct(): lax.ppermute(value, axis, exchange_pairs(size, step))]
    ppermute x0 -> x30, waiting for transfers between devices: none -> 25.8 us  [all_sum_direct(): lax.ppermute(value, axis, exchange_pairs(size, step))]
    ppermute x20 -> x5, waiting for transfers between devices: 40 us -> 23.1 us  [all_sum(): value = value + lax.ppermute(value, axis, exchange_pairs(size, step))]
    ppermute x15, starting transfers between devices: 19.4 us -> 12.5 us  [gather_blocks(): lax.ppermute(held, axis, exchange_pairs(size, step))]
    ppermute x15, waiting for transfers between devices: 30.9 us -> 37.6 us  [scatter_sum(): lax.ppermute(sent, axis, exchange_pairs(size, step)).astype(held.dtype)]
    ppermute x15, starting transfers between devices: 23.7 us -> 17.2 us  [scatter_sum(): lax.ppermute(sent, axis, exchange_pairs(size, step)).astype(held.dtype)]
    ppermute x15, waiting for transfers between devices: 27.9 us -> 34.1 us  [gather_blocks(): lax.ppermute(held, axis, exchange_pairs(size, step))]
  transfers between devices with their start and end apart: 50 -> 65, of which waited for: 29 -> 33; matrix products, arithmetic and copies ran while one was open for 8% -> 11% of each run, Pallas kernels for 9% -> 8%
where the time goes in v7:
time: 278 us
  waiting for transfers between devices  121 us (44%)
  starting transfers between devices  66.5 us (24%)
  Pallas kernels  49.2 us (18%)
  other arithmetic  24.6 us (9%)
  local copies, waits for them, and re-layouts  11.1 us (4%)
  matrix products  3.88 us (1%)
    pallas_call x2, Pallas kernels, tile_products(): pl.pallas_call(tile_kernel, grid_spec=grid_spec, out_shape=[jax.ShapeDtyp...  49.2 us
    ppermute x15, waiting for transfers between devices, scatter_sum(): lax.ppermute(sent, axis, exchange_pairs(size, step)).astype(held.dtype)  37.6 us
    ppermute x30, starting transfers between devices, all_sum_direct(): lax.ppermute(value, axis, exchange_pairs(size, step))  36.4 us
    ppermute x15, waiting for transfers between devices, gather_blocks(): lax.ppermute(held, axis, exchange_pairs(size, step))  34.1 us
    ppermute x30, waiting for transfers between devices, all_sum_direct(): lax.ppermute(value, axis, exchange_pairs(size, step))  25.8 us
    ppermute x5, waiting for transfers between devices, all_sum(): value = value + lax.ppermute(value, axis, exchange_pairs(size, step))  23.1 us
    ppermute x15, starting transfers between devices, scatter_sum(): lax.ppermute(sent, axis, exchange_pairs(size, step)).astype(held.dtype)  17.2 us
    ppermute x15, starting transfers between devices, gather_blocks(): lax.ppermute(held, axis, exchange_pairs(size, step))  12.5 us
  transfers between devices with their start and end apart: 65, of which 33 were waited for; matrix products, arithmetic and copies ran while one was open for 11% of the time, Pallas kernels for 8%

profile of v7, /device:TPU:0, one launch (start us, length us, event | category | flops | bytes accessed | tf_op | source)
XLA Modules:
  0.0 278.2 jit_solution(15379690272197372145)
XLA Ops:
  2.4 2.6 collective-permute-start.1
  5.1 0.9 bitcast_bitcast_fusion.1
  6.0 2.9 %collective-permute-start.13 = (bf16[6,64,128]{2,1,0:T(8,128)(2,1)S(1)}, bf16[6,64,128]{2,1,0:T(8,128)(2,1)S(1)}, u32[]{:S(2)}, u32[]{:S(2)}) collective-permute-start(bf16[6,64,128]{2,1,0:T(8,128)(2,1)S(1)} %bitcast_bitcast_fusion.1), channel_id=1, source_target_pairs={{0,4},{1,5},{2,6},{3,7},{4,0},{5,1},{6,2},{7,3},{8,12},{9,13},{10,... | collective-permute-start | bytes 294920 | tf_op jit(solution)/shard_map/ppermute | solution.py:125
  8.9 1.5 collective-permute-start.18
  12.6 1.6 collective-permute-start.3
  14.2 1.6 collective-permute-start.4
  16.9 1.3 collective-permute-done.4
  18.2 2.2 collective-permute-start.7
  20.5 1.7 collective-permute-start.8
  22.3 2.3 collective-permute-start.9
  24.6 1.7 collective-permute-done.8
  26.3 2.6 collective-permute-done.9
  29.8 5.8 %cholesky.16 = f32[64,64]{1,0:T(8,128)S(1)} custom-call(f32[64,64]{1,0:T(8,128)S(1)} %fusion.19), custom_call_target="Cholesky" | custom-call | tf_op jit(solution)/shard_map/jit(cholesky)/cholesky | solution.py:212
  37.0 4.9 %custom-call.6 = f32[1,64,64]{1,2,0:T(8,128)S(1)} custom-call(f32[1,64,64]{2,1,0:T(8,128)S(1)} %fusion.15), custom_call_target="InvertDiagBlocksLowerTriangular" | custom-call | tf_op jit(solution)/shard_map/triangular_solve | solution.py:213
  43.0 2.7 collective-permute-start.14
  45.7 3.0 %collective-permute-done.10 = bf16[6,64,128]{2,1,0:T(8,128)(2,1)S(1)} collective-permute-done((bf16[6,64,128]{2,1,0:T(8,128)(2,1)S(1)}, bf16[6,64,128]{2,1,0:T(8,128)(2,1)S(1)}, u32[]{:S(2)}, u32[]{:S(2)}) %collective-permute-start.10) | collective-permute-done | bytes 98336 | tf_op jit(solution)/shard_map/ppermute | solution.py:125
  48.7 1.1 collective-permute-start.11
  49.8 2.2 collective-permute-done.14
  52.1 1.0 collective-permute-start.15
  53.1 1.4 collective-permute-done.11
  54.5 1.1 collective-permute-start.12
  58.1 4.8 %collective-permute-done.15 = bf16[24,64,128]{2,1,0:T(8,128)(2,1)S(1)} collective-permute-done((bf16[24,64,128]{2,1,0:T(8,128)(2,1)S(1)}, bf16[24,64,128]{2,1,0:T(8,128)(2,1)S(1)}, u32[]{:S(2)}, u32[]{:S(2)}) %collective-permute-start.15) | collective-permute-done | bytes 393248 | tf_op jit(solution)/shard_map/ppermute | solution.py:125
  62.9 4.2 %collective-permute-done.12 = bf16[24,64,128]{2,1,0:T(8,128)(2,1)S(1)} collective-permute-done((bf16[24,64,128]{2,1,0:T(8,128)(2,1)S(1)}, bf16[24,64,128]{2,1,0:T(8,128)(2,1)S(1)}, u32[]{:S(2)}, u32[]{:S(2)}) %collective-permute-start.12) | collective-permute-done | bytes 393248 | tf_op jit(solution)/shard_map/ppermute | solution.py:125
  67.2 4.4 %maximum_maximum_fusion.rin_ref = bf16[48,128,128]{2,1,0:T(8,128)(2,1)} fusion(bf16[24,64,128]{2,1,0:T(8,128)(2,1)S(1)} %collective-permute-done.15, bf16[12,64,128]{2,1,0:T(8,128)(2,1)S(1)} %collective-permute-done.14, bf16[6,64,128]{2,1,0:T(8,128)(2,1)S(1)} %collective-permute-done.13, bf16[6,64,128]{2,1,0:T(8,128)(2,1)S(1)} %bitcast_bitcast_fusion.1, ...), kind=kLoop, calls=%fused_computation.6 | loop fusion | flops 12582912 | bytes 3145728 | tf_op jit(solution)/shard_map/concatenate | solution.py:218
  71.6 25.6 %shard_map.93 = (f32[48,64,128]{2,1,0:T(8,128)S(1)}, f32[24,64,128]{2,1,0:T(8,128)S(1)}, f32[48,64,128]{2,1,0:T(8,128)S(1)}, f32[24,64,128]{2,1,0:T(8,128)S(1)}) custom-call(s32[576]{0:T(1024)S(1)} %get-tuple-element.38.rows_ref, s32[576]{0:T(1024)S(1)} %get-tuple-element.39.cols_ref, s32[1]{0:T(128)} %bitcast.130.cnt_ref, bf16[576,128,128]{2,1,0:T(8,128)(2,1)} %bitcast.132, ...), custom_call_target="tpu_custom_call" | custom-call | flops 4831838208 | bytes 25952256 | tf_op jit(solution)/shard_map/pallas_call | solution.py:94
  97.3 5.6 %collective-permute-start.20 = (bf16[24,64,128]{2,1,0:T(8,128)(2,1)S(1)}, bf16[24,64,128]{2,1,0:T(8,128)(2,1)S(1)}, u32[]{:S(2)}, u32[]{:S(2)}) collective-permute-start(bf16[24,64,128]{2,1,0:T(8,128)(2,1)S(1)} %slice.497), channel_id=1, source_target_pairs={{0,1},{1,0},{2,3},{3,2},{4,5},{5,4},{6,7},{7,6},{8,9},{9,8},{10,11... | collective-permute-start | bytes 1179656 | tf_op jit(solution)/shard_map/ppermute | solution.py:139
  102.9 5.6 %collective-permute-done.20 = bf16[24,64,128]{2,1,0:T(8,128)(2,1)S(1)} collective-permute-done((bf16[24,64,128]{2,1,0:T(8,128)(2,1)S(1)}, bf16[24,64,128]{2,1,0:T(8,128)(2,1)S(1)}, u32[]{:S(2)}, u32[]{:S(2)}) %collective-permute-start.20) | collective-permute-done | bytes 393248 | tf_op jit(solution)/shard_map/ppermute | solution.py:139
  109.0 9.7 %collective-permute-done.21 = f32[12,64,128]{2,1,0:T(8,128)S(1)} collective-permute-done((f32[12,64,128]{2,1,0:T(8,128)S(1)}, f32[12,64,128]{2,1,0:T(8,128)S(1)}, u32[]{:S(2)}, u32[]{:S(2)}) %collective-permute-start.21) | collective-permute-done | bytes 393248 | tf_op jit(solution)/shard_map/ppermute | solution.py:139
  118.9 2.0 collective-permute-start.45
  121.0 5.9 %collective-permute-done.22 = f32[6,64,128]{2,1,0:T(8,128)S(1)} collective-permute-done((f32[6,64,128]{2,1,0:T(8,128)S(1)}, f32[6,64,128]{2,1,0:T(8,128)S(1)}, u32[]{:S(2)}, u32[]{:S(2)}) %collective-permute-start.22) | collective-permute-done | bytes 196640 | tf_op jit(solution)/shard_map/ppermute | solution.py:139
  127.5 1.8 collective-permute-start.27
  129.5 2.1 collective-permute-done.26
  132.8 1.5 collective-permute-start.28
  134.3 1.0 slice_add_fusion.3
  135.4 1.3 collective-permute-start.49
  136.7 2.0 collective-permute-start.30
  139.4 2.9 %collective-permute-done.29 = f32[64,64]{1,0:T(8,128)S(1)} collective-permute-done((f32[64,64]{1,0:T(8,128)S(1)}, f32[64,64]{1,0:T(8,128)S(1)}, u32[]{:S(2)}, u32[]{:S(2)}) %collective-permute-start.29) | collective-permute-done | bytes 16416 | tf_op jit(solution)/shard_map/ppermute | solution.py:159
  142.2 1.0 collective-permute-start.32
  143.8 2.2 collective-permute-start.33
  146.6 1.6 collective-permute-start.34
  150.1 3.1 %collective-permute-done.34 = f32[64,64]{1,0:T(8,128)S(1)} collective-permute-done((f32[64,64]{1,0:T(8,128)S(1)}, f32[64,64]{1,0:T(8,128)S(1)}, u32[]{:S(2)}, u32[]{:S(2)}) %collective-permute-start.34) | collective-permute-done | bytes 16416 | tf_op jit(solution)/shard_map/ppermute | solution.py:159
  153.9 1.5 gather_fusion.5
  156.2 1.0 slice_add_fusion
  157.3 2.9 %collective-permute-start.47 = (f32[6,64,128]{2,1,0:T(8,128)S(1)}, f32[6,64,128]{2,1,0:T(8,128)S(1)}, u32[]{:S(2)}, u32[]{:S(2)}) collective-permute-start(f32[6,64,128]{2,1,0:T(8,128)S(1)} %slice.343), channel_id=1, source_target_pairs={{0,4},{1,5},{2,6},{3,7},{4,0},{5,1},{6,2},{7,3},{8,12},{9,13},{10,... | collective-permute-start | bytes 589832 | tf_op jit(solution)/shard_map/ppermute | solution.py:139
  160.2 6.6 %collective-permute-done.35 = bf16[6,64,128]{2,1,0:T(8,128)(2,1)S(1)} collective-permute-done((bf16[6,64,128]{2,1,0:T(8,128)(2,1)S(1)}, bf16[6,64,128]{2,1,0:T(8,128)(2,1)S(1)}, u32[]{:S(2)}, u32[]{:S(2)}) %collective-permute-start.35) | collective-permute-done | bytes 98336 | tf_op jit(solution)/shard_map/ppermute | solution.py:125
  167.7 4.9 %collective-permute-done.36 = bf16[12,64,128]{2,1,0:T(8,128)(2,1)S(1)} collective-permute-done((bf16[12,64,128]{2,1,0:T(8,128)(2,1)S(1)}, bf16[12,64,128]{2,1,0:T(8,128)(2,1)S(1)}, u32[]{:S(2)}, u32[]{:S(2)}) %collective-permute-start.36) | collective-permute-done | bytes 196640 | tf_op jit(solution)/shard_map/ppermute | solution.py:125
  174.8 5.7 %collective-permute-done.37 = bf16[24,64,128]{2,1,0:T(8,128)(2,1)S(1)} collective-permute-done((bf16[24,64,128]{2,1,0:T(8,128)(2,1)S(1)}, bf16[24,64,128]{2,1,0:T(8,128)(2,1)S(1)}, u32[]{:S(2)}, u32[]{:S(2)}) %collective-permute-start.37) | collective-permute-done | bytes 393248 | tf_op jit(solution)/shard_map/ppermute | solution.py:125
  180.6 23.6 %shard_map.94 = (f32[48,64,128]{2,1,0:T(8,128)S(1)}, f32[24,64,128]{2,1,0:T(8,128)S(1)}) custom-call(s32[576]{0:T(1024)S(1)} %get-tuple-element.38.rows_ref, s32[576]{0:T(1024)S(1)} %get-tuple-element.39.cols_ref, s32[1]{0:T(128)} %bitcast.131.cnt_ref, bf16[576,128,128]{2,1,0:T(8,128)(2,1)} %bitcast.133, bf16[48,64,128]{2,1,0:T(8,128)(2,1)S(1)} %pad_maximum_fusion.rin_ref, ...), custom_call_target="tpu_custom_call" | custom-call | flops 2415919104 | bytes 22413312 | tf_op jit(solution)/shard_map/pallas_call | solution.py:94
  204.3 4.7 %collective-permute-start.40 = (bf16[24,64,128]{2,1,0:T(8,128)(2,1)S(1)}, bf16[24,64,128]{2,1,0:T(8,128)(2,1)S(1)}, u32[]{:S(2)}, u32[]{:S(2)}) collective-permute-start(bf16[24,64,128]{2,1,0:T(8,128)(2,1)S(1)} %slice.496), channel_id=1, source_target_pairs={{0,1},{1,0},{2,3},{3,2},{4,5},{5,4},{6,7},{7,6},{8,9},{9,8},{10,11... | collective-permute-start | bytes 1179656 | tf_op jit(solution)/shard_map/ppermute | solution.py:139
  209.3 6.7 %collective-permute-done.51 = f32[192,320]{1,0:T(8,128)S(1)} collective-permute-done((f32[192,320]{1,0:T(8,128)S(1)}, f32[192,320]{1,0:T(8,128)S(1)}, u32[]{:S(2)}, u32[]{:S(2)}) %collective-permute-start.51) | collective-permute-done | bytes 245792 | tf_op jit(solution)/shard_map/ppermute | solution.py:149
  216.4 6.3 %collective-permute-done.52 = f32[192,320]{1,0:T(8,128)S(1)} collective-permute-done((f32[192,320]{1,0:T(8,128)S(1)}, f32[192,320]{1,0:T(8,128)S(1)}, u32[]{:S(2)}, u32[]{:S(2)}) %collective-permute-start.52) | collective-permute-done | bytes 245792 | tf_op jit(solution)/shard_map/ppermute | solution.py:149
  223.1 5.3 %collective-permute-done.41 = f32[12,64,128]{2,1,0:T(8,128)S(1)} collective-permute-done((f32[12,64,128]{2,1,0:T(8,128)S(1)}, f32[12,64,128]{2,1,0:T(8,128)S(1)}, u32[]{:S(2)}, u32[]{:S(2)}) %collective-permute-start.41) | collective-permute-done | bytes 393248 | tf_op jit(solution)/shard_map/ppermute | solution.py:139
  228.5 7.6 %collective-permute-done.53 = f32[192,320]{1,0:T(8,128)S(1)} collective-permute-done((f32[192,320]{1,0:T(8,128)S(1)}, f32[192,320]{1,0:T(8,128)S(1)}, u32[]{:S(2)}, u32[]{:S(2)}) %collective-permute-start.53) | collective-permute-done | bytes 245792 | tf_op jit(solution)/shard_map/ppermute | solution.py:149
  236.2 11.0 %collective-permute-done.42 = f32[6,64,128]{2,1,0:T(8,128)S(1)} collective-permute-done((f32[6,64,128]{2,1,0:T(8,128)S(1)}, f32[6,64,128]{2,1,0:T(8,128)S(1)}, u32[]{:S(2)}, u32[]{:S(2)}) %collective-permute-start.42) | collective-permute-done | bytes 196640 | tf_op jit(solution)/shard_map/ppermute | solution.py:139
  248.1 1.7 collective-permute-start.57
  249.9 2.5 collective-permute-done.54
  252.4 1.3 collective-permute-done.56
  253.6 1.2 collective-permute-done.57
  255.6 1.3 collective-permute-start.58
  257.7 2.2 collective-permute-start.60
  259.9 3.6 %collective-permute-start.62 = (f32[192,64]{1,0:T(8,128)S(1)}, f32[192,64]{1,0:T(8,128)S(1)}, u32[]{:S(2)}, u32[]{:S(2)}) collective-permute-start(f32[192,64]{1,0:T(8,128)S(1)} %bitcast.141), channel_id=1, source_target_pairs={{0,5},{1,4},{2,7},{3,6},{4,1},{5,0},{6,3},{7,2},{8,13},{9,12},{10,... | collective-permute-start | bytes 147464 | tf_op jit(solution)/shard_map/ppermute | solution.py:159
  263.8 3.9 %collective-permute-start.64 = (f32[192,64]{1,0:T(8,128)S(1)}, f32[192,64]{1,0:T(8,128)S(1)}, u32[]{:S(2)}, u32[]{:S(2)}) collective-permute-start(f32[192,64]{1,0:T(8,128)S(1)} %bitcast.143), channel_id=1, source_target_pairs={{0,7},{1,6},{2,5},{3,4},{4,3},{5,2},{6,1},{7,0},{8,15},{9,14},{10,... | collective-permute-start | bytes 147464 | tf_op jit(solution)/shard_map/ppermute | solution.py:159
  267.7 6.4 %collective-permute-done.61 = f32[192,64]{1,0:T(8,128)S(1)} collective-permute-done((f32[192,64]{1,0:T(8,128)S(1)}, f32[192,64]{1,0:T(8,128)S(1)}, u32[]{:S(2)}, u32[]{:S(2)}) %collective-permute-start.61) | collective-permute-done | bytes 49184 | tf_op jit(solution)/shard_map/ppermute | solution.py:159
  274.2 2.3 collective-permute-done.62
  (199 shorter events, 27.1 us)
Async XLA Ops:
  1.9 10.0 %collective-permute-start = (f32[64,64]{1,0:T(8,128)S(1)}, f32[64,64]{1,0:T(8,128)S(1)}, u32[]{:S(2)}, u32[]{:S(2)}) collective-permute-start(f32[64,64]{1,0:T(8,128)S(1)} %convolution_multiply_fusion.5), channel_id=1, source_target_pairs={{0,8},{8,0},{16,24},{24,16},{1,9},{9,1},{17,25},{25,17},{2,10},{10... | collective-permute-start | bytes 49160 | tf_op jit(solution)/shard_map/ppermute | solution.py:159
  2.4 9.5 %collective-permute-start.1 = (f32[64,64]{1,0:T(8,128)S(1)}, f32[64,64]{1,0:T(8,128)S(1)}, u32[]{:S(2)}, u32[]{:S(2)}) collective-permute-start(f32[64,64]{1,0:T(8,128)S(1)} %convolution_multiply_fusion.5), channel_id=1, source_target_pairs={{0,16},{8,24},{16,0},{24,8},{1,17},{9,25},{17,1},{25,9},{2,18},{10... | collective-permute-start | bytes 49160 | tf_op jit(solution)/shard_map/ppermute | solution.py:159
  5.0 6.9 %collective-permute-start.2 = (f32[64,64]{1,0:T(8,128)S(1)}, f32[64,64]{1,0:T(8,128)S(1)}, u32[]{:S(2)}, u32[]{:S(2)}) collective-permute-start(f32[64,64]{1,0:T(8,128)S(1)} %convolution_multiply_fusion.5), channel_id=1, source_target_pairs={{0,24},{8,16},{16,8},{24,0},{1,25},{9,17},{17,9},{25,1},{2,26},{10... | collective-permute-start | bytes 49160 | tf_op jit(solution)/shard_map/ppermute | solution.py:159
  6.0 37.0 %collective-permute-start.13 = (bf16[6,64,128]{2,1,0:T(8,128)(2,1)S(1)}, bf16[6,64,128]{2,1,0:T(8,128)(2,1)S(1)}, u32[]{:S(2)}, u32[]{:S(2)}) collective-permute-start(bf16[6,64,128]{2,1,0:T(8,128)(2,1)S(1)} %bitcast_bitcast_fusion.1), channel_id=1, source_target_pairs={{0,4},{1,5},{2,6},{3,7},{4,0},{5,1},{6,2},{7,3},{8,12},{9,13},{10,... | collective-permute-start | bytes 294920 | tf_op jit(solution)/shard_map/ppermute | solution.py:125
  8.9 34.1 %collective-permute-start.18 = (bf16[6,64,128]{2,1,0:T(8,128)(2,1)S(1)}, bf16[6,64,128]{2,1,0:T(8,128)(2,1)S(1)}, u32[]{:S(2)}, u32[]{:S(2)}) collective-permute-start(bf16[6,64,128]{2,1,0:T(8,128)(2,1)S(1)} %bitcast_bitcast_fusion.1), channel_id=1, source_target_pairs={{0,16},{8,24},{16,0},{24,8},{1,17},{9,25},{17,1},{25,9},{2,18},{10... | collective-permute-start | bytes 294920 | tf_op jit(solution)/shard_map/ppermute | solution.py:125
  12.6 4.0 %collective-permute-start.3 = (f32[64,64]{1,0:T(8,128)S(1)}, f32[64,64]{1,0:T(8,128)S(1)}, u32[]{:S(2)}, u32[]{:S(2)}) collective-permute-start(f32[64,64]{1,0:T(8,128)S(1)} %bitcast.154), channel_id=1, source_target_pairs={{0,1},{1,0},{2,3},{3,2},{4,5},{5,4},{6,7},{7,6},{8,9},{9,8},{10,11... | collective-permute-start | bytes 49160 | tf_op jit(solution)/shard_map/ppermute | solution.py:159
  14.2 4.1 %collective-permute-start.4 = (f32[64,64]{1,0:T(8,128)S(1)}, f32[64,64]{1,0:T(8,128)S(1)}, u32[]{:S(2)}, u32[]{:S(2)}) collective-permute-start(f32[64,64]{1,0:T(8,128)S(1)} %bitcast.155), channel_id=1, source_target_pairs={{0,2},{1,3},{2,0},{3,1},{4,6},{5,7},{6,4},{7,5},{8,10},{9,11},{10,... | collective-permute-start | bytes 49160 | tf_op jit(solution)/shard_map/ppermute | solution.py:159
  15.7 4.8 %collective-permute-start.5 = (f32[64,64]{1,0:T(8,128)S(1)}, f32[64,64]{1,0:T(8,128)S(1)}, u32[]{:S(2)}, u32[]{:S(2)}) collective-permute-start(f32[64,64]{1,0:T(8,128)S(1)} %bitcast.156), channel_id=1, source_target_pairs={{0,3},{1,2},{2,1},{3,0},{4,7},{5,6},{6,5},{7,4},{8,11},{9,10},{10,... | collective-permute-start | bytes 49160 | tf_op jit(solution)/shard_map/ppermute | solution.py:159
  16.6 5.7 %collective-permute-start.6 = (f32[64,64]{1,0:T(8,128)S(1)}, f32[64,64]{1,0:T(8,128)S(1)}, u32[]{:S(2)}, u32[]{:S(2)}) collective-permute-start(f32[64,64]{1,0:T(8,128)S(1)} %bitcast.157), channel_id=1, source_target_pairs={{0,4},{1,5},{2,6},{3,7},{4,0},{5,1},{6,2},{7,3},{8,12},{9,13},{10,... | collective-permute-start | bytes 49160 | tf_op jit(solution)/shard_map/ppermute | solution.py:159
  18.2 6.3 %collective-permute-start.7 = (f32[64,64]{1,0:T(8,128)S(1)}, f32[64,64]{1,0:T(8,128)S(1)}, u32[]{:S(2)}, u32[]{:S(2)}) collective-permute-start(f32[64,64]{1,0:T(8,128)S(1)} %bitcast.158), channel_id=1, source_target_pairs={{0,5},{1,4},{2,7},{3,6},{4,1},{5,0},{6,3},{7,2},{8,13},{9,12},{10,... | collective-permute-start | bytes 49160 | tf_op jit(solution)/shard_map/ppermute | solution.py:159
  20.5 5.7 %collective-permute-start.8 = (f32[64,64]{1,0:T(8,128)S(1)}, f32[64,64]{1,0:T(8,128)S(1)}, u32[]{:S(2)}, u32[]{:S(2)}) collective-permute-start(f32[64,64]{1,0:T(8,128)S(1)} %bitcast.159), channel_id=1, source_target_pairs={{0,6},{1,7},{2,4},{3,5},{4,2},{5,3},{6,0},{7,1},{8,14},{9,15},{10,... | collective-permute-start | bytes 49160 | tf_op jit(solution)/shard_map/ppermute | solution.py:159
  22.3 6.6 %collective-permute-start.9 = (f32[64,64]{1,0:T(8,128)S(1)}, f32[64,64]{1,0:T(8,128)S(1)}, u32[]{:S(2)}, u32[]{:S(2)}) collective-permute-start(f32[64,64]{1,0:T(8,128)S(1)} %bitcast.160), channel_id=1, source_target_pairs={{0,7},{1,6},{2,5},{3,4},{4,3},{5,2},{6,1},{7,0},{8,15},{9,14},{10,... | collective-permute-start | bytes 49160 | tf_op jit(solution)/shard_map/ppermute | solution.py:159
  42.3 6.4 %collective-permute-start.10 = (bf16[6,64,128]{2,1,0:T(8,128)(2,1)S(1)}, bf16[6,64,128]{2,1,0:T(8,128)(2,1)S(1)}, u32[]{:S(2)}, u32[]{:S(2)}) collective-permute-start(bf16[6,64,128]{2,1,0:T(8,128)(2,1)S(1)} %bitcast_bitcast_fusion.2), channel_id=1, source_target_pairs={{0,4},{1,5},{2,6},{3,7},{4,0},{5,1},{6,2},{7,3},{8,12},{9,13},{10,... | collective-permute-start | bytes 294920 | tf_op jit(solution)/shard_map/ppermute | solution.py:125
  42.4 6.3 %collective-permute-start.16 = (bf16[6,64,128]{2,1,0:T(8,128)(2,1)S(1)}, bf16[6,64,128]{2,1,0:T(8,128)(2,1)S(1)}, u32[]{:S(2)}, u32[]{:S(2)}) collective-permute-start(bf16[6,64,128]{2,1,0:T(8,128)(2,1)S(1)} %bitcast_bitcast_fusion.2), channel_id=1, source_target_pairs={{0,16},{8,24},{16,0},{24,8},{1,17},{9,25},{17,1},{25,9},{2,18},{10... | collective-permute-start | bytes 294920 | tf_op jit(solution)/shard_map/ppermute | solution.py:125
  43.0 9.0 %collective-permute-start.14 = (bf16[12,64,128]{2,1,0:T(8,128)(2,1)S(1)}, bf16[12,64,128]{2,1,0:T(8,128)(2,1)S(1)}, u32[]{:S(2)}, u32[]{:S(2)}) collective-permute-start(bf16[12,64,128]{2,1,0:T(8,128)(2,1)S(1)} %get-tuple-element.37), channel_id=1, source_target_pairs={{0,2},{1,3},{2,0},{3,1},{4,6},{5,7},{6,4},{7,5},{8,10},{9,11},{10,... | collective-permute-start | bytes 589832 | tf_op jit(solution)/shard_map/ppermute | solution.py:125
  48.7 5.7 %collective-permute-start.11 = (bf16[12,64,128]{2,1,0:T(8,128)(2,1)S(1)}, bf16[12,64,128]{2,1,0:T(8,128)(2,1)S(1)}, u32[]{:S(2)}, u32[]{:S(2)}) collective-permute-start(bf16[12,64,128]{2,1,0:T(8,128)(2,1)S(1)} %get-tuple-element.35), channel_id=1, source_target_pairs={{0,2},{1,3},{2,0},{3,1},{4,6},{5,7},{6,4},{7,5},{8,10},{9,11},{10,... | collective-permute-start | bytes 589832 | tf_op jit(solution)/shard_map/ppermute | solution.py:125
  52.1 10.9 %collective-permute-start.15 = (bf16[24,64,128]{2,1,0:T(8,128)(2,1)S(1)}, bf16[24,64,128]{2,1,0:T(8,128)(2,1)S(1)}, u32[]{:S(2)}, u32[]{:S(2)}) collective-permute-start(bf16[24,64,128]{2,1,0:T(8,128)(2,1)S(1)} %pad_maximum_fusion.5), channel_id=1, source_target_pairs={{0,1},{1,0},{2,3},{3,2},{4,5},{5,4},{6,7},{7,6},{8,9},{9,8},{10,11... | collective-permute-start | bytes 1179656 | tf_op jit(solution)/shard_map/ppermute | solution.py:125
  54.5 12.7 %collective-permute-start.12 = (bf16[24,64,128]{2,1,0:T(8,128)(2,1)S(1)}, bf16[24,64,128]{2,1,0:T(8,128)(2,1)S(1)}, u32[]{:S(2)}, u32[]{:S(2)}) collective-permute-start(bf16[24,64,128]{2,1,0:T(8,128)(2,1)S(1)} %pad_maximum_fusion.4), channel_id=1, source_target_pairs={{0,1},{1,0},{2,3},{3,2},{4,5},{5,4},{6,7},{7,6},{8,9},{9,8},{10,11... | collective-permute-start | bytes 1179656 | tf_op jit(solution)/shard_map/ppermute | solution.py:125
  56.3 1.7 collective-permute-start.17
  97.3 11.3 %collective-permute-start.20 = (bf16[24,64,128]{2,1,0:T(8,128)(2,1)S(1)}, bf16[24,64,128]{2,1,0:T(8,128)(2,1)S(1)}, u32[]{:S(2)}, u32[]{:S(2)}) collective-permute-start(bf16[24,64,128]{2,1,0:T(8,128)(2,1)S(1)} %slice.497), channel_id=1, source_target_pairs={{0,1},{1,0},{2,3},{3,2},{4,5},{5,4},{6,7},{7,6},{8,9},{9,8},{10,11... | collective-permute-start | bytes 1179656 | tf_op jit(solution)/shard_map/ppermute | solution.py:139
  102.8 6.0 %collective-permute-start.23 = (f32[12,64,128]{2,1,0:T(8,128)S(1)}, f32[12,64,128]{2,1,0:T(8,128)S(1)}, u32[]{:S(2)}, u32[]{:S(2)}) collective-permute-start(f32[12,64,128]{2,1,0:T(8,128)S(1)} %slice.239), channel_id=1, source_target_pairs={{0,8},{8,0},{16,24},{24,16},{1,9},{9,1},{17,25},{25,17},{2,10},{10... | collective-permute-start | bytes 1179656 | tf_op jit(solution)/shard_map/ppermute | solution.py:139
  108.7 9.9 %collective-permute-start.21 = (f32[12,64,128]{2,1,0:T(8,128)S(1)}, f32[12,64,128]{2,1,0:T(8,128)S(1)}, u32[]{:S(2)}, u32[]{:S(2)}) collective-permute-start(f32[12,64,128]{2,1,0:T(8,128)S(1)} %slice.315), channel_id=1, source_target_pairs={{0,2},{1,3},{2,0},{3,1},{4,6},{5,7},{6,4},{7,5},{8,10},{9,11},{10,... | collective-permute-start | bytes 1179656 | tf_op jit(solution)/shard_map/ppermute | solution.py:139
  108.9 12.1 %collective-permute-start.24 = (f32[6,64,128]{2,1,0:T(8,128)S(1)}, f32[6,64,128]{2,1,0:T(8,128)S(1)}, u32[]{:S(2)}, u32[]{:S(2)}) collective-permute-start(f32[6,64,128]{2,1,0:T(8,128)S(1)} %slice.319), channel_id=1, source_target_pairs={{0,16},{8,24},{16,0},{24,8},{1,17},{9,25},{17,1},{25,9},{2,18},{10... | collective-permute-start | bytes 589832 | tf_op jit(solution)/shard_map/ppermute | solution.py:139
  118.7 8.2 %collective-permute-start.22 = (f32[6,64,128]{2,1,0:T(8,128)S(1)}, f32[6,64,128]{2,1,0:T(8,128)S(1)}, u32[]{:S(2)}, u32[]{:S(2)}) collective-permute-start(f32[6,64,128]{2,1,0:T(8,128)S(1)} %slice.317), channel_id=1, source_target_pairs={{0,4},{1,5},{2,6},{3,7},{4,0},{5,1},{6,2},{7,3},{8,12},{9,13},{10,... | collective-permute-start | bytes 589832 | tf_op jit(solution)/shard_map/ppermute | solution.py:139
  118.9 10.3 %collective-permute-start.45 = (bf16[24,64,128]{2,1,0:T(8,128)(2,1)S(1)}, bf16[24,64,128]{2,1,0:T(8,128)(2,1)S(1)}, u32[]{:S(2)}, u32[]{:S(2)}) collective-permute-start(bf16[24,64,128]{2,1,0:T(8,128)(2,1)S(1)} %slice.495), channel_id=1, source_target_pairs={{0,1},{1,0},{2,3},{3,2},{4,5},{5,4},{6,7},{7,6},{8,9},{9,8},{10,11... | collective-permute-start | bytes 1179656 | tf_op jit(solution)/shard_map/ppermute | solution.py:139
  120.9 13.4 %collective-permute-start.48 = (f32[12,64,128]{2,1,0:T(8,128)S(1)}, f32[12,64,128]{2,1,0:T(8,128)}, u32[]{:S(2)}, u32[]{:S(2)}) collective-permute-start(f32[12,64,128]{2,1,0:T(8,128)S(1)} %slice.271), channel_id=1, source_target_pairs={{0,8},{8,0},{16,24},{24,16},{1,9},{9,1},{17,25},{25,17},{2,10},{10... | collective-permute-start | bytes 1179656 | tf_op jit(solution)/shard_map/ppermute | solution.py:139
  127.3 2.2 collective-permute-start.25
  127.4 4.2 %collective-permute-start.26 = (f32[64,64]{1,0:T(8,128)S(1)}, f32[64,64]{1,0:T(8,128)S(1)}, u32[]{:S(2)}, u32[]{:S(2)}) collective-permute-start(f32[64,64]{1,0:T(8,128)S(1)} %convolution_multiply_fusion.4), channel_id=1, source_target_pairs={{0,16},{8,24},{16,0},{24,8},{1,17},{9,25},{17,1},{25,9},{2,18},{10... | collective-permute-start | bytes 49160 | tf_op jit(solution)/shard_map/ppermute | solution.py:159
  127.5 4.1 %collective-permute-start.27 = (f32[64,64]{1,0:T(8,128)S(1)}, f32[64,64]{1,0:T(8,128)S(1)}, u32[]{:S(2)}, u32[]{:S(2)}) collective-permute-start(f32[64,64]{1,0:T(8,128)S(1)} %convolution_multiply_fusion.4), channel_id=1, source_target_pairs={{0,24},{8,16},{16,8},{24,0},{1,25},{9,17},{17,9},{25,1},{2,26},{10... | collective-permute-start | bytes 49160 | tf_op jit(solution)/shard_map/ppermute | solution.py:159
  129.4 26.9 %collective-permute-start.46 = (f32[12,64,128]{2,1,0:T(8,128)S(1)}, f32[12,64,128]{2,1,0:T(8,128)}, u32[]{:S(2)}, u32[]{:S(2)}) collective-permute-start(f32[12,64,128]{2,1,0:T(8,128)S(1)} %slice.341), channel_id=1, source_target_pairs={{0,2},{1,3},{2,0},{3,1},{4,6},{5,7},{6,4},{7,5},{8,10},{9,11},{10,... | collective-permute-start | bytes 1179656 | tf_op jit(solution)/shard_map/ppermute | solution.py:139
  132.8 5.9 %collective-permute-start.28 = (f32[64,64]{1,0:T(8,128)S(1)}, f32[64,64]{1,0:T(8,128)S(1)}, u32[]{:S(2)}, u32[]{:S(2)}) collective-permute-start(f32[64,64]{1,0:T(8,128)S(1)} %bitcast.147), channel_id=1, source_target_pairs={{0,1},{1,0},{2,3},{3,2},{4,5},{5,4},{6,7},{7,6},{8,9},{9,8},{10,11... | collective-permute-start | bytes 49160 | tf_op jit(solution)/shard_map/ppermute | solution.py:159
  135.4 38.6 %collective-permute-start.49 = (f32[6,64,128]{2,1,0:T(8,128)S(1)}, f32[6,64,128]{2,1,0:T(8,128)S(1)}, u32[]{:S(2)}, u32[]{:S(2)}) collective-permute-start(f32[6,64,128]{2,1,0:T(8,128)S(1)} %slice.345), channel_id=1, source_target_pairs={{0,16},{8,24},{16,0},{24,8},{1,17},{9,25},{17,1},{25,9},{2,18},{10... | collective-permute-start | bytes 589832 | tf_op jit(solution)/shard_map/ppermute | solution.py:139
  136.7 5.5 %collective-permute-start.29 = (f32[64,64]{1,0:T(8,128)S(1)}, f32[64,64]{1,0:T(8,128)S(1)}, u32[]{:S(2)}, u32[]{:S(2)}) collective-permute-start(f32[64,64]{1,0:T(8,128)S(1)} %bitcast.148), channel_id=1, source_target_pairs={{0,2},{1,3},{2,0},{3,1},{4,6},{5,7},{6,4},{7,5},{8,10},{9,11},{10,... | collective-permute-start | bytes 49160 | tf_op jit(solution)/shard_map/ppermute | solution.py:159
  136.7 7.1 %collective-permute-start.30 = (f32[64,64]{1,0:T(8,128)S(1)}, f32[64,64]{1,0:T(8,128)S(1)}, u32[]{:S(2)}, u32[]{:S(2)}) collective-permute-start(f32[64,64]{1,0:T(8,128)S(1)} %bitcast.149), channel_id=1, source_target_pairs={{0,3},{1,2},{2,1},{3,0},{4,7},{5,6},{6,5},{7,4},{8,11},{9,10},{10,... | collective-permute-start | bytes 49160 | tf_op jit(solution)/shard_map/ppermute | solution.py:159
  138.7 7.9 %collective-permute-start.31 = (f32[64,64]{1,0:T(8,128)S(1)}, f32[64,64]{1,0:T(8,128)S(1)}, u32[]{:S(2)}, u32[]{:S(2)}) collective-permute-start(f32[64,64]{1,0:T(8,128)S(1)} %bitcast.150), channel_id=1, source_target_pairs={{0,4},{1,5},{2,6},{3,7},{4,0},{5,1},{6,2},{7,3},{8,12},{9,13},{10,... | collective-permute-start | bytes 49160 | tf_op jit(solution)/shard_map/ppermute | solution.py:159
  142.2 6.6 %collective-permute-start.32 = (f32[64,64]{1,0:T(8,128)S(1)}, f32[64,64]{1,0:T(8,128)S(1)}, u32[]{:S(2)}, u32[]{:S(2)}) collective-permute-start(f32[64,64]{1,0:T(8,128)S(1)} %bitcast.151), channel_id=1, source_target_pairs={{0,5},{1,4},{2,7},{3,6},{4,1},{5,0},{6,3},{7,2},{8,13},{9,12},{10,... | collective-permute-start | bytes 49160 | tf_op jit(solution)/shard_map/ppermute | solution.py:159
  143.8 5.7 %collective-permute-start.33 = (f32[64,64]{1,0:T(8,128)S(1)}, f32[64,64]{1,0:T(8,128)S(1)}, u32[]{:S(2)}, u32[]{:S(2)}) collective-permute-start(f32[64,64]{1,0:T(8,128)S(1)} %bitcast.152), channel_id=1, source_target_pairs={{0,6},{1,7},{2,4},{3,5},{4,2},{5,3},{6,0},{7,1},{8,14},{9,15},{10,... | collective-permute-start | bytes 49160 | tf_op jit(solution)/shard_map/ppermute | solution.py:159
  146.6 6.6 %collective-permute-start.34 = (f32[64,64]{1,0:T(8,128)S(1)}, f32[64,64]{1,0:T(8,128)S(1)}, u32[]{:S(2)}, u32[]{:S(2)}) collective-permute-start(f32[64,64]{1,0:T(8,128)S(1)} %bitcast.153), channel_id=1, source_target_pairs={{0,7},{1,6},{2,5},{3,4},{4,3},{5,2},{6,1},{7,0},{8,15},{9,14},{10,... | collective-permute-start | bytes 49160 | tf_op jit(solution)/shard_map/ppermute | solution.py:159
  155.9 10.9 %collective-permute-start.35 = (bf16[6,64,128]{2,1,0:T(8,128)(2,1)S(1)}, bf16[6,64,128]{2,1,0:T(8,128)(2,1)S(1)}, u32[]{:S(2)}, u32[]{:S(2)}) collective-permute-start(bf16[6,64,128]{2,1,0:T(8,128)(2,1)S(1)} %bitcast_bitcast_fusion), channel_id=1, source_target_pairs={{0,4},{1,5},{2,6},{3,7},{4,0},{5,1},{6,2},{7,3},{8,12},{9,13},{10,... | collective-permute-start | bytes 294920 | tf_op jit(solution)/shard_map/ppermute | solution.py:125
  156.0 10.9 %collective-permute-start.38 = (bf16[6,64,128]{2,1,0:T(8,128)(2,1)S(1)}, bf16[6,64,128]{2,1,0:T(8,128)(2,1)S(1)}, u32[]{:S(2)}, u32[]{:S(2)}) collective-permute-start(bf16[6,64,128]{2,1,0:T(8,128)(2,1)S(1)} %bitcast_bitcast_fusion), channel_id=1, source_target_pairs={{0,16},{8,24},{16,0},{24,8},{1,17},{9,25},{17,1},{25,9},{2,18},{10... | collective-permute-start | bytes 294920 | tf_op jit(solution)/shard_map/ppermute | solution.py:125
  157.3 16.7 %collective-permute-start.47 = (f32[6,64,128]{2,1,0:T(8,128)S(1)}, f32[6,64,128]{2,1,0:T(8,128)S(1)}, u32[]{:S(2)}, u32[]{:S(2)}) collective-permute-start(f32[6,64,128]{2,1,0:T(8,128)S(1)} %slice.343), channel_id=1, source_target_pairs={{0,4},{1,5},{2,6},{3,7},{4,0},{5,1},{6,2},{7,3},{8,12},{9,13},{10,... | collective-permute-start | bytes 589832 | tf_op jit(solution)/shard_map/ppermute | solution.py:139
  166.9 5.7 %collective-permute-start.36 = (bf16[12,64,128]{2,1,0:T(8,128)(2,1)S(1)}, bf16[12,64,128]{2,1,0:T(8,128)(2,1)S(1)}, u32[]{:S(2)}, u32[]{:S(2)}) collective-permute-start(bf16[12,64,128]{2,1,0:T(8,128)(2,1)S(1)} %get-tuple-element.33), channel_id=1, source_target_pairs={{0,2},{1,3},{2,0},{3,1},{4,6},{5,7},{6,4},{7,5},{8,10},{9,11},{10,... | collective-permute-start | bytes 589832 | tf_op jit(solution)/shard_map/ppermute | solution.py:125
  167.0 5.7 %collective-permute-start.39 = (bf16[12,64,128]{2,1,0:T(8,128)(2,1)S(1)}, bf16[12,64,128]{2,1,0:T(8,128)(2,1)S(1)}, u32[]{:S(2)}, u32[]{:S(2)}) collective-permute-start(bf16[12,64,128]{2,1,0:T(8,128)(2,1)S(1)} %get-tuple-element.32), channel_id=1, source_target_pairs={{0,8},{8,0},{16,24},{24,16},{1,9},{9,1},{17,25},{25,17},{2,10},{10... | collective-permute-start | bytes 589832 | tf_op jit(solution)/shard_map/ppermute | solution.py:125
  172.7 7.8 %collective-permute-start.37 = (bf16[24,64,128]{2,1,0:T(8,128)(2,1)S(1)}, bf16[24,64,128]{2,1,0:T(8,128)(2,1)S(1)}, u32[]{:S(2)}, u32[]{:S(2)}) collective-permute-start(bf16[24,64,128]{2,1,0:T(8,128)(2,1)S(1)} %get-tuple-element.31), channel_id=1, source_target_pairs={{0,1},{1,0},{2,3},{3,2},{4,5},{5,4},{6,7},{7,6},{8,9},{9,8},{10,11... | collective-permute-start | bytes 1179656 | tf_op jit(solution)/shard_map/ppermute | solution.py:125
  174.8 34.3 %collective-permute-start.50 = (f32[192,320]{1,0:T(8,128)S(1)}, f32[192,320]{1,0:T(8,128)S(1)}, u32[]{:S(2)}, u32[]{:S(2)}) collective-permute-start(f32[192,320]{1,0:T(8,128)S(1)} %pad_maximum_fusion.7), channel_id=1, source_target_pairs={{0,8},{8,0},{16,24},{24,16},{1,9},{9,1},{17,25},{25,17},{2,10},{10... | collective-permute-start | bytes 737288 | tf_op jit(solution)/shard_map/ppermute | solution.py:149
  204.3 11.9 %collective-permute-start.40 = (bf16[24,64,128]{2,1,0:T(8,128)(2,1)S(1)}, bf16[24,64,128]{2,1,0:T(8,128)(2,1)S(1)}, u32[]{:S(2)}, u32[]{:S(2)}) collective-permute-start(bf16[24,64,128]{2,1,0:T(8,128)(2,1)S(1)} %slice.496), channel_id=1, source_target_pairs={{0,1},{1,0},{2,3},{3,2},{4,5},{5,4},{6,7},{7,6},{8,9},{9,8},{10,11... | collective-permute-start | bytes 1179656 | tf_op jit(solution)/shard_map/ppermute | solution.py:139
  209.2 6.8 %collective-permute-start.51 = (f32[192,320]{1,0:T(8,128)S(1)}, f32[192,320]{1,0:T(8,128)S(1)}, u32[]{:S(2)}, u32[]{:S(2)}) collective-permute-start(f32[192,320]{1,0:T(8,128)S(1)} %fusion.39), channel_id=1, source_target_pairs={{0,16},{8,24},{16,0},{24,8},{1,17},{9,25},{17,1},{25,9},{2,18},{10... | collective-permute-start | bytes 737288 | tf_op jit(solution)/shard_map/ppermute | solution.py:149
  216.0 6.8 %collective-permute-start.52 = (f32[192,320]{1,0:T(8,128)S(1)}, f32[192,320]{1,0:T(8,128)S(1)}, u32[]{:S(2)}, u32[]{:S(2)}) collective-permute-start(f32[192,320]{1,0:T(8,128)S(1)} %add.314), channel_id=1, source_target_pairs={{0,1},{1,0},{2,3},{3,2},{4,5},{5,4},{6,7},{7,6},{8,9},{9,8},{10,11... | collective-permute-start | bytes 737288 | tf_op jit(solution)/shard_map/ppermute | solution.py:149
  216.1 6.8 %collective-permute-start.43 = (f32[12,64,128]{2,1,0:T(8,128)S(1)}, f32[12,64,128]{2,1,0:T(8,128)S(1)}, u32[]{:S(2)}, u32[]{:S(2)}) collective-permute-start(f32[12,64,128]{2,1,0:T(8,128)S(1)} %slice.261), channel_id=1, source_target_pairs={{0,8},{8,0},{16,24},{24,16},{1,9},{9,1},{17,25},{25,17},{2,10},{10... | collective-permute-start | bytes 1179656 | tf_op jit(solution)/shard_map/ppermute | solution.py:139
  216.4 12.0 %collective-permute-start.41 = (f32[12,64,128]{2,1,0:T(8,128)S(1)}, f32[12,64,128]{2,1,0:T(8,128)S(1)}, u32[]{:S(2)}, u32[]{:S(2)}) collective-permute-start(f32[12,64,128]{2,1,0:T(8,128)S(1)} %slice.334), channel_id=1, source_target_pairs={{0,2},{1,3},{2,0},{3,1},{4,6},{5,7},{6,4},{7,5},{8,10},{9,11},{10,... | collective-permute-start | bytes 1179656 | tf_op jit(solution)/shard_map/ppermute | solution.py:139
  222.8 13.2 %collective-permute-start.53 = (f32[192,320]{1,0:T(8,128)S(1)}, f32[192,320]{1,0:T(8,128)S(1)}, u32[]{:S(2)}, u32[]{:S(2)}) collective-permute-start(f32[192,320]{1,0:T(8,128)S(1)} %add.315), channel_id=1, source_target_pairs={{0,2},{1,3},{2,0},{3,1},{4,6},{5,7},{6,4},{7,5},{8,10},{9,11},{10,... | collective-permute-start | bytes 737288 | tf_op jit(solution)/shard_map/ppermute | solution.py:149
  223.0 13.2 %collective-permute-start.44 = (f32[6,64,128]{2,1,0:T(8,128)S(1)}, f32[6,64,128]{2,1,0:T(8,128)S(1)}, u32[]{:S(2)}, u32[]{:S(2)}) collective-permute-start(f32[6,64,128]{2,1,0:T(8,128)S(1)} %slice.338), channel_id=1, source_target_pairs={{0,16},{8,24},{16,0},{24,8},{1,17},{9,25},{17,1},{25,9},{2,18},{10... | collective-permute-start | bytes 589832 | tf_op jit(solution)/shard_map/ppermute | solution.py:139
  228.4 18.8 %collective-permute-start.42 = (f32[6,64,128]{2,1,0:T(8,128)S(1)}, f32[6,64,128]{2,1,0:T(8,128)S(1)}, u32[]{:S(2)}, u32[]{:S(2)}) collective-permute-start(f32[6,64,128]{2,1,0:T(8,128)S(1)} %slice.336), channel_id=1, source_target_pairs={{0,4},{1,5},{2,6},{3,7},{4,0},{5,1},{6,2},{7,3},{8,12},{9,13},{10,... | collective-permute-start | bytes 589832 | tf_op jit(solution)/shard_map/ppermute | solution.py:139
  236.1 16.2 %collective-permute-start.54 = (f32[192,320]{1,0:T(8,128)S(1)}, f32[192,320]{1,0:T(8,128)S(1)}, u32[]{:S(2)}, u32[]{:S(2)}) collective-permute-start(f32[192,320]{1,0:T(8,128)S(1)} %add.316), channel_id=1, source_target_pairs={{0,4},{1,5},{2,6},{3,7},{4,0},{5,1},{6,2},{7,3},{8,12},{9,13},{10,... | collective-permute-start | bytes 737288 | tf_op jit(solution)/shard_map/ppermute | solution.py:149
  247.9 4.5 %collective-permute-start.55 = (f32[192,64]{1,0:T(8,128)S(1)}, f32[192,64]{1,0:T(8,128)S(1)}, u32[]{:S(2)}, u32[]{:S(2)}) collective-permute-start(f32[192,64]{1,0:T(8,128)S(1)} %convolution_multiply_fusion.1), channel_id=1, source_target_pairs={{0,8},{8,0},{16,24},{24,16},{1,9},{9,1},{17,25},{25,17},{2,10},{10... | collective-permute-start | bytes 147464 | tf_op jit(solution)/shard_map/ppermute | solution.py:159
  248.0 5.7 %collective-permute-start.56 = (f32[192,64]{1,0:T(8,128)S(1)}, f32[192,64]{1,0:T(8,128)S(1)}, u32[]{:S(2)}, u32[]{:S(2)}) collective-permute-start(f32[192,64]{1,0:T(8,128)S(1)} %convolution_multiply_fusion.1), channel_id=1, source_target_pairs={{0,16},{8,24},{16,0},{24,8},{1,17},{9,25},{17,1},{25,9},{2,18},{10... | collective-permute-start | bytes 147464 | tf_op jit(solution)/shard_map/ppermute | solution.py:159
  248.1 6.7 %collective-permute-start.57 = (f32[192,64]{1,0:T(8,128)S(1)}, f32[192,64]{1,0:T(8,128)S(1)}, u32[]{:S(2)}, u32[]{:S(2)}) collective-permute-start(f32[192,64]{1,0:T(8,128)S(1)} %convolution_multiply_fusion.1), channel_id=1, source_target_pairs={{0,24},{8,16},{16,8},{24,0},{1,25},{9,17},{17,9},{25,1},{2,26},{10... | collective-permute-start | bytes 147464 | tf_op jit(solution)/shard_map/ppermute | solution.py:159
  255.6 7.9 %collective-permute-start.58 = (f32[192,64]{1,0:T(8,128)S(1)}, f32[192,64]{1,0:T(8,128)S(1)}, u32[]{:S(2)}, u32[]{:S(2)}) collective-permute-start(f32[192,64]{1,0:T(8,128)S(1)} %bitcast.137), channel_id=1, source_target_pairs={{0,1},{1,0},{2,3},{3,2},{4,5},{5,4},{6,7},{7,6},{8,9},{9,8},{10,11... | collective-permute-start | bytes 147464 | tf_op jit(solution)/shard_map/ppermute | solution.py:159
  257.7 6.1 %collective-permute-start.59 = (f32[192,64]{1,0:T(8,128)S(1)}, f32[192,64]{1,0:T(8,128)S(1)}, u32[]{:S(2)}, u32[]{:S(2)}) collective-permute-start(f32[192,64]{1,0:T(8,128)S(1)} %bitcast.138), channel_id=1, source_target_pairs={{0,2},{1,3},{2,0},{3,1},{4,6},{5,7},{6,4},{7,5},{8,10},{9,11},{10,... | collective-permute-start | bytes 147464 | tf_op jit(solution)/shard_map/ppermute | solution.py:159
  257.7 10.0 %collective-permute-start.60 = (f32[192,64]{1,0:T(8,128)S(1)}, f32[192,64]{1,0:T(8,128)S(1)}, u32[]{:S(2)}, u32[]{:S(2)}) collective-permute-start(f32[192,64]{1,0:T(8,128)S(1)} %bitcast.139), channel_id=1, source_target_pairs={{0,3},{1,2},{2,1},{3,0},{4,7},{5,6},{6,5},{7,4},{8,11},{9,10},{10,... | collective-permute-start | bytes 147464 | tf_op jit(solution)/shard_map/ppermute | solution.py:159
  259.9 14.2 %collective-permute-start.61 = (f32[192,64]{1,0:T(8,128)S(1)}, f32[192,64]{1,0:T(8,128)S(1)}, u32[]{:S(2)}, u32[]{:S(2)}) collective-permute-start(f32[192,64]{1,0:T(8,128)S(1)} %bitcast.140), channel_id=1, source_target_pairs={{0,4},{1,5},{2,6},{3,7},{4,0},{5,1},{6,2},{7,3},{8,12},{9,13},{10,... | collective-permute-start | bytes 147464 | tf_op jit(solution)/shard_map/ppermute | solution.py:159
  259.9 16.6 %collective-permute-start.62 = (f32[192,64]{1,0:T(8,128)S(1)}, f32[192,64]{1,0:T(8,128)S(1)}, u32[]{:S(2)}, u32[]{:S(2)}) collective-permute-start(f32[192,64]{1,0:T(8,128)S(1)} %bitcast.141), channel_id=1, source_target_pairs={{0,5},{1,4},{2,7},{3,6},{4,1},{5,0},{6,3},{7,2},{8,13},{9,12},{10,... | collective-permute-start | bytes 147464 | tf_op jit(solution)/shard_map/ppermute | solution.py:159
  263.5 13.0 %collective-permute-start.63 = (f32[192,64]{1,0:T(8,128)S(1)}, f32[192,64]{1,0:T(8,128)S(1)}, u32[]{:S(2)}, u32[]{:S(2)}) collective-permute-start(f32[192,64]{1,0:T(8,128)S(1)} %bitcast.142), channel_id=1, source_target_pairs={{0,6},{1,7},{2,4},{3,5},{4,2},{5,3},{6,0},{7,1},{8,14},{9,15},{10,... | collective-permute-start | bytes 147464 | tf_op jit(solution)/shard_map/ppermute | solution.py:159
  263.8 12.7 %collective-permute-start.64 = (f32[192,64]{1,0:T(8,128)S(1)}, f32[192,64]{1,0:T(8,128)S(1)}, u32[]{:S(2)}, u32[]{:S(2)}) collective-permute-start(f32[192,64]{1,0:T(8,128)S(1)} %bitcast.143), channel_id=1, source_target_pairs={{0,7},{1,6},{2,5},{3,4},{4,3},{5,2},{6,1},{7,0},{8,15},{9,14},{10,... | collective-permute-start | bytes 147464 | tf_op jit(solution)/shard_map/ppermute | solution.py:159
  (7 other events, 147.0 us)

commit v8 on v6

--- a/solution.py
+++ b/solution.py
@@ -8,7 +8,7 @@
 from jax.sharding import PartitionSpec as P
 
 GROUP = 64
-UNROLL = 32
+UNROLL = 64
 
 
 def tile_kernel(rows_ref, cols_ref, cnt_ref, vals_ref, rin_ref, cin_ref, *out_refs):
@@ -199,11 +199,12 @@
     orthonormal = lax.linalg.triangular_solve(cholesky_factor, block_x, left_side=True, lower=True)
     tile = tile_vals.shape[-1]
     dir_rows, dir_cols = gathered(block_p.astype(jnp.bfloat16), tile)
+    p_rows, p_cols = tile_products(
+        dir_rows, dir_cols, slot_rows, slot_cols, live_count, slot_vals, (block_p.shape[0],)
+    )
     ortho_rows, ortho_cols = gathered(orthonormal.astype(jnp.bfloat16), tile)
-    x_rows, x_cols, p_rows, p_cols = tile_products(
-        jnp.concatenate([ortho_rows, dir_rows], axis=1),
-        jnp.concatenate([ortho_cols, dir_cols], axis=1),
-        slot_rows, slot_cols, live_count, slot_vals, (width_k, block_p.shape[0]),
+    x_rows, x_cols = tile_products(
+        ortho_rows, ortho_cols, slot_rows, slot_cols, live_count, slot_vals, (width_k,)
     )
     image_x = owned(x_rows, x_cols)
     rayleigh = all_sum(product(orthonormal, image_x))

time: 256 us -> 272 us (1.062); the launches traced: 255 us -> 274 us
  starting transfers between devices: 80.9 us -> 50.5 us
  Pallas kernels: 45.8 us -> 75 us
  waiting for transfers between devices: 98.9 us -> 125 us
  other arithmetic: 21.3 us -> 15.7 us
    pallas_call x2 -> x3, Pallas kernels: 45.8 us -> 75 us  [tile_products(): pl.pallas_call(tile_kernel, grid_spec=grid_spec, out_shape=[jax.ShapeDtyp...]
    ppermute x20, starting transfers between devices: 37.8 us -> 24.8 us  [all_sum(): value = value + lax.ppermute(value, axis, exchange_pairs(size, step))]
    ppermute x20, waiting for transfers between devices: 40 us -> 52.7 us  [all_sum(): value = value + lax.ppermute(value, axis, exchange_pairs(size, step))]
    ppermute x15, starting transfers between devices: 23.7 us -> 11.5 us  [scatter_sum(): lax.ppermute(sent, axis, exchange_pairs(size, step)).astype(held.dtype)]
    ppermute x15, waiting for transfers between devices: 27.9 us -> 36.5 us  [gather_blocks(): lax.ppermute(held, axis, exchange_pairs(size, step))]
    ppermute x15, starting transfers between devices: 19.4 us -> 14.2 us  [gather_blocks(): lax.ppermute(held, axis, exchange_pairs(size, step))]
    ppermute x15, waiting for transfers between devices: 30.9 us -> 36 us  [scatter_sum(): lax.ppermute(sent, axis, exchange_pairs(size, step)).astype(held.dtype)]
    concatenate x2 -> x0, other arithmetic: 4.49 us -> none  [the longest x1 4.43 us: per_device(): jnp.concatenate([ortho_rows, dir_rows], axis=1)]
  transfers between devices with their start and end apart: 50 -> 50, of which waited for: 29 -> 31; matrix products, arithmetic and copies ran while one was open for 8% -> 7% of each run, Pallas kernels for 9% -> 27%
where the time goes in v8:
time: 272 us; the launch traced here: 274 us
  waiting for transfers between devices  125 us (46%)
  Pallas kernels  75 us (28%)
  starting transfers between devices  50.5 us (19%)
  other arithmetic  15.7 us (6%)
  matrix products  3.81 us (1%)
    pallas_call x3, Pallas kernels, tile_products(): pl.pallas_call(tile_kernel, grid_spec=grid_spec, out_shape=[jax.ShapeDtyp...  75 us
    ppermute x20, waiting for transfers between devices, all_sum(): value = value + lax.ppermute(value, axis, exchange_pairs(size, step))  52.7 us
    ppermute x15, waiting for transfers between devices, gather_blocks(): lax.ppermute(held, axis, exchange_pairs(size, step))  36.5 us
    ppermute x15, waiting for transfers between devices, scatter_sum(): lax.ppermute(sent, axis, exchange_pairs(size, step)).astype(held.dtype)  36 us
    ppermute x20, starting transfers between devices, all_sum(): value = value + lax.ppermute(value, axis, exchange_pairs(size, step))  24.8 us
    ppermute x15, starting transfers between devices, gather_blocks(): lax.ppermute(held, axis, exchange_pairs(size, step))  14.2 us
    ppermute x15, starting transfers between devices, scatter_sum(): lax.ppermute(sent, axis, exchange_pairs(size, step)).astype(held.dtype)  11.5 us
    another operation x3, other arithmetic, per_device(): cholesky_factor = jnp.linalg.cholesky(gram_x)  6.52 us
  transfers between devices with their start and end apart: 50, of which 31 were waited for; matrix products, arithmetic and copies ran while one was open for 7% of the time, Pallas kernels for 27%

profile of v8, /device:TPU:0, one launch (start us, length us, event | category | flops | bytes accessed | tf_op | source)
XLA Modules:
  0.0 274.5 jit_solution(7470221300787994246)
XLA Ops:
  0.7 0.9 copy-done
  2.4 0.9 collective-permute-done
  3.3 2.9 %collective-permute-start.1 = (f32[64,64]{0,1:T(8,128)S(1)}, f32[64,64]{0,1:T(8,128)S(1)}, u32[]{:S(2)}, u32[]{:S(2)}) collective-permute-start(f32[64,64]{0,1:T(8,128)S(1)} %add.147), channel_id=1, source_target_pairs={{0,16},{8,24},{16,0},{24,8},{1,17},{9,25},{17,1},{25,9},{2,18},{10... | collective-permute-start | bytes 49160 | tf_op jit(solution)/shard_map/ppermute | solution.py:149
  6.1 1.9 collective-permute-done.1
  8.0 2.0 collective-permute-start.2
  10.0 1.9 collective-permute-done.2
  11.9 2.1 collective-permute-start.3
  14.0 1.9 collective-permute-done.3
  15.9 3.0 %collective-permute-start.4 = (f32[64,64]{0,1:T(8,128)S(1)}, f32[64,64]{0,1:T(8,128)S(1)}, u32[]{:S(2)}, u32[]{:S(2)}) collective-permute-start(f32[64,64]{0,1:T(8,128)S(1)} %add.150), channel_id=1, source_target_pairs={{0,4},{1,5},{2,6},{3,7},{4,0},{5,1},{6,2},{7,3},{8,12},{9,13},{10,... | collective-permute-start | bytes 49160 | tf_op jit(solution)/shard_map/ppermute | solution.py:149
  19.0 0.9 bitcast_bitcast_fusion
  19.9 1.6 collective-permute-start.33
  21.9 5.8 %cholesky.16 = f32[64,64]{1,0:T(8,128)S(1)} custom-call(f32[64,64]{1,0:T(8,128)S(1)} %fusion.21), custom_call_target="Cholesky" | custom-call | tf_op jit(solution)/shard_map/jit(cholesky)/cholesky | solution.py:198
  28.5 0.7 fusion.18
  29.1 4.9 %custom-call.6 = f32[1,64,64]{1,2,0:T(8,128)S(1)} custom-call(f32[1,64,64]{2,1,0:T(8,128)S(1)} %fusion.18), custom_call_target="InvertDiagBlocksLowerTriangular" | custom-call | tf_op jit(solution)/shard_map/triangular_solve | solution.py:199
  34.4 2.7 collective-permute-start.8
  37.1 0.9 collective-permute-start.5
  38.0 1.7 collective-permute-done.8
  39.7 3.7 %collective-permute-done.5 = bf16[6,64,128]{2,1,0:T(8,128)(2,1)S(1)} collective-permute-done((bf16[6,64,128]{2,1,0:T(8,128)(2,1)S(1)}, bf16[6,64,128]{2,1,0:T(8,128)(2,1)S(1)}, u32[]{:S(2)}, u32[]{:S(2)}) %collective-permute-start.5) | collective-permute-done | bytes 98336 | tf_op jit(solution)/shard_map/ppermute | solution.py:125
  43.6 1.3 collective-permute-done.9
  44.9 5.9 %collective-permute-done.6 = bf16[12,64,128]{2,1,0:T(8,128)(2,1)S(1)} collective-permute-done((bf16[12,64,128]{2,1,0:T(8,128)(2,1)S(1)}, bf16[12,64,128]{2,1,0:T(8,128)(2,1)S(1)}, u32[]{:S(2)}, u32[]{:S(2)}) %collective-permute-start.6) | collective-permute-done | bytes 196640 | tf_op jit(solution)/shard_map/ppermute | solution.py:125
  50.9 1.6 collective-permute-start.7
  53.6 8.0 %collective-permute-done.7 = bf16[24,64,128]{2,1,0:T(8,128)(2,1)S(1)} collective-permute-done((bf16[24,64,128]{2,1,0:T(8,128)(2,1)S(1)}, bf16[24,64,128]{2,1,0:T(8,128)(2,1)S(1)}, u32[]{:S(2)}, u32[]{:S(2)}) %collective-permute-start.7) | collective-permute-done | bytes 393248 | tf_op jit(solution)/shard_map/ppermute | solution.py:125
  61.7 25.0 %shard_map.93 = (f32[48,64,128]{2,1,0:T(8,128)S(1)}, f32[24,64,128]{2,1,0:T(8,128)S(1)}) custom-call(s32[576]{0:T(1024)S(1)} %get-tuple-element.34.rows_ref, s32[576]{0:T(1024)S(1)} %get-tuple-element.35.cols_ref, s32[1]{0:T(128)} %bitcast.61.cnt_ref, bf16[576,128,128]{2,1,0:T(8,128)(2,1)} %bitcast.64, bf16[48,64,128]{2,1,0:T(8,128)(2,1)S(1)} %pad_maximum_fusion.rin_ref, ...), custom_call_target="tpu_custom_call" | custom-call | flops 2415919104 | bytes 22413312 | tf_op jit(solution)/shard_map/pallas_call | solution.py:94
  87.0 2.1 collective-permute-start.32
  89.2 5.5 %collective-permute-done.10 = bf16[24,64,128]{2,1,0:T(8,128)(2,1)S(1)} collective-permute-done((bf16[24,64,128]{2,1,0:T(8,128)(2,1)S(1)}, bf16[24,64,128]{2,1,0:T(8,128)(2,1)S(1)}, u32[]{:S(2)}, u32[]{:S(2)}) %collective-permute-start.10) | collective-permute-done | bytes 393248 | tf_op jit(solution)/shard_map/ppermute | solution.py:139
  94.8 3.8 %collective-permute-start.11 = (f32[12,64,128]{2,1,0:T(8,128)S(1)}, f32[12,64,128]{2,1,0:T(8,128)S(1)}, u32[]{:S(2)}, u32[]{:S(2)}) collective-permute-start(f32[12,64,128]{2,1,0:T(8,128)S(1)} %slice.147), channel_id=1, source_target_pairs={{0,2},{1,3},{2,0},{3,1},{4,6},{5,7},{6,4},{7,5},{8,10},{9,11},{10,... | collective-permute-start | bytes 1179656 | tf_op jit(solution)/shard_map/ppermute | solution.py:139
  99.2 7.4 %collective-permute-done.11 = f32[12,64,128]{2,1,0:T(8,128)S(1)} collective-permute-done((f32[12,64,128]{2,1,0:T(8,128)S(1)}, f32[12,64,128]{2,1,0:T(8,128)S(1)}, u32[]{:S(2)}, u32[]{:S(2)}) %collective-permute-start.11) | collective-permute-done | bytes 393248 | tf_op jit(solution)/shard_map/ppermute | solution.py:139
  106.6 1.2 collective-permute-start.12
  107.8 24.9 %shard_map.95 = (f32[48,64,128]{2,1,0:T(8,128)S(1)}, f32[24,64,128]{2,1,0:T(8,128)S(1)}) custom-call(s32[576]{0:T(1024)S(1)} %get-tuple-element.34.rows_ref, s32[576]{0:T(1024)S(1)} %get-tuple-element.35.cols_ref, s32[1]{0:T(128)} %bitcast.63.cnt_ref, bf16[576,128,128]{2,1,0:T(8,128)(2,1)} %bitcast.65, bf16[48,64,128]{2,1,0:T(8,128)(2,1)S(1)} %pad_maximum_fusion.2.rin_ref, ...), custom_call_target="tpu_custom_call" | custom-call | flops 2415919104 | bytes 22413312 | tf_op jit(solution)/shard_map/pallas_call | solution.py:94
  133.9 0.9 collective-permute-done.15
  134.7 3.9 %collective-permute-done.16 = f32[64,64]{0,1:T(8,128)S(1)} collective-permute-done((f32[64,64]{0,1:T(8,128)S(1)}, f32[64,64]{0,1:T(8,128)S(1)}, u32[]{:S(2)}, u32[]{:S(2)}) %collective-permute-start.16) | collective-permute-done | bytes 16416 | tf_op jit(solution)/shard_map/ppermute | solution.py:149
  138.6 1.8 collective-permute-start.17
  140.5 4.6 %collective-permute-done.17 = f32[64,64]{0,1:T(8,128)S(1)} collective-permute-done((f32[64,64]{0,1:T(8,128)S(1)}, f32[64,64]{0,1:T(8,128)S(1)}, u32[]{:S(2)}, u32[]{:S(2)}) %collective-permute-start.17) | collective-permute-done | bytes 16416 | tf_op jit(solution)/shard_map/ppermute | solution.py:149
  145.1 1.7 collective-permute-start.18
  147.0 2.0 collective-permute-done.18
  149.2 1.9 collective-permute-start.36
  151.1 2.8 %collective-permute-done.19 = f32[64,64]{0,1:T(8,128)S(1)} collective-permute-done((f32[64,64]{0,1:T(8,128)S(1)}, f32[64,64]{0,1:T(8,128)S(1)}, u32[]{:S(2)}, u32[]{:S(2)}) %collective-permute-start.19) | collective-permute-done | bytes 16416 | tf_op jit(solution)/shard_map/ppermute | solution.py:149
  154.8 7.0 %collective-permute-done.36 = f32[12,64,128]{2,1,0:T(8,128)S(1)} collective-permute-done((f32[12,64,128]{2,1,0:T(8,128)S(1)}, f32[12,64,128]{2,1,0:T(8,128)S(1)}, u32[]{:S(2)}, u32[]{:S(2)}) %collective-permute-start.36) | collective-permute-done | bytes 393248 | tf_op jit(solution)/shard_map/ppermute | solution.py:139
  161.9 1.6 collective-permute-start.37
  163.6 2.5 collective-permute-start.21
  166.8 7.7 %collective-permute-done.21 = bf16[12,64,128]{2,1,0:T(8,128)(2,1)S(1)} collective-permute-done((bf16[12,64,128]{2,1,0:T(8,128)(2,1)S(1)}, bf16[12,64,128]{2,1,0:T(8,128)(2,1)S(1)}, u32[]{:S(2)}, u32[]{:S(2)}) %collective-permute-start.21) | collective-permute-done | bytes 196640 | tf_op jit(solution)/shard_map/ppermute | solution.py:125
  174.6 1.4 collective-permute-start.22
  177.6 8.0 %collective-permute-done.22 = bf16[24,64,128]{2,1,0:T(8,128)(2,1)S(1)} collective-permute-done((bf16[24,64,128]{2,1,0:T(8,128)(2,1)S(1)}, bf16[24,64,128]{2,1,0:T(8,128)(2,1)S(1)}, u32[]{:S(2)}, u32[]{:S(2)}) %collective-permute-start.22) | collective-permute-done | bytes 393248 | tf_op jit(solution)/shard_map/ppermute | solution.py:125
  185.7 25.1 %shard_map.94 = (f32[48,64,128]{2,1,0:T(8,128)S(1)}, f32[24,64,128]{2,1,0:T(8,128)S(1)}) custom-call(s32[576]{0:T(1024)S(1)} %get-tuple-element.34.rows_ref, s32[576]{0:T(1024)S(1)} %get-tuple-element.35.cols_ref, s32[1]{0:T(128)} %bitcast.62.cnt_ref, bf16[576,128,128]{2,1,0:T(8,128)(2,1)} %bitcast.66, bf16[48,64,128]{2,1,0:T(8,128)(2,1)S(1)} %pad_maximum_fusion.1.rin_ref, ...), custom_call_target="tpu_custom_call" | custom-call | flops 2415919104 | bytes 22413312 | tf_op jit(solution)/shard_map/pallas_call | solution.py:94
  211.1 6.7 %collective-permute-done.41 = f32[192,320]{1,0:T(8,128)S(1)} collective-permute-done((f32[192,320]{1,0:T(8,128)S(1)}, f32[192,320]{1,0:T(8,128)S(1)}, u32[]{:S(2)}, u32[]{:S(2)}) %collective-permute-start.41) | collective-permute-done | bytes 245792 | tf_op jit(solution)/shard_map/ppermute | solution.py:149
  217.9 2.1 collective-permute-start.42
  220.1 0.8 collective-permute-done.25
  221.0 1.3 collective-permute-start.26
  222.4 2.3 collective-permute-done.42
  224.7 2.4 collective-permute-start.43
  227.2 5.9 %collective-permute-done.26 = f32[12,64,128]{2,1,0:T(8,128)S(1)} collective-permute-done((f32[12,64,128]{2,1,0:T(8,128)S(1)}, f32[12,64,128]{2,1,0:T(8,128)S(1)}, u32[]{:S(2)}, u32[]{:S(2)}) %collective-permute-start.26) | collective-permute-done | bytes 393248 | tf_op jit(solution)/shard_map/ppermute | solution.py:139
  233.2 1.1 collective-permute-start.27
  234.3 6.1 %collective-permute-done.43 = f32[192,320]{1,0:T(8,128)S(1)} collective-permute-done((f32[192,320]{1,0:T(8,128)S(1)}, f32[192,320]{1,0:T(8,128)S(1)}, u32[]{:S(2)}, u32[]{:S(2)}) %collective-permute-start.43) | collective-permute-done | bytes 245792 | tf_op jit(solution)/shard_map/ppermute | solution.py:149
  240.5 9.3 %collective-permute-done.27 = f32[6,64,128]{2,1,0:T(8,128)S(1)} collective-permute-done((f32[6,64,128]{2,1,0:T(8,128)S(1)}, f32[6,64,128]{2,1,0:T(8,128)S(1)}, u32[]{:S(2)}, u32[]{:S(2)}) %collective-permute-start.27) | collective-permute-done | bytes 196640 | tf_op jit(solution)/shard_map/ppermute | solution.py:139
  250.6 1.3 collective-permute-done.45
  251.9 1.0 collective-permute-start.46
  252.9 3.9 %collective-permute-done.46 = f32[192,64]{1,0:T(8,128)S(1)} collective-permute-done((f32[192,64]{1,0:T(8,128)S(1)}, f32[192,64]{1,0:T(8,128)S(1)}, u32[]{:S(2)}, u32[]{:S(2)}) %collective-permute-start.46) | collective-permute-done | bytes 49184 | tf_op jit(solution)/shard_map/ppermute | solution.py:149
  256.8 3.2 %collective-permute-start.47 = (f32[192,64]{1,0:T(8,128)S(1)}, f32[192,64]{1,0:T(8,128)S(1)}, u32[]{:S(2)}, u32[]{:S(2)}) collective-permute-start(f32[192,64]{1,0:T(8,128)S(1)} %add.182), channel_id=1, source_target_pairs={{0,1},{1,0},{2,3},{3,2},{4,5},{5,4},{6,7},{7,6},{8,9},{9,8},{10,11... | collective-permute-start | bytes 147464 | tf_op jit(solution)/shard_map/ppermute | solution.py:149
  260.0 2.6 collective-permute-done.47
  262.8 4.6 %collective-permute-done.48 = f32[192,64]{1,0:T(8,128)S(1)} collective-permute-done((f32[192,64]{1,0:T(8,128)S(1)}, f32[192,64]{1,0:T(8,128)S(1)}, u32[]{:S(2)}, u32[]{:S(2)}) %collective-permute-start.48) | collective-permute-done | bytes 49184 | tf_op jit(solution)/shard_map/ppermute | solution.py:149
  267.4 1.2 collective-permute-start.49
  268.7 0.7 slice.168
  269.3 4.3 %collective-permute-done.49 = f32[192,64]{1,0:T(8,128)S(1)} collective-permute-done((f32[192,64]{1,0:T(8,128)S(1)}, f32[192,64]{1,0:T(8,128)S(1)}, u32[]{:S(2)}, u32[]{:S(2)}) %collective-permute-start.49) | collective-permute-done | bytes 49184 | tf_op jit(solution)/shard_map/ppermute | solution.py:149
  273.7 0.8 pad_maximum_fusion.17
  (132 shorter events, 10.9 us)
Async XLA Ops:
  0.6 0.9 copy-start
  0.6 37.3 %copy-start.4 = (s32[1,1,576]{2,1,0:T(1,128)S(1)}, s32[1,1,576]{2,1,0:T(1,128)}, u32[]{:S(2)}) copy-start(s32[1,1,576]{2,1,0:T(1,128)} %param.8) | copy-start | bytes 6916
  0.7 42.9 %copy-start.5 = (s32[1,1,576]{2,1,0:T(1,128)S(1)}, s32[1,1,576]{2,1,0:T(1,128)}, u32[]{:S(2)}) copy-start(s32[1,1,576]{2,1,0:T(1,128)} %param.9) | copy-start | bytes 6916
  1.9 1.4 collective-permute-start
  3.3 4.8 %collective-permute-start.1 = (f32[64,64]{0,1:T(8,128)S(1)}, f32[64,64]{0,1:T(8,128)S(1)}, u32[]{:S(2)}, u32[]{:S(2)}) collective-permute-start(f32[64,64]{0,1:T(8,128)S(1)} %add.147), channel_id=1, source_target_pairs={{0,16},{8,24},{16,0},{24,8},{1,17},{9,25},{17,1},{25,9},{2,18},{10... | collective-permute-start | bytes 49160 | tf_op jit(solution)/shard_map/ppermute | solution.py:149
  8.0 3.9 %collective-permute-start.2 = (f32[64,64]{0,1:T(8,128)S(1)}, f32[64,64]{0,1:T(8,128)S(1)}, u32[]{:S(2)}, u32[]{:S(2)}) collective-permute-start(f32[64,64]{0,1:T(8,128)S(1)} %add.148), channel_id=1, source_target_pairs={{0,1},{1,0},{2,3},{3,2},{4,5},{5,4},{6,7},{7,6},{8,9},{9,8},{10,11... | collective-permute-start | bytes 49160 | tf_op jit(solution)/shard_map/ppermute | solution.py:149
  11.9 4.0 %collective-permute-start.3 = (f32[64,64]{0,1:T(8,128)S(1)}, f32[64,64]{0,1:T(8,128)S(1)}, u32[]{:S(2)}, u32[]{:S(2)}) collective-permute-start(f32[64,64]{0,1:T(8,128)S(1)} %add.149), channel_id=1, source_target_pairs={{0,2},{1,3},{2,0},{3,1},{4,6},{5,7},{6,4},{7,5},{8,10},{9,11},{10,... | collective-permute-start | bytes 49160 | tf_op jit(solution)/shard_map/ppermute | solution.py:149
  15.9 5.9 %collective-permute-start.4 = (f32[64,64]{0,1:T(8,128)S(1)}, f32[64,64]{0,1:T(8,128)S(1)}, u32[]{:S(2)}, u32[]{:S(2)}) collective-permute-start(f32[64,64]{0,1:T(8,128)S(1)} %add.150), channel_id=1, source_target_pairs={{0,4},{1,5},{2,6},{3,7},{4,0},{5,1},{6,2},{7,3},{8,12},{9,13},{10,... | collective-permute-start | bytes 49160 | tf_op jit(solution)/shard_map/ppermute | solution.py:149
  19.9 33.2 %collective-permute-start.33 = (bf16[6,64,128]{2,1,0:T(8,128)(2,1)S(1)}, bf16[6,64,128]{2,1,0:T(8,128)(2,1)S(1)}, u32[]{:S(2)}, u32[]{:S(2)}) collective-permute-start(bf16[6,64,128]{2,1,0:T(8,128)(2,1)S(1)} %bitcast_bitcast_fusion), channel_id=1, source_target_pairs={{0,16},{8,24},{16,0},{24,8},{1,17},{9,25},{17,1},{25,9},{2,18},{10... | collective-permute-start | bytes 294920 | tf_op jit(solution)/shard_map/ppermute | solution.py:125
  21.5 31.6 %collective-permute-start.30 = (bf16[6,64,128]{2,1,0:T(8,128)(2,1)S(1)}, bf16[6,64,128]{2,1,0:T(8,128)(2,1)S(1)}, u32[]{:S(2)}, u32[]{:S(2)}) collective-permute-start(bf16[6,64,128]{2,1,0:T(8,128)(2,1)S(1)} %bitcast_bitcast_fusion), channel_id=1, source_target_pairs={{0,4},{1,5},{2,6},{3,7},{4,0},{5,1},{6,2},{7,3},{8,12},{9,13},{10,... | collective-permute-start | bytes 294920 | tf_op jit(solution)/shard_map/ppermute | solution.py:125
  34.4 5.2 %collective-permute-start.8 = (bf16[6,64,128]{2,1,0:T(8,128)(2,1)S(1)}, bf16[6,64,128]{2,1,0:T(8,128)(2,1)S(1)}, u32[]{:S(2)}, u32[]{:S(2)}) collective-permute-start(bf16[6,64,128]{2,1,0:T(8,128)(2,1)S(1)} %bitcast_bitcast_fusion.2), channel_id=1, source_target_pairs={{0,16},{8,24},{16,0},{24,8},{1,17},{9,25},{17,1},{25,9},{2,18},{10... | collective-permute-start | bytes 294920 | tf_op jit(solution)/shard_map/ppermute | solution.py:125
  37.1 6.3 %collective-permute-start.5 = (bf16[6,64,128]{2,1,0:T(8,128)(2,1)S(1)}, bf16[6,64,128]{2,1,0:T(8,128)(2,1)S(1)}, u32[]{:S(2)}, u32[]{:S(2)}) collective-permute-start(bf16[6,64,128]{2,1,0:T(8,128)(2,1)S(1)} %bitcast_bitcast_fusion.2), channel_id=1, source_target_pairs={{0,4},{1,5},{2,6},{3,7},{4,0},{5,1},{6,2},{7,3},{8,12},{9,13},{10,... | collective-permute-start | bytes 294920 | tf_op jit(solution)/shard_map/ppermute | solution.py:125
  43.4 1.5 collective-permute-start.9
  43.5 7.3 %collective-permute-start.6 = (bf16[12,64,128]{2,1,0:T(8,128)(2,1)S(1)}, bf16[12,64,128]{2,1,0:T(8,128)(2,1)S(1)}, u32[]{:S(2)}, u32[]{:S(2)}) collective-permute-start(bf16[12,64,128]{2,1,0:T(8,128)(2,1)S(1)} %get-tuple-element.33), channel_id=1, source_target_pairs={{0,2},{1,3},{2,0},{3,1},{4,6},{5,7},{6,4},{7,5},{8,10},{9,11},{10,... | collective-permute-start | bytes 589832 | tf_op jit(solution)/shard_map/ppermute | solution.py:125
  50.9 10.7 %collective-permute-start.7 = (bf16[24,64,128]{2,1,0:T(8,128)(2,1)S(1)}, bf16[24,64,128]{2,1,0:T(8,128)(2,1)S(1)}, u32[]{:S(2)}, u32[]{:S(2)}) collective-permute-start(bf16[24,64,128]{2,1,0:T(8,128)(2,1)S(1)} %get-tuple-element.31), channel_id=1, source_target_pairs={{0,1},{1,0},{2,3},{3,2},{4,5},{5,4},{6,7},{7,6},{8,9},{9,8},{10,11... | collective-permute-start | bytes 1179656 | tf_op jit(solution)/shard_map/ppermute | solution.py:125
  53.2 33.7 %collective-permute-start.34 = (bf16[12,64,128]{2,1,0:T(8,128)(2,1)S(1)}, bf16[12,64,128]{2,1,0:T(8,128)(2,1)S(1)}, u32[]{:S(2)}, u32[]{:S(2)}) collective-permute-start(bf16[12,64,128]{2,1,0:T(8,128)(2,1)S(1)} %get-tuple-element.24), channel_id=1, source_target_pairs={{0,8},{8,0},{16,24},{24,16},{1,9},{9,1},{17,25},{25,17},{2,10},{10... | collective-permute-start | bytes 589832 | tf_op jit(solution)/shard_map/ppermute | solution.py:125
  53.3 33.6 %collective-permute-start.31 = (bf16[12,64,128]{2,1,0:T(8,128)(2,1)S(1)}, bf16[12,64,128]{2,1,0:T(8,128)(2,1)S(1)}, u32[]{:S(2)}, u32[]{:S(2)}) collective-permute-start(bf16[12,64,128]{2,1,0:T(8,128)(2,1)S(1)} %get-tuple-element.25), channel_id=1, source_target_pairs={{0,2},{1,3},{2,0},{3,1},{4,6},{5,7},{6,4},{7,5},{8,10},{9,11},{10,... | collective-permute-start | bytes 589832 | tf_op jit(solution)/shard_map/ppermute | solution.py:125
  86.8 7.9 %collective-permute-start.10 = (bf16[24,64,128]{2,1,0:T(8,128)(2,1)S(1)}, bf16[24,64,128]{2,1,0:T(8,128)(2,1)S(1)}, u32[]{:S(2)}, u32[]{:S(2)}) collective-permute-start(bf16[24,64,128]{2,1,0:T(8,128)(2,1)S(1)} %slice.207), channel_id=1, source_target_pairs={{0,1},{1,0},{2,3},{3,2},{4,5},{5,4},{6,7},{7,6},{8,9},{9,8},{10,11... | collective-permute-start | bytes 1179656 | tf_op jit(solution)/shard_map/ppermute | solution.py:139
  87.0 11.9 %collective-permute-start.32 = (bf16[24,64,128]{2,1,0:T(8,128)(2,1)S(1)}, bf16[24,64,128]{2,1,0:T(8,128)(2,1)S(1)}, u32[]{:S(2)}, u32[]{:S(2)}) collective-permute-start(bf16[24,64,128]{2,1,0:T(8,128)(2,1)S(1)} %get-tuple-element.23), channel_id=1, source_target_pairs={{0,1},{1,0},{2,3},{3,2},{4,5},{5,4},{6,7},{7,6},{8,9},{9,8},{10,11... | collective-permute-start | bytes 1179656 | tf_op jit(solution)/shard_map/ppermute | solution.py:125
  89.1 9.9 %collective-permute-start.13 = (f32[12,64,128]{2,1,0:T(8,128)S(1)}, f32[12,64,128]{2,1,0:T(8,128)S(1)}, u32[]{:S(2)}, u32[]{:S(2)}) collective-permute-start(f32[12,64,128]{2,1,0:T(8,128)S(1)} %slice.119), channel_id=1, source_target_pairs={{0,8},{8,0},{16,24},{24,16},{1,9},{9,1},{17,25},{25,17},{2,10},{10... | collective-permute-start | bytes 1179656 | tf_op jit(solution)/shard_map/ppermute | solution.py:139
  94.8 11.7 %collective-permute-start.11 = (f32[12,64,128]{2,1,0:T(8,128)S(1)}, f32[12,64,128]{2,1,0:T(8,128)S(1)}, u32[]{:S(2)}, u32[]{:S(2)}) collective-permute-start(f32[12,64,128]{2,1,0:T(8,128)S(1)} %slice.147), channel_id=1, source_target_pairs={{0,2},{1,3},{2,0},{3,1},{4,6},{5,7},{6,4},{7,5},{8,10},{9,11},{10,... | collective-permute-start | bytes 1179656 | tf_op jit(solution)/shard_map/ppermute | solution.py:139
  99.1 33.8 %collective-permute-start.14 = (f32[6,64,128]{2,1,0:T(8,128)S(1)}, f32[6,64,128]{2,1,0:T(8,128)S(1)}, u32[]{:S(2)}, u32[]{:S(2)}) collective-permute-start(f32[6,64,128]{2,1,0:T(8,128)S(1)} %slice.151), channel_id=1, source_target_pairs={{0,16},{8,24},{16,0},{24,8},{1,17},{9,25},{17,1},{25,9},{2,18},{10... | collective-permute-start | bytes 589832 | tf_op jit(solution)/shard_map/ppermute | solution.py:139
  106.6 26.3 %collective-permute-start.12 = (f32[6,64,128]{2,1,0:T(8,128)S(1)}, f32[6,64,128]{2,1,0:T(8,128)S(1)}, u32[]{:S(2)}, u32[]{:S(2)}) collective-permute-start(f32[6,64,128]{2,1,0:T(8,128)S(1)} %slice.149), channel_id=1, source_target_pairs={{0,4},{1,5},{2,6},{3,7},{4,0},{5,1},{6,2},{7,3},{8,12},{9,13},{10,... | collective-permute-start | bytes 589832 | tf_op jit(solution)/shard_map/ppermute | solution.py:139
  132.7 14.1 %collective-permute-start.38 = (f32[12,64,128]{2,1,0:T(8,128)S(1)}, f32[12,64,128]{2,1,0:T(8,128)S(1)}, u32[]{:S(2)}, u32[]{:S(2)}) collective-permute-start(f32[12,64,128]{2,1,0:T(8,128)S(1)} %slice.139), channel_id=1, source_target_pairs={{0,8},{8,0},{16,24},{24,16},{1,9},{9,1},{17,25},{25,17},{2,10},{10... | collective-permute-start | bytes 1179656 | tf_op jit(solution)/shard_map/ppermute | solution.py:139
  132.8 16.2 %collective-permute-start.35 = (bf16[24,64,128]{2,1,0:T(8,128)(2,1)S(1)}, bf16[24,64,128]{2,1,0:T(8,128)(2,1)S(1)}, u32[]{:S(2)}, u32[]{:S(2)}) collective-permute-start(bf16[24,64,128]{2,1,0:T(8,128)(2,1)S(1)} %slice.205), channel_id=1, source_target_pairs={{0,1},{1,0},{2,3},{3,2},{4,5},{5,4},{6,7},{7,6},{8,9},{9,8},{10,11... | collective-permute-start | bytes 1179656 | tf_op jit(solution)/shard_map/ppermute | solution.py:139
  133.3 1.4 collective-permute-start.15
  134.7 3.9 %collective-permute-start.16 = (f32[64,64]{0,1:T(8,128)S(1)}, f32[64,64]{0,1:T(8,128)S(1)}, u32[]{:S(2)}, u32[]{:S(2)}) collective-permute-start(f32[64,64]{0,1:T(8,128)S(1)} %add.159), channel_id=1, source_target_pairs={{0,16},{8,24},{16,0},{24,8},{1,17},{9,25},{17,1},{25,9},{2,18},{10... | collective-permute-start | bytes 49160 | tf_op jit(solution)/shard_map/ppermute | solution.py:149
  138.6 6.5 %collective-permute-start.17 = (f32[64,64]{0,1:T(8,128)S(1)}, f32[64,64]{0,1:T(8,128)S(1)}, u32[]{:S(2)}, u32[]{:S(2)}) collective-permute-start(f32[64,64]{0,1:T(8,128)S(1)} %add.160), channel_id=1, source_target_pairs={{0,1},{1,0},{2,3},{3,2},{4,5},{5,4},{6,7},{7,6},{8,9},{9,8},{10,11... | collective-permute-start | bytes 49160 | tf_op jit(solution)/shard_map/ppermute | solution.py:149
  145.1 3.9 %collective-permute-start.18 = (f32[64,64]{0,1:T(8,128)S(1)}, f32[64,64]{0,1:T(8,128)S(1)}, u32[]{:S(2)}, u32[]{:S(2)}) collective-permute-start(f32[64,64]{0,1:T(8,128)S(1)} %add.161), channel_id=1, source_target_pairs={{0,2},{1,3},{2,0},{3,1},{4,6},{5,7},{6,4},{7,5},{8,10},{9,11},{10,... | collective-permute-start | bytes 49160 | tf_op jit(solution)/shard_map/ppermute | solution.py:149
  146.9 29.8 %collective-permute-start.39 = (f32[6,64,128]{2,1,0:T(8,128)S(1)}, f32[6,64,128]{2,1,0:T(8,128)S(1)}, u32[]{:S(2)}, u32[]{:S(2)}) collective-permute-start(f32[6,64,128]{2,1,0:T(8,128)S(1)} %slice.165), channel_id=1, source_target_pairs={{0,16},{8,24},{16,0},{24,8},{1,17},{9,25},{17,1},{25,9},{2,18},{10... | collective-permute-start | bytes 589832 | tf_op jit(solution)/shard_map/ppermute | solution.py:139
  149.0 4.9 %collective-permute-start.19 = (f32[64,64]{0,1:T(8,128)S(1)}, f32[64,64]{0,1:T(8,128)S(1)}, u32[]{:S(2)}, u32[]{:S(2)}) collective-permute-start(f32[64,64]{0,1:T(8,128)S(1)} %add.162), channel_id=1, source_target_pairs={{0,4},{1,5},{2,6},{3,7},{4,0},{5,1},{6,2},{7,3},{8,12},{9,13},{10,... | collective-permute-start | bytes 49160 | tf_op jit(solution)/shard_map/ppermute | solution.py:149
  149.2 17.0 %copy-start.2 = (f32[64,768]{1,0:T(8,128)S(1)}, f32[64,768]{1,0:T(8,128)}, u32[]{:S(2)}) copy-start(f32[64,768]{1,0:T(8,128)} %param.7) | copy-start | bytes 589828
  149.2 12.6 %collective-permute-start.36 = (f32[12,64,128]{2,1,0:T(8,128)S(1)}, f32[12,64,128]{2,1,0:T(8,128)S(1)}, u32[]{:S(2)}, u32[]{:S(2)}) collective-permute-start(f32[12,64,128]{2,1,0:T(8,128)S(1)} %slice.161), channel_id=1, source_target_pairs={{0,2},{1,3},{2,0},{3,1},{4,6},{5,7},{6,4},{7,5},{8,10},{9,11},{10,... | collective-permute-start | bytes 1179656 | tf_op jit(solution)/shard_map/ppermute | solution.py:139
  154.3 95.6 %copy-start.1 = (f32[64,768]{1,0:T(8,128)}, f32[64,768]{1,0:T(8,128)S(1)}, u32[]{:S(2)}) copy-start(f32[64,768]{1,0:T(8,128)S(1)} %convolution_subtract_fusion) | copy-start | bytes 589828
  154.3 9.2 %collective-permute-start.23 = (bf16[6,64,128]{2,1,0:T(8,128)(2,1)S(1)}, bf16[6,64,128]{2,1,0:T(8,128)(2,1)S(1)}, u32[]{:S(2)}, u32[]{:S(2)}) collective-permute-start(bf16[6,64,128]{2,1,0:T(8,128)(2,1)S(1)} %bitcast_bitcast_fusion.1), channel_id=1, source_target_pairs={{0,16},{8,24},{16,0},{24,8},{1,17},{9,25},{17,1},{25,9},{2,18},{10... | collective-permute-start | bytes 294920 | tf_op jit(solution)/shard_map/ppermute | solution.py:125
  154.5 9.0 %collective-permute-start.20 = (bf16[6,64,128]{2,1,0:T(8,128)(2,1)S(1)}, bf16[6,64,128]{2,1,0:T(8,128)(2,1)S(1)}, u32[]{:S(2)}, u32[]{:S(2)}) collective-permute-start(bf16[6,64,128]{2,1,0:T(8,128)(2,1)S(1)} %bitcast_bitcast_fusion.1), channel_id=1, source_target_pairs={{0,4},{1,5},{2,6},{3,7},{4,0},{5,1},{6,2},{7,3},{8,12},{9,13},{10,... | collective-permute-start | bytes 294920 | tf_op jit(solution)/shard_map/ppermute | solution.py:125
  161.9 14.8 %collective-permute-start.37 = (f32[6,64,128]{2,1,0:T(8,128)S(1)}, f32[6,64,128]{2,1,0:T(8,128)S(1)}, u32[]{:S(2)}, u32[]{:S(2)}) collective-permute-start(f32[6,64,128]{2,1,0:T(8,128)S(1)} %slice.163), channel_id=1, source_target_pairs={{0,4},{1,5},{2,6},{3,7},{4,0},{5,1},{6,2},{7,3},{8,12},{9,13},{10,... | collective-permute-start | bytes 589832 | tf_op jit(solution)/shard_map/ppermute | solution.py:139
  163.6 3.2 %collective-permute-start.24 = (bf16[12,64,128]{2,1,0:T(8,128)(2,1)S(1)}, bf16[12,64,128]{2,1,0:T(8,128)(2,1)S(1)}, u32[]{:S(2)}, u32[]{:S(2)}) collective-permute-start(bf16[12,64,128]{2,1,0:T(8,128)(2,1)S(1)} %get-tuple-element.28), channel_id=1, source_target_pairs={{0,8},{8,0},{16,24},{24,16},{1,9},{9,1},{17,25},{25,17},{2,10},{10... | collective-permute-start | bytes 589832 | tf_op jit(solution)/shard_map/ppermute | solution.py:125
  163.6 10.9 %collective-permute-start.21 = (bf16[12,64,128]{2,1,0:T(8,128)(2,1)S(1)}, bf16[12,64,128]{2,1,0:T(8,128)(2,1)S(1)}, u32[]{:S(2)}, u32[]{:S(2)}) collective-permute-start(bf16[12,64,128]{2,1,0:T(8,128)(2,1)S(1)} %get-tuple-element.29), channel_id=1, source_target_pairs={{0,2},{1,3},{2,0},{3,1},{4,6},{5,7},{6,4},{7,5},{8,10},{9,11},{10,... | collective-permute-start | bytes 589832 | tf_op jit(solution)/shard_map/ppermute | solution.py:125
  174.6 10.9 %collective-permute-start.22 = (bf16[24,64,128]{2,1,0:T(8,128)(2,1)S(1)}, bf16[24,64,128]{2,1,0:T(8,128)(2,1)S(1)}, u32[]{:S(2)}, u32[]{:S(2)}) collective-permute-start(bf16[24,64,128]{2,1,0:T(8,128)(2,1)S(1)} %get-tuple-element.27), channel_id=1, source_target_pairs={{0,1},{1,0},{2,3},{3,2},{4,5},{5,4},{6,7},{7,6},{8,9},{9,8},{10,11... | collective-permute-start | bytes 1179656 | tf_op jit(solution)/shard_map/ppermute | solution.py:125
  177.5 33.4 %collective-permute-start.40 = (f32[192,320]{1,0:T(8,128)S(1)}, f32[192,320]{1,0:T(8,128)S(1)}, u32[]{:S(2)}, u32[]{:S(2)}) collective-permute-start(f32[192,320]{1,0:T(8,128)S(1)} %pad_maximum_fusion.10), channel_id=1, source_target_pairs={{0,8},{8,0},{16,24},{24,16},{1,9},{9,1},{17,25},{25,17},{2,10},{10... | collective-permute-start | bytes 737288 | tf_op jit(solution)/shard_map/ppermute | solution.py:149
  210.8 10.0 %collective-permute-start.25 = (bf16[24,64,128]{2,1,0:T(8,128)(2,1)S(1)}, bf16[24,64,128]{2,1,0:T(8,128)(2,1)S(1)}, u32[]{:S(2)}, u32[]{:S(2)}) collective-permute-start(bf16[24,64,128]{2,1,0:T(8,128)(2,1)S(1)} %slice.206), channel_id=1, source_target_pairs={{0,1},{1,0},{2,3},{3,2},{4,5},{5,4},{6,7},{7,6},{8,9},{9,8},{10,11... | collective-permute-start | bytes 1179656 | tf_op jit(solution)/shard_map/ppermute | solution.py:139
  211.0 6.8 %collective-permute-start.41 = (f32[192,320]{1,0:T(8,128)S(1)}, f32[192,320]{1,0:T(8,128)S(1)}, u32[]{:S(2)}, u32[]{:S(2)}) collective-permute-start(f32[192,320]{1,0:T(8,128)S(1)} %fusion.38), channel_id=1, source_target_pairs={{0,16},{8,24},{16,0},{24,8},{1,17},{9,25},{17,1},{25,9},{2,18},{10... | collective-permute-start | bytes 737288 | tf_op jit(solution)/shard_map/ppermute | solution.py:149
  217.9 6.8 %collective-permute-start.42 = (f32[192,320]{1,0:T(8,128)S(1)}, f32[192,320]{1,0:T(8,128)S(1)}, u32[]{:S(2)}, u32[]{:S(2)}) collective-permute-start(f32[192,320]{1,0:T(8,128)S(1)} %add.177), channel_id=1, source_target_pairs={{0,1},{1,0},{2,3},{3,2},{4,5},{5,4},{6,7},{7,6},{8,9},{9,8},{10,11... | collective-permute-start | bytes 737288 | tf_op jit(solution)/shard_map/ppermute | solution.py:149
  220.0 7.1 %collective-permute-start.28 = (f32[12,64,128]{2,1,0:T(8,128)S(1)}, f32[12,64,128]{2,1,0:T(8,128)S(1)}, u32[]{:S(2)}, u32[]{:S(2)}) collective-permute-start(f32[12,64,128]{2,1,0:T(8,128)S(1)} %slice.129), channel_id=1, source_target_pairs={{0,8},{8,0},{16,24},{24,16},{1,9},{9,1},{17,25},{25,17},{2,10},{10... | collective-permute-start | bytes 1179656 | tf_op jit(solution)/shard_map/ppermute | solution.py:139
  221.0 12.1 %collective-permute-start.26 = (f32[12,64,128]{2,1,0:T(8,128)S(1)}, f32[12,64,128]{2,1,0:T(8,128)S(1)}, u32[]{:S(2)}, u32[]{:S(2)}) collective-permute-start(f32[12,64,128]{2,1,0:T(8,128)S(1)} %slice.154), channel_id=1, source_target_pairs={{0,2},{1,3},{2,0},{3,1},{4,6},{5,7},{6,4},{7,5},{8,10},{9,11},{10,... | collective-permute-start | bytes 1179656 | tf_op jit(solution)/shard_map/ppermute | solution.py:139
  224.7 15.7 %collective-permute-start.43 = (f32[192,320]{1,0:T(8,128)S(1)}, f32[192,320]{1,0:T(8,128)S(1)}, u32[]{:S(2)}, u32[]{:S(2)}) collective-permute-start(f32[192,320]{1,0:T(8,128)S(1)} %add.178), channel_id=1, source_target_pairs={{0,2},{1,3},{2,0},{3,1},{4,6},{5,7},{6,4},{7,5},{8,10},{9,11},{10,... | collective-permute-start | bytes 737288 | tf_op jit(solution)/shard_map/ppermute | solution.py:149
  227.1 13.4 %collective-permute-start.29 = (f32[6,64,128]{2,1,0:T(8,128)S(1)}, f32[6,64,128]{2,1,0:T(8,128)S(1)}, u32[]{:S(2)}, u32[]{:S(2)}) collective-permute-start(f32[6,64,128]{2,1,0:T(8,128)S(1)} %slice.158), channel_id=1, source_target_pairs={{0,16},{8,24},{16,0},{24,8},{1,17},{9,25},{17,1},{25,9},{2,18},{10... | collective-permute-start | bytes 589832 | tf_op jit(solution)/shard_map/ppermute | solution.py:139
  233.2 16.7 %collective-permute-start.27 = (f32[6,64,128]{2,1,0:T(8,128)S(1)}, f32[6,64,128]{2,1,0:T(8,128)S(1)}, u32[]{:S(2)}, u32[]{:S(2)}) collective-permute-start(f32[6,64,128]{2,1,0:T(8,128)S(1)} %slice.156), channel_id=1, source_target_pairs={{0,4},{1,5},{2,6},{3,7},{4,0},{5,1},{6,2},{7,3},{8,12},{9,13},{10,... | collective-permute-start | bytes 589832 | tf_op jit(solution)/shard_map/ppermute | solution.py:139
  240.4 22.3 %collective-permute-start.44 = (f32[192,320]{1,0:T(8,128)S(1)}, f32[192,320]{1,0:T(8,128)S(1)}, u32[]{:S(2)}, u32[]{:S(2)}) collective-permute-start(f32[192,320]{1,0:T(8,128)S(1)} %add.179), channel_id=1, source_target_pairs={{0,4},{1,5},{2,6},{3,7},{4,0},{5,1},{6,2},{7,3},{8,12},{9,13},{10,... | collective-permute-start | bytes 737288 | tf_op jit(solution)/shard_map/ppermute | solution.py:149
  249.9 18.8 %copy-start.3 = (f32[64,768]{1,0:T(8,128)}, f32[64,768]{1,0:T(8,128)S(1)}, u32[]{:S(2)}) copy-start(f32[64,768]{1,0:T(8,128)S(1)} %copy_bitcast_fusion) | copy-start | bytes 589828
  250.5 1.4 collective-permute-start.45
  251.9 4.9 %collective-permute-start.46 = (f32[192,64]{1,0:T(8,128)S(1)}, f32[192,64]{1,0:T(8,128)S(1)}, u32[]{:S(2)}, u32[]{:S(2)}) collective-permute-start(f32[192,64]{1,0:T(8,128)S(1)} %add.181), channel_id=1, source_target_pairs={{0,16},{8,24},{16,0},{24,8},{1,17},{9,25},{17,1},{25,9},{2,18},{10... | collective-permute-start | bytes 147464 | tf_op jit(solution)/shard_map/ppermute | solution.py:149
  256.8 5.8 %collective-permute-start.47 = (f32[192,64]{1,0:T(8,128)S(1)}, f32[192,64]{1,0:T(8,128)S(1)}, u32[]{:S(2)}, u32[]{:S(2)}) collective-permute-start(f32[192,64]{1,0:T(8,128)S(1)} %add.182), channel_id=1, source_target_pairs={{0,1},{1,0},{2,3},{3,2},{4,5},{5,4},{6,7},{7,6},{8,9},{9,8},{10,11... | collective-permute-start | bytes 147464 | tf_op jit(solution)/shard_map/ppermute | solution.py:149
  262.7 4.7 %collective-permute-start.48 = (f32[192,64]{1,0:T(8,128)S(1)}, f32[192,64]{1,0:T(8,128)S(1)}, u32[]{:S(2)}, u32[]{:S(2)}) collective-permute-start(f32[192,64]{1,0:T(8,128)S(1)} %add.183), channel_id=1, source_target_pairs={{0,2},{1,3},{2,0},{3,1},{4,6},{5,7},{6,4},{7,5},{8,10},{9,11},{10,... | collective-permute-start | bytes 147464 | tf_op jit(solution)/shard_map/ppermute | solution.py:149
  267.4 6.3 %collective-permute-start.49 = (f32[192,64]{1,0:T(8,128)S(1)}, f32[192,64]{1,0:T(8,128)S(1)}, u32[]{:S(2)}, u32[]{:S(2)}) collective-permute-start(f32[192,64]{1,0:T(8,128)S(1)} %add.184), channel_id=1, source_target_pairs={{0,4},{1,5},{2,6},{3,7},{4,0},{5,1},{6,2},{7,3},{8,12},{9,13},{10,... | collective-permute-start | bytes 147464 | tf_op jit(solution)/shard_map/ppermute | solution.py:149

commit v9 on v6

--- a/solution.py
+++ b/solution.py
@@ -8,7 +8,7 @@
 from jax.sharding import PartitionSpec as P
 
 GROUP = 64
-UNROLL = 32
+UNROLL = 64
 
 
 def tile_kernel(rows_ref, cols_ref, cnt_ref, vals_ref, rin_ref, cin_ref, *out_refs):

time: 256 us -> 251 us (0.980); the launches traced: 255 us -> 254 us
    ppermute x20, waiting for transfers between devices: 40 us -> 45.3 us  [all_sum(): value = value + lax.ppermute(value, axis, exchange_pairs(size, step))]
    ppermute x15, waiting for transfers between devices: 30.9 us -> 27.1 us  [scatter_sum(): lax.ppermute(sent, axis, exchange_pairs(size, step)).astype(held.dtype)]
where the time goes in v9:
time: 251 us; the launch traced here: 254 us
  waiting for transfers between devices  100 us (40%)
  starting transfers between devices  79.7 us (32%)
  Pallas kernels  45 us (18%)
  other arithmetic  21.3 us (8%)
  matrix products  3.81 us (2%)
    ppermute x20, waiting for transfers between devices, all_sum(): value = value + lax.ppermute(value, axis, exchange_pairs(size, step))  45.3 us
    pallas_call x2, Pallas kernels, tile_products(): pl.pallas_call(tile_kernel, grid_spec=grid_spec, out_shape=[jax.ShapeDtyp...  45 us
    ppermute x20, starting transfers between devices, all_sum(): value = value + lax.ppermute(value, axis, exchange_pairs(size, step))  35.5 us
    ppermute x15, waiting for transfers between devices, gather_blocks(): lax.ppermute(held, axis, exchange_pairs(size, step))  27.7 us
    ppermute x15, waiting for transfers between devices, scatter_sum(): lax.ppermute(sent, axis, exchange_pairs(size, step)).astype(held.dtype)  27.1 us
    ppermute x15, starting transfers between devices, scatter_sum(): lax.ppermute(sent, axis, exchange_pairs(size, step)).astype(held.dtype)  24.5 us
    ppermute x15, starting transfers between devices, gather_blocks(): lax.ppermute(held, axis, exchange_pairs(size, step))  19.7 us
    another operation x3, other arithmetic, per_device(): cholesky_factor = jnp.linalg.cholesky(gram_x)  6.52 us
  transfers between devices with their start and end apart: 50, of which 29 were waited for; matrix products, arithmetic and copies ran while one was open for 8% of the time, Pallas kernels for 9%

profile of v9, /device:TPU:0, one launch (start us, length us, event | category | flops | bytes accessed | tf_op | source)
XLA Modules:
  0.0 254.1 jit_solution(10847637401471933095)
XLA Ops:
  0.6 0.9 copy-done
  2.4 0.9 collective-permute-done
  3.3 2.9 %collective-permute-start.1 = (f32[64,64]{0,1:T(8,128)S(1)}, f32[64,64]{0,1:T(8,128)S(1)}, u32[]{:S(2)}, u32[]{:S(2)}) collective-permute-start(f32[64,64]{0,1:T(8,128)S(1)} %add.147), channel_id=1, source_target_pairs={{0,16},{8,24},{16,0},{24,8},{1,17},{9,25},{17,1},{25,9},{2,18},{10... | collective-permute-start | bytes 49160 | tf_op jit(solution)/shard_map/ppermute | solution.py:149
  6.1 1.9 collective-permute-done.1
  8.0 2.0 collective-permute-start.2
  10.0 0.9 bitcast_bitcast_fusion.1
  11.0 1.6 collective-permute-start.13
  12.6 2.6 %collective-permute-start.8 = (bf16[6,64,128]{2,1,0:T(8,128)(2,1)S(1)}, bf16[6,64,128]{2,1,0:T(8,128)(2,1)S(1)}, u32[]{:S(2)}, u32[]{:S(2)}) collective-permute-start(bf16[6,64,128]{2,1,0:T(8,128)(2,1)S(1)} %bitcast_bitcast_fusion.1), channel_id=1, source_target_pairs={{0,4},{1,5},{2,6},{3,7},{4,0},{5,1},{6,2},{7,3},{8,12},{9,13},{10,... | collective-permute-start | bytes 294920 | tf_op jit(solution)/shard_map/ppermute | solution.py:125
  15.2 1.6 collective-permute-start.3
  17.5 1.6 collective-permute-done.3
  19.1 0.9 collective-permute-start.4
  20.7 3.2 %collective-permute-done.4 = f32[64,64]{0,1:T(8,128)S(1)} collective-permute-done((f32[64,64]{0,1:T(8,128)S(1)}, f32[64,64]{0,1:T(8,128)S(1)}, u32[]{:S(2)}, u32[]{:S(2)}) %collective-permute-start.4) | collective-permute-done | bytes 16416 | tf_op jit(solution)/shard_map/ppermute | solution.py:149
  24.1 5.8 %cholesky.16 = f32[64,64]{1,0:T(8,128)S(1)} custom-call(f32[64,64]{1,0:T(8,128)S(1)} %fusion.17), custom_call_target="Cholesky" | custom-call | tf_op jit(solution)/shard_map/jit(cholesky)/cholesky | solution.py:198
  31.2 4.9 %custom-call.6 = f32[1,64,64]{1,2,0:T(8,128)S(1)} custom-call(f32[1,64,64]{2,1,0:T(8,128)S(1)} %fusion.14), custom_call_target="InvertDiagBlocksLowerTriangular" | custom-call | tf_op jit(solution)/shard_map/triangular_solve | solution.py:199
  37.1 0.9 collective-permute-start.5
  38.1 1.9 collective-permute-start.9
  39.9 1.3 collective-permute-done.11
  41.3 1.5 collective-permute-done.5
  42.8 2.6 %collective-permute-start.6 = (bf16[12,64,128]{2,1,0:T(8,128)(2,1)S(1)}, bf16[12,64,128]{2,1,0:T(8,128)(2,1)S(1)}, u32[]{:S(2)}, u32[]{:S(2)}) collective-permute-start(bf16[12,64,128]{2,1,0:T(8,128)(2,1)S(1)} %get-tuple-element.27), channel_id=1, source_target_pairs={{0,2},{1,3},{2,0},{3,1},{4,6},{5,7},{6,4},{7,5},{8,10},{9,11},{10,... | collective-permute-start | bytes 589832 | tf_op jit(solution)/shard_map/ppermute | solution.py:125
  45.5 0.8 collective-permute-start.10
  46.3 2.7 %collective-permute-done.6 = bf16[12,64,128]{2,1,0:T(8,128)(2,1)S(1)} collective-permute-done((bf16[12,64,128]{2,1,0:T(8,128)(2,1)S(1)}, bf16[12,64,128]{2,1,0:T(8,128)(2,1)S(1)}, u32[]{:S(2)}, u32[]{:S(2)}) %collective-permute-start.6) | collective-permute-done | bytes 196640 | tf_op jit(solution)/shard_map/ppermute | solution.py:125
  49.1 0.8 collective-permute-start.7
  51.2 0.9 collective-permute-done.14
  52.5 2.6 %collective-permute-done.10 = bf16[24,64,128]{2,1,0:T(8,128)(2,1)S(1)} collective-permute-done((bf16[24,64,128]{2,1,0:T(8,128)(2,1)S(1)}, bf16[24,64,128]{2,1,0:T(8,128)(2,1)S(1)}, u32[]{:S(2)}, u32[]{:S(2)}) %collective-permute-start.10) | collective-permute-done | bytes 393248 | tf_op jit(solution)/shard_map/ppermute | solution.py:125
  55.1 4.2 %collective-permute-done.7 = bf16[24,64,128]{2,1,0:T(8,128)(2,1)S(1)} collective-permute-done((bf16[24,64,128]{2,1,0:T(8,128)(2,1)S(1)}, bf16[24,64,128]{2,1,0:T(8,128)(2,1)S(1)}, u32[]{:S(2)}, u32[]{:S(2)}) %collective-permute-start.7) | collective-permute-done | bytes 393248 | tf_op jit(solution)/shard_map/ppermute | solution.py:125
  59.3 4.4 %maximum_maximum_fusion.rin_ref = bf16[48,128,128]{2,1,0:T(8,128)(2,1)} fusion(bf16[24,64,128]{2,1,0:T(8,128)(2,1)S(1)} %collective-permute-done.10, bf16[12,64,128]{2,1,0:T(8,128)(2,1)S(1)} %collective-permute-done.9, bf16[6,64,128]{2,1,0:T(8,128)(2,1)S(1)} %collective-permute-done.8, bf16[6,64,128]{2,1,0:T(8,128)(2,1)S(1)} %bitcast_bitcast_fusion.1, ...), kind=kLoop, calls=%fused_computation | loop fusion | flops 12582912 | bytes 3145728 | tf_op jit(solution)/shard_map/concatenate | solution.py:204
  63.7 23.3 %shard_map.93 = (f32[48,64,128]{2,1,0:T(8,128)S(1)}, f32[24,64,128]{2,1,0:T(8,128)S(1)}, f32[48,64,128]{2,1,0:T(8,128)S(1)}, f32[24,64,128]{2,1,0:T(8,128)S(1)}) custom-call(s32[576]{0:T(1024)S(1)} %get-tuple-element.30.rows_ref, s32[576]{0:T(1024)S(1)} %get-tuple-element.31.cols_ref, s32[1]{0:T(128)} %bitcast.61.cnt_ref, bf16[576,128,128]{2,1,0:T(8,128)(2,1)} %bitcast.63, ...), custom_call_target="tpu_custom_call" | custom-call | flops 4831838208 | bytes 25952256 | tf_op jit(solution)/shard_map/pallas_call | solution.py:94
  87.3 7.6 %collective-permute-done.15 = bf16[24,64,128]{2,1,0:T(8,128)(2,1)S(1)} collective-permute-done((bf16[24,64,128]{2,1,0:T(8,128)(2,1)S(1)}, bf16[24,64,128]{2,1,0:T(8,128)(2,1)S(1)}, u32[]{:S(2)}, u32[]{:S(2)}) %collective-permute-start.15) | collective-permute-done | bytes 393248 | tf_op jit(solution)/shard_map/ppermute | solution.py:139
  95.1 3.9 %collective-permute-start.16 = (f32[12,64,128]{2,1,0:T(8,128)S(1)}, f32[12,64,128]{2,1,0:T(8,128)S(1)}, u32[]{:S(2)}, u32[]{:S(2)}) collective-permute-start(f32[12,64,128]{2,1,0:T(8,128)S(1)} %slice.147), channel_id=1, source_target_pairs={{0,2},{1,3},{2,0},{3,1},{4,6},{5,7},{6,4},{7,5},{8,10},{9,11},{10,... | collective-permute-start | bytes 1179656 | tf_op jit(solution)/shard_map/ppermute | solution.py:139
  99.2 7.1 %collective-permute-done.16 = f32[12,64,128]{2,1,0:T(8,128)S(1)} collective-permute-done((f32[12,64,128]{2,1,0:T(8,128)S(1)}, f32[12,64,128]{2,1,0:T(8,128)S(1)}, u32[]{:S(2)}, u32[]{:S(2)}) %collective-permute-start.16) | collective-permute-done | bytes 393248 | tf_op jit(solution)/shard_map/ppermute | solution.py:139
  106.3 5.3 %collective-permute-start.17 = (f32[6,64,128]{2,1,0:T(8,128)S(1)}, f32[6,64,128]{2,1,0:T(8,128)S(1)}, u32[]{:S(2)}, u32[]{:S(2)}) collective-permute-start(f32[6,64,128]{2,1,0:T(8,128)S(1)} %slice.149), channel_id=1, source_target_pairs={{0,4},{1,5},{2,6},{3,7},{4,0},{5,1},{6,2},{7,3},{8,12},{9,13},{10,... | collective-permute-start | bytes 589832 | tf_op jit(solution)/shard_map/ppermute | solution.py:139
  111.8 1.5 collective-permute-start.35
  113.4 4.0 %collective-permute-done.17 = f32[6,64,128]{2,1,0:T(8,128)S(1)} collective-permute-done((f32[6,64,128]{2,1,0:T(8,128)S(1)}, f32[6,64,128]{2,1,0:T(8,128)S(1)}, u32[]{:S(2)}, u32[]{:S(2)}) %collective-permute-start.17) | collective-permute-done | bytes 196640 | tf_op jit(solution)/shard_map/ppermute | solution.py:139
  117.8 1.2 collective-permute-done.20
  119.0 3.9 %collective-permute-done.21 = f32[64,64]{0,1:T(8,128)S(1)} collective-permute-done((f32[64,64]{0,1:T(8,128)S(1)}, f32[64,64]{0,1:T(8,128)S(1)}, u32[]{:S(2)}, u32[]{:S(2)}) %collective-permute-start.21) | collective-permute-done | bytes 16416 | tf_op jit(solution)/shard_map/ppermute | solution.py:149
  123.0 1.5 collective-permute-start.22
  124.4 2.4 collective-permute-done.22
  126.9 1.0 collective-permute-start.23
  128.0 2.8 %collective-permute-done.23 = f32[64,64]{0,1:T(8,128)S(1)} collective-permute-done((f32[64,64]{0,1:T(8,128)S(1)}, f32[64,64]{0,1:T(8,128)S(1)}, u32[]{:S(2)}, u32[]{:S(2)}) %collective-permute-start.23) | collective-permute-done | bytes 16416 | tf_op jit(solution)/shard_map/ppermute | solution.py:149
  130.8 2.7 %collective-permute-start.24 = (f32[64,64]{0,1:T(8,128)S(1)}, f32[64,64]{0,1:T(8,128)S(1)}, u32[]{:S(2)}, u32[]{:S(2)}) collective-permute-start(f32[64,64]{0,1:T(8,128)S(1)} %add.162), channel_id=1, source_target_pairs={{0,4},{1,5},{2,6},{3,7},{4,0},{5,1},{6,2},{7,3},{8,12},{9,13},{10,... | collective-permute-start | bytes 49160 | tf_op jit(solution)/shard_map/ppermute | solution.py:149
  133.7 2.1 collective-permute-start.36
  136.2 3.0 %collective-permute-start.25 = (bf16[6,64,128]{2,1,0:T(8,128)(2,1)S(1)}, bf16[6,64,128]{2,1,0:T(8,128)(2,1)S(1)}, u32[]{:S(2)}, u32[]{:S(2)}) collective-permute-start(bf16[6,64,128]{2,1,0:T(8,128)(2,1)S(1)} %bitcast_bitcast_fusion), channel_id=1, source_target_pairs={{0,4},{1,5},{2,6},{3,7},{4,0},{5,1},{6,2},{7,3},{8,12},{9,13},{10,... | collective-permute-start | bytes 294920 | tf_op jit(solution)/shard_map/ppermute | solution.py:125
  139.2 4.7 %collective-permute-done.36 = f32[12,64,128]{2,1,0:T(8,128)S(1)} collective-permute-done((f32[12,64,128]{2,1,0:T(8,128)S(1)}, f32[12,64,128]{2,1,0:T(8,128)S(1)}, u32[]{:S(2)}, u32[]{:S(2)}) %collective-permute-start.36) | collective-permute-done | bytes 393248 | tf_op jit(solution)/shard_map/ppermute | solution.py:139
  144.0 1.5 collective-permute-start.37
  145.6 2.7 %collective-permute-start.26 = (bf16[12,64,128]{2,1,0:T(8,128)(2,1)S(1)}, bf16[12,64,128]{2,1,0:T(8,128)(2,1)S(1)}, u32[]{:S(2)}, u32[]{:S(2)}) collective-permute-start(bf16[12,64,128]{2,1,0:T(8,128)(2,1)S(1)} %get-tuple-element.25), channel_id=1, source_target_pairs={{0,2},{1,3},{2,0},{3,1},{4,6},{5,7},{6,4},{7,5},{8,10},{9,11},{10,... | collective-permute-start | bytes 589832 | tf_op jit(solution)/shard_map/ppermute | solution.py:125
  148.9 5.9 %collective-permute-done.26 = bf16[12,64,128]{2,1,0:T(8,128)(2,1)S(1)} collective-permute-done((bf16[12,64,128]{2,1,0:T(8,128)(2,1)S(1)}, bf16[12,64,128]{2,1,0:T(8,128)(2,1)S(1)}, u32[]{:S(2)}, u32[]{:S(2)}) %collective-permute-start.26) | collective-permute-done | bytes 196640 | tf_op jit(solution)/shard_map/ppermute | solution.py:125
  154.9 1.5 collective-permute-start.27
  157.9 8.1 %collective-permute-done.27 = bf16[24,64,128]{2,1,0:T(8,128)(2,1)S(1)} collective-permute-done((bf16[24,64,128]{2,1,0:T(8,128)(2,1)S(1)}, bf16[24,64,128]{2,1,0:T(8,128)(2,1)S(1)}, u32[]{:S(2)}, u32[]{:S(2)}) %collective-permute-start.27) | collective-permute-done | bytes 393248 | tf_op jit(solution)/shard_map/ppermute | solution.py:125
  166.1 21.7 %shard_map.94 = (f32[48,64,128]{2,1,0:T(8,128)S(1)}, f32[24,64,128]{2,1,0:T(8,128)S(1)}) custom-call(s32[576]{0:T(1024)S(1)} %get-tuple-element.30.rows_ref, s32[576]{0:T(1024)S(1)} %get-tuple-element.31.cols_ref, s32[1]{0:T(128)} %bitcast.62.cnt_ref, bf16[576,128,128]{2,1,0:T(8,128)(2,1)} %bitcast.64, bf16[48,64,128]{2,1,0:T(8,128)(2,1)S(1)} %pad_maximum_fusion.rin_ref, ...), custom_call_target="tpu_custom_call" | custom-call | flops 2415919104 | bytes 22413312 | tf_op jit(solution)/shard_map/pallas_call | solution.py:94
  188.2 8.9 %collective-permute-done.41 = f32[192,320]{1,0:T(8,128)S(1)} collective-permute-done((f32[192,320]{1,0:T(8,128)S(1)}, f32[192,320]{1,0:T(8,128)S(1)}, u32[]{:S(2)}, u32[]{:S(2)}) %collective-permute-start.41) | collective-permute-done | bytes 245792 | tf_op jit(solution)/shard_map/ppermute | solution.py:149
  197.8 2.1 collective-permute-start.31
  199.9 5.4 %collective-permute-done.42 = f32[192,320]{1,0:T(8,128)S(1)} collective-permute-done((f32[192,320]{1,0:T(8,128)S(1)}, f32[192,320]{1,0:T(8,128)S(1)}, u32[]{:S(2)}, u32[]{:S(2)}) %collective-permute-start.42) | collective-permute-done | bytes 245792 | tf_op jit(solution)/shard_map/ppermute | solution.py:149
  206.1 3.7 %collective-permute-done.31 = f32[12,64,128]{2,1,0:T(8,128)S(1)} collective-permute-done((f32[12,64,128]{2,1,0:T(8,128)S(1)}, f32[12,64,128]{2,1,0:T(8,128)S(1)}, u32[]{:S(2)}, u32[]{:S(2)}) %collective-permute-start.31) | collective-permute-done | bytes 393248 | tf_op jit(solution)/shard_map/ppermute | solution.py:139
  209.9 6.9 %collective-permute-start.32 = (f32[6,64,128]{2,1,0:T(8,128)S(1)}, f32[6,64,128]{2,1,0:T(8,128)S(1)}, u32[]{:S(2)}, u32[]{:S(2)}) collective-permute-start(f32[6,64,128]{2,1,0:T(8,128)S(1)} %slice.156), channel_id=1, source_target_pairs={{0,4},{1,5},{2,6},{3,7},{4,0},{5,1},{6,2},{7,3},{8,12},{9,13},{10,... | collective-permute-start | bytes 589832 | tf_op jit(solution)/shard_map/ppermute | solution.py:139
  216.8 6.2 %collective-permute-start.44 = (f32[192,320]{1,0:T(8,128)S(1)}, f32[192,320]{1,0:T(8,128)S(1)}, u32[]{:S(2)}, u32[]{:S(2)}) collective-permute-start(f32[192,320]{1,0:T(8,128)S(1)} %add.179), channel_id=1, source_target_pairs={{0,4},{1,5},{2,6},{3,7},{4,0},{5,1},{6,2},{7,3},{8,12},{9,13},{10,... | collective-permute-start | bytes 737288 | tf_op jit(solution)/shard_map/ppermute | solution.py:149
  223.8 1.3 collective-permute-done.45
  225.2 4.8 %collective-permute-done.46 = f32[192,64]{1,0:T(8,128)S(1)} collective-permute-done((f32[192,64]{1,0:T(8,128)S(1)}, f32[192,64]{1,0:T(8,128)S(1)}, u32[]{:S(2)}, u32[]{:S(2)}) %collective-permute-start.46) | collective-permute-done | bytes 49184 | tf_op jit(solution)/shard_map/ppermute | solution.py:149
  230.0 2.1 collective-permute-start.47
  232.1 2.6 %collective-permute-done.47 = f32[192,64]{1,0:T(8,128)S(1)} collective-permute-done((f32[192,64]{1,0:T(8,128)S(1)}, f32[192,64]{1,0:T(8,128)S(1)}, u32[]{:S(2)}, u32[]{:S(2)}) %collective-permute-start.47) | collective-permute-done | bytes 49184 | tf_op jit(solution)/shard_map/ppermute | solution.py:149
  234.7 9.9 %collective-permute-start.48 = (f32[192,64]{1,0:T(8,128)S(1)}, f32[192,64]{1,0:T(8,128)S(1)}, u32[]{:S(2)}, u32[]{:S(2)}) collective-permute-start(f32[192,64]{1,0:T(8,128)S(1)} %add.183), channel_id=1, source_target_pairs={{0,2},{1,3},{2,0},{3,1},{4,6},{5,7},{6,4},{7,5},{8,10},{9,11},{10,... | collective-permute-start | bytes 147464 | tf_op jit(solution)/shard_map/ppermute | solution.py:149
  244.7 2.6 %collective-permute-done.48 = f32[192,64]{1,0:T(8,128)S(1)} collective-permute-done((f32[192,64]{1,0:T(8,128)S(1)}, f32[192,64]{1,0:T(8,128)S(1)}, u32[]{:S(2)}, u32[]{:S(2)}) %collective-permute-start.48) | collective-permute-done | bytes 49184 | tf_op jit(solution)/shard_map/ppermute | solution.py:149
  247.2 3.4 %collective-permute-start.49 = (f32[192,64]{1,0:T(8,128)S(1)}, f32[192,64]{1,0:T(8,128)S(1)}, u32[]{:S(2)}, u32[]{:S(2)}) collective-permute-start(f32[192,64]{1,0:T(8,128)S(1)} %add.184), channel_id=1, source_target_pairs={{0,4},{1,5},{2,6},{3,7},{4,0},{5,1},{6,2},{7,3},{8,12},{9,13},{10,... | collective-permute-start | bytes 147464 | tf_op jit(solution)/shard_map/ppermute | solution.py:149
  251.5 1.8 collective-permute-done.49
  253.3 0.8 pad_maximum_fusion.13
  (131 shorter events, 13.7 us)
Async XLA Ops:
  0.6 0.9 copy-start
  1.9 43.5 %copy-start.4 = (s32[1,1,576]{2,1,0:T(1,128)S(1)}, s32[1,1,576]{2,1,0:T(1,128)}, u32[]{:S(2)}) copy-start(s32[1,1,576]{2,1,0:T(1,128)} %param.8) | copy-start | bytes 6916
  1.9 1.4 collective-permute-start
  3.3 4.8 %collective-permute-start.1 = (f32[64,64]{0,1:T(8,128)S(1)}, f32[64,64]{0,1:T(8,128)S(1)}, u32[]{:S(2)}, u32[]{:S(2)}) collective-permute-start(f32[64,64]{0,1:T(8,128)S(1)} %add.147), channel_id=1, source_target_pairs={{0,16},{8,24},{16,0},{24,8},{1,17},{9,25},{17,1},{25,9},{2,18},{10... | collective-permute-start | bytes 49160 | tf_op jit(solution)/shard_map/ppermute | solution.py:149
  8.0 7.1 %collective-permute-start.2 = (f32[64,64]{0,1:T(8,128)S(1)}, f32[64,64]{0,1:T(8,128)S(1)}, u32[]{:S(2)}, u32[]{:S(2)}) collective-permute-start(f32[64,64]{0,1:T(8,128)S(1)} %add.148), channel_id=1, source_target_pairs={{0,1},{1,0},{2,3},{3,2},{4,5},{5,4},{6,7},{7,6},{8,9},{9,8},{10,11... | collective-permute-start | bytes 49160 | tf_op jit(solution)/shard_map/ppermute | solution.py:149
  11.0 27.1 %collective-permute-start.13 = (bf16[6,64,128]{2,1,0:T(8,128)(2,1)S(1)}, bf16[6,64,128]{2,1,0:T(8,128)(2,1)S(1)}, u32[]{:S(2)}, u32[]{:S(2)}) collective-permute-start(bf16[6,64,128]{2,1,0:T(8,128)(2,1)S(1)} %bitcast_bitcast_fusion.1), channel_id=1, source_target_pairs={{0,16},{8,24},{16,0},{24,8},{1,17},{9,25},{17,1},{25,9},{2,18},{10... | collective-permute-start | bytes 294920 | tf_op jit(solution)/shard_map/ppermute | solution.py:125
  12.6 25.5 %collective-permute-start.8 = (bf16[6,64,128]{2,1,0:T(8,128)(2,1)S(1)}, bf16[6,64,128]{2,1,0:T(8,128)(2,1)S(1)}, u32[]{:S(2)}, u32[]{:S(2)}) collective-permute-start(bf16[6,64,128]{2,1,0:T(8,128)(2,1)S(1)} %bitcast_bitcast_fusion.1), channel_id=1, source_target_pairs={{0,4},{1,5},{2,6},{3,7},{4,0},{5,1},{6,2},{7,3},{8,12},{9,13},{10,... | collective-permute-start | bytes 294920 | tf_op jit(solution)/shard_map/ppermute | solution.py:125
  15.2 4.0 %collective-permute-start.3 = (f32[64,64]{0,1:T(8,128)S(1)}, f32[64,64]{0,1:T(8,128)S(1)}, u32[]{:S(2)}, u32[]{:S(2)}) collective-permute-start(f32[64,64]{0,1:T(8,128)S(1)} %add.149), channel_id=1, source_target_pairs={{0,2},{1,3},{2,0},{3,1},{4,6},{5,7},{6,4},{7,5},{8,10},{9,11},{10,... | collective-permute-start | bytes 49160 | tf_op jit(solution)/shard_map/ppermute | solution.py:149
  19.1 4.8 %collective-permute-start.4 = (f32[64,64]{0,1:T(8,128)S(1)}, f32[64,64]{0,1:T(8,128)S(1)}, u32[]{:S(2)}, u32[]{:S(2)}) collective-permute-start(f32[64,64]{0,1:T(8,128)S(1)} %add.150), channel_id=1, source_target_pairs={{0,4},{1,5},{2,6},{3,7},{4,0},{5,1},{6,2},{7,3},{8,12},{9,13},{10,... | collective-permute-start | bytes 49160 | tf_op jit(solution)/shard_map/ppermute | solution.py:149
  36.5 13.4 %copy-start.5 = (s32[1,1,576]{2,1,0:T(1,128)S(1)}, s32[1,1,576]{2,1,0:T(1,128)}, u32[]{:S(2)}) copy-start(s32[1,1,576]{2,1,0:T(1,128)} %param.9) | copy-start | bytes 6916
  36.6 4.7 %collective-permute-start.11 = (bf16[6,64,128]{2,1,0:T(8,128)(2,1)S(1)}, bf16[6,64,128]{2,1,0:T(8,128)(2,1)S(1)}, u32[]{:S(2)}, u32[]{:S(2)}) collective-permute-start(bf16[6,64,128]{2,1,0:T(8,128)(2,1)S(1)} %bitcast_bitcast_fusion.2), channel_id=1, source_target_pairs={{0,16},{8,24},{16,0},{24,8},{1,17},{9,25},{17,1},{25,9},{2,18},{10... | collective-permute-start | bytes 294920 | tf_op jit(solution)/shard_map/ppermute | solution.py:125
  37.1 5.6 %collective-permute-start.5 = (bf16[6,64,128]{2,1,0:T(8,128)(2,1)S(1)}, bf16[6,64,128]{2,1,0:T(8,128)(2,1)S(1)}, u32[]{:S(2)}, u32[]{:S(2)}) collective-permute-start(bf16[6,64,128]{2,1,0:T(8,128)(2,1)S(1)} %bitcast_bitcast_fusion.2), channel_id=1, source_target_pairs={{0,4},{1,5},{2,6},{3,7},{4,0},{5,1},{6,2},{7,3},{8,12},{9,13},{10,... | collective-permute-start | bytes 294920 | tf_op jit(solution)/shard_map/ppermute | solution.py:125
  38.1 7.4 %collective-permute-start.9 = (bf16[12,64,128]{2,1,0:T(8,128)(2,1)S(1)}, bf16[12,64,128]{2,1,0:T(8,128)(2,1)S(1)}, u32[]{:S(2)}, u32[]{:S(2)}) collective-permute-start(bf16[12,64,128]{2,1,0:T(8,128)(2,1)S(1)} %get-tuple-element.29), channel_id=1, source_target_pairs={{0,2},{1,3},{2,0},{3,1},{4,6},{5,7},{6,4},{7,5},{8,10},{9,11},{10,... | collective-permute-start | bytes 589832 | tf_op jit(solution)/shard_map/ppermute | solution.py:125
  42.8 6.2 %collective-permute-start.6 = (bf16[12,64,128]{2,1,0:T(8,128)(2,1)S(1)}, bf16[12,64,128]{2,1,0:T(8,128)(2,1)S(1)}, u32[]{:S(2)}, u32[]{:S(2)}) collective-permute-start(bf16[12,64,128]{2,1,0:T(8,128)(2,1)S(1)} %get-tuple-element.27), channel_id=1, source_target_pairs={{0,2},{1,3},{2,0},{3,1},{4,6},{5,7},{6,4},{7,5},{8,10},{9,11},{10,... | collective-permute-start | bytes 589832 | tf_op jit(solution)/shard_map/ppermute | solution.py:125
  45.5 9.6 %collective-permute-start.10 = (bf16[24,64,128]{2,1,0:T(8,128)(2,1)S(1)}, bf16[24,64,128]{2,1,0:T(8,128)(2,1)S(1)}, u32[]{:S(2)}, u32[]{:S(2)}) collective-permute-start(bf16[24,64,128]{2,1,0:T(8,128)(2,1)S(1)} %pad_maximum_fusion.5), channel_id=1, source_target_pairs={{0,1},{1,0},{2,3},{3,2},{4,5},{5,4},{6,7},{7,6},{8,9},{9,8},{10,11... | collective-permute-start | bytes 1179656 | tf_op jit(solution)/shard_map/ppermute | solution.py:125
  49.1 10.2 %collective-permute-start.7 = (bf16[24,64,128]{2,1,0:T(8,128)(2,1)S(1)}, bf16[24,64,128]{2,1,0:T(8,128)(2,1)S(1)}, u32[]{:S(2)}, u32[]{:S(2)}) collective-permute-start(bf16[24,64,128]{2,1,0:T(8,128)(2,1)S(1)} %pad_maximum_fusion.4), channel_id=1, source_target_pairs={{0,1},{1,0},{2,3},{3,2},{4,5},{5,4},{6,7},{7,6},{8,9},{9,8},{10,11... | collective-permute-start | bytes 1179656 | tf_op jit(solution)/shard_map/ppermute | solution.py:125
  50.6 1.5 collective-permute-start.14
  50.7 1.7 collective-permute-start.12
  87.1 7.8 %collective-permute-start.15 = (bf16[24,64,128]{2,1,0:T(8,128)(2,1)S(1)}, bf16[24,64,128]{2,1,0:T(8,128)(2,1)S(1)}, u32[]{:S(2)}, u32[]{:S(2)}) collective-permute-start(bf16[24,64,128]{2,1,0:T(8,128)(2,1)S(1)} %slice.207), channel_id=1, source_target_pairs={{0,1},{1,0},{2,3},{3,2},{4,5},{5,4},{6,7},{7,6},{8,9},{9,8},{10,11... | collective-permute-start | bytes 1179656 | tf_op jit(solution)/shard_map/ppermute | solution.py:139
  87.2 11.8 %collective-permute-start.18 = (f32[12,64,128]{2,1,0:T(8,128)S(1)}, f32[12,64,128]{2,1,0:T(8,128)S(1)}, u32[]{:S(2)}, u32[]{:S(2)}) collective-permute-start(f32[12,64,128]{2,1,0:T(8,128)S(1)} %slice.119), channel_id=1, source_target_pairs={{0,8},{8,0},{16,24},{24,16},{1,9},{9,1},{17,25},{25,17},{2,10},{10... | collective-permute-start | bytes 1179656 | tf_op jit(solution)/shard_map/ppermute | solution.py:139
  95.1 11.2 %collective-permute-start.16 = (f32[12,64,128]{2,1,0:T(8,128)S(1)}, f32[12,64,128]{2,1,0:T(8,128)S(1)}, u32[]{:S(2)}, u32[]{:S(2)}) collective-permute-start(f32[12,64,128]{2,1,0:T(8,128)S(1)} %slice.147), channel_id=1, source_target_pairs={{0,2},{1,3},{2,0},{3,1},{4,6},{5,7},{6,4},{7,5},{8,10},{9,11},{10,... | collective-permute-start | bytes 1179656 | tf_op jit(solution)/shard_map/ppermute | solution.py:139
  99.1 14.3 %collective-permute-start.19 = (f32[6,64,128]{2,1,0:T(8,128)S(1)}, f32[6,64,128]{2,1,0:T(8,128)S(1)}, u32[]{:S(2)}, u32[]{:S(2)}) collective-permute-start(f32[6,64,128]{2,1,0:T(8,128)S(1)} %slice.151), channel_id=1, source_target_pairs={{0,16},{8,24},{16,0},{24,8},{1,17},{9,25},{17,1},{25,9},{2,18},{10... | collective-permute-start | bytes 589832 | tf_op jit(solution)/shard_map/ppermute | solution.py:139
  106.3 11.1 %collective-permute-start.17 = (f32[6,64,128]{2,1,0:T(8,128)S(1)}, f32[6,64,128]{2,1,0:T(8,128)S(1)}, u32[]{:S(2)}, u32[]{:S(2)}) collective-permute-start(f32[6,64,128]{2,1,0:T(8,128)S(1)} %slice.149), channel_id=1, source_target_pairs={{0,4},{1,5},{2,6},{3,7},{4,0},{5,1},{6,2},{7,3},{8,12},{9,13},{10,... | collective-permute-start | bytes 589832 | tf_op jit(solution)/shard_map/ppermute | solution.py:139
  111.7 16.1 %collective-permute-start.38 = (f32[12,64,128]{2,1,0:T(8,128)S(1)}, f32[12,64,128]{2,1,0:T(8,128)S(1)}, u32[]{:S(2)}, u32[]{:S(2)}) collective-permute-start(f32[12,64,128]{2,1,0:T(8,128)S(1)} %slice.139), channel_id=1, source_target_pairs={{0,8},{8,0},{16,24},{24,16},{1,9},{9,1},{17,25},{25,17},{2,10},{10... | collective-permute-start | bytes 1179656 | tf_op jit(solution)/shard_map/ppermute | solution.py:139
  111.8 21.7 %collective-permute-start.35 = (bf16[24,64,128]{2,1,0:T(8,128)(2,1)S(1)}, bf16[24,64,128]{2,1,0:T(8,128)(2,1)S(1)}, u32[]{:S(2)}, u32[]{:S(2)}) collective-permute-start(bf16[24,64,128]{2,1,0:T(8,128)(2,1)S(1)} %slice.205), channel_id=1, source_target_pairs={{0,1},{1,0},{2,3},{3,2},{4,5},{5,4},{6,7},{7,6},{8,9},{9,8},{10,11... | collective-permute-start | bytes 1179656 | tf_op jit(solution)/shard_map/ppermute | solution.py:139
  117.8 1.3 collective-permute-start.20
  119.0 3.9 %collective-permute-start.21 = (f32[64,64]{0,1:T(8,128)S(1)}, f32[64,64]{0,1:T(8,128)S(1)}, u32[]{:S(2)}, u32[]{:S(2)}) collective-permute-start(f32[64,64]{0,1:T(8,128)S(1)} %add.159), channel_id=1, source_target_pairs={{0,16},{8,24},{16,0},{24,8},{1,17},{9,25},{17,1},{25,9},{2,18},{10... | collective-permute-start | bytes 49160 | tf_op jit(solution)/shard_map/ppermute | solution.py:149
  123.0 3.9 %collective-permute-start.22 = (f32[64,64]{0,1:T(8,128)S(1)}, f32[64,64]{0,1:T(8,128)S(1)}, u32[]{:S(2)}, u32[]{:S(2)}) collective-permute-start(f32[64,64]{0,1:T(8,128)S(1)} %add.160), channel_id=1, source_target_pairs={{0,1},{1,0},{2,3},{3,2},{4,5},{5,4},{6,7},{7,6},{8,9},{9,8},{10,11... | collective-permute-start | bytes 49160 | tf_op jit(solution)/shard_map/ppermute | solution.py:149
  126.9 3.9 %collective-permute-start.23 = (f32[64,64]{0,1:T(8,128)S(1)}, f32[64,64]{0,1:T(8,128)S(1)}, u32[]{:S(2)}, u32[]{:S(2)}) collective-permute-start(f32[64,64]{0,1:T(8,128)S(1)} %add.161), channel_id=1, source_target_pairs={{0,2},{1,3},{2,0},{3,1},{4,6},{5,7},{6,4},{7,5},{8,10},{9,11},{10,... | collective-permute-start | bytes 49160 | tf_op jit(solution)/shard_map/ppermute | solution.py:149
  128.0 29.1 %collective-permute-start.39 = (f32[6,64,128]{2,1,0:T(8,128)S(1)}, f32[6,64,128]{2,1,0:T(8,128)S(1)}, u32[]{:S(2)}, u32[]{:S(2)}) collective-permute-start(f32[6,64,128]{2,1,0:T(8,128)S(1)} %slice.165), channel_id=1, source_target_pairs={{0,16},{8,24},{16,0},{24,8},{1,17},{9,25},{17,1},{25,9},{2,18},{10... | collective-permute-start | bytes 589832 | tf_op jit(solution)/shard_map/ppermute | solution.py:139
  130.8 5.0 %collective-permute-start.24 = (f32[64,64]{0,1:T(8,128)S(1)}, f32[64,64]{0,1:T(8,128)S(1)}, u32[]{:S(2)}, u32[]{:S(2)}) collective-permute-start(f32[64,64]{0,1:T(8,128)S(1)} %add.162), channel_id=1, source_target_pairs={{0,4},{1,5},{2,6},{3,7},{4,0},{5,1},{6,2},{7,3},{8,12},{9,13},{10,... | collective-permute-start | bytes 49160 | tf_op jit(solution)/shard_map/ppermute | solution.py:149
  133.7 14.6 %copy-start.2 = (f32[64,768]{1,0:T(8,128)S(1)}, f32[64,768]{1,0:T(8,128)}, u32[]{:S(2)}) copy-start(f32[64,768]{1,0:T(8,128)} %param.7) | copy-start | bytes 589828
  133.7 10.2 %collective-permute-start.36 = (f32[12,64,128]{2,1,0:T(8,128)S(1)}, f32[12,64,128]{2,1,0:T(8,128)S(1)}, u32[]{:S(2)}, u32[]{:S(2)}) collective-permute-start(f32[12,64,128]{2,1,0:T(8,128)S(1)} %slice.161), channel_id=1, source_target_pairs={{0,2},{1,3},{2,0},{3,1},{4,6},{5,7},{6,4},{7,5},{8,10},{9,11},{10,... | collective-permute-start | bytes 1179656 | tf_op jit(solution)/shard_map/ppermute | solution.py:139
  136.1 87.0 %copy-start.1 = (f32[64,768]{1,0:T(8,128)}, f32[64,768]{1,0:T(8,128)S(1)}, u32[]{:S(2)}) copy-start(f32[64,768]{1,0:T(8,128)S(1)} %convolution_subtract_fusion) | copy-start | bytes 589828
  136.1 9.3 %collective-permute-start.28 = (bf16[6,64,128]{2,1,0:T(8,128)(2,1)S(1)}, bf16[6,64,128]{2,1,0:T(8,128)(2,1)S(1)}, u32[]{:S(2)}, u32[]{:S(2)}) collective-permute-start(bf16[6,64,128]{2,1,0:T(8,128)(2,1)S(1)} %bitcast_bitcast_fusion), channel_id=1, source_target_pairs={{0,16},{8,24},{16,0},{24,8},{1,17},{9,25},{17,1},{25,9},{2,18},{10... | collective-permute-start | bytes 294920 | tf_op jit(solution)/shard_map/ppermute | solution.py:125
  136.2 9.2 %collective-permute-start.25 = (bf16[6,64,128]{2,1,0:T(8,128)(2,1)S(1)}, bf16[6,64,128]{2,1,0:T(8,128)(2,1)S(1)}, u32[]{:S(2)}, u32[]{:S(2)}) collective-permute-start(bf16[6,64,128]{2,1,0:T(8,128)(2,1)S(1)} %bitcast_bitcast_fusion), channel_id=1, source_target_pairs={{0,4},{1,5},{2,6},{3,7},{4,0},{5,1},{6,2},{7,3},{8,12},{9,13},{10,... | collective-permute-start | bytes 294920 | tf_op jit(solution)/shard_map/ppermute | solution.py:125
  144.0 13.1 %collective-permute-start.37 = (f32[6,64,128]{2,1,0:T(8,128)S(1)}, f32[6,64,128]{2,1,0:T(8,128)S(1)}, u32[]{:S(2)}, u32[]{:S(2)}) collective-permute-start(f32[6,64,128]{2,1,0:T(8,128)S(1)} %slice.163), channel_id=1, source_target_pairs={{0,4},{1,5},{2,6},{3,7},{4,0},{5,1},{6,2},{7,3},{8,12},{9,13},{10,... | collective-permute-start | bytes 589832 | tf_op jit(solution)/shard_map/ppermute | solution.py:139
  145.5 3.4 %collective-permute-start.29 = (bf16[12,64,128]{2,1,0:T(8,128)(2,1)S(1)}, bf16[12,64,128]{2,1,0:T(8,128)(2,1)S(1)}, u32[]{:S(2)}, u32[]{:S(2)}) collective-permute-start(bf16[12,64,128]{2,1,0:T(8,128)(2,1)S(1)} %get-tuple-element.24), channel_id=1, source_target_pairs={{0,8},{8,0},{16,24},{24,16},{1,9},{9,1},{17,25},{25,17},{2,10},{10... | collective-permute-start | bytes 589832 | tf_op jit(solution)/shard_map/ppermute | solution.py:125
  145.6 9.2 %collective-permute-start.26 = (bf16[12,64,128]{2,1,0:T(8,128)(2,1)S(1)}, bf16[12,64,128]{2,1,0:T(8,128)(2,1)S(1)}, u32[]{:S(2)}, u32[]{:S(2)}) collective-permute-start(bf16[12,64,128]{2,1,0:T(8,128)(2,1)S(1)} %get-tuple-element.25), channel_id=1, source_target_pairs={{0,2},{1,3},{2,0},{3,1},{4,6},{5,7},{6,4},{7,5},{8,10},{9,11},{10,... | collective-permute-start | bytes 589832 | tf_op jit(solution)/shard_map/ppermute | solution.py:125
  154.9 11.2 %collective-permute-start.27 = (bf16[24,64,128]{2,1,0:T(8,128)(2,1)S(1)}, bf16[24,64,128]{2,1,0:T(8,128)(2,1)S(1)}, u32[]{:S(2)}, u32[]{:S(2)}) collective-permute-start(bf16[24,64,128]{2,1,0:T(8,128)(2,1)S(1)} %get-tuple-element.23), channel_id=1, source_target_pairs={{0,1},{1,0},{2,3},{3,2},{4,5},{5,4},{6,7},{7,6},{8,9},{9,8},{10,11... | collective-permute-start | bytes 1179656 | tf_op jit(solution)/shard_map/ppermute | solution.py:125
  157.9 30.2 %collective-permute-start.40 = (f32[192,320]{1,0:T(8,128)S(1)}, f32[192,320]{1,0:T(8,128)S(1)}, u32[]{:S(2)}, u32[]{:S(2)}) collective-permute-start(f32[192,320]{1,0:T(8,128)S(1)} %pad_maximum_fusion.6), channel_id=1, source_target_pairs={{0,8},{8,0},{16,24},{24,16},{1,9},{9,1},{17,25},{25,17},{2,10},{10... | collective-permute-start | bytes 737288 | tf_op jit(solution)/shard_map/ppermute | solution.py:149
  187.9 9.7 %collective-permute-start.30 = (bf16[24,64,128]{2,1,0:T(8,128)(2,1)S(1)}, bf16[24,64,128]{2,1,0:T(8,128)(2,1)S(1)}, u32[]{:S(2)}, u32[]{:S(2)}) collective-permute-start(bf16[24,64,128]{2,1,0:T(8,128)(2,1)S(1)} %slice.206), channel_id=1, source_target_pairs={{0,1},{1,0},{2,3},{3,2},{4,5},{5,4},{6,7},{7,6},{8,9},{9,8},{10,11... | collective-permute-start | bytes 1179656 | tf_op jit(solution)/shard_map/ppermute | solution.py:139
  188.1 9.0 %collective-permute-start.41 = (f32[192,320]{1,0:T(8,128)S(1)}, f32[192,320]{1,0:T(8,128)S(1)}, u32[]{:S(2)}, u32[]{:S(2)}) collective-permute-start(f32[192,320]{1,0:T(8,128)S(1)} %fusion.34), channel_id=1, source_target_pairs={{0,16},{8,24},{16,0},{24,8},{1,17},{9,25},{17,1},{25,9},{2,18},{10... | collective-permute-start | bytes 737288 | tf_op jit(solution)/shard_map/ppermute | solution.py:149
  197.2 8.1 %collective-permute-start.42 = (f32[192,320]{1,0:T(8,128)S(1)}, f32[192,320]{1,0:T(8,128)S(1)}, u32[]{:S(2)}, u32[]{:S(2)}) collective-permute-start(f32[192,320]{1,0:T(8,128)S(1)} %add.177), channel_id=1, source_target_pairs={{0,1},{1,0},{2,3},{3,2},{4,5},{5,4},{6,7},{7,6},{8,9},{9,8},{10,11... | collective-permute-start | bytes 737288 | tf_op jit(solution)/shard_map/ppermute | solution.py:149
  197.5 7.8 %collective-permute-start.33 = (f32[12,64,128]{2,1,0:T(8,128)S(1)}, f32[12,64,128]{2,1,0:T(8,128)S(1)}, u32[]{:S(2)}, u32[]{:S(2)}) collective-permute-start(f32[12,64,128]{2,1,0:T(8,128)S(1)} %slice.129), channel_id=1, source_target_pairs={{0,8},{8,0},{16,24},{24,16},{1,9},{9,1},{17,25},{25,17},{2,10},{10... | collective-permute-start | bytes 1179656 | tf_op jit(solution)/shard_map/ppermute | solution.py:139
  197.8 12.0 %collective-permute-start.31 = (f32[12,64,128]{2,1,0:T(8,128)S(1)}, f32[12,64,128]{2,1,0:T(8,128)S(1)}, u32[]{:S(2)}, u32[]{:S(2)}) collective-permute-start(f32[12,64,128]{2,1,0:T(8,128)S(1)} %slice.154), channel_id=1, source_target_pairs={{0,2},{1,3},{2,0},{3,1},{4,6},{5,7},{6,4},{7,5},{8,10},{9,11},{10,... | collective-permute-start | bytes 1179656 | tf_op jit(solution)/shard_map/ppermute | solution.py:139
  205.3 11.4 %collective-permute-start.43 = (f32[192,320]{1,0:T(8,128)S(1)}, f32[192,320]{1,0:T(8,128)S(1)}, u32[]{:S(2)}, u32[]{:S(2)}) collective-permute-start(f32[192,320]{1,0:T(8,128)S(1)} %add.178), channel_id=1, source_target_pairs={{0,2},{1,3},{2,0},{3,1},{4,6},{5,7},{6,4},{7,5},{8,10},{9,11},{10,... | collective-permute-start | bytes 737288 | tf_op jit(solution)/shard_map/ppermute | solution.py:149
  205.5 17.5 %collective-permute-start.34 = (f32[6,64,128]{2,1,0:T(8,128)S(1)}, f32[6,64,128]{2,1,0:T(8,128)S(1)}, u32[]{:S(2)}, u32[]{:S(2)}) collective-permute-start(f32[6,64,128]{2,1,0:T(8,128)S(1)} %slice.158), channel_id=1, source_target_pairs={{0,16},{8,24},{16,0},{24,8},{1,17},{9,25},{17,1},{25,9},{2,18},{10... | collective-permute-start | bytes 589832 | tf_op jit(solution)/shard_map/ppermute | solution.py:139
  209.9 13.1 %collective-permute-start.32 = (f32[6,64,128]{2,1,0:T(8,128)S(1)}, f32[6,64,128]{2,1,0:T(8,128)S(1)}, u32[]{:S(2)}, u32[]{:S(2)}) collective-permute-start(f32[6,64,128]{2,1,0:T(8,128)S(1)} %slice.156), channel_id=1, source_target_pairs={{0,4},{1,5},{2,6},{3,7},{4,0},{5,1},{6,2},{7,3},{8,12},{9,13},{10,... | collective-permute-start | bytes 589832 | tf_op jit(solution)/shard_map/ppermute | solution.py:139
  216.8 27.9 %collective-permute-start.44 = (f32[192,320]{1,0:T(8,128)S(1)}, f32[192,320]{1,0:T(8,128)S(1)}, u32[]{:S(2)}, u32[]{:S(2)}) collective-permute-start(f32[192,320]{1,0:T(8,128)S(1)} %add.179), channel_id=1, source_target_pairs={{0,4},{1,5},{2,6},{3,7},{4,0},{5,1},{6,2},{7,3},{8,12},{9,13},{10,... | collective-permute-start | bytes 737288 | tf_op jit(solution)/shard_map/ppermute | solution.py:149
  223.1 27.7 %copy-start.3 = (f32[64,768]{1,0:T(8,128)}, f32[64,768]{1,0:T(8,128)S(1)}, u32[]{:S(2)}) copy-start(f32[64,768]{1,0:T(8,128)S(1)} %copy_bitcast_fusion) | copy-start | bytes 589828
  223.7 1.4 collective-permute-start.45
  225.1 4.9 %collective-permute-start.46 = (f32[192,64]{1,0:T(8,128)S(1)}, f32[192,64]{1,0:T(8,128)S(1)}, u32[]{:S(2)}, u32[]{:S(2)}) collective-permute-start(f32[192,64]{1,0:T(8,128)S(1)} %add.181), channel_id=1, source_target_pairs={{0,16},{8,24},{16,0},{24,8},{1,17},{9,25},{17,1},{25,9},{2,18},{10... | collective-permute-start | bytes 147464 | tf_op jit(solution)/shard_map/ppermute | solution.py:149
  230.0 4.7 %collective-permute-start.47 = (f32[192,64]{1,0:T(8,128)S(1)}, f32[192,64]{1,0:T(8,128)S(1)}, u32[]{:S(2)}, u32[]{:S(2)}) collective-permute-start(f32[192,64]{1,0:T(8,128)S(1)} %add.182), channel_id=1, source_target_pairs={{0,1},{1,0},{2,3},{3,2},{4,5},{5,4},{6,7},{7,6},{8,9},{9,8},{10,11... | collective-permute-start | bytes 147464 | tf_op jit(solution)/shard_map/ppermute | solution.py:149
  234.7 12.5 %collective-permute-start.48 = (f32[192,64]{1,0:T(8,128)S(1)}, f32[192,64]{1,0:T(8,128)S(1)}, u32[]{:S(2)}, u32[]{:S(2)}) collective-permute-start(f32[192,64]{1,0:T(8,128)S(1)} %add.183), channel_id=1, source_target_pairs={{0,2},{1,3},{2,0},{3,1},{4,6},{5,7},{6,4},{7,5},{8,10},{9,11},{10,... | collective-permute-start | bytes 147464 | tf_op jit(solution)/shard_map/ppermute | solution.py:149
  247.2 6.0 %collective-permute-start.49 = (f32[192,64]{1,0:T(8,128)S(1)}, f32[192,64]{1,0:T(8,128)S(1)}, u32[]{:S(2)}, u32[]{:S(2)}) collective-permute-start(f32[192,64]{1,0:T(8,128)S(1)} %add.184), channel_id=1, source_target_pairs={{0,4},{1,5},{2,6},{3,7},{4,0},{5,1},{6,2},{7,3},{8,12},{9,13},{10,... | collective-permute-start | bytes 147464 | tf_op jit(solution)/shard_map/ppermute | solution.py:149
